TPU v7x, 256 devices: a whole 4x4x8 slice. The times are simulated.
256 devices in a mesh: gx: 32 (over x, y, core), gy: 8 (over z).
Axes of the slice: x: 4, y: 4, z: 8, core: 2. Of those that a mesh axis runs over, the one named last changes fastest.
Arguments:
- orbitals: float32 [64, 128, 64, 128], P(None, 'gx', 'gy'), may hold values from -60 to 60, as said below
- potential: float32 [128, 64, 128], P('gx', 'gy'), may hold values from 0.2 to 2
Outputs:
- basis: float32 [64, 128, 64, 128], P(None, 'gx', 'gy')
- factor: float32 [64, 64], replicated
Inputs may be any that keep to these rules, and one draw needn't show every extreme that they name: `orbitals`: Real-valued entries.
All inputs are finite; a program needn't handle non-finite values.
Results may differ from a plain program's by a relative error of at most 0.00011.
Values sent between devices are 32-bit elements; how exact they have to be, the bound alone decides.
No kernel may reach another device: no remote copies, remote signals or barrier semaphores. Data moves between devices by JAX's collectives and lax.ppermute only.
A program may use at most 64 MiB of HBM per device.

v0:
```python
import jax
import jax.numpy as jnp
from jax import lax
from jax.sharding import PartitionSpec as P


def extended(cells, sides, width):
    for axis, dim in sides:
        count = lax.axis_size(axis)
        head = lax.slice_in_dim(cells, 0, width, axis=dim)
        tail = lax.slice_in_dim(cells, cells.shape[dim] - width, cells.shape[dim], axis=dim)
        cells = jnp.concatenate(
            [
                lax.ppermute(tail, axis, [(i, (i + 1) % count) for i in range(count)]),
                cells,
                lax.ppermute(head, axis, [((i + 1) % count, i) for i in range(count)]),
            ],
            axis=dim,
        )
    return cells


def apply_ham(padded, pot):
    core = padded[:, 2:-2, 2:-2]
    total = -7.5 * core
    total = total + 4.0 / 3.0 * (padded[:, 3:-1, 2:-2] + padded[:, 1:-3, 2:-2])
    total = total - 1.0 / 12.0 * (padded[:, 4:, 2:-2] + padded[:, :-4, 2:-2])
    total = total + 4.0 / 3.0 * (padded[:, 2:-2, 3:-1] + padded[:, 2:-2, 1:-3])
    total = total - 1.0 / 12.0 * (padded[:, 2:-2, 4:] + padded[:, 2:-2, :-4])
    total = total + 4.0 / 3.0 * (jnp.roll(core, 1, 3) + jnp.roll(core, -1, 3))
    total = total - 1.0 / 12.0 * (jnp.roll(core, 2, 3) + jnp.roll(core, -2, 3))
    return -0.5 * total + pot[None] * core


def with_faces(field):
    return extended(field, (("gx", 1), ("gy", 2)), 2)


def upper_factor(gram):
    order = gram.shape[0]
    index = jnp.arange(order)

    def column_step(col, lower):
        row_now = lax.dynamic_slice_in_dim(lower, col, 1, 0)[0]
        target = lax.dynamic_slice_in_dim(gram, col, 1, 1)[:, 0]
        column = target - jnp.dot(
            lower, row_now, precision=lax.Precision.HIGHEST, preferred_element_type=jnp.float32
        )
        pivot = jnp.sqrt(jnp.sum(jnp.where(index == col, column, 0.0)))
        values = jnp.where(index == col, pivot, column / pivot)
        values = jnp.where(index >= col, values, 0.0)
        return jnp.where(index[None, :] == col, values[:, None], lower)

    lower = lax.fori_loop(0, order, column_step, jnp.zeros_like(gram))
    return lower.T


def upper_inverse(upper):
    order = upper.shape[0]
    index = jnp.arange(order)

    def row_step(step, inverse):
        row = order - 1 - step
        upper_row = lax.dynamic_slice_in_dim(upper, row, 1, 0)[0]
        pivot = jnp.sum(jnp.where(index == row, upper_row, 0.0))
        rest = jnp.dot(
            upper_row, inverse, precision=lax.Precision.HIGHEST, preferred_element_type=jnp.float32
        )
        unit = jnp.where(index == row, 1.0, 0.0).astype(jnp.float32)
        new_row = (unit - rest) / pivot
        return jnp.where(index[:, None] == row, new_row[None, :], inverse)

    return lax.fori_loop(0, order, row_step, jnp.zeros_like(upper))


def shards(orbitals, potential):
    first = (apply_ham(with_faces(orbitals), potential) - 5.5 * orbitals) / 4.5
    applied = apply_ham(with_faces(first), potential)
    filtered = 2.0 * (applied - 5.5 * first) / 4.5 - orbitals
    width = filtered.shape[0]
    flat = filtered.reshape(width, -1)
    cells = flat.shape[1] * lax.axis_size("gx") * lax.axis_size("gy")
    local_gram = (
        jnp.dot(flat, flat.T, precision=lax.Precision.HIGHEST, preferred_element_type=jnp.float32)
        / cells
    )
    factor = upper_factor(lax.psum(local_gram, ("gx", "gy")))
    inverse = upper_inverse(factor)
    solved = jnp.dot(
        inverse.T, flat, precision=lax.Precision.HIGHEST, preferred_element_type=jnp.float32
    )
    basis = (solved * jnp.sqrt(jnp.float32(cells))).reshape(filtered.shape)
    return (basis, factor)


def solution(mesh):
    return jax.shard_map(
        shards,
        mesh=mesh,
        in_specs=(P(None, "gx", "gy", None), P("gx", "gy", None)),
        out_specs=(P(None, "gx", "gy", None), P()),
        check_vma=False,
    )
```

profile of v0, /device:TPU:32, one launch (start us, length us, event | category | flops | bytes accessed | tf_op | source)
XLA Modules:
  0.0 353.0 jit_solution(158170441676691293)
XLA Ops:
  0.6 2.4 fusion.60
  3.0 4.6 %collective-permute-start = (f32[64,2,8,128]{3,2,1,0:T(8,128)}, f32[64,2,8,128]{3,2,1,0:T(8,128)S(1)}, u32[]{:S(2)}, u32[]{:S(2)}) collective-permute-start(f32[64,2,8,128]{3,2,1,0:T(8,128)} %get-tuple-element.279), channel_id=1, source_target_pairs={{8,0},{16,8},{24,16},{32,24},{40,32},{48,40},{56,48},{64,56},{72,6... | collective-permute-start | bytes 1572872 | tf_op jit(solution)/shard_map/ppermute | solution.py:16
  9.7 5.0 %collective-permute-done = f32[64,2,8,128]{3,2,1,0:T(8,128)S(1)} collective-permute-done((f32[64,2,8,128]{3,2,1,0:T(8,128)}, f32[64,2,8,128]{3,2,1,0:T(8,128)S(1)}, u32[]{:S(2)}, u32[]{:S(2)}) %collective-permute-start) | collective-permute-done | bytes 524320 | tf_op jit(solution)/shard_map/ppermute | solution.py:16
  14.9 4.8 %collective-permute-done.1 = f32[64,2,8,128]{3,2,1,0:T(8,128)S(1)} collective-permute-done((f32[64,2,8,128]{3,2,1,0:T(8,128)}, f32[64,2,8,128]{3,2,1,0:T(8,128)S(1)}, u32[]{:S(2)}, u32[]{:S(2)}) %collective-permute-start.1) | collective-permute-done | bytes 524320 | tf_op jit(solution)/shard_map/ppermute | solution.py:14
  20.6 1.9 collective-permute-start.3
  23.8 5.9 %collective-permute-done.2 = f32[64,8,2,128]{3,1,2,0:T(8,128)S(1)} collective-permute-done((f32[64,8,2,128]{3,1,2,0:T(8,128)S(1)}, f32[64,8,2,128]{3,1,2,0:T(8,128)S(1)}, u32[]{:S(2)}, u32[]{:S(2)}) %collective-permute-start.2) | collective-permute-done | bytes 524320 | tf_op jit(solution)/shard_map/ppermute | solution.py:16
  29.7 3.9 %collective-permute-done.3 = f32[64,8,2,128]{3,1,2,0:T(8,128)S(1)} collective-permute-done((f32[64,8,2,128]{3,1,2,0:T(8,128)S(1)}, f32[64,8,2,128]{3,1,2,0:T(8,128)S(1)}, u32[]{:S(2)}, u32[]{:S(2)}) %collective-permute-start.3) | collective-permute-done | bytes 524320 | tf_op jit(solution)/shard_map/ppermute | solution.py:14
  33.6 7.3 %broadcast_multiply_fusion = (f32[64,4,8,128]{3,1,2,0:T(4,128)S(1)}, f32[64,4,8,128]{3,1,2,0:T(4,128)S(1)}) fusion(f32[64,4,8,128]{3,1,2,0:T(4,128)S(1)} %copy.55, f32[4,8,128]{2,0,1:T(4,128)S(1)} %copy.71, f32[64,4,8,2]{3,1,2,0:T(4,128)S(1)} %get-tuple-element.285, f32[64,4,8,126]{3,1,2,0:T(4,128)S(1)} %get-tuple-element.287, ...), kind=kLoop, calls=%fused_computation.105 | loop fusion | flops 11796480 | bytes 9453568 | tf_op jit(solution)/shard_map/div | solution.py:77
  41.4 2.5 collective-permute-start.4
  45.6 5.1 %collective-permute-done.4 = f32[64,2,8,128]{3,2,1,0:T(8,128)S(1)} collective-permute-done((f32[64,2,8,128]{3,2,1,0:T(8,128)S(1)}, f32[64,2,8,128]{3,2,1,0:T(8,128)S(1)}, u32[]{:S(2)}, u32[]{:S(2)}) %collective-permute-start.4) | collective-permute-done | bytes 524320 | tf_op jit(solution)/shard_map/ppermute | solution.py:16
  50.9 5.2 %collective-permute-done.5 = f32[64,2,8,128]{3,2,1,0:T(8,128)S(1)} collective-permute-done((f32[64,2,8,128]{3,2,1,0:T(8,128)S(1)}, f32[64,2,8,128]{3,2,1,0:T(8,128)S(1)}, u32[]{:S(2)}, u32[]{:S(2)}) %collective-permute-start.5) | collective-permute-done | bytes 524320 | tf_op jit(solution)/shard_map/ppermute | solution.py:14
  56.8 3.3 collective-permute-start.6
  61.4 5.4 %collective-permute-done.6 = f32[64,8,2,128]{3,1,2,0:T(8,128)S(1)} collective-permute-done((f32[64,8,2,128]{3,1,2,0:T(8,128)S(1)}, f32[64,8,2,128]{3,1,2,0:T(8,128)S(1)}, u32[]{:S(2)}, u32[]{:S(2)}) %collective-permute-start.6) | collective-permute-done | bytes 524320 | tf_op jit(solution)/shard_map/ppermute | solution.py:16
  66.8 2.5 collective-permute-done.7
  69.3 7.5 %multiply_subtract_fusion = f32[64,4,8,128]{3,1,2,0:T(4,128)S(1)} fusion(f32[64,4,8,128]{3,1,2,0:T(4,128)S(1)} %get-tuple-element.261, f32[64,4,8,2]{3,1,2,0:T(4,128)S(1)} %get-tuple-element.275, f32[64,4,8,126]{3,1,2,0:T(4,128)S(1)} %get-tuple-element.277, f32[64,4,8,126]{3,1,2,0:T(4,128)S(1)} %get-tuple-element.276, ...), kind=kLoop, calls=%fused_computation.97 | loop fusion | flops 12058624 | bytes 10502144 | tf_op jit(solution)/shard_map/sub | solution.py:79
  76.8 2.1 fusion.17
  78.9 74.7 %psum.7 = f32[64,64]{1,0:T(8,128)S(1)} all-reduce(f32[64,64]{1,0:T(8,128)S(1)} %fusion.17), channel_id=1, replica_groups=mesh['gx'=32,'gy'=8] {'gx','gy'}, use_global_device_ids=true, to_apply=%region_0.1 | all-reduce | flops 4096 | bytes 32768 | tf_op jit(solution)/shard_map/psum | solution.py:87
  153.8 101.3 %while.32 = (s32[]{:T(128)}, f32[64,64]{1,0:T(8,128)S(1)}, f32[64,64]{0,1:T(8,128)S(1)}, s32[]{:T(128)}, s32[]{:T(128)}) while((s32[]{:T(128)}, f32[64,64]{1,0:T(8,128)S(1)}, f32[64,64]{0,1:T(8,128)S(1)}, s32[]{:T(128)}, s32[]{:T(128)}) %tuple.94), condition=%wide.region_3.4_spmd.clone.clone, body=%wide.region_1.3_spmd.clone.clone.sunk | while | flops 62082 | bytes 102112 | solution.py:54
  255.1 95.1 %while.31 = (s32[]{:T(128)}, f32[64,64]{1,0:T(8,128)S(1)}, f32[64,64]{1,0:T(8,128)S(1)}, s32[]{:T(128)}, s32[]{:T(128)}, /*index=5*/s32[]{:T(128)}, s32[]{:T(128)}) while((s32[]{:T(128)}, f32[64,64]{1,0:T(8,128)S(1)}, f32[64,64]{1,0:T(8,128)S(1)}, s32[]{:T(128)}, s32[]{:T(128)}, /*index=5*/s32[]{:T(128)}, s32[]{:T(128)}) %tuple.100), condition=%wide.region_6.7_spmd.clone, body=%wide.region_4.6_spmd.clone.sunk | while | flops 61958 | bytes 67106 | solution.py:73
  257.2 0.8 fusion.75
  258.7 0.8 fusion.75
  260.2 0.8 fusion.75
  350.2 1.6 fusion.16
  351.8 1.2 copy.89
  (609 shorter events, 156.7 us)
Async XLA Ops:
  0.6 7.0 %copy-start = (f32[64,4,8,128]{3,2,1,0:T(8,128)S(1)}, f32[64,4,8,128]{3,2,1,0:T(8,128)}, u32[]{:S(2)}) copy-start(f32[64,4,8,128]{3,2,1,0:T(8,128)} %param.6) | copy-start | bytes 3145732
  3.0 11.7 %collective-permute-start = (f32[64,2,8,128]{3,2,1,0:T(8,128)}, f32[64,2,8,128]{3,2,1,0:T(8,128)S(1)}, u32[]{:S(2)}, u32[]{:S(2)}) collective-permute-start(f32[64,2,8,128]{3,2,1,0:T(8,128)} %get-tuple-element.279), channel_id=1, source_target_pairs={{8,0},{16,8},{24,16},{32,24},{40,32},{48,40},{56,48},{64,56},{72,6... | collective-permute-start | bytes 1572872 | tf_op jit(solution)/shard_map/ppermute | solution.py:16
  7.6 0.7 copy-start.1
  7.6 12.1 %collective-permute-start.1 = (f32[64,2,8,128]{3,2,1,0:T(8,128)}, f32[64,2,8,128]{3,2,1,0:T(8,128)S(1)}, u32[]{:S(2)}, u32[]{:S(2)}) collective-permute-start(f32[64,2,8,128]{3,2,1,0:T(8,128)} %get-tuple-element.278), channel_id=1, source_target_pairs={{0,8},{8,16},{16,24},{24,32},{32,40},{40,48},{48,56},{56,64},{64,7... | collective-permute-start | bytes 1572872 | tf_op jit(solution)/shard_map/ppermute | solution.py:14
  20.4 9.3 %collective-permute-start.2 = (f32[64,8,2,128]{3,1,2,0:T(8,128)S(1)}, f32[64,8,2,128]{3,1,2,0:T(8,128)S(1)}, u32[]{:S(2)}, u32[]{:S(2)}) collective-permute-start(f32[64,8,2,128]{3,1,2,0:T(8,128)S(1)} %get-tuple-element.266), channel_id=1, source_target_pairs={{1,0},{2,1},{3,2},{4,3},{5,4},{6,5},{7,6},{0,7},{9,8},{10,9},{11,1... | collective-permute-start | bytes 1572872 | tf_op jit(solution)/shard_map/ppermute | solution.py:16
  20.6 13.0 %collective-permute-start.3 = (f32[64,8,2,128]{3,1,2,0:T(8,128)S(1)}, f32[64,8,2,128]{3,1,2,0:T(8,128)S(1)}, u32[]{:S(2)}, u32[]{:S(2)}) collective-permute-start(f32[64,8,2,128]{3,1,2,0:T(8,128)S(1)} %get-tuple-element.267), channel_id=1, source_target_pairs={{0,1},{1,2},{2,3},{3,4},{4,5},{5,6},{6,7},{7,0},{8,9},{9,10},{10,1... | collective-permute-start | bytes 1572872 | tf_op jit(solution)/shard_map/ppermute | solution.py:14
  41.4 9.2 %collective-permute-start.4 = (f32[64,2,8,128]{3,2,1,0:T(8,128)S(1)}, f32[64,2,8,128]{3,2,1,0:T(8,128)S(1)}, u32[]{:S(2)}, u32[]{:S(2)}) collective-permute-start(f32[64,2,8,128]{3,2,1,0:T(8,128)S(1)} %copy.74), channel_id=1, source_target_pairs={{8,0},{16,8},{24,16},{32,24},{40,32},{48,40},{56,48},{64,56},{72,6... | collective-permute-start | bytes 1572872 | tf_op jit(solution)/shard_map/ppermute | solution.py:16
  44.0 12.2 %collective-permute-start.5 = (f32[64,2,8,128]{3,2,1,0:T(8,128)S(1)}, f32[64,2,8,128]{3,2,1,0:T(8,128)S(1)}, u32[]{:S(2)}, u32[]{:S(2)}) collective-permute-start(f32[64,2,8,128]{3,2,1,0:T(8,128)S(1)} %copy.76), channel_id=1, source_target_pairs={{0,8},{8,16},{16,24},{24,32},{32,40},{40,48},{48,56},{56,64},{64,7... | collective-permute-start | bytes 1572872 | tf_op jit(solution)/shard_map/ppermute | solution.py:14
  56.8 10.0 %collective-permute-start.6 = (f32[64,8,2,128]{3,1,2,0:T(8,128)S(1)}, f32[64,8,2,128]{3,1,2,0:T(8,128)S(1)}, u32[]{:S(2)}, u32[]{:S(2)}) collective-permute-start(f32[64,8,2,128]{3,1,2,0:T(8,128)S(1)} %get-tuple-element.264), channel_id=1, source_target_pairs={{1,0},{2,1},{3,2},{4,3},{5,4},{6,5},{7,6},{0,7},{9,8},{10,9},{11,1... | collective-permute-start | bytes 1572872 | tf_op jit(solution)/shard_map/ppermute | solution.py:16
  60.1 9.2 %collective-permute-start.7 = (f32[64,8,2,128]{3,1,2,0:T(8,128)S(1)}, f32[64,8,2,128]{3,1,2,0:T(8,128)S(1)}, u32[]{:S(2)}, u32[]{:S(2)}) collective-permute-start(f32[64,8,2,128]{3,1,2,0:T(8,128)S(1)} %get-tuple-element.265), channel_id=1, source_target_pairs={{0,1},{1,2},{2,3},{3,4},{4,5},{5,6},{6,7},{7,0},{8,9},{9,10},{10,1... | collective-permute-start | bytes 1572872 | tf_op jit(solution)/shard_map/ppermute | solution.py:14
  350.2 1.6 copy-start.2
where the time goes:
time: 355 us; the launch traced here: 353 us
  matrix products  103 us (29%)
  blocking collectives  74.7 us (21%)
  other arithmetic  66.1 us (19%)
  loops' own time  46 us (13%)
  waiting for transfers between devices  37.9 us (11%)
  starting transfers between devices  12.9 us (4%)
  local copies, waits for them, and re-layouts  11.1 us (3%)
    psum x1, blocking collectives, shards(): factor = upper_factor(lax.psum(local_gram, ('gx', 'gy')))  74.7 us
    dot_general x64, matrix products, row_step(): jnp.dot(upper_row, inverse, precision=lax.Precision.HIGHEST, preferred_el...  50.1 us
    dot_general x64, matrix products, column_step(): jnp.dot(lower, row_now, precision=lax.Precision.HIGHEST, preferred_elemen...  49.5 us
    another operation x1, loops' own time, upper_factor(): lower = lax.fori_loop(0, order, column_step, jnp.zeros_like(gram))  45.6 us
    reduce_sum x64, other arithmetic, row_step(): pivot = jnp.sum(jnp.where(index == row, upper_row, 0.0))  39.3 us
    ppermute x4, waiting for transfers between devices, extended(): lax.ppermute(head, axis, [((i + 1) % count, i) for i in range(count)])  21.4 us
    ppermute x4, waiting for transfers between devices, extended(): lax.ppermute(tail, axis, [(i, (i + 1) % count) for i in range(count)])  16.5 us
    ppermute x4, starting transfers between devices, extended(): lax.ppermute(head, axis, [((i + 1) % count, i) for i in range(count)])  10.7 us
  transfers between devices with their start and end apart: 8, of which 8 were waited for; matrix products, arithmetic and copies ran while one was open for 2% of the time, Pallas kernels for 0%

commit v1 on v0

v1 whole, which is shorter than its diff:
```python
import jax
import jax.numpy as jnp
from jax import lax
from jax.experimental import pallas as pl
from jax.experimental.pallas import tpu as pltpu
from jax.sharding import PartitionSpec as P


def extended(cells, sides, width):
    for axis, dim in sides:
        count = lax.axis_size(axis)
        head = lax.slice_in_dim(cells, 0, width, axis=dim)
        tail = lax.slice_in_dim(cells, cells.shape[dim] - width, cells.shape[dim], axis=dim)
        cells = jnp.concatenate(
            [
                lax.ppermute(tail, axis, [(i, (i + 1) % count) for i in range(count)]),
                cells,
                lax.ppermute(head, axis, [((i + 1) % count, i) for i in range(count)]),
            ],
            axis=dim,
        )
    return cells


def apply_ham(padded, pot):
    core = padded[:, 2:-2, 2:-2]
    total = -7.5 * core
    total = total + 4.0 / 3.0 * (padded[:, 3:-1, 2:-2] + padded[:, 1:-3, 2:-2])
    total = total - 1.0 / 12.0 * (padded[:, 4:, 2:-2] + padded[:, :-4, 2:-2])
    total = total + 4.0 / 3.0 * (padded[:, 2:-2, 3:-1] + padded[:, 2:-2, 1:-3])
    total = total - 1.0 / 12.0 * (padded[:, 2:-2, 4:] + padded[:, 2:-2, :-4])
    total = total + 4.0 / 3.0 * (jnp.roll(core, 1, 3) + jnp.roll(core, -1, 3))
    total = total - 1.0 / 12.0 * (jnp.roll(core, 2, 3) + jnp.roll(core, -2, 3))
    return -0.5 * total + pot[None] * core


def with_faces(field):
    return extended(field, (("gx", 1), ("gy", 2)), 2)


def factor_kernel(aug_ref, out_ref):
    order = aug_ref.shape[0]
    groups = order // 8
    blocks = [aug_ref[pl.ds(8 * i, 8), :] for i in range(groups)]
    sub = lax.broadcasted_iota(jnp.int32, blocks[0].shape, 0)
    lane = lax.broadcasted_iota(jnp.int32, blocks[0].shape, 1)
    for k in range(order):
        home, place = divmod(k, 8)
        row = jnp.sum(jnp.where(sub == place, blocks[home], 0.0), axis=0, keepdims=True)
        pivot = jnp.sum(jnp.where(lane[:1] == k, row, 0.0), axis=1, keepdims=True)
        scale = 1.0 / jnp.sqrt(pivot)
        scaled = row * scale
        for j in range(home, groups):
            block = blocks[j]
            column = jnp.sum(jnp.where(lane == k, block, 0.0), axis=1, keepdims=True) * scale
            if j == home:
                column = jnp.where(sub[:, :1] > place, column, 0.0)
                block = jnp.where(sub == place, scaled, block - column * scaled)
            else:
                block = block - column * scaled
            blocks[j] = block
    for i in range(groups):
        keep = (lane >= order) | (lane >= sub + 8 * i)
        out_ref[pl.ds(8 * i, 8), :] = jnp.where(keep, blocks[i], 0.0)


def factor_and_inverse(gram):
    order = gram.shape[0]
    sym = 0.5 * (gram + gram.T)
    aug = jnp.concatenate([sym, jnp.eye(order, dtype=jnp.float32)], axis=1)
    out = pl.pallas_call(
        factor_kernel,
        out_shape=jax.ShapeDtypeStruct(aug.shape, jnp.float32),
        in_specs=[pl.BlockSpec(memory_space=pltpu.VMEM)],
        out_specs=pl.BlockSpec(memory_space=pltpu.VMEM),
    )(aug)
    return out[:, :order], out[:, order:]


def shards(orbitals, potential):
    first = (apply_ham(with_faces(orbitals), potential) - 5.5 * orbitals) / 4.5
    applied = apply_ham(with_faces(first), potential)
    filtered = 2.0 * (applied - 5.5 * first) / 4.5 - orbitals
    width = filtered.shape[0]
    flat = filtered.reshape(width, -1)
    cells = flat.shape[1] * lax.axis_size("gx") * lax.axis_size("gy")
    local_gram = (
        jnp.dot(flat, flat.T, precision=lax.Precision.HIGHEST, preferred_element_type=jnp.float32)
        / cells
    )
    factor, lower_inverse = factor_and_inverse(lax.psum(local_gram, ("gx", "gy")))
    solved = jnp.dot(
        lower_inverse, flat, precision=lax.Precision.HIGHEST, preferred_element_type=jnp.float32
    )
    basis = (solved * jnp.sqrt(jnp.float32(cells))).reshape(filtered.shape)
    return (basis, factor)


def solution(mesh):
    return jax.shard_map(
        shards,
        mesh=mesh,
        in_specs=(P(None, "gx", "gy", None), P("gx", "gy", None)),
        out_specs=(P(None, "gx", "gy", None), P()),
        check_vma=False,
    )
```

time: 355 us -> 166 us (0.47)
  matrix products: 103 us -> 4.4 us
  other arithmetic: 66.1 us -> 16.2 us
  loops' own time: 46 us -> 0 us
  Pallas kernels: 0 us -> 8.65 us
    dot_general x129 -> x1, matrix products: 101 us -> 2.35 us  [shards(): jnp.dot(lower_inverse, flat, precision=lax.Precision.HIGHEST, preferred_e...]
    another operation x2 -> x0, loops' own time: 46.1 us -> none  [the longest x1 45.6 us: upper_factor(): lower = lax.fori_loop(0, order, column_step, jnp.zeros_like(gram))]
    reduce_sum x64 -> x0, other arithmetic: 39.3 us -> none  [row_step(): pivot = jnp.sum(jnp.where(index == row, upper_row, 0.0))]
    select_n x192 -> x0, other arithmetic: 10.1 us -> none  [the longest x64 4.88 us: row_step(): return jnp.where(index[:, None] == row, new_row[None, :], inverse)]
    pallas_call x0 -> x1, Pallas kernels: none -> 8.65 us  [factor_and_inverse(): pl.pallas_call(factor_kernel, out_shape=jax.ShapeDtypeStruct(aug.shape, j...]
  transfers between devices with their start and end apart: 8 -> 8, of which waited for: 8 -> 8; matrix products, arithmetic and copies ran while one was open for 2% -> 4% of each run, Pallas kernels for 0% -> 0%
where the time goes in v1:
time: 166 us; the launch traced here: 165 us
  blocking collectives  74.5 us (45%)
  waiting for transfers between devices  37.6 us (23%)
  other arithmetic  16.2 us (10%)
  starting transfers between devices  13 us (8%)
  local copies, waits for them, and re-layouts  10.1 us (6%)
  Pallas kernels  8.65 us (5%)
  matrix products  4.4 us (3%)
    psum x1, blocking collectives, shards(): lax.psum(local_gram, ('gx', 'gy'))  74.5 us
    ppermute x4, waiting for transfers between devices, extended(): lax.ppermute(head, axis, [((i + 1) % count, i) for i in range(count)])  21 us
    ppermute x4, waiting for transfers between devices, extended(): lax.ppermute(tail, axis, [(i, (i + 1) % count) for i in range(count)])  16.6 us
    ppermute x4, starting transfers between devices, extended(): lax.ppermute(head, axis, [((i + 1) % count, i) for i in range(count)])  10.8 us
    pallas_call x1, Pallas kernels, factor_and_inverse(): pl.pallas_call(factor_kernel, out_shape=jax.ShapeDtypeStruct(aug.shape, j...  8.65 us
    sub x1, other arithmetic, shards(): filtered = 2.0 * (applied - 5.5 * first) / 4.5 - orbitals  7.45 us
    div x1, other arithmetic, shards(): first = (apply_ham(with_faces(orbitals), potential) - 5.5 * orbitals) / 4.5  7.38 us
  transfers between devices with their start and end apart: 8, of which 8 were waited for; matrix products, arithmetic and copies ran while one was open for 4% of the time, Pallas kernels for 0%

profile of v1, /device:TPU:32, one launch (start us, length us, event | category | flops | bytes accessed | tf_op | source)
XLA Modules:
  0.0 165.2 jit_solution(15629306752864410489)
XLA Ops:
  0.6 1.4 fusion.47
  2.0 4.7 %collective-permute-start = (f32[64,2,8,128]{3,2,1,0:T(8,128)S(1)}, f32[64,2,8,128]{3,2,1,0:T(8,128)S(1)}, u32[]{:S(2)}, u32[]{:S(2)}) collective-permute-start(f32[64,2,8,128]{3,2,1,0:T(8,128)S(1)} %get-tuple-element.19), channel_id=1, source_target_pairs={{8,0},{16,8},{24,16},{32,24},{40,32},{48,40},{56,48},{64,56},{72,6... | collective-permute-start | bytes 1572872 | tf_op jit(solution)/shard_map/ppermute | solution.py:18
  8.1 0.6 fusion.49
  8.8 4.6 %collective-permute-done = f32[64,2,8,128]{3,2,1,0:T(8,128)S(1)} collective-permute-done((f32[64,2,8,128]{3,2,1,0:T(8,128)S(1)}, f32[64,2,8,128]{3,2,1,0:T(8,128)S(1)}, u32[]{:S(2)}, u32[]{:S(2)}) %collective-permute-start) | collective-permute-done | bytes 524320 | tf_op jit(solution)/shard_map/ppermute | solution.py:18
  13.7 5.0 %collective-permute-done.1 = f32[64,2,8,128]{3,2,1,0:T(8,128)S(1)} collective-permute-done((f32[64,2,8,128]{3,2,1,0:T(8,128)S(1)}, f32[64,2,8,128]{3,2,1,0:T(8,128)S(1)}, u32[]{:S(2)}, u32[]{:S(2)}) %collective-permute-start.1) | collective-permute-done | bytes 524320 | tf_op jit(solution)/shard_map/ppermute | solution.py:16
  19.5 1.9 %collective-permute-start.3 = (f32[64,8,2,128]{3,1,2,0:T(8,128)S(1)}, f32[64,8,2,128]{3,1,2,0:T(8,128)S(1)}, u32[]{:S(2)}, u32[]{:S(2)}) collective-permute-start(f32[64,8,2,128]{3,1,2,0:T(8,128)S(1)} %get-tuple-element.7), channel_id=1, source_target_pairs={{0,1},{1,2},{2,3},{3,4},{4,5},{5,6},{6,7},{7,0},{8,9},{9,10},{10,1... | collective-permute-start | bytes 1572872 | tf_op jit(solution)/shard_map/ppermute | solution.py:16
  22.0 0.6 fusion.51
  22.7 5.9 %collective-permute-done.2 = f32[64,8,2,128]{3,1,2,0:T(8,128)S(1)} collective-permute-done((f32[64,8,2,128]{3,1,2,0:T(8,128)S(1)}, f32[64,8,2,128]{3,1,2,0:T(8,128)S(1)}, u32[]{:S(2)}, u32[]{:S(2)}) %collective-permute-start.2) | collective-permute-done | bytes 524320 | tf_op jit(solution)/shard_map/ppermute | solution.py:18
  28.6 3.9 %collective-permute-done.3 = f32[64,8,2,128]{3,1,2,0:T(8,128)S(1)} collective-permute-done((f32[64,8,2,128]{3,1,2,0:T(8,128)S(1)}, f32[64,8,2,128]{3,1,2,0:T(8,128)S(1)}, u32[]{:S(2)}, u32[]{:S(2)}) %collective-permute-start.3) | collective-permute-done | bytes 524320 | tf_op jit(solution)/shard_map/ppermute | solution.py:16
  32.5 7.4 %broadcast_multiply_fusion = (f32[64,4,8,128]{3,1,2,0:T(4,128)S(1)}, f32[64,4,8,128]{3,1,2,0:T(4,128)S(1)}) fusion(f32[64,4,8,128]{3,1,2,0:T(4,128)S(1)} %copy.55, f32[4,8,128]{2,0,1:T(4,128)S(1)} %copy.71, f32[64,4,8,2]{3,1,2,0:T(4,128)S(1)} %get-tuple-element.25, f32[64,4,8,126]{3,1,2,0:T(4,128)S(1)} %get-tuple-element.27, ...), kind=kLoop, calls=%fused_computation.79 | loop fusion | flops 11796480 | bytes 9453568 | tf_op jit(solution)/shard_map/div | solution.py:81
  40.3 2.5 %collective-permute-start.4 = (f32[64,2,8,128]{3,2,1,0:T(8,128)S(1)}, f32[64,2,8,128]{3,2,1,0:T(8,128)S(1)}, u32[]{:S(2)}, u32[]{:S(2)}) collective-permute-start(f32[64,2,8,128]{3,2,1,0:T(8,128)S(1)} %copy.74), channel_id=1, source_target_pairs={{8,0},{16,8},{24,16},{32,24},{40,32},{48,40},{56,48},{64,56},{72,6... | collective-permute-start | bytes 1572872 | tf_op jit(solution)/shard_map/ppermute | solution.py:18
  43.8 0.6 fusion.44
  44.5 5.1 %collective-permute-done.4 = f32[64,2,8,128]{3,2,1,0:T(8,128)S(1)} collective-permute-done((f32[64,2,8,128]{3,2,1,0:T(8,128)S(1)}, f32[64,2,8,128]{3,2,1,0:T(8,128)S(1)}, u32[]{:S(2)}, u32[]{:S(2)}) %collective-permute-start.4) | collective-permute-done | bytes 524320 | tf_op jit(solution)/shard_map/ppermute | solution.py:18
  49.9 5.2 %collective-permute-done.5 = f32[64,2,8,128]{3,2,1,0:T(8,128)S(1)} collective-permute-done((f32[64,2,8,128]{3,2,1,0:T(8,128)S(1)}, f32[64,2,8,128]{3,2,1,0:T(8,128)S(1)}, u32[]{:S(2)}, u32[]{:S(2)}) %collective-permute-start.5) | collective-permute-done | bytes 524320 | tf_op jit(solution)/shard_map/ppermute | solution.py:16
  55.7 3.3 %collective-permute-start.6 = (f32[64,8,2,128]{3,1,2,0:T(8,128)S(1)}, f32[64,8,2,128]{3,1,2,0:T(8,128)S(1)}, u32[]{:S(2)}, u32[]{:S(2)}) collective-permute-start(f32[64,8,2,128]{3,1,2,0:T(8,128)S(1)} %get-tuple-element.4), channel_id=1, source_target_pairs={{1,0},{2,1},{3,2},{4,3},{5,4},{6,5},{7,6},{0,7},{9,8},{10,9},{11,1... | collective-permute-start | bytes 1572872 | tf_op jit(solution)/shard_map/ppermute | solution.py:18
  60.3 5.4 %collective-permute-done.6 = f32[64,8,2,128]{3,1,2,0:T(8,128)S(1)} collective-permute-done((f32[64,8,2,128]{3,1,2,0:T(8,128)S(1)}, f32[64,8,2,128]{3,1,2,0:T(8,128)S(1)}, u32[]{:S(2)}, u32[]{:S(2)}) %collective-permute-start.6) | collective-permute-done | bytes 524320 | tf_op jit(solution)/shard_map/ppermute | solution.py:18
  65.7 2.5 %collective-permute-done.7 = f32[64,8,2,128]{3,1,2,0:T(8,128)S(1)} collective-permute-done((f32[64,8,2,128]{3,1,2,0:T(8,128)S(1)}, f32[64,8,2,128]{3,1,2,0:T(8,128)S(1)}, u32[]{:S(2)}, u32[]{:S(2)}) %collective-permute-start.7) | collective-permute-done | bytes 524320 | tf_op jit(solution)/shard_map/ppermute | solution.py:16
  68.2 7.5 %multiply_subtract_fusion = f32[64,4,8,128]{3,1,2,0:T(4,128)S(1)} fusion(f32[64,4,8,128]{3,1,2,0:T(4,128)S(1)} %get-tuple-element.3, f32[64,4,8,2]{3,1,2,0:T(4,128)S(1)} %get-tuple-element.15, f32[64,4,8,126]{3,1,2,0:T(4,128)S(1)} %get-tuple-element.17, f32[64,4,8,126]{3,1,2,0:T(4,128)S(1)} %get-tuple-element.16, f32[64,4,8,2]{3,1,2,0:T(4,128)S(1)} %get-tuple-element.14, ...), kind=kLoop, calls=%fused_computation.71 | loop fusion | flops 12058624 | bytes 10502144 | tf_op jit(solution)/shard_map/sub | solution.py:83
  75.7 2.0 %fusion.1 = f32[64,64]{0,1:T(8,128)S(1)} fusion(f32[64,4,8,128]{3,1,2,0:T(4,128)S(1)} %multiply_subtract_fusion), kind=kOutput, calls=%fused_computation.11 | convolution fusion | flops 201330688 | bytes 1064960 | tf_op jit(solution)/shard_map/dot_general | solution.py:88
  77.8 74.5 %psum.7 = f32[64,64]{0,1:T(8,128)S(1)} all-reduce(f32[64,64]{0,1:T(8,128)S(1)} %fusion.1), channel_id=1, replica_groups=mesh['gx'=32,'gy'=8] {'gx','gy'}, use_global_device_ids=true, to_apply=%region_0.1 | all-reduce | flops 4096 | bytes 32768 | tf_op jit(solution)/shard_map/psum | solution.py:91
  152.4 0.7 pad_maximum_fusion.22.aug_ref
  153.1 8.6 %shard_map.41 = f32[64,128]{1,0:T(8,128)} custom-call(f32[64,128]{1,0:T(8,128)} %pad_maximum_fusion.22.aug_ref), custom_call_target="tpu_custom_call" | custom-call | tf_op jit(solution)/shard_map/pallas_call | solution.py:71
  161.7 2.3 %fusion = f32[8,8,32,128]{3,1,2,0:T(8,128)S(1)} fusion(f32[8,8,32,128]{3,2,1,0:T(8,128)S(1)} %bitcast.18, f32[64,128]{1,0:T(8,128)} %shard_map.41), kind=kOutput, calls=%fused_computation.9 | convolution fusion | flops 201588736 | bytes 2129920 | tf_op jit(solution)/shard_map/dot_general | solution.py:92
  164.1 1.2 copy.90
  (30 shorter events, 6.8 us)
Async XLA Ops:
  0.6 6.1 %copy-start = (f32[64,4,8,128]{3,2,1,0:T(8,128)S(1)}, f32[64,4,8,128]{3,2,1,0:T(8,128)}, u32[]{:S(2)}) copy-start(f32[64,4,8,128]{3,2,1,0:T(8,128)} %param.2) | copy-start | bytes 3145732
  2.0 11.4 %collective-permute-start = (f32[64,2,8,128]{3,2,1,0:T(8,128)S(1)}, f32[64,2,8,128]{3,2,1,0:T(8,128)S(1)}, u32[]{:S(2)}, u32[]{:S(2)}) collective-permute-start(f32[64,2,8,128]{3,2,1,0:T(8,128)S(1)} %get-tuple-element.19), channel_id=1, source_target_pairs={{8,0},{16,8},{24,16},{32,24},{40,32},{48,40},{56,48},{64,56},{72,6... | collective-permute-start | bytes 1572872 | tf_op jit(solution)/shard_map/ppermute | solution.py:18
  6.7 0.7 copy-start.1
  6.7 11.9 %collective-permute-start.1 = (f32[64,2,8,128]{3,2,1,0:T(8,128)S(1)}, f32[64,2,8,128]{3,2,1,0:T(8,128)S(1)}, u32[]{:S(2)}, u32[]{:S(2)}) collective-permute-start(f32[64,2,8,128]{3,2,1,0:T(8,128)S(1)} %get-tuple-element.18), channel_id=1, source_target_pairs={{0,8},{8,16},{16,24},{24,32},{32,40},{40,48},{48,56},{56,64},{64,7... | collective-permute-start | bytes 1572872 | tf_op jit(solution)/shard_map/ppermute | solution.py:16
  19.3 9.3 %collective-permute-start.2 = (f32[64,8,2,128]{3,1,2,0:T(8,128)S(1)}, f32[64,8,2,128]{3,1,2,0:T(8,128)S(1)}, u32[]{:S(2)}, u32[]{:S(2)}) collective-permute-start(f32[64,8,2,128]{3,1,2,0:T(8,128)S(1)} %get-tuple-element.6), channel_id=1, source_target_pairs={{1,0},{2,1},{3,2},{4,3},{5,4},{6,5},{7,6},{0,7},{9,8},{10,9},{11,1... | collective-permute-start | bytes 1572872 | tf_op jit(solution)/shard_map/ppermute | solution.py:18
  19.5 13.0 %collective-permute-start.3 = (f32[64,8,2,128]{3,1,2,0:T(8,128)S(1)}, f32[64,8,2,128]{3,1,2,0:T(8,128)S(1)}, u32[]{:S(2)}, u32[]{:S(2)}) collective-permute-start(f32[64,8,2,128]{3,1,2,0:T(8,128)S(1)} %get-tuple-element.7), channel_id=1, source_target_pairs={{0,1},{1,2},{2,3},{3,4},{4,5},{5,6},{6,7},{7,0},{8,9},{9,10},{10,1... | collective-permute-start | bytes 1572872 | tf_op jit(solution)/shard_map/ppermute | solution.py:16
  40.3 9.2 %collective-permute-start.4 = (f32[64,2,8,128]{3,2,1,0:T(8,128)S(1)}, f32[64,2,8,128]{3,2,1,0:T(8,128)S(1)}, u32[]{:S(2)}, u32[]{:S(2)}) collective-permute-start(f32[64,2,8,128]{3,2,1,0:T(8,128)S(1)} %copy.74), channel_id=1, source_target_pairs={{8,0},{16,8},{24,16},{32,24},{40,32},{48,40},{56,48},{64,56},{72,6... | collective-permute-start | bytes 1572872 | tf_op jit(solution)/shard_map/ppermute | solution.py:18
  42.9 12.2 %collective-permute-start.5 = (f32[64,2,8,128]{3,2,1,0:T(8,128)S(1)}, f32[64,2,8,128]{3,2,1,0:T(8,128)S(1)}, u32[]{:S(2)}, u32[]{:S(2)}) collective-permute-start(f32[64,2,8,128]{3,2,1,0:T(8,128)S(1)} %copy.76), channel_id=1, source_target_pairs={{0,8},{8,16},{16,24},{24,32},{32,40},{40,48},{48,56},{56,64},{64,7... | collective-permute-start | bytes 1572872 | tf_op jit(solution)/shard_map/ppermute | solution.py:16
  55.7 10.0 %collective-permute-start.6 = (f32[64,8,2,128]{3,1,2,0:T(8,128)S(1)}, f32[64,8,2,128]{3,1,2,0:T(8,128)S(1)}, u32[]{:S(2)}, u32[]{:S(2)}) collective-permute-start(f32[64,8,2,128]{3,1,2,0:T(8,128)S(1)} %get-tuple-element.4), channel_id=1, source_target_pairs={{1,0},{2,1},{3,2},{4,3},{5,4},{6,5},{7,6},{0,7},{9,8},{10,9},{11,1... | collective-permute-start | bytes 1572872 | tf_op jit(solution)/shard_map/ppermute | solution.py:18
  59.0 9.2 %collective-permute-start.7 = (f32[64,8,2,128]{3,1,2,0:T(8,128)S(1)}, f32[64,8,2,128]{3,1,2,0:T(8,128)S(1)}, u32[]{:S(2)}, u32[]{:S(2)}) collective-permute-start(f32[64,8,2,128]{3,1,2,0:T(8,128)S(1)} %get-tuple-element.5), channel_id=1, source_target_pairs={{0,1},{1,2},{2,3},{3,4},{4,5},{5,6},{6,7},{7,0},{8,9},{9,10},{10,1... | collective-permute-start | bytes 1572872 | tf_op jit(solution)/shard_map/ppermute | solution.py:16

commit v2 on v1

--- a/solution.py
+++ b/solution.py
@@ -77,6 +77,17 @@
     return out[:, :order], out[:, order:]
 
 
+def butterfly_sum(value, axis):
+    count = lax.axis_size(axis)
+    if count & (count - 1):
+        return lax.psum(value, axis)
+    mask = 1
+    while mask < count:
+        value = value + lax.ppermute(value, axis, [(i, i ^ mask) for i in range(count)])
+        mask *= 2
+    return value
+
+
 def shards(orbitals, potential):
     first = (apply_ham(with_faces(orbitals), potential) - 5.5 * orbitals) / 4.5
     applied = apply_ham(with_faces(first), potential)
@@ -88,7 +99,9 @@
         jnp.dot(flat, flat.T, precision=lax.Precision.HIGHEST, preferred_element_type=jnp.float32)
         / cells
     )
-    factor, lower_inverse = factor_and_inverse(lax.psum(local_gram, ("gx", "gy")))
+    packed = local_gram.reshape(-1, 128)
+    gram = butterfly_sum(butterfly_sum(packed, "gy"), "gx").reshape(local_gram.shape)
+    factor, lower_inverse = factor_and_inverse(gram)
     solved = jnp.dot(
         lower_inverse, flat, precision=lax.Precision.HIGHEST, preferred_element_type=jnp.float32
     )

time: 166 us -> 126 us (0.76)
  blocking collectives: 74.5 us -> 0 us
  waiting for transfers between devices: 37.6 us -> 69.8 us
  starting transfers between devices: 13 us -> 15.9 us
    psum x1 -> x0, blocking collectives: 74.5 us -> none  [shards(): lax.psum(local_gram, ('gx', 'gy'))]
    ppermute x0 -> x8, waiting for transfers between devices: none -> 32.2 us  [butterfly_sum(): lax.ppermute(value, axis, [(i, i ^ mask) for i in range(count)])]
    ppermute x0 -> x8, starting transfers between devices: none -> 2.91 us  [butterfly_sum(): lax.ppermute(value, axis, [(i, i ^ mask) for i in range(count)])]
  transfers between devices with their start and end apart: 8 -> 16, of which waited for: 8 -> 16; matrix products, arithmetic and copies ran while one was open for 4% -> 5% of each run, Pallas kernels for 0% -> 0%
where the time goes in v2:
time: 126 us
  waiting for transfers between devices  69.8 us (55%)
  other arithmetic  16.3 us (13%)
  starting transfers between devices  15.9 us (13%)
  local copies, waits for them, and re-layouts  10.2 us (8%)
  Pallas kernels  8.65 us (7%)
  matrix products  4.45 us (4%)
    ppermute x8, waiting for transfers between devices, butterfly_sum(): lax.ppermute(value, axis, [(i, i ^ mask) for i in range(count)])  32.2 us
    ppermute x4, waiting for transfers between devices, extended(): lax.ppermute(head, axis, [((i + 1) % count, i) for i in range(count)])  21 us
    ppermute x4, waiting for transfers between devices, extended(): lax.ppermute(tail, axis, [(i, (i + 1) % count) for i in range(count)])  16.6 us
    ppermute x4, starting transfers between devices, extended(): lax.ppermute(head, axis, [((i + 1) % count, i) for i in range(count)])  10.8 us
    pallas_call x1, Pallas kernels, factor_and_inverse(): pl.pallas_call(factor_kernel, out_shape=jax.ShapeDtypeStruct(aug.shape, j...  8.65 us
    sub x1, other arithmetic, shards(): filtered = 2.0 * (applied - 5.5 * first) / 4.5 - orbitals  7.45 us
    div x1, other arithmetic, shards(): first = (apply_ham(with_faces(orbitals), potential) - 5.5 * orbitals) / 4.5  7.38 us
    ppermute x8, starting transfers between devices, butterfly_sum(): lax.ppermute(value, axis, [(i, i ^ mask) for i in range(count)])  2.91 us
  transfers between devices with their start and end apart: 16, of which 16 were waited for; matrix products, arithmetic and copies ran while one was open for 5% of the time, Pallas kernels for 0%

profile of v2, /device:TPU:32, one launch (start us, length us, event | category | flops | bytes accessed | tf_op | source)
XLA Modules:
  0.0 126.2 jit_solution(6629029291490872603)
XLA Ops:
  2.0 4.7 %collective-permute-start = (f32[64,2,8,128]{3,2,1,0:T(8,128)S(1)}, f32[64,2,8,128]{3,2,1,0:T(8,128)S(1)}, u32[]{:S(2)}, u32[]{:S(2)}) collective-permute-start(f32[64,2,8,128]{3,2,1,0:T(8,128)S(1)} %get-tuple-element.19), channel_id=1, source_target_pairs={{8,0},{16,8},{24,16},{32,24},{40,32},{48,40},{56,48},{64,56},{72,6... | collective-permute-start | bytes 1572872 | tf_op jit(solution)/shard_map/ppermute | solution.py:18
  8.8 4.7 %collective-permute-done = f32[64,2,8,128]{3,2,1,0:T(8,128)S(1)} collective-permute-done((f32[64,2,8,128]{3,2,1,0:T(8,128)S(1)}, f32[64,2,8,128]{3,2,1,0:T(8,128)S(1)}, u32[]{:S(2)}, u32[]{:S(2)}) %collective-permute-start) | collective-permute-done | bytes 524320 | tf_op jit(solution)/shard_map/ppermute | solution.py:18
  13.7 5.0 %collective-permute-done.1 = f32[64,2,8,128]{3,2,1,0:T(8,128)S(1)} collective-permute-done((f32[64,2,8,128]{3,2,1,0:T(8,128)S(1)}, f32[64,2,8,128]{3,2,1,0:T(8,128)S(1)}, u32[]{:S(2)}, u32[]{:S(2)}) %collective-permute-start.1) | collective-permute-done | bytes 524320 | tf_op jit(solution)/shard_map/ppermute | solution.py:16
  19.5 1.9 %collective-permute-start.3 = (f32[64,8,2,128]{3,1,2,0:T(8,128)S(1)}, f32[64,8,2,128]{3,1,2,0:T(8,128)S(1)}, u32[]{:S(2)}, u32[]{:S(2)}) collective-permute-start(f32[64,8,2,128]{3,1,2,0:T(8,128)S(1)} %get-tuple-element.7), channel_id=1, source_target_pairs={{0,1},{1,2},{2,3},{3,4},{4,5},{5,6},{6,7},{7,0},{8,9},{9,10},{10,1... | collective-permute-start | bytes 1572872 | tf_op jit(solution)/shard_map/ppermute | solution.py:16
  22.7 5.9 %collective-permute-done.2 = f32[64,8,2,128]{3,1,2,0:T(8,128)S(1)} collective-permute-done((f32[64,8,2,128]{3,1,2,0:T(8,128)S(1)}, f32[64,8,2,128]{3,1,2,0:T(8,128)S(1)}, u32[]{:S(2)}, u32[]{:S(2)}) %collective-permute-start.2) | collective-permute-done | bytes 524320 | tf_op jit(solution)/shard_map/ppermute | solution.py:18
  28.6 3.9 %collective-permute-done.3 = f32[64,8,2,128]{3,1,2,0:T(8,128)S(1)} collective-permute-done((f32[64,8,2,128]{3,1,2,0:T(8,128)S(1)}, f32[64,8,2,128]{3,1,2,0:T(8,128)S(1)}, u32[]{:S(2)}, u32[]{:S(2)}) %collective-permute-start.3) | collective-permute-done | bytes 524320 | tf_op jit(solution)/shard_map/ppermute | solution.py:16
  32.5 7.4 %broadcast_multiply_fusion = (f32[64,4,8,128]{3,1,2,0:T(4,128)S(1)}, f32[64,4,8,128]{3,1,2,0:T(4,128)S(1)}) fusion(f32[64,4,8,128]{3,1,2,0:T(4,128)S(1)} %copy.55, f32[4,8,128]{2,0,1:T(4,128)S(1)} %copy.71, f32[64,4,8,2]{3,1,2,0:T(4,128)S(1)} %get-tuple-element.25, f32[64,4,8,126]{3,1,2,0:T(4,128)S(1)} %get-tuple-element.27, ...), kind=kLoop, calls=%fused_computation.79 | loop fusion | flops 11796480 | bytes 9453568 | tf_op jit(solution)/shard_map/div | solution.py:92
  40.3 2.5 %collective-permute-start.4 = (f32[64,2,8,128]{3,2,1,0:T(8,128)S(1)}, f32[64,2,8,128]{3,2,1,0:T(8,128)S(1)}, u32[]{:S(2)}, u32[]{:S(2)}) collective-permute-start(f32[64,2,8,128]{3,2,1,0:T(8,128)S(1)} %copy.74), channel_id=1, source_target_pairs={{8,0},{16,8},{24,16},{32,24},{40,32},{48,40},{56,48},{64,56},{72,6... | collective-permute-start | bytes 1572872 | tf_op jit(solution)/shard_map/ppermute | solution.py:18
  44.5 5.1 %collective-permute-done.4 = f32[64,2,8,128]{3,2,1,0:T(8,128)S(1)} collective-permute-done((f32[64,2,8,128]{3,2,1,0:T(8,128)S(1)}, f32[64,2,8,128]{3,2,1,0:T(8,128)S(1)}, u32[]{:S(2)}, u32[]{:S(2)}) %collective-permute-start.4) | collective-permute-done | bytes 524320 | tf_op jit(solution)/shard_map/ppermute | solution.py:18
  49.9 5.2 %collective-permute-done.5 = f32[64,2,8,128]{3,2,1,0:T(8,128)S(1)} collective-permute-done((f32[64,2,8,128]{3,2,1,0:T(8,128)S(1)}, f32[64,2,8,128]{3,2,1,0:T(8,128)S(1)}, u32[]{:S(2)}, u32[]{:S(2)}) %collective-permute-start.5) | collective-permute-done | bytes 524320 | tf_op jit(solution)/shard_map/ppermute | solution.py:16
  55.7 3.3 %collective-permute-start.6 = (f32[64,8,2,128]{3,1,2,0:T(8,128)S(1)}, f32[64,8,2,128]{3,1,2,0:T(8,128)S(1)}, u32[]{:S(2)}, u32[]{:S(2)}) collective-permute-start(f32[64,8,2,128]{3,1,2,0:T(8,128)S(1)} %get-tuple-element.4), channel_id=1, source_target_pairs={{1,0},{2,1},{3,2},{4,3},{5,4},{6,5},{7,6},{0,7},{9,8},{10,9},{11,1... | collective-permute-start | bytes 1572872 | tf_op jit(solution)/shard_map/ppermute | solution.py:18
  60.3 5.4 %collective-permute-done.6 = f32[64,8,2,128]{3,1,2,0:T(8,128)S(1)} collective-permute-done((f32[64,8,2,128]{3,1,2,0:T(8,128)S(1)}, f32[64,8,2,128]{3,1,2,0:T(8,128)S(1)}, u32[]{:S(2)}, u32[]{:S(2)}) %collective-permute-start.6) | collective-permute-done | bytes 524320 | tf_op jit(solution)/shard_map/ppermute | solution.py:18
  65.7 2.5 %collective-permute-done.7 = f32[64,8,2,128]{3,1,2,0:T(8,128)S(1)} collective-permute-done((f32[64,8,2,128]{3,1,2,0:T(8,128)S(1)}, f32[64,8,2,128]{3,1,2,0:T(8,128)S(1)}, u32[]{:S(2)}, u32[]{:S(2)}) %collective-permute-start.7) | collective-permute-done | bytes 524320 | tf_op jit(solution)/shard_map/ppermute | solution.py:16
  68.2 7.5 %multiply_subtract_fusion = f32[64,4,8,128]{3,1,2,0:T(4,128)S(1)} fusion(f32[64,4,8,128]{3,1,2,0:T(4,128)S(1)} %get-tuple-element.3, f32[64,4,8,2]{3,1,2,0:T(4,128)S(1)} %get-tuple-element.15, f32[64,4,8,126]{3,1,2,0:T(4,128)S(1)} %get-tuple-element.17, f32[64,4,8,126]{3,1,2,0:T(4,128)S(1)} %get-tuple-element.16, f32[64,4,8,2]{3,1,2,0:T(4,128)S(1)} %get-tuple-element.14, ...), kind=kLoop, calls=%fused_computation.71 | loop fusion | flops 12058624 | bytes 10502144 | tf_op jit(solution)/shard_map/sub | solution.py:94
  75.7 2.1 %fusion.1 = f32[64,64]{1,0:T(8,128)S(1)} fusion(f32[64,4,8,128]{3,1,2,0:T(4,128)S(1)} %multiply_subtract_fusion), kind=kOutput, calls=%fused_computation.11 | convolution fusion | flops 201330688 | bytes 1064960 | tf_op jit(solution)/shard_map/dot_general | solution.py:99
  79.2 2.4 %collective-permute-done.8 = f32[32,128]{1,0:T(8,128)S(1)} collective-permute-done((f32[32,128]{1,0:T(8,128)S(1)}, f32[32,128]{1,0:T(8,128)S(1)}, u32[]{:S(2)}, u32[]{:S(2)}) %collective-permute-start.8) | collective-permute-done | bytes 16416 | tf_op jit(solution)/shard_map/ppermute | solution.py:86
  81.6 4.6 %collective-permute-done.9 = f32[32,128]{1,0:T(8,128)S(1)} collective-permute-done((f32[32,128]{1,0:T(8,128)S(1)}, f32[32,128]{1,0:T(8,128)S(1)}, u32[]{:S(2)}, u32[]{:S(2)}) %collective-permute-start.9) | collective-permute-done | bytes 16416 | tf_op jit(solution)/shard_map/ppermute | solution.py:86
  87.9 6.1 %collective-permute-done.10 = f32[32,128]{1,0:T(8,128)S(1)} collective-permute-done((f32[32,128]{1,0:T(8,128)S(1)}, f32[32,128]{1,0:T(8,128)S(1)}, u32[]{:S(2)}, u32[]{:S(2)}) %collective-permute-start.10) | collective-permute-done | bytes 16416 | tf_op jit(solution)/shard_map/ppermute | solution.py:86
  95.1 3.7 %collective-permute-done.12 = f32[32,128]{1,0:T(8,128)S(1)} collective-permute-done((f32[32,128]{1,0:T(8,128)S(1)}, f32[32,128]{1,0:T(8,128)S(1)}, u32[]{:S(2)}, u32[]{:S(2)}) %collective-permute-start.12) | collective-permute-done | bytes 16416 | tf_op jit(solution)/shard_map/ppermute | solution.py:86
  98.9 5.2 %collective-permute-done.13 = f32[32,128]{1,0:T(8,128)S(1)} collective-permute-done((f32[32,128]{1,0:T(8,128)S(1)}, f32[32,128]{1,0:T(8,128)S(1)}, u32[]{:S(2)}, u32[]{:S(2)}) %collective-permute-start.13) | collective-permute-done | bytes 16416 | tf_op jit(solution)/shard_map/ppermute | solution.py:86
  104.1 3.7 %collective-permute-done.14 = f32[32,128]{1,0:T(8,128)S(1)} collective-permute-done((f32[32,128]{1,0:T(8,128)S(1)}, f32[32,128]{1,0:T(8,128)S(1)}, u32[]{:S(2)}, u32[]{:S(2)}) %collective-permute-start.14) | collective-permute-done | bytes 16416 | tf_op jit(solution)/shard_map/ppermute | solution.py:86
  108.0 5.1 %collective-permute-done.15 = f32[32,128]{1,0:T(8,128)S(1)} collective-permute-done((f32[32,128]{1,0:T(8,128)S(1)}, f32[32,128]{1,0:T(8,128)S(1)}, u32[]{:S(2)}, u32[]{:S(2)}) %collective-permute-start.15) | collective-permute-done | bytes 16416 | tf_op jit(solution)/shard_map/ppermute | solution.py:86
  114.0 8.6 %shard_map.41 = f32[64,128]{1,0:T(8,128)} custom-call(f32[64,128]{1,0:T(8,128)} %pad_maximum_fusion.22.aug_ref), custom_call_target="tpu_custom_call" | custom-call | tf_op jit(solution)/shard_map/pallas_call | solution.py:71
  122.6 2.3 %fusion = f32[8,8,32,128]{3,1,2,0:T(8,128)S(1)} fusion(f32[8,8,32,128]{3,2,1,0:T(8,128)S(1)} %bitcast.20, f32[64,128]{1,0:T(8,128)} %shard_map.41), kind=kOutput, calls=%fused_computation.9 | convolution fusion | flops 201588736 | bytes 2129920 | tf_op jit(solution)/shard_map/dot_general | solution.py:105
  (55 shorter events, 16.2 us)
Async XLA Ops:
  0.6 6.1 %copy-start = (f32[64,4,8,128]{3,2,1,0:T(8,128)S(1)}, f32[64,4,8,128]{3,2,1,0:T(8,128)}, u32[]{:S(2)}) copy-start(f32[64,4,8,128]{3,2,1,0:T(8,128)} %param.2) | copy-start | bytes 3145732
  2.0 11.4 %collective-permute-start = (f32[64,2,8,128]{3,2,1,0:T(8,128)S(1)}, f32[64,2,8,128]{3,2,1,0:T(8,128)S(1)}, u32[]{:S(2)}, u32[]{:S(2)}) collective-permute-start(f32[64,2,8,128]{3,2,1,0:T(8,128)S(1)} %get-tuple-element.19), channel_id=1, source_target_pairs={{8,0},{16,8},{24,16},{32,24},{40,32},{48,40},{56,48},{64,56},{72,6... | collective-permute-start | bytes 1572872 | tf_op jit(solution)/shard_map/ppermute | solution.py:18
  6.7 0.7 copy-start.1
  6.7 11.9 %collective-permute-start.1 = (f32[64,2,8,128]{3,2,1,0:T(8,128)S(1)}, f32[64,2,8,128]{3,2,1,0:T(8,128)S(1)}, u32[]{:S(2)}, u32[]{:S(2)}) collective-permute-start(f32[64,2,8,128]{3,2,1,0:T(8,128)S(1)} %get-tuple-element.18), channel_id=1, source_target_pairs={{0,8},{8,16},{16,24},{24,32},{32,40},{40,48},{48,56},{56,64},{64,7... | collective-permute-start | bytes 1572872 | tf_op jit(solution)/shard_map/ppermute | solution.py:16
  19.3 9.3 %collective-permute-start.2 = (f32[64,8,2,128]{3,1,2,0:T(8,128)S(1)}, f32[64,8,2,128]{3,1,2,0:T(8,128)S(1)}, u32[]{:S(2)}, u32[]{:S(2)}) collective-permute-start(f32[64,8,2,128]{3,1,2,0:T(8,128)S(1)} %get-tuple-element.6), channel_id=1, source_target_pairs={{1,0},{2,1},{3,2},{4,3},{5,4},{6,5},{7,6},{0,7},{9,8},{10,9},{11,1... | collective-permute-start | bytes 1572872 | tf_op jit(solution)/shard_map/ppermute | solution.py:18
  19.5 13.0 %collective-permute-start.3 = (f32[64,8,2,128]{3,1,2,0:T(8,128)S(1)}, f32[64,8,2,128]{3,1,2,0:T(8,128)S(1)}, u32[]{:S(2)}, u32[]{:S(2)}) collective-permute-start(f32[64,8,2,128]{3,1,2,0:T(8,128)S(1)} %get-tuple-element.7), channel_id=1, source_target_pairs={{0,1},{1,2},{2,3},{3,4},{4,5},{5,6},{6,7},{7,0},{8,9},{9,10},{10,1... | collective-permute-start | bytes 1572872 | tf_op jit(solution)/shard_map/ppermute | solution.py:16
  40.3 9.2 %collective-permute-start.4 = (f32[64,2,8,128]{3,2,1,0:T(8,128)S(1)}, f32[64,2,8,128]{3,2,1,0:T(8,128)S(1)}, u32[]{:S(2)}, u32[]{:S(2)}) collective-permute-start(f32[64,2,8,128]{3,2,1,0:T(8,128)S(1)} %copy.74), channel_id=1, source_target_pairs={{8,0},{16,8},{24,16},{32,24},{40,32},{48,40},{56,48},{64,56},{72,6... | collective-permute-start | bytes 1572872 | tf_op jit(solution)/shard_map/ppermute | solution.py:18
  42.9 12.2 %collective-permute-start.5 = (f32[64,2,8,128]{3,2,1,0:T(8,128)S(1)}, f32[64,2,8,128]{3,2,1,0:T(8,128)S(1)}, u32[]{:S(2)}, u32[]{:S(2)}) collective-permute-start(f32[64,2,8,128]{3,2,1,0:T(8,128)S(1)} %copy.76), channel_id=1, source_target_pairs={{0,8},{8,16},{16,24},{24,32},{32,40},{40,48},{48,56},{56,64},{64,7... | collective-permute-start | bytes 1572872 | tf_op jit(solution)/shard_map/ppermute | solution.py:16
  55.7 10.0 %collective-permute-start.6 = (f32[64,8,2,128]{3,1,2,0:T(8,128)S(1)}, f32[64,8,2,128]{3,1,2,0:T(8,128)S(1)}, u32[]{:S(2)}, u32[]{:S(2)}) collective-permute-start(f32[64,8,2,128]{3,1,2,0:T(8,128)S(1)} %get-tuple-element.4), channel_id=1, source_target_pairs={{1,0},{2,1},{3,2},{4,3},{5,4},{6,5},{7,6},{0,7},{9,8},{10,9},{11,1... | collective-permute-start | bytes 1572872 | tf_op jit(solution)/shard_map/ppermute | solution.py:18
  59.0 9.2 %collective-permute-start.7 = (f32[64,8,2,128]{3,1,2,0:T(8,128)S(1)}, f32[64,8,2,128]{3,1,2,0:T(8,128)S(1)}, u32[]{:S(2)}, u32[]{:S(2)}) collective-permute-start(f32[64,8,2,128]{3,1,2,0:T(8,128)S(1)} %get-tuple-element.5), channel_id=1, source_target_pairs={{0,1},{1,2},{2,3},{3,4},{4,5},{5,6},{6,7},{7,0},{8,9},{9,10},{10,1... | collective-permute-start | bytes 1572872 | tf_op jit(solution)/shard_map/ppermute | solution.py:16
  77.9 3.8 %collective-permute-start.8 = (f32[32,128]{1,0:T(8,128)S(1)}, f32[32,128]{1,0:T(8,128)S(1)}, u32[]{:S(2)}, u32[]{:S(2)}) collective-permute-start(f32[32,128]{1,0:T(8,128)S(1)} %reshape.17), channel_id=1, source_target_pairs={{0,1},{1,0},{2,3},{3,2},{4,5},{5,4},{6,7},{7,6},{8,9},{9,8},{10,11... | collective-permute-start | bytes 49160 | tf_op jit(solution)/shard_map/ppermute | solution.py:86
  81.6 4.7 %collective-permute-start.9 = (f32[32,128]{1,0:T(8,128)S(1)}, f32[32,128]{1,0:T(8,128)S(1)}, u32[]{:S(2)}, u32[]{:S(2)}) collective-permute-start(f32[32,128]{1,0:T(8,128)S(1)} %add.107), channel_id=1, source_target_pairs={{0,2},{1,3},{2,0},{3,1},{4,6},{5,7},{6,4},{7,5},{8,10},{9,11},{10,... | collective-permute-start | bytes 49160 | tf_op jit(solution)/shard_map/ppermute | solution.py:86
  86.3 7.6 %collective-permute-start.10 = (f32[32,128]{1,0:T(8,128)S(1)}, f32[32,128]{1,0:T(8,128)S(1)}, u32[]{:S(2)}, u32[]{:S(2)}) collective-permute-start(f32[32,128]{1,0:T(8,128)S(1)} %add.108), channel_id=1, source_target_pairs={{0,4},{1,5},{2,6},{3,7},{4,0},{5,1},{6,2},{7,3},{8,12},{9,13},{10,... | collective-permute-start | bytes 49160 | tf_op jit(solution)/shard_map/ppermute | solution.py:86
  93.9 1.2 collective-permute-start.11
  95.1 3.7 %collective-permute-start.12 = (f32[32,128]{1,0:T(8,128)S(1)}, f32[32,128]{1,0:T(8,128)S(1)}, u32[]{:S(2)}, u32[]{:S(2)}) collective-permute-start(f32[32,128]{1,0:T(8,128)S(1)} %add.110), channel_id=1, source_target_pairs={{0,16},{8,24},{16,0},{24,8},{32,48},{40,56},{48,32},{56,40},{64,80... | collective-permute-start | bytes 49160 | tf_op jit(solution)/shard_map/ppermute | solution.py:86
  98.9 5.2 %collective-permute-start.13 = (f32[32,128]{1,0:T(8,128)S(1)}, f32[32,128]{1,0:T(8,128)S(1)}, u32[]{:S(2)}, u32[]{:S(2)}) collective-permute-start(f32[32,128]{1,0:T(8,128)S(1)} %add.111), channel_id=1, source_target_pairs={{0,32},{8,40},{16,48},{24,56},{32,0},{40,8},{48,16},{56,24},{64,96... | collective-permute-start | bytes 49160 | tf_op jit(solution)/shard_map/ppermute | solution.py:86
  104.1 3.7 %collective-permute-start.14 = (f32[32,128]{1,0:T(8,128)S(1)}, f32[32,128]{1,0:T(8,128)S(1)}, u32[]{:S(2)}, u32[]{:S(2)}) collective-permute-start(f32[32,128]{1,0:T(8,128)S(1)} %add.112), channel_id=1, source_target_pairs={{0,64},{8,72},{16,80},{24,88},{32,96},{40,104},{48,112},{56,120},{... | collective-permute-start | bytes 49160 | tf_op jit(solution)/shard_map/ppermute | solution.py:86
  107.9 5.2 %collective-permute-start.15 = (f32[32,128]{1,0:T(8,128)S(1)}, f32[32,128]{1,0:T(8,128)S(1)}, u32[]{:S(2)}, u32[]{:S(2)}) collective-permute-start(f32[32,128]{1,0:T(8,128)S(1)} %add.113), channel_id=1, source_target_pairs={{0,128},{8,136},{16,144},{24,152},{32,160},{40,168},{48,176},{56,1... | collective-permute-start | bytes 49160 | tf_op jit(solution)/shard_map/ppermute | solution.py:86

commit v3 on v2

--- a/solution.py
+++ b/solution.py
@@ -6,36 +6,27 @@
 from jax.sharding import PartitionSpec as P
 
 
-def extended(cells, sides, width):
-    for axis, dim in sides:
-        count = lax.axis_size(axis)
-        head = lax.slice_in_dim(cells, 0, width, axis=dim)
-        tail = lax.slice_in_dim(cells, cells.shape[dim] - width, cells.shape[dim], axis=dim)
-        cells = jnp.concatenate(
-            [
-                lax.ppermute(tail, axis, [(i, (i + 1) % count) for i in range(count)]),
-                cells,
-                lax.ppermute(head, axis, [((i + 1) % count, i) for i in range(count)]),
-            ],
-            axis=dim,
-        )
-    return cells
+def faces(cells, axis, dim, width):
+    count = lax.axis_size(axis)
+    size = cells.shape[dim]
+    head = lax.slice_in_dim(cells, 0, width, axis=dim)
+    tail = lax.slice_in_dim(cells, size - width, size, axis=dim)
+    before = lax.ppermute(tail, axis, [(i, (i + 1) % count) for i in range(count)])
+    after = lax.ppermute(head, axis, [((i + 1) % count, i) for i in range(count)])
+    return jnp.concatenate([before, cells, after], axis=dim)
 
 
-def apply_ham(padded, pot):
-    core = padded[:, 2:-2, 2:-2]
+def apply_ham(core, pot):
+    along_x = faces(core, "gx", 1, 2)
+    along_y = faces(core, "gy", 2, 2)
     total = -7.5 * core
-    total = total + 4.0 / 3.0 * (padded[:, 3:-1, 2:-2] + padded[:, 1:-3, 2:-2])
-    total = total - 1.0 / 12.0 * (padded[:, 4:, 2:-2] + padded[:, :-4, 2:-2])
-    total = total + 4.0 / 3.0 * (padded[:, 2:-2, 3:-1] + padded[:, 2:-2, 1:-3])
-    total = total - 1.0 / 12.0 * (padded[:, 2:-2, 4:] + padded[:, 2:-2, :-4])
+    total = total + 4.0 / 3.0 * (along_x[:, 3:-1] + along_x[:, 1:-3])
+    total = total - 1.0 / 12.0 * (along_x[:, 4:] + along_x[:, :-4])
+    total = total + 4.0 / 3.0 * (along_y[:, :, 3:-1] + along_y[:, :, 1:-3])
+    total = total - 1.0 / 12.0 * (along_y[:, :, 4:] + along_y[:, :, :-4])
     total = total + 4.0 / 3.0 * (jnp.roll(core, 1, 3) + jnp.roll(core, -1, 3))
     total = total - 1.0 / 12.0 * (jnp.roll(core, 2, 3) + jnp.roll(core, -2, 3))
     return -0.5 * total + pot[None] * core
-
-
-def with_faces(field):
-    return extended(field, (("gx", 1), ("gy", 2)), 2)
 
 
 def factor_kernel(aug_ref, out_ref):
@@ -89,8 +80,8 @@
 
 
 def shards(orbitals, potential):
-    first = (apply_ham(with_faces(orbitals), potential) - 5.5 * orbitals) / 4.5
-    applied = apply_ham(with_faces(first), potential)
+    first = (apply_ham(orbitals, potential) - 5.5 * orbitals) / 4.5
+    applied = apply_ham(first, potential)
     filtered = 2.0 * (applied - 5.5 * first) / 4.5 - orbitals
     width = filtered.shape[0]
     flat = filtered.reshape(width, -1)

time: 126 us -> 90.8 us (0.72)
  waiting for transfers between devices: 69.8 us -> 36.7 us
  other arithmetic: 16.3 us -> 5.91 us
  starting transfers between devices: 15.9 us -> 22.1 us
  local copies, waits for them, and re-layouts: 10.2 us -> 12.9 us
    ppermute x8, waiting for transfers between devices: 37.6 us -> 9.14 us  [the longest x4 5.55 us: faces(): lax.ppermute(tail, axis, [(i, (i + 1) % count) for i in range(count)])]
    ppermute x8, starting transfers between devices: 2.91 us -> 8.58 us  [butterfly_sum(): lax.ppermute(value, axis, [(i, i ^ mask) for i in range(count)])]
    unnamed x7 -> x20, local copies, waits for them, and re-layouts: 1.87 us -> 7.34 us
    sub x1, other arithmetic: 7.45 us -> 2.5 us  [shards(): filtered = 2.0 * (applied - 5.5 * first) / 4.5 - orbitals]
    div x1, other arithmetic: 7.38 us -> 2.65 us  [shards(): first = (apply_ham(orbitals, potential) - 5.5 * orbitals) / 4.5]
    ppermute x8, waiting for transfers between devices: 32.2 us -> 27.5 us  [butterfly_sum(): lax.ppermute(value, axis, [(i, i ^ mask) for i in range(count)])]
  transfers between devices with their start and end apart: 16 -> 16, of which waited for: 16 -> 11; matrix products, arithmetic and copies ran while one was open for 5% -> 10% of each run, Pallas kernels for 0% -> 0%
where the time goes in v3:
time: 90.8 us; the launch traced here: 90.5 us
  waiting for transfers between devices  36.7 us (40%)
  starting transfers between devices  22.1 us (24%)
  local copies, waits for them, and re-layouts  12.9 us (14%)
  Pallas kernels  8.65 us (10%)
  other arithmetic  5.91 us (7%)
  matrix products  3.31 us (4%)
  between operations  0.96 us (1%)
    ppermute x8, waiting for transfers between devices, butterfly_sum(): lax.ppermute(value, axis, [(i, i ^ mask) for i in range(count)])  27.5 us
    ppermute x4, starting transfers between devices, faces(): lax.ppermute(head, axis, [((i + 1) % count, i) for i in range(count)])  10 us
    pallas_call x1, Pallas kernels, factor_and_inverse(): pl.pallas_call(factor_kernel, out_shape=jax.ShapeDtypeStruct(aug.shape, j...  8.65 us
    ppermute x8, starting transfers between devices, butterfly_sum(): lax.ppermute(value, axis, [(i, i ^ mask) for i in range(count)])  8.58 us
    unnamed x20, local copies, waits for them, and re-layouts  7.34 us
    ppermute x4, waiting for transfers between devices, faces(): lax.ppermute(tail, axis, [(i, (i + 1) % count) for i in range(count)])  5.55 us
    ppermute x4, waiting for transfers between devices, faces(): lax.ppermute(head, axis, [((i + 1) % count, i) for i in range(count)])  3.59 us
    ppermute x4, starting transfers between devices, faces(): lax.ppermute(tail, axis, [(i, (i + 1) % count) for i in range(count)])  3.52 us
  transfers between devices with their start and end apart: 16, of which 11 were waited for; matrix products, arithmetic and copies ran while one was open for 10% of the time, Pallas kernels for 0%

profile of v3, /device:TPU:32, one launch (start us, length us, event | category | flops | bytes accessed | tf_op | source)
XLA Modules:
  0.0 90.5 jit_solution(10857641036622004985)
XLA Ops:
  0.6 1.4 %fusion.54 = (f32[64,2,8,128]{3,2,1,0:T(8,128)S(1)}, f32[64,2,8,128]{3,2,1,0:T(8,128)S(1)}) fusion(f32[64,4,8,128]{3,2,1,0:T(8,128)} %param.2), kind=kLoop, calls=%fused_computation.88 | loop fusion | bytes 2097152 | tf_op jit(solution)/shard_map/slice | solution.py:12
  2.5 2.0 %collective-permute-start.3 = (f32[64,4,2,128]{3,0,2,1:T(8,128)S(1)}, f32[64,4,2,128]{3,0,2,1:T(8,128)S(1)}, u32[]{:S(2)}, u32[]{:S(2)}) collective-permute-start(f32[64,4,2,128]{3,0,2,1:T(8,128)S(1)} %copy.66), channel_id=1, source_target_pairs={{0,1},{1,2},{2,3},{3,4},{4,5},{5,6},{6,7},{7,0},{8,9},{9,10},{10,1... | collective-permute-start | bytes 786440 | tf_op jit(solution)/shard_map/ppermute | solution.py:14
  4.7 4.8 %collective-permute-start = (f32[64,2,8,128]{3,0,2,1:T(8,128)S(1)}, f32[64,2,8,128]{3,0,2,1:T(8,128)S(1)}, u32[]{:S(2)}, u32[]{:S(2)}) collective-permute-start(f32[64,2,8,128]{3,0,2,1:T(8,128)S(1)} %copy.69), channel_id=1, source_target_pairs={{8,0},{16,8},{24,16},{32,24},{40,32},{48,40},{56,48},{64,56},{72,6... | collective-permute-start | bytes 1572872 | tf_op jit(solution)/shard_map/ppermute | solution.py:15
  17.5 2.7 %broadcast_multiply_fusion = (f32[64,4,8,128]{3,0,2,1:T(8,128)S(1)}, f32[64,4,8,128]{3,0,2,1:T(8,128)S(1)}) fusion(f32[4,8,128]{2,1,0:T(8,128)S(1)} %copy-done.1, f32[64,4,8,2]{3,0,2,1:T(8,128)S(1)} %copy.76, f32[64,4,8,126]{3,0,2,1:T(8,128)S(1)} %copy.77, f32[64,4,8,126]{3,0,2,1:T(8,128)S(1)} %copy.74, f32[64,4,8,2]{3,0,2,1:T(8,128)S(1)} %copy.75, ...), kind=kLoop, calls=%fused_computation.66 | loop fusion | flops 7602176 | bytes 15745024 | tf_op jit(solution)/shard_map/div | solution.py:83
  21.1 4.1 %collective-permute-start.4 = (f32[64,2,8,128]{3,0,2,1:T(8,128)S(1)}, f32[64,2,8,128]{3,0,2,1:T(8,128)S(1)}, u32[]{:S(2)}, u32[]{:S(2)}) collective-permute-start(f32[64,2,8,128]{3,0,2,1:T(8,128)S(1)} %get-tuple-element.12), channel_id=1, source_target_pairs={{8,0},{16,8},{24,16},{32,24},{40,32},{48,40},{56,48},{64,56},{72,6... | collective-permute-start | bytes 1572872 | tf_op jit(solution)/shard_map/ppermute | solution.py:15
  25.8 1.4 %collective-permute-start.7 = (f32[64,4,2,128]{3,0,2,1:T(8,128)S(1)}, f32[64,4,2,128]{3,0,2,1:T(8,128)S(1)}, u32[]{:S(2)}, u32[]{:S(2)}) collective-permute-start(f32[64,4,2,128]{3,0,2,1:T(8,128)S(1)} %get-tuple-element.15), channel_id=1, source_target_pairs={{0,1},{1,2},{2,3},{3,4},{4,5},{5,6},{6,7},{7,0},{8,9},{9,10},{10,1... | collective-permute-start | bytes 786440 | tf_op jit(solution)/shard_map/ppermute | solution.py:14
  28.0 3.6 %collective-permute-done.6 = f32[64,4,2,128]{3,0,2,1:T(8,128)S(1)} collective-permute-done((f32[64,4,2,128]{3,0,2,1:T(8,128)S(1)}, f32[64,4,2,128]{3,0,2,1:T(8,128)S(1)}, u32[]{:S(2)}, u32[]{:S(2)}) %collective-permute-start.6) | collective-permute-done | bytes 262176 | tf_op jit(solution)/shard_map/ppermute | solution.py:15
  31.5 2.3 %collective-permute-done.7 = f32[64,4,2,128]{3,0,2,1:T(8,128)S(1)} collective-permute-done((f32[64,4,2,128]{3,0,2,1:T(8,128)S(1)}, f32[64,4,2,128]{3,0,2,1:T(8,128)S(1)}, u32[]{:S(2)}, u32[]{:S(2)}) %collective-permute-start.7) | collective-permute-done | bytes 262176 | tf_op jit(solution)/shard_map/ppermute | solution.py:14
  33.9 3.2 %collective-permute-done.5 = f32[64,2,8,128]{3,0,2,1:T(8,128)S(1)} collective-permute-done((f32[64,2,8,128]{3,0,2,1:T(8,128)S(1)}, f32[64,2,8,128]{3,0,2,1:T(8,128)S(1)}, u32[]{:S(2)}, u32[]{:S(2)}) %collective-permute-start.5) | collective-permute-done | bytes 524320 | tf_op jit(solution)/shard_map/ppermute | solution.py:14
  37.1 2.5 %fusion.13 = f32[64,4,8,128]{3,0,2,1:T(8,128)S(1)} fusion(f32[64,4,2,128]{3,0,2,1:T(8,128)S(1)} %collective-permute-done.7, f32[64,4,8,128]{3,0,2,1:T(8,128)S(1)} %get-tuple-element.2, f32[64,4,2,128]{3,0,2,1:T(8,128)S(1)} %collective-permute-done.6, f32[64,2,8,128]{3,0,2,1:T(8,128)S(1)} %collective-permute-done.5, ...), kind=kLoop, calls=%fused_computation.23 | loop fusion | flops 9961472 | bytes 9977856 | tf_op jit(solution)/shard_map/sub | solution.py:85
  39.6 1.0 %fusion.1 = f32[64,64]{1,0:T(8,128)S(1)} fusion(f32[64,4,8,128]{3,0,2,1:T(8,128)S(1)} %fusion.13), kind=kOutput, calls=%fused_computation.11 | convolution fusion | flops 201330688 | bytes 1064960 | tf_op jit(solution)/shard_map/dot_general | solution.py:90
  40.9 3.5 %collective-permute-done.8 = f32[32,128]{1,0:T(8,128)S(1)} collective-permute-done((f32[32,128]{1,0:T(8,128)S(1)}, f32[32,128]{1,0:T(8,128)S(1)}, u32[]{:S(2)}, u32[]{:S(2)}) %collective-permute-start.8) | collective-permute-done | bytes 16416 | tf_op jit(solution)/shard_map/ppermute | solution.py:77
  44.4 4.5 %collective-permute-start.9 = (f32[32,128]{1,0:T(8,128)S(1)}, f32[32,128]{1,0:T(8,128)S(1)}, u32[]{:S(2)}, u32[]{:S(2)}) collective-permute-start(f32[32,128]{1,0:T(8,128)S(1)} %add.107), channel_id=1, source_target_pairs={{0,2},{1,3},{2,0},{3,1},{4,6},{5,7},{6,4},{7,5},{8,10},{9,11},{10,... | collective-permute-start | bytes 49160 | tf_op jit(solution)/shard_map/ppermute | solution.py:77
  48.9 1.7 %collective-permute-done.9 = f32[32,128]{1,0:T(8,128)S(1)} collective-permute-done((f32[32,128]{1,0:T(8,128)S(1)}, f32[32,128]{1,0:T(8,128)S(1)}, u32[]{:S(2)}, u32[]{:S(2)}) %collective-permute-start.9) | collective-permute-done | bytes 16416 | tf_op jit(solution)/shard_map/ppermute | solution.py:77
  50.6 3.8 %collective-permute-start.10 = (f32[32,128]{1,0:T(8,128)S(1)}, f32[32,128]{1,0:T(8,128)S(1)}, u32[]{:S(2)}, u32[]{:S(2)}) collective-permute-start(f32[32,128]{1,0:T(8,128)S(1)} %add.108), channel_id=1, source_target_pairs={{0,4},{1,5},{2,6},{3,7},{4,0},{5,1},{6,2},{7,3},{8,12},{9,13},{10,... | collective-permute-start | bytes 49160 | tf_op jit(solution)/shard_map/ppermute | solution.py:77
  54.5 3.8 %collective-permute-done.10 = f32[32,128]{1,0:T(8,128)S(1)} collective-permute-done((f32[32,128]{1,0:T(8,128)S(1)}, f32[32,128]{1,0:T(8,128)S(1)}, u32[]{:S(2)}, u32[]{:S(2)}) %collective-permute-start.10) | collective-permute-done | bytes 16416 | tf_op jit(solution)/shard_map/ppermute | solution.py:77
  58.3 1.2 %collective-permute-done.11 = f32[32,128]{1,0:T(8,128)S(1)} collective-permute-done((f32[32,128]{1,0:T(8,128)S(1)}, f32[32,128]{1,0:T(8,128)S(1)}, u32[]{:S(2)}, u32[]{:S(2)}) %collective-permute-start.11) | collective-permute-done | bytes 16416 | tf_op jit(solution)/shard_map/ppermute | solution.py:77
  59.5 3.7 %collective-permute-done.12 = f32[32,128]{1,0:T(8,128)S(1)} collective-permute-done((f32[32,128]{1,0:T(8,128)S(1)}, f32[32,128]{1,0:T(8,128)S(1)}, u32[]{:S(2)}, u32[]{:S(2)}) %collective-permute-start.12) | collective-permute-done | bytes 16416 | tf_op jit(solution)/shard_map/ppermute | solution.py:77
  63.2 5.2 %collective-permute-done.13 = f32[32,128]{1,0:T(8,128)S(1)} collective-permute-done((f32[32,128]{1,0:T(8,128)S(1)}, f32[32,128]{1,0:T(8,128)S(1)}, u32[]{:S(2)}, u32[]{:S(2)}) %collective-permute-start.13) | collective-permute-done | bytes 16416 | tf_op jit(solution)/shard_map/ppermute | solution.py:77
  68.5 3.7 %collective-permute-done.14 = f32[32,128]{1,0:T(8,128)S(1)} collective-permute-done((f32[32,128]{1,0:T(8,128)S(1)}, f32[32,128]{1,0:T(8,128)S(1)}, u32[]{:S(2)}, u32[]{:S(2)}) %collective-permute-start.14) | collective-permute-done | bytes 16416 | tf_op jit(solution)/shard_map/ppermute | solution.py:77
  72.8 4.6 %collective-permute-done.15 = f32[32,128]{1,0:T(8,128)S(1)} collective-permute-done((f32[32,128]{1,0:T(8,128)S(1)}, f32[32,128]{1,0:T(8,128)S(1)}, u32[]{:S(2)}, u32[]{:S(2)}) %collective-permute-start.15) | collective-permute-done | bytes 16416 | tf_op jit(solution)/shard_map/ppermute | solution.py:77
  78.3 8.6 %shard_map.41 = f32[64,128]{1,0:T(8,128)} custom-call(f32[64,128]{1,0:T(8,128)} %pad_maximum_fusion.4.aug_ref), custom_call_target="tpu_custom_call" | custom-call | tf_op jit(solution)/shard_map/pallas_call | solution.py:62
  87.0 2.3 %fusion = f32[8,8,32,128]{3,1,2,0:T(8,128)S(1)} fusion(f32[8,8,32,128]{3,2,1,0:T(8,128)S(1)} %bitcast.22, f32[64,128]{1,0:T(8,128)} %shard_map.41), kind=kOutput, calls=%fused_computation.5 | convolution fusion | flops 201588736 | bytes 2129920 | tf_op jit(solution)/shard_map/dot_general | solution.py:96
  89.3 1.2 %copy.55 = f32[8,8,32,128]{3,2,1,0:T(8,128)} copy(f32[8,8,32,128]{3,1,2,0:T(8,128)S(1)} %fusion) | data formatting | bytes 2097152
  (63 shorter events, 12.5 us)
Async XLA Ops:
  0.6 1.7 %copy-start = (f32[64,4,8,128]{3,2,1,0:T(8,128)S(1)}, f32[64,4,8,128]{3,2,1,0:T(8,128)}, u32[]{:S(2)}) copy-start(f32[64,4,8,128]{3,2,1,0:T(8,128)} %param.2) | copy-start | bytes 3145732
  2.2 14.5 %collective-permute-start.1 = (f32[64,2,8,128]{3,0,2,1:T(8,128)S(1)}, f32[64,2,8,128]{3,0,2,1:T(8,128)S(1)}, u32[]{:S(2)}, u32[]{:S(2)}) collective-permute-start(f32[64,2,8,128]{3,0,2,1:T(8,128)S(1)} %copy.68), channel_id=1, source_target_pairs={{0,8},{8,16},{16,24},{24,32},{32,40},{40,48},{48,56},{56,64},{64,7... | collective-permute-start | bytes 1572872 | tf_op jit(solution)/shard_map/ppermute | solution.py:14
  2.5 14.1 %collective-permute-start.3 = (f32[64,4,2,128]{3,0,2,1:T(8,128)S(1)}, f32[64,4,2,128]{3,0,2,1:T(8,128)S(1)}, u32[]{:S(2)}, u32[]{:S(2)}) collective-permute-start(f32[64,4,2,128]{3,0,2,1:T(8,128)S(1)} %copy.66), channel_id=1, source_target_pairs={{0,1},{1,2},{2,3},{3,4},{4,5},{5,6},{6,7},{7,0},{8,9},{9,10},{10,1... | collective-permute-start | bytes 786440 | tf_op jit(solution)/shard_map/ppermute | solution.py:14
  4.7 12.7 %collective-permute-start = (f32[64,2,8,128]{3,0,2,1:T(8,128)S(1)}, f32[64,2,8,128]{3,0,2,1:T(8,128)S(1)}, u32[]{:S(2)}, u32[]{:S(2)}) collective-permute-start(f32[64,2,8,128]{3,0,2,1:T(8,128)S(1)} %copy.69), channel_id=1, source_target_pairs={{8,0},{16,8},{24,16},{32,24},{40,32},{48,40},{56,48},{64,56},{72,6... | collective-permute-start | bytes 1572872 | tf_op jit(solution)/shard_map/ppermute | solution.py:15
  9.6 7.9 %collective-permute-start.2 = (f32[64,4,2,128]{3,0,2,1:T(8,128)S(1)}, f32[64,4,2,128]{3,0,2,1:T(8,128)S(1)}, u32[]{:S(2)}, u32[]{:S(2)}) collective-permute-start(f32[64,4,2,128]{3,0,2,1:T(8,128)S(1)} %copy.67), channel_id=1, source_target_pairs={{1,0},{2,1},{3,2},{4,3},{5,4},{6,5},{7,6},{0,7},{9,8},{10,9},{11,1... | collective-permute-start | bytes 786440 | tf_op jit(solution)/shard_map/ppermute | solution.py:15
  15.9 0.7 copy-start.1
  21.1 12.8 %collective-permute-start.4 = (f32[64,2,8,128]{3,0,2,1:T(8,128)S(1)}, f32[64,2,8,128]{3,0,2,1:T(8,128)S(1)}, u32[]{:S(2)}, u32[]{:S(2)}) collective-permute-start(f32[64,2,8,128]{3,0,2,1:T(8,128)S(1)} %get-tuple-element.12), channel_id=1, source_target_pairs={{8,0},{16,8},{24,16},{32,24},{40,32},{48,40},{56,48},{64,56},{72,6... | collective-permute-start | bytes 1572872 | tf_op jit(solution)/shard_map/ppermute | solution.py:15
  25.2 11.9 %collective-permute-start.5 = (f32[64,2,8,128]{3,0,2,1:T(8,128)S(1)}, f32[64,2,8,128]{3,0,2,1:T(8,128)S(1)}, u32[]{:S(2)}, u32[]{:S(2)}) collective-permute-start(f32[64,2,8,128]{3,0,2,1:T(8,128)S(1)} %get-tuple-element.13), channel_id=1, source_target_pairs={{0,8},{8,16},{16,24},{24,32},{32,40},{40,48},{48,56},{56,64},{64,7... | collective-permute-start | bytes 1572872 | tf_op jit(solution)/shard_map/ppermute | solution.py:14
  25.2 6.4 %collective-permute-start.6 = (f32[64,4,2,128]{3,0,2,1:T(8,128)S(1)}, f32[64,4,2,128]{3,0,2,1:T(8,128)S(1)}, u32[]{:S(2)}, u32[]{:S(2)}) collective-permute-start(f32[64,4,2,128]{3,0,2,1:T(8,128)S(1)} %get-tuple-element.14), channel_id=1, source_target_pairs={{1,0},{2,1},{3,2},{4,3},{5,4},{6,5},{7,6},{0,7},{9,8},{10,9},{11,1... | collective-permute-start | bytes 786440 | tf_op jit(solution)/shard_map/ppermute | solution.py:15
  25.8 8.1 %collective-permute-start.7 = (f32[64,4,2,128]{3,0,2,1:T(8,128)S(1)}, f32[64,4,2,128]{3,0,2,1:T(8,128)S(1)}, u32[]{:S(2)}, u32[]{:S(2)}) collective-permute-start(f32[64,4,2,128]{3,0,2,1:T(8,128)S(1)} %get-tuple-element.15), channel_id=1, source_target_pairs={{0,1},{1,2},{2,3},{3,4},{4,5},{5,6},{6,7},{7,0},{8,9},{9,10},{10,1... | collective-permute-start | bytes 786440 | tf_op jit(solution)/shard_map/ppermute | solution.py:14
  40.6 3.8 %collective-permute-start.8 = (f32[32,128]{1,0:T(8,128)S(1)}, f32[32,128]{1,0:T(8,128)S(1)}, u32[]{:S(2)}, u32[]{:S(2)}) collective-permute-start(f32[32,128]{1,0:T(8,128)S(1)} %reshape.17), channel_id=1, source_target_pairs={{0,1},{1,0},{2,3},{3,2},{4,5},{5,4},{6,7},{7,6},{8,9},{9,8},{10,11... | collective-permute-start | bytes 49160 | tf_op jit(solution)/shard_map/ppermute | solution.py:77
  44.4 6.2 %collective-permute-start.9 = (f32[32,128]{1,0:T(8,128)S(1)}, f32[32,128]{1,0:T(8,128)S(1)}, u32[]{:S(2)}, u32[]{:S(2)}) collective-permute-start(f32[32,128]{1,0:T(8,128)S(1)} %add.107), channel_id=1, source_target_pairs={{0,2},{1,3},{2,0},{3,1},{4,6},{5,7},{6,4},{7,5},{8,10},{9,11},{10,... | collective-permute-start | bytes 49160 | tf_op jit(solution)/shard_map/ppermute | solution.py:77
  50.6 7.6 %collective-permute-start.10 = (f32[32,128]{1,0:T(8,128)S(1)}, f32[32,128]{1,0:T(8,128)S(1)}, u32[]{:S(2)}, u32[]{:S(2)}) collective-permute-start(f32[32,128]{1,0:T(8,128)S(1)} %add.108), channel_id=1, source_target_pairs={{0,4},{1,5},{2,6},{3,7},{4,0},{5,1},{6,2},{7,3},{8,12},{9,13},{10,... | collective-permute-start | bytes 49160 | tf_op jit(solution)/shard_map/ppermute | solution.py:77
  58.3 1.2 %collective-permute-start.11 = (f32[32,128]{1,0:T(8,128)S(1)}, f32[32,128]{1,0:T(8,128)S(1)}, u32[]{:S(2)}, u32[]{:S(2)}) collective-permute-start(f32[32,128]{1,0:T(8,128)S(1)} %add.109), channel_id=1, source_target_pairs={{0,8},{8,0},{16,24},{24,16},{32,40},{40,32},{48,56},{56,48},{64,72... | collective-permute-start | bytes 49160 | tf_op jit(solution)/shard_map/ppermute | solution.py:77
  59.5 3.7 %collective-permute-start.12 = (f32[32,128]{1,0:T(8,128)S(1)}, f32[32,128]{1,0:T(8,128)S(1)}, u32[]{:S(2)}, u32[]{:S(2)}) collective-permute-start(f32[32,128]{1,0:T(8,128)S(1)} %add.110), channel_id=1, source_target_pairs={{0,16},{8,24},{16,0},{24,8},{32,48},{40,56},{48,32},{56,40},{64,80... | collective-permute-start | bytes 49160 | tf_op jit(solution)/shard_map/ppermute | solution.py:77
  63.2 5.2 %collective-permute-start.13 = (f32[32,128]{1,0:T(8,128)S(1)}, f32[32,128]{1,0:T(8,128)S(1)}, u32[]{:S(2)}, u32[]{:S(2)}) collective-permute-start(f32[32,128]{1,0:T(8,128)S(1)} %add.111), channel_id=1, source_target_pairs={{0,32},{8,40},{16,48},{24,56},{32,0},{40,8},{48,16},{56,24},{64,96... | collective-permute-start | bytes 49160 | tf_op jit(solution)/shard_map/ppermute | solution.py:77
  68.5 3.7 %collective-permute-start.14 = (f32[32,128]{1,0:T(8,128)S(1)}, f32[32,128]{1,0:T(8,128)S(1)}, u32[]{:S(2)}, u32[]{:S(2)}) collective-permute-start(f32[32,128]{1,0:T(8,128)S(1)} %add.112), channel_id=1, source_target_pairs={{0,64},{8,72},{16,80},{24,88},{32,96},{40,104},{48,112},{56,120},{... | collective-permute-start | bytes 49160 | tf_op jit(solution)/shard_map/ppermute | solution.py:77
  72.2 5.2 %collective-permute-start.15 = (f32[32,128]{1,0:T(8,128)S(1)}, f32[32,128]{1,0:T(8,128)S(1)}, u32[]{:S(2)}, u32[]{:S(2)}) collective-permute-start(f32[32,128]{1,0:T(8,128)S(1)} %add.113), channel_id=1, source_target_pairs={{0,128},{8,136},{16,144},{24,152},{32,160},{40,168},{48,176},{56,1... | collective-permute-start | bytes 49160 | tf_op jit(solution)/shard_map/ppermute | solution.py:77

commit v4 on v3

--- a/solution.py
+++ b/solution.py
@@ -37,13 +37,12 @@
     lane = lax.broadcasted_iota(jnp.int32, blocks[0].shape, 1)
     for k in range(order):
         home, place = divmod(k, 8)
-        row = jnp.sum(jnp.where(sub == place, blocks[home], 0.0), axis=0, keepdims=True)
-        pivot = jnp.sum(jnp.where(lane[:1] == k, row, 0.0), axis=1, keepdims=True)
-        scale = 1.0 / jnp.sqrt(pivot)
+        row = blocks[home][place:place + 1, :]
+        scale = 1.0 / jnp.sqrt(row[:, k:k + 1])
         scaled = row * scale
         for j in range(home, groups):
             block = blocks[j]
-            column = jnp.sum(jnp.where(lane == k, block, 0.0), axis=1, keepdims=True) * scale
+            column = block[:, k:k + 1] * scale
             if j == home:
                 column = jnp.where(sub[:, :1] > place, column, 0.0)
                 block = jnp.where(sub == place, scaled, block - column * scaled)
@@ -83,20 +82,22 @@
     first = (apply_ham(orbitals, potential) - 5.5 * orbitals) / 4.5
     applied = apply_ham(first, potential)
     filtered = 2.0 * (applied - 5.5 * first) / 4.5 - orbitals
-    width = filtered.shape[0]
-    flat = filtered.reshape(width, -1)
-    cells = flat.shape[1] * lax.axis_size("gx") * lax.axis_size("gy")
+    count = filtered.shape[1] * filtered.shape[2] * filtered.shape[3]
+    cells = count * lax.axis_size("gx") * lax.axis_size("gy")
     local_gram = (
-        jnp.dot(flat, flat.T, precision=lax.Precision.HIGHEST, preferred_element_type=jnp.float32)
+        jnp.einsum(
+            "kxyz,mxyz->km", filtered, filtered,
+            precision=lax.Precision.HIGHEST, preferred_element_type=jnp.float32,
+        )
         / cells
     )
     packed = local_gram.reshape(-1, 128)
     gram = butterfly_sum(butterfly_sum(packed, "gy"), "gx").reshape(local_gram.shape)
     factor, lower_inverse = factor_and_inverse(gram)
-    solved = jnp.dot(
-        lower_inverse, flat, precision=lax.Precision.HIGHEST, preferred_element_type=jnp.float32
+    basis = jnp.einsum(
+        "mk,kxyz->mxyz", lower_inverse * jnp.sqrt(jnp.float32(cells)), filtered,
+        precision=lax.Precision.HIGHEST, preferred_element_type=jnp.float32,
     )
-    basis = (solved * jnp.sqrt(jnp.float32(cells))).reshape(filtered.shape)
     return (basis, factor)
 
 

time: 90.8 us -> 89.4 us (0.985)
  Pallas kernels: 8.65 us -> 7.58 us
    pallas_call x1, Pallas kernels: 8.65 us -> 7.58 us  [factor_and_inverse(): pl.pallas_call(factor_kernel, out_shape=jax.ShapeDtypeStruct(aug.shape, j...]
  transfers between devices with their start and end apart: 16 -> 16, of which waited for: 11 -> 11; matrix products, arithmetic and copies ran while one was open for 10% -> 9% of each run, Pallas kernels for 0% -> 0%
where the time goes in v4:
time: 89.4 us; the launch traced here: 89.1 us
  waiting for transfers between devices  37.3 us (42%)
  starting transfers between devices  22.1 us (25%)
  local copies, waits for them, and re-layouts  12.7 us (14%)
  Pallas kernels  7.58 us (8%)
  other arithmetic  5.77 us (6%)
  matrix products  2.76 us (3%)
  between operations  0.96 us (1%)
    ppermute x8, waiting for transfers between devices, butterfly_sum(): lax.ppermute(value, axis, [(i, i ^ mask) for i in range(count)])  28.1 us
    ppermute x4, starting transfers between devices, faces(): lax.ppermute(head, axis, [((i + 1) % count, i) for i in range(count)])  10 us
    ppermute x8, starting transfers between devices, butterfly_sum(): lax.ppermute(value, axis, [(i, i ^ mask) for i in range(count)])  8.58 us
    unnamed x20, local copies, waits for them, and re-layouts  7.76 us
    pallas_call x1, Pallas kernels, factor_and_inverse(): pl.pallas_call(factor_kernel, out_shape=jax.ShapeDtypeStruct(aug.shape, j...  7.58 us
    ppermute x4, waiting for transfers between devices, faces(): lax.ppermute(tail, axis, [(i, (i + 1) % count) for i in range(count)])  5.55 us
    ppermute x4, waiting for transfers between devices, faces(): lax.ppermute(head, axis, [((i + 1) % count, i) for i in range(count)])  3.59 us
    ppermute x4, starting transfers between devices, faces(): lax.ppermute(tail, axis, [(i, (i + 1) % count) for i in range(count)])  3.52 us
  transfers between devices with their start and end apart: 16, of which 11 were waited for; matrix products, arithmetic and copies ran while one was open for 9% of the time, Pallas kernels for 0%

profile of v4, /device:TPU:32, one launch (start us, length us, event | category | flops | bytes accessed | tf_op | source)
XLA Modules:
  0.0 89.1 jit_solution(16265428521283747602)
XLA Ops:
  0.6 1.4 %fusion.55 = (f32[64,2,8,128]{3,2,1,0:T(8,128)S(1)}, f32[64,2,8,128]{3,2,1,0:T(8,128)S(1)}) fusion(f32[64,4,8,128]{3,2,1,0:T(8,128)} %param.2), kind=kLoop, calls=%fused_computation.88 | loop fusion | bytes 2097152 | tf_op jit(solution)/shard_map/slice | solution.py:12
  2.5 2.0 %collective-permute-start.3 = (f32[64,4,2,128]{3,0,2,1:T(8,128)S(1)}, f32[64,4,2,128]{3,0,2,1:T(8,128)S(1)}, u32[]{:S(2)}, u32[]{:S(2)}) collective-permute-start(f32[64,4,2,128]{3,0,2,1:T(8,128)S(1)} %copy.44), channel_id=1, source_target_pairs={{0,1},{1,2},{2,3},{3,4},{4,5},{5,6},{6,7},{7,0},{8,9},{9,10},{10,1... | collective-permute-start | bytes 786440 | tf_op jit(solution)/shard_map/ppermute | solution.py:14
  4.7 4.8 %collective-permute-start = (f32[64,2,8,128]{3,0,2,1:T(8,128)S(1)}, f32[64,2,8,128]{3,0,2,1:T(8,128)S(1)}, u32[]{:S(2)}, u32[]{:S(2)}) collective-permute-start(f32[64,2,8,128]{3,0,2,1:T(8,128)S(1)} %copy.47), channel_id=1, source_target_pairs={{8,0},{16,8},{24,16},{32,24},{40,32},{48,40},{56,48},{64,56},{72,6... | collective-permute-start | bytes 1572872 | tf_op jit(solution)/shard_map/ppermute | solution.py:15
  17.5 2.5 %broadcast_multiply_fusion = (f32[64,4,8,128]{3,0,2,1:T(8,128)S(1)}, f32[64,4,8,128]{3,0,2,1:T(8,128)S(1)}) fusion(f32[4,8,128]{2,1,0:T(8,128)S(1)} %copy-done.1, f32[64,4,8,2]{3,0,2,1:T(8,128)S(1)} %copy.54, f32[64,4,8,126]{3,0,2,1:T(8,128)S(1)} %copy.55, f32[64,4,8,126]{3,0,2,1:T(8,128)S(1)} %copy.52, f32[64,4,8,2]{3,0,2,1:T(8,128)S(1)} %copy.53, ...), kind=kLoop, calls=%fused_computation.62 | loop fusion | flops 7602176 | bytes 15745024 | tf_op jit(solution)/shard_map/div | solution.py:82
  20.9 4.1 %collective-permute-start.4 = (f32[64,2,8,128]{3,0,2,1:T(8,128)S(1)}, f32[64,2,8,128]{3,0,2,1:T(8,128)S(1)}, u32[]{:S(2)}, u32[]{:S(2)}) collective-permute-start(f32[64,2,8,128]{3,0,2,1:T(8,128)S(1)} %get-tuple-element.18), channel_id=1, source_target_pairs={{8,0},{16,8},{24,16},{32,24},{40,32},{48,40},{56,48},{64,56},{72,6... | collective-permute-start | bytes 1572872 | tf_op jit(solution)/shard_map/ppermute | solution.py:15
  25.6 1.4 %collective-permute-start.7 = (f32[64,4,2,128]{3,0,2,1:T(8,128)S(1)}, f32[64,4,2,128]{3,0,2,1:T(8,128)S(1)}, u32[]{:S(2)}, u32[]{:S(2)}) collective-permute-start(f32[64,4,2,128]{3,0,2,1:T(8,128)S(1)} %get-tuple-element.21), channel_id=1, source_target_pairs={{0,1},{1,2},{2,3},{3,4},{4,5},{5,6},{6,7},{7,0},{8,9},{9,10},{10,1... | collective-permute-start | bytes 786440 | tf_op jit(solution)/shard_map/ppermute | solution.py:14
  27.8 3.6 %collective-permute-done.6 = f32[64,4,2,128]{3,0,2,1:T(8,128)S(1)} collective-permute-done((f32[64,4,2,128]{3,0,2,1:T(8,128)S(1)}, f32[64,4,2,128]{3,0,2,1:T(8,128)S(1)}, u32[]{:S(2)}, u32[]{:S(2)}) %collective-permute-start.6) | collective-permute-done | bytes 262176 | tf_op jit(solution)/shard_map/ppermute | solution.py:15
  31.4 2.3 %collective-permute-done.7 = f32[64,4,2,128]{3,0,2,1:T(8,128)S(1)} collective-permute-done((f32[64,4,2,128]{3,0,2,1:T(8,128)S(1)}, f32[64,4,2,128]{3,0,2,1:T(8,128)S(1)}, u32[]{:S(2)}, u32[]{:S(2)}) %collective-permute-start.7) | collective-permute-done | bytes 262176 | tf_op jit(solution)/shard_map/ppermute | solution.py:14
  33.7 3.2 %collective-permute-done.5 = f32[64,2,8,128]{3,0,2,1:T(8,128)S(1)} collective-permute-done((f32[64,2,8,128]{3,0,2,1:T(8,128)S(1)}, f32[64,2,8,128]{3,0,2,1:T(8,128)S(1)}, u32[]{:S(2)}, u32[]{:S(2)}) %collective-permute-start.5) | collective-permute-done | bytes 524320 | tf_op jit(solution)/shard_map/ppermute | solution.py:14
  37.0 2.5 %fusion.12 = f32[64,4,8,128]{3,0,2,1:T(8,128)S(1)} fusion(f32[64,4,2,128]{3,0,2,1:T(8,128)S(1)} %collective-permute-done.7, f32[64,4,8,128]{3,0,2,1:T(8,128)S(1)} %get-tuple-element.8, f32[64,4,2,128]{3,0,2,1:T(8,128)S(1)} %collective-permute-done.6, f32[64,2,8,128]{3,0,2,1:T(8,128)S(1)} %collective-permute-done.5, ...), kind=kLoop, calls=%fused_computation.21 | loop fusion | flops 9961472 | bytes 9977856 | tf_op jit(solution)/shard_map/sub | solution.py:84
  39.5 1.0 %fusion = f32[64,64]{1,0:T(8,128)S(1)} fusion(f32[64,4,8,128]{3,0,2,1:T(8,128)S(1)} %fusion.12), kind=kOutput, calls=%fused_computation.9 | convolution fusion | flops 201330688 | bytes 1064960 | tf_op jit(solution)/shard_map/kxyz,mxyz->km/dot_general | solution.py:88
  40.8 3.5 %collective-permute-done.8 = f32[32,128]{1,0:T(8,128)S(1)} collective-permute-done((f32[32,128]{1,0:T(8,128)S(1)}, f32[32,128]{1,0:T(8,128)S(1)}, u32[]{:S(2)}, u32[]{:S(2)}) %collective-permute-start.8) | collective-permute-done | bytes 16416 | tf_op jit(solution)/shard_map/ppermute | solution.py:76
  44.3 4.5 %collective-permute-start.9 = (f32[32,128]{1,0:T(8,128)S(1)}, f32[32,128]{1,0:T(8,128)S(1)}, u32[]{:S(2)}, u32[]{:S(2)}) collective-permute-start(f32[32,128]{1,0:T(8,128)S(1)} %add.107), channel_id=1, source_target_pairs={{0,2},{1,3},{2,0},{3,1},{4,6},{5,7},{6,4},{7,5},{8,10},{9,11},{10,... | collective-permute-start | bytes 49160 | tf_op jit(solution)/shard_map/ppermute | solution.py:76
  48.8 1.7 %collective-permute-done.9 = f32[32,128]{1,0:T(8,128)S(1)} collective-permute-done((f32[32,128]{1,0:T(8,128)S(1)}, f32[32,128]{1,0:T(8,128)S(1)}, u32[]{:S(2)}, u32[]{:S(2)}) %collective-permute-start.9) | collective-permute-done | bytes 16416 | tf_op jit(solution)/shard_map/ppermute | solution.py:76
  50.5 3.8 %collective-permute-start.10 = (f32[32,128]{1,0:T(8,128)S(1)}, f32[32,128]{1,0:T(8,128)S(1)}, u32[]{:S(2)}, u32[]{:S(2)}) collective-permute-start(f32[32,128]{1,0:T(8,128)S(1)} %add.108), channel_id=1, source_target_pairs={{0,4},{1,5},{2,6},{3,7},{4,0},{5,1},{6,2},{7,3},{8,12},{9,13},{10,... | collective-permute-start | bytes 49160 | tf_op jit(solution)/shard_map/ppermute | solution.py:76
  54.3 3.8 %collective-permute-done.10 = f32[32,128]{1,0:T(8,128)S(1)} collective-permute-done((f32[32,128]{1,0:T(8,128)S(1)}, f32[32,128]{1,0:T(8,128)S(1)}, u32[]{:S(2)}, u32[]{:S(2)}) %collective-permute-start.10) | collective-permute-done | bytes 16416 | tf_op jit(solution)/shard_map/ppermute | solution.py:76
  58.1 1.2 %collective-permute-done.11 = f32[32,128]{1,0:T(8,128)S(1)} collective-permute-done((f32[32,128]{1,0:T(8,128)S(1)}, f32[32,128]{1,0:T(8,128)S(1)}, u32[]{:S(2)}, u32[]{:S(2)}) %collective-permute-start.11) | collective-permute-done | bytes 16416 | tf_op jit(solution)/shard_map/ppermute | solution.py:76
  59.3 3.7 %collective-permute-done.12 = f32[32,128]{1,0:T(8,128)S(1)} collective-permute-done((f32[32,128]{1,0:T(8,128)S(1)}, f32[32,128]{1,0:T(8,128)S(1)}, u32[]{:S(2)}, u32[]{:S(2)}) %collective-permute-start.12) | collective-permute-done | bytes 16416 | tf_op jit(solution)/shard_map/ppermute | solution.py:76
  63.1 5.2 %collective-permute-done.13 = f32[32,128]{1,0:T(8,128)S(1)} collective-permute-done((f32[32,128]{1,0:T(8,128)S(1)}, f32[32,128]{1,0:T(8,128)S(1)}, u32[]{:S(2)}, u32[]{:S(2)}) %collective-permute-start.13) | collective-permute-done | bytes 16416 | tf_op jit(solution)/shard_map/ppermute | solution.py:76
  68.3 3.7 %collective-permute-done.14 = f32[32,128]{1,0:T(8,128)S(1)} collective-permute-done((f32[32,128]{1,0:T(8,128)S(1)}, f32[32,128]{1,0:T(8,128)S(1)}, u32[]{:S(2)}, u32[]{:S(2)}) %collective-permute-start.14) | collective-permute-done | bytes 16416 | tf_op jit(solution)/shard_map/ppermute | solution.py:76
  72.1 5.2 %collective-permute-done.15 = f32[32,128]{1,0:T(8,128)S(1)} collective-permute-done((f32[32,128]{1,0:T(8,128)S(1)}, f32[32,128]{1,0:T(8,128)S(1)}, u32[]{:S(2)}, u32[]{:S(2)}) %collective-permute-start.15) | collective-permute-done | bytes 16416 | tf_op jit(solution)/shard_map/ppermute | solution.py:76
  78.2 7.6 %shard_map.41 = f32[64,128]{1,0:T(8,128)} custom-call(f32[64,128]{1,0:T(8,128)} %pad_maximum_fusion.4.aug_ref), custom_call_target="tpu_custom_call" | custom-call | tf_op jit(solution)/shard_map/pallas_call | solution.py:61
  85.8 1.8 %fusion.42 = f32[64,4,8,128]{3,0,2,1:T(8,128)S(1)} fusion(f32[64,4,8,128]{3,0,2,1:T(8,128)S(1)} %fusion.12, f32[64,128]{1,0:T(8,128)} %shard_map.41), kind=kOutput, calls=%fused_computation.65 | convolution fusion | flops 201330688 | bytes 2129920 | tf_op jit(solution)/shard_map/mk,kxyz->mxyz/dot_general | solution.py:97
  87.6 1.6 %copy.35 = f32[64,4,8,128]{3,2,1,0:T(8,128)} copy(f32[64,4,8,128]{3,0,2,1:T(8,128)S(1)} %fusion.42) | data formatting | bytes 2097152
  (62 shorter events, 11.9 us)
Async XLA Ops:
  0.6 1.7 %copy-start = (f32[64,4,8,128]{3,2,1,0:T(8,128)S(1)}, f32[64,4,8,128]{3,2,1,0:T(8,128)}, u32[]{:S(2)}) copy-start(f32[64,4,8,128]{3,2,1,0:T(8,128)} %param.2) | copy-start | bytes 3145732
  2.2 14.5 %collective-permute-start.1 = (f32[64,2,8,128]{3,0,2,1:T(8,128)S(1)}, f32[64,2,8,128]{3,0,2,1:T(8,128)S(1)}, u32[]{:S(2)}, u32[]{:S(2)}) collective-permute-start(f32[64,2,8,128]{3,0,2,1:T(8,128)S(1)} %copy.46), channel_id=1, source_target_pairs={{0,8},{8,16},{16,24},{24,32},{32,40},{40,48},{48,56},{56,64},{64,7... | collective-permute-start | bytes 1572872 | tf_op jit(solution)/shard_map/ppermute | solution.py:14
  2.5 14.1 %collective-permute-start.3 = (f32[64,4,2,128]{3,0,2,1:T(8,128)S(1)}, f32[64,4,2,128]{3,0,2,1:T(8,128)S(1)}, u32[]{:S(2)}, u32[]{:S(2)}) collective-permute-start(f32[64,4,2,128]{3,0,2,1:T(8,128)S(1)} %copy.44), channel_id=1, source_target_pairs={{0,1},{1,2},{2,3},{3,4},{4,5},{5,6},{6,7},{7,0},{8,9},{9,10},{10,1... | collective-permute-start | bytes 786440 | tf_op jit(solution)/shard_map/ppermute | solution.py:14
  4.7 12.7 %collective-permute-start = (f32[64,2,8,128]{3,0,2,1:T(8,128)S(1)}, f32[64,2,8,128]{3,0,2,1:T(8,128)S(1)}, u32[]{:S(2)}, u32[]{:S(2)}) collective-permute-start(f32[64,2,8,128]{3,0,2,1:T(8,128)S(1)} %copy.47), channel_id=1, source_target_pairs={{8,0},{16,8},{24,16},{32,24},{40,32},{48,40},{56,48},{64,56},{72,6... | collective-permute-start | bytes 1572872 | tf_op jit(solution)/shard_map/ppermute | solution.py:15
  9.6 7.9 %collective-permute-start.2 = (f32[64,4,2,128]{3,0,2,1:T(8,128)S(1)}, f32[64,4,2,128]{3,0,2,1:T(8,128)S(1)}, u32[]{:S(2)}, u32[]{:S(2)}) collective-permute-start(f32[64,4,2,128]{3,0,2,1:T(8,128)S(1)} %copy.45), channel_id=1, source_target_pairs={{1,0},{2,1},{3,2},{4,3},{5,4},{6,5},{7,6},{0,7},{9,8},{10,9},{11,1... | collective-permute-start | bytes 786440 | tf_op jit(solution)/shard_map/ppermute | solution.py:15
  15.9 0.7 copy-start.1
  20.9 12.8 %collective-permute-start.4 = (f32[64,2,8,128]{3,0,2,1:T(8,128)S(1)}, f32[64,2,8,128]{3,0,2,1:T(8,128)S(1)}, u32[]{:S(2)}, u32[]{:S(2)}) collective-permute-start(f32[64,2,8,128]{3,0,2,1:T(8,128)S(1)} %get-tuple-element.18), channel_id=1, source_target_pairs={{8,0},{16,8},{24,16},{32,24},{40,32},{48,40},{56,48},{64,56},{72,6... | collective-permute-start | bytes 1572872 | tf_op jit(solution)/shard_map/ppermute | solution.py:15
  25.0 11.9 %collective-permute-start.5 = (f32[64,2,8,128]{3,0,2,1:T(8,128)S(1)}, f32[64,2,8,128]{3,0,2,1:T(8,128)S(1)}, u32[]{:S(2)}, u32[]{:S(2)}) collective-permute-start(f32[64,2,8,128]{3,0,2,1:T(8,128)S(1)} %get-tuple-element.19), channel_id=1, source_target_pairs={{0,8},{8,16},{16,24},{24,32},{32,40},{40,48},{48,56},{56,64},{64,7... | collective-permute-start | bytes 1572872 | tf_op jit(solution)/shard_map/ppermute | solution.py:14
  25.0 6.4 %collective-permute-start.6 = (f32[64,4,2,128]{3,0,2,1:T(8,128)S(1)}, f32[64,4,2,128]{3,0,2,1:T(8,128)S(1)}, u32[]{:S(2)}, u32[]{:S(2)}) collective-permute-start(f32[64,4,2,128]{3,0,2,1:T(8,128)S(1)} %get-tuple-element.20), channel_id=1, source_target_pairs={{1,0},{2,1},{3,2},{4,3},{5,4},{6,5},{7,6},{0,7},{9,8},{10,9},{11,1... | collective-permute-start | bytes 786440 | tf_op jit(solution)/shard_map/ppermute | solution.py:15
  25.6 8.1 %collective-permute-start.7 = (f32[64,4,2,128]{3,0,2,1:T(8,128)S(1)}, f32[64,4,2,128]{3,0,2,1:T(8,128)S(1)}, u32[]{:S(2)}, u32[]{:S(2)}) collective-permute-start(f32[64,4,2,128]{3,0,2,1:T(8,128)S(1)} %get-tuple-element.21), channel_id=1, source_target_pairs={{0,1},{1,2},{2,3},{3,4},{4,5},{5,6},{6,7},{7,0},{8,9},{9,10},{10,1... | collective-permute-start | bytes 786440 | tf_op jit(solution)/shard_map/ppermute | solution.py:14
  40.5 3.8 %collective-permute-start.8 = (f32[32,128]{1,0:T(8,128)S(1)}, f32[32,128]{1,0:T(8,128)S(1)}, u32[]{:S(2)}, u32[]{:S(2)}) collective-permute-start(f32[32,128]{1,0:T(8,128)S(1)} %reshape.11), channel_id=1, source_target_pairs={{0,1},{1,0},{2,3},{3,2},{4,5},{5,4},{6,7},{7,6},{8,9},{9,8},{10,11... | collective-permute-start | bytes 49160 | tf_op jit(solution)/shard_map/ppermute | solution.py:76
  44.3 6.2 %collective-permute-start.9 = (f32[32,128]{1,0:T(8,128)S(1)}, f32[32,128]{1,0:T(8,128)S(1)}, u32[]{:S(2)}, u32[]{:S(2)}) collective-permute-start(f32[32,128]{1,0:T(8,128)S(1)} %add.107), channel_id=1, source_target_pairs={{0,2},{1,3},{2,0},{3,1},{4,6},{5,7},{6,4},{7,5},{8,10},{9,11},{10,... | collective-permute-start | bytes 49160 | tf_op jit(solution)/shard_map/ppermute | solution.py:76
  50.5 7.6 %collective-permute-start.10 = (f32[32,128]{1,0:T(8,128)S(1)}, f32[32,128]{1,0:T(8,128)S(1)}, u32[]{:S(2)}, u32[]{:S(2)}) collective-permute-start(f32[32,128]{1,0:T(8,128)S(1)} %add.108), channel_id=1, source_target_pairs={{0,4},{1,5},{2,6},{3,7},{4,0},{5,1},{6,2},{7,3},{8,12},{9,13},{10,... | collective-permute-start | bytes 49160 | tf_op jit(solution)/shard_map/ppermute | solution.py:76
  58.1 1.2 %collective-permute-start.11 = (f32[32,128]{1,0:T(8,128)S(1)}, f32[32,128]{1,0:T(8,128)S(1)}, u32[]{:S(2)}, u32[]{:S(2)}) collective-permute-start(f32[32,128]{1,0:T(8,128)S(1)} %add.109), channel_id=1, source_target_pairs={{0,8},{8,0},{16,24},{24,16},{32,40},{40,32},{48,56},{56,48},{64,72... | collective-permute-start | bytes 49160 | tf_op jit(solution)/shard_map/ppermute | solution.py:76
  59.3 3.7 %collective-permute-start.12 = (f32[32,128]{1,0:T(8,128)S(1)}, f32[32,128]{1,0:T(8,128)S(1)}, u32[]{:S(2)}, u32[]{:S(2)}) collective-permute-start(f32[32,128]{1,0:T(8,128)S(1)} %add.110), channel_id=1, source_target_pairs={{0,16},{8,24},{16,0},{24,8},{32,48},{40,56},{48,32},{56,40},{64,80... | collective-permute-start | bytes 49160 | tf_op jit(solution)/shard_map/ppermute | solution.py:76
  63.1 5.2 %collective-permute-start.13 = (f32[32,128]{1,0:T(8,128)S(1)}, f32[32,128]{1,0:T(8,128)S(1)}, u32[]{:S(2)}, u32[]{:S(2)}) collective-permute-start(f32[32,128]{1,0:T(8,128)S(1)} %add.111), channel_id=1, source_target_pairs={{0,32},{8,40},{16,48},{24,56},{32,0},{40,8},{48,16},{56,24},{64,96... | collective-permute-start | bytes 49160 | tf_op jit(solution)/shard_map/ppermute | solution.py:76
  68.3 3.7 %collective-permute-start.14 = (f32[32,128]{1,0:T(8,128)S(1)}, f32[32,128]{1,0:T(8,128)S(1)}, u32[]{:S(2)}, u32[]{:S(2)}) collective-permute-start(f32[32,128]{1,0:T(8,128)S(1)} %add.112), channel_id=1, source_target_pairs={{0,64},{8,72},{16,80},{24,88},{32,96},{40,104},{48,112},{56,120},{... | collective-permute-start | bytes 49160 | tf_op jit(solution)/shard_map/ppermute | solution.py:76
  72.1 5.2 %collective-permute-start.15 = (f32[32,128]{1,0:T(8,128)S(1)}, f32[32,128]{1,0:T(8,128)S(1)}, u32[]{:S(2)}, u32[]{:S(2)}) collective-permute-start(f32[32,128]{1,0:T(8,128)S(1)} %add.113), channel_id=1, source_target_pairs={{0,128},{8,136},{16,144},{24,152},{32,160},{40,168},{48,176},{56,1... | collective-permute-start | bytes 49160 | tf_op jit(solution)/shard_map/ppermute | solution.py:76

commit v5 on v4

--- a/solution.py
+++ b/solution.py
@@ -67,14 +67,26 @@
     return out[:, :order], out[:, order:]
 
 
+def ring_rounds(stride):
+    def flip(i):
+        return i ^ stride
+
+    def mirror(i):
+        return i + (3 - 2 * ((i // stride) % 4)) * stride
+
+    return [flip, mirror]
+
+
 def butterfly_sum(value, axis):
     count = lax.axis_size(axis)
     if count & (count - 1):
         return lax.psum(value, axis)
-    mask = 1
-    while mask < count:
-        value = value + lax.ppermute(value, axis, [(i, i ^ mask) for i in range(count)])
-        mask *= 2
+    if count == 32:
+        rounds = [lambda i: i ^ 1] + ring_rounds(2) + ring_rounds(8)
+    else:
+        rounds = [lambda i, mask=1 << b: i ^ mask for b in range(count.bit_length() - 1)]
+    for partner in rounds:
+        value = value + lax.ppermute(value, axis, [(i, partner(i)) for i in range(count)])
     return value
 
 

time: 89.4 us -> 88.9 us (level)
  no operation moved by 1% of the time
where the time goes in v5:
time: 88.9 us; the launch traced here: 88.6 us
  waiting for transfers between devices  36.7 us (41%)
  starting transfers between devices  22.1 us (25%)
  local copies, waits for them, and re-layouts  12.7 us (14%)
  Pallas kernels  7.58 us (9%)
  other arithmetic  5.77 us (6%)
  matrix products  2.76 us (3%)
  between operations  0.96 us (1%)
    ppermute x8, waiting for transfers between devices, butterfly_sum(): lax.ppermute(value, axis, [(i, partner(i)) for i in range(count)])  27.6 us
    ppermute x4, starting transfers between devices, faces(): lax.ppermute(head, axis, [((i + 1) % count, i) for i in range(count)])  10 us
    ppermute x8, starting transfers between devices, butterfly_sum(): lax.ppermute(value, axis, [(i, partner(i)) for i in range(count)])  8.58 us
    unnamed x20, local copies, waits for them, and re-layouts  7.76 us
    pallas_call x1, Pallas kernels, factor_and_inverse(): pl.pallas_call(factor_kernel, out_shape=jax.ShapeDtypeStruct(aug.shape, j...  7.58 us
    ppermute x4, waiting for transfers between devices, faces(): lax.ppermute(tail, axis, [(i, (i + 1) % count) for i in range(count)])  5.55 us
    ppermute x4, waiting for transfers between devices, faces(): lax.ppermute(head, axis, [((i + 1) % count, i) for i in range(count)])  3.59 us
    ppermute x4, starting transfers between devices, faces(): lax.ppermute(tail, axis, [(i, (i + 1) % count) for i in range(count)])  3.52 us
  transfers between devices with their start and end apart: 16, of which 11 were waited for; matrix products, arithmetic and copies ran while one was open for 9% of the time, Pallas kernels for 0%

profile of v5, /device:TPU:32, one launch (start us, length us, event | category | flops | bytes accessed | tf_op | source)
XLA Modules:
  0.0 88.6 jit_solution(18141500448712010669)
XLA Ops:
  0.6 1.4 %fusion.55 = (f32[64,2,8,128]{3,2,1,0:T(8,128)S(1)}, f32[64,2,8,128]{3,2,1,0:T(8,128)S(1)}) fusion(f32[64,4,8,128]{3,2,1,0:T(8,128)} %param.2), kind=kLoop, calls=%fused_computation.88 | loop fusion | bytes 2097152 | tf_op jit(solution)/shard_map/slice | solution.py:12
  2.5 2.0 %collective-permute-start.3 = (f32[64,4,2,128]{3,0,2,1:T(8,128)S(1)}, f32[64,4,2,128]{3,0,2,1:T(8,128)S(1)}, u32[]{:S(2)}, u32[]{:S(2)}) collective-permute-start(f32[64,4,2,128]{3,0,2,1:T(8,128)S(1)} %copy.44), channel_id=1, source_target_pairs={{0,1},{1,2},{2,3},{3,4},{4,5},{5,6},{6,7},{7,0},{8,9},{9,10},{10,1... | collective-permute-start | bytes 786440 | tf_op jit(solution)/shard_map/ppermute | solution.py:14
  4.7 4.8 %collective-permute-start = (f32[64,2,8,128]{3,0,2,1:T(8,128)S(1)}, f32[64,2,8,128]{3,0,2,1:T(8,128)S(1)}, u32[]{:S(2)}, u32[]{:S(2)}) collective-permute-start(f32[64,2,8,128]{3,0,2,1:T(8,128)S(1)} %copy.47), channel_id=1, source_target_pairs={{8,0},{16,8},{24,16},{32,24},{40,32},{48,40},{56,48},{64,56},{72,6... | collective-permute-start | bytes 1572872 | tf_op jit(solution)/shard_map/ppermute | solution.py:15
  17.5 2.5 %broadcast_multiply_fusion = (f32[64,4,8,128]{3,0,2,1:T(8,128)S(1)}, f32[64,4,8,128]{3,0,2,1:T(8,128)S(1)}) fusion(f32[4,8,128]{2,1,0:T(8,128)S(1)} %copy-done.1, f32[64,4,8,2]{3,0,2,1:T(8,128)S(1)} %copy.54, f32[64,4,8,126]{3,0,2,1:T(8,128)S(1)} %copy.55, f32[64,4,8,126]{3,0,2,1:T(8,128)S(1)} %copy.52, f32[64,4,8,2]{3,0,2,1:T(8,128)S(1)} %copy.53, ...), kind=kLoop, calls=%fused_computation.62 | loop fusion | flops 7602176 | bytes 15745024 | tf_op jit(solution)/shard_map/div | solution.py:94
  20.9 4.1 %collective-permute-start.4 = (f32[64,2,8,128]{3,0,2,1:T(8,128)S(1)}, f32[64,2,8,128]{3,0,2,1:T(8,128)S(1)}, u32[]{:S(2)}, u32[]{:S(2)}) collective-permute-start(f32[64,2,8,128]{3,0,2,1:T(8,128)S(1)} %get-tuple-element.18), channel_id=1, source_target_pairs={{8,0},{16,8},{24,16},{32,24},{40,32},{48,40},{56,48},{64,56},{72,6... | collective-permute-start | bytes 1572872 | tf_op jit(solution)/shard_map/ppermute | solution.py:15
  25.6 1.4 %collective-permute-start.7 = (f32[64,4,2,128]{3,0,2,1:T(8,128)S(1)}, f32[64,4,2,128]{3,0,2,1:T(8,128)S(1)}, u32[]{:S(2)}, u32[]{:S(2)}) collective-permute-start(f32[64,4,2,128]{3,0,2,1:T(8,128)S(1)} %get-tuple-element.21), channel_id=1, source_target_pairs={{0,1},{1,2},{2,3},{3,4},{4,5},{5,6},{6,7},{7,0},{8,9},{9,10},{10,1... | collective-permute-start | bytes 786440 | tf_op jit(solution)/shard_map/ppermute | solution.py:14
  27.8 3.6 %collective-permute-done.6 = f32[64,4,2,128]{3,0,2,1:T(8,128)S(1)} collective-permute-done((f32[64,4,2,128]{3,0,2,1:T(8,128)S(1)}, f32[64,4,2,128]{3,0,2,1:T(8,128)S(1)}, u32[]{:S(2)}, u32[]{:S(2)}) %collective-permute-start.6) | collective-permute-done | bytes 262176 | tf_op jit(solution)/shard_map/ppermute | solution.py:15
  31.4 2.3 %collective-permute-done.7 = f32[64,4,2,128]{3,0,2,1:T(8,128)S(1)} collective-permute-done((f32[64,4,2,128]{3,0,2,1:T(8,128)S(1)}, f32[64,4,2,128]{3,0,2,1:T(8,128)S(1)}, u32[]{:S(2)}, u32[]{:S(2)}) %collective-permute-start.7) | collective-permute-done | bytes 262176 | tf_op jit(solution)/shard_map/ppermute | solution.py:14
  33.7 3.2 %collective-permute-done.5 = f32[64,2,8,128]{3,0,2,1:T(8,128)S(1)} collective-permute-done((f32[64,2,8,128]{3,0,2,1:T(8,128)S(1)}, f32[64,2,8,128]{3,0,2,1:T(8,128)S(1)}, u32[]{:S(2)}, u32[]{:S(2)}) %collective-permute-start.5) | collective-permute-done | bytes 524320 | tf_op jit(solution)/shard_map/ppermute | solution.py:14
  37.0 2.5 %fusion.12 = f32[64,4,8,128]{3,0,2,1:T(8,128)S(1)} fusion(f32[64,4,2,128]{3,0,2,1:T(8,128)S(1)} %collective-permute-done.7, f32[64,4,8,128]{3,0,2,1:T(8,128)S(1)} %get-tuple-element.8, f32[64,4,2,128]{3,0,2,1:T(8,128)S(1)} %collective-permute-done.6, f32[64,2,8,128]{3,0,2,1:T(8,128)S(1)} %collective-permute-done.5, ...), kind=kLoop, calls=%fused_computation.21 | loop fusion | flops 9961472 | bytes 9977856 | tf_op jit(solution)/shard_map/sub | solution.py:96
  39.5 1.0 %fusion = f32[64,64]{1,0:T(8,128)S(1)} fusion(f32[64,4,8,128]{3,0,2,1:T(8,128)S(1)} %fusion.12), kind=kOutput, calls=%fused_computation.9 | convolution fusion | flops 201330688 | bytes 1064960 | tf_op jit(solution)/shard_map/kxyz,mxyz->km/dot_general | solution.py:100
  40.8 3.5 %collective-permute-done.8 = f32[32,128]{1,0:T(8,128)S(1)} collective-permute-done((f32[32,128]{1,0:T(8,128)S(1)}, f32[32,128]{1,0:T(8,128)S(1)}, u32[]{:S(2)}, u32[]{:S(2)}) %collective-permute-start.8) | collective-permute-done | bytes 16416 | tf_op jit(solution)/shard_map/ppermute | solution.py:89
  44.3 4.5 %collective-permute-start.9 = (f32[32,128]{1,0:T(8,128)S(1)}, f32[32,128]{1,0:T(8,128)S(1)}, u32[]{:S(2)}, u32[]{:S(2)}) collective-permute-start(f32[32,128]{1,0:T(8,128)S(1)} %add.107), channel_id=1, source_target_pairs={{0,2},{1,3},{2,0},{3,1},{4,6},{5,7},{6,4},{7,5},{8,10},{9,11},{10,... | collective-permute-start | bytes 49160 | tf_op jit(solution)/shard_map/ppermute | solution.py:89
  48.8 1.7 %collective-permute-done.9 = f32[32,128]{1,0:T(8,128)S(1)} collective-permute-done((f32[32,128]{1,0:T(8,128)S(1)}, f32[32,128]{1,0:T(8,128)S(1)}, u32[]{:S(2)}, u32[]{:S(2)}) %collective-permute-start.9) | collective-permute-done | bytes 16416 | tf_op jit(solution)/shard_map/ppermute | solution.py:89
  50.5 3.8 %collective-permute-start.10 = (f32[32,128]{1,0:T(8,128)S(1)}, f32[32,128]{1,0:T(8,128)S(1)}, u32[]{:S(2)}, u32[]{:S(2)}) collective-permute-start(f32[32,128]{1,0:T(8,128)S(1)} %add.108), channel_id=1, source_target_pairs={{0,4},{1,5},{2,6},{3,7},{4,0},{5,1},{6,2},{7,3},{8,12},{9,13},{10,... | collective-permute-start | bytes 49160 | tf_op jit(solution)/shard_map/ppermute | solution.py:89
  54.3 3.8 %collective-permute-done.10 = f32[32,128]{1,0:T(8,128)S(1)} collective-permute-done((f32[32,128]{1,0:T(8,128)S(1)}, f32[32,128]{1,0:T(8,128)S(1)}, u32[]{:S(2)}, u32[]{:S(2)}) %collective-permute-start.10) | collective-permute-done | bytes 16416 | tf_op jit(solution)/shard_map/ppermute | solution.py:89
  58.1 1.2 %collective-permute-done.11 = f32[32,128]{1,0:T(8,128)S(1)} collective-permute-done((f32[32,128]{1,0:T(8,128)S(1)}, f32[32,128]{1,0:T(8,128)S(1)}, u32[]{:S(2)}, u32[]{:S(2)}) %collective-permute-start.11) | collective-permute-done | bytes 16416 | tf_op jit(solution)/shard_map/ppermute | solution.py:89
  59.3 3.7 %collective-permute-done.12 = f32[32,128]{1,0:T(8,128)S(1)} collective-permute-done((f32[32,128]{1,0:T(8,128)S(1)}, f32[32,128]{1,0:T(8,128)S(1)}, u32[]{:S(2)}, u32[]{:S(2)}) %collective-permute-start.12) | collective-permute-done | bytes 16416 | tf_op jit(solution)/shard_map/ppermute | solution.py:89
  63.1 4.9 %collective-permute-done.13 = f32[32,128]{1,0:T(8,128)S(1)} collective-permute-done((f32[32,128]{1,0:T(8,128)S(1)}, f32[32,128]{1,0:T(8,128)S(1)}, u32[]{:S(2)}, u32[]{:S(2)}) %collective-permute-start.13) | collective-permute-done | bytes 16416 | tf_op jit(solution)/shard_map/ppermute | solution.py:89
  68.0 3.7 %collective-permute-done.14 = f32[32,128]{1,0:T(8,128)S(1)} collective-permute-done((f32[32,128]{1,0:T(8,128)S(1)}, f32[32,128]{1,0:T(8,128)S(1)}, u32[]{:S(2)}, u32[]{:S(2)}) %collective-permute-start.14) | collective-permute-done | bytes 16416 | tf_op jit(solution)/shard_map/ppermute | solution.py:89
  71.8 4.9 %collective-permute-done.15 = f32[32,128]{1,0:T(8,128)S(1)} collective-permute-done((f32[32,128]{1,0:T(8,128)S(1)}, f32[32,128]{1,0:T(8,128)S(1)}, u32[]{:S(2)}, u32[]{:S(2)}) %collective-permute-start.15) | collective-permute-done | bytes 16416 | tf_op jit(solution)/shard_map/ppermute | solution.py:89
  77.6 7.6 %shard_map.41 = f32[64,128]{1,0:T(8,128)} custom-call(f32[64,128]{1,0:T(8,128)} %pad_maximum_fusion.4.aug_ref), custom_call_target="tpu_custom_call" | custom-call | tf_op jit(solution)/shard_map/pallas_call | solution.py:61
  85.2 1.8 %fusion.42 = f32[64,4,8,128]{3,0,2,1:T(8,128)S(1)} fusion(f32[64,4,8,128]{3,0,2,1:T(8,128)S(1)} %fusion.12, f32[64,128]{1,0:T(8,128)} %shard_map.41), kind=kOutput, calls=%fused_computation.65 | convolution fusion | flops 201330688 | bytes 2129920 | tf_op jit(solution)/shard_map/mk,kxyz->mxyz/dot_general | solution.py:109
  87.0 1.6 %copy.35 = f32[64,4,8,128]{3,2,1,0:T(8,128)} copy(f32[64,4,8,128]{3,0,2,1:T(8,128)S(1)} %fusion.42) | data formatting | bytes 2097152
  (62 shorter events, 11.9 us)
Async XLA Ops:
  0.6 1.7 %copy-start = (f32[64,4,8,128]{3,2,1,0:T(8,128)S(1)}, f32[64,4,8,128]{3,2,1,0:T(8,128)}, u32[]{:S(2)}) copy-start(f32[64,4,8,128]{3,2,1,0:T(8,128)} %param.2) | copy-start | bytes 3145732
  2.2 14.5 %collective-permute-start.1 = (f32[64,2,8,128]{3,0,2,1:T(8,128)S(1)}, f32[64,2,8,128]{3,0,2,1:T(8,128)S(1)}, u32[]{:S(2)}, u32[]{:S(2)}) collective-permute-start(f32[64,2,8,128]{3,0,2,1:T(8,128)S(1)} %copy.46), channel_id=1, source_target_pairs={{0,8},{8,16},{16,24},{24,32},{32,40},{40,48},{48,56},{56,64},{64,7... | collective-permute-start | bytes 1572872 | tf_op jit(solution)/shard_map/ppermute | solution.py:14
  2.5 14.1 %collective-permute-start.3 = (f32[64,4,2,128]{3,0,2,1:T(8,128)S(1)}, f32[64,4,2,128]{3,0,2,1:T(8,128)S(1)}, u32[]{:S(2)}, u32[]{:S(2)}) collective-permute-start(f32[64,4,2,128]{3,0,2,1:T(8,128)S(1)} %copy.44), channel_id=1, source_target_pairs={{0,1},{1,2},{2,3},{3,4},{4,5},{5,6},{6,7},{7,0},{8,9},{9,10},{10,1... | collective-permute-start | bytes 786440 | tf_op jit(solution)/shard_map/ppermute | solution.py:14
  4.7 12.7 %collective-permute-start = (f32[64,2,8,128]{3,0,2,1:T(8,128)S(1)}, f32[64,2,8,128]{3,0,2,1:T(8,128)S(1)}, u32[]{:S(2)}, u32[]{:S(2)}) collective-permute-start(f32[64,2,8,128]{3,0,2,1:T(8,128)S(1)} %copy.47), channel_id=1, source_target_pairs={{8,0},{16,8},{24,16},{32,24},{40,32},{48,40},{56,48},{64,56},{72,6... | collective-permute-start | bytes 1572872 | tf_op jit(solution)/shard_map/ppermute | solution.py:15
  9.6 7.9 %collective-permute-start.2 = (f32[64,4,2,128]{3,0,2,1:T(8,128)S(1)}, f32[64,4,2,128]{3,0,2,1:T(8,128)S(1)}, u32[]{:S(2)}, u32[]{:S(2)}) collective-permute-start(f32[64,4,2,128]{3,0,2,1:T(8,128)S(1)} %copy.45), channel_id=1, source_target_pairs={{1,0},{2,1},{3,2},{4,3},{5,4},{6,5},{7,6},{0,7},{9,8},{10,9},{11,1... | collective-permute-start | bytes 786440 | tf_op jit(solution)/shard_map/ppermute | solution.py:15
  15.9 0.7 copy-start.1
  20.9 12.8 %collective-permute-start.4 = (f32[64,2,8,128]{3,0,2,1:T(8,128)S(1)}, f32[64,2,8,128]{3,0,2,1:T(8,128)S(1)}, u32[]{:S(2)}, u32[]{:S(2)}) collective-permute-start(f32[64,2,8,128]{3,0,2,1:T(8,128)S(1)} %get-tuple-element.18), channel_id=1, source_target_pairs={{8,0},{16,8},{24,16},{32,24},{40,32},{48,40},{56,48},{64,56},{72,6... | collective-permute-start | bytes 1572872 | tf_op jit(solution)/shard_map/ppermute | solution.py:15
  25.0 11.9 %collective-permute-start.5 = (f32[64,2,8,128]{3,0,2,1:T(8,128)S(1)}, f32[64,2,8,128]{3,0,2,1:T(8,128)S(1)}, u32[]{:S(2)}, u32[]{:S(2)}) collective-permute-start(f32[64,2,8,128]{3,0,2,1:T(8,128)S(1)} %get-tuple-element.19), channel_id=1, source_target_pairs={{0,8},{8,16},{16,24},{24,32},{32,40},{40,48},{48,56},{56,64},{64,7... | collective-permute-start | bytes 1572872 | tf_op jit(solution)/shard_map/ppermute | solution.py:14
  25.0 6.4 %collective-permute-start.6 = (f32[64,4,2,128]{3,0,2,1:T(8,128)S(1)}, f32[64,4,2,128]{3,0,2,1:T(8,128)S(1)}, u32[]{:S(2)}, u32[]{:S(2)}) collective-permute-start(f32[64,4,2,128]{3,0,2,1:T(8,128)S(1)} %get-tuple-element.20), channel_id=1, source_target_pairs={{1,0},{2,1},{3,2},{4,3},{5,4},{6,5},{7,6},{0,7},{9,8},{10,9},{11,1... | collective-permute-start | bytes 786440 | tf_op jit(solution)/shard_map/ppermute | solution.py:15
  25.6 8.1 %collective-permute-start.7 = (f32[64,4,2,128]{3,0,2,1:T(8,128)S(1)}, f32[64,4,2,128]{3,0,2,1:T(8,128)S(1)}, u32[]{:S(2)}, u32[]{:S(2)}) collective-permute-start(f32[64,4,2,128]{3,0,2,1:T(8,128)S(1)} %get-tuple-element.21), channel_id=1, source_target_pairs={{0,1},{1,2},{2,3},{3,4},{4,5},{5,6},{6,7},{7,0},{8,9},{9,10},{10,1... | collective-permute-start | bytes 786440 | tf_op jit(solution)/shard_map/ppermute | solution.py:14
  40.5 3.8 %collective-permute-start.8 = (f32[32,128]{1,0:T(8,128)S(1)}, f32[32,128]{1,0:T(8,128)S(1)}, u32[]{:S(2)}, u32[]{:S(2)}) collective-permute-start(f32[32,128]{1,0:T(8,128)S(1)} %reshape.11), channel_id=1, source_target_pairs={{0,1},{1,0},{2,3},{3,2},{4,5},{5,4},{6,7},{7,6},{8,9},{9,8},{10,11... | collective-permute-start | bytes 49160 | tf_op jit(solution)/shard_map/ppermute | solution.py:89
  44.3 6.2 %collective-permute-start.9 = (f32[32,128]{1,0:T(8,128)S(1)}, f32[32,128]{1,0:T(8,128)S(1)}, u32[]{:S(2)}, u32[]{:S(2)}) collective-permute-start(f32[32,128]{1,0:T(8,128)S(1)} %add.107), channel_id=1, source_target_pairs={{0,2},{1,3},{2,0},{3,1},{4,6},{5,7},{6,4},{7,5},{8,10},{9,11},{10,... | collective-permute-start | bytes 49160 | tf_op jit(solution)/shard_map/ppermute | solution.py:89
  50.5 7.6 %collective-permute-start.10 = (f32[32,128]{1,0:T(8,128)S(1)}, f32[32,128]{1,0:T(8,128)S(1)}, u32[]{:S(2)}, u32[]{:S(2)}) collective-permute-start(f32[32,128]{1,0:T(8,128)S(1)} %add.108), channel_id=1, source_target_pairs={{0,4},{1,5},{2,6},{3,7},{4,0},{5,1},{6,2},{7,3},{8,12},{9,13},{10,... | collective-permute-start | bytes 49160 | tf_op jit(solution)/shard_map/ppermute | solution.py:89
  58.1 1.2 %collective-permute-start.11 = (f32[32,128]{1,0:T(8,128)S(1)}, f32[32,128]{1,0:T(8,128)S(1)}, u32[]{:S(2)}, u32[]{:S(2)}) collective-permute-start(f32[32,128]{1,0:T(8,128)S(1)} %add.109), channel_id=1, source_target_pairs={{0,8},{8,0},{16,24},{24,16},{32,40},{40,32},{48,56},{56,48},{64,72... | collective-permute-start | bytes 49160 | tf_op jit(solution)/shard_map/ppermute | solution.py:89
  59.3 3.7 %collective-permute-start.12 = (f32[32,128]{1,0:T(8,128)S(1)}, f32[32,128]{1,0:T(8,128)S(1)}, u32[]{:S(2)}, u32[]{:S(2)}) collective-permute-start(f32[32,128]{1,0:T(8,128)S(1)} %add.110), channel_id=1, source_target_pairs={{0,16},{8,24},{16,0},{24,8},{32,48},{40,56},{48,32},{56,40},{64,80... | collective-permute-start | bytes 49160 | tf_op jit(solution)/shard_map/ppermute | solution.py:89
  63.1 4.9 %collective-permute-start.13 = (f32[32,128]{1,0:T(8,128)S(1)}, f32[32,128]{1,0:T(8,128)S(1)}, u32[]{:S(2)}, u32[]{:S(2)}) collective-permute-start(f32[32,128]{1,0:T(8,128)S(1)} %add.111), channel_id=1, source_target_pairs={{0,48},{8,56},{16,32},{24,40},{32,16},{40,24},{48,0},{56,8},{64,11... | collective-permute-start | bytes 49160 | tf_op jit(solution)/shard_map/ppermute | solution.py:89
  68.0 3.7 %collective-permute-start.14 = (f32[32,128]{1,0:T(8,128)S(1)}, f32[32,128]{1,0:T(8,128)S(1)}, u32[]{:S(2)}, u32[]{:S(2)}) collective-permute-start(f32[32,128]{1,0:T(8,128)S(1)} %add.112), channel_id=1, source_target_pairs={{0,64},{8,72},{16,80},{24,88},{32,96},{40,104},{48,112},{56,120},{... | collective-permute-start | bytes 49160 | tf_op jit(solution)/shard_map/ppermute | solution.py:89
  71.8 4.9 %collective-permute-start.15 = (f32[32,128]{1,0:T(8,128)S(1)}, f32[32,128]{1,0:T(8,128)S(1)}, u32[]{:S(2)}, u32[]{:S(2)}) collective-permute-start(f32[32,128]{1,0:T(8,128)S(1)} %add.113), channel_id=1, source_target_pairs={{0,192},{8,200},{16,208},{24,216},{32,224},{40,232},{48,240},{56,2... | collective-permute-start | bytes 49160 | tf_op jit(solution)/shard_map/ppermute | solution.py:89

commit v6 on v5

--- a/solution.py
+++ b/solution.py
@@ -38,20 +38,18 @@
     for k in range(order):
         home, place = divmod(k, 8)
         row = blocks[home][place:place + 1, :]
-        scale = 1.0 / jnp.sqrt(row[:, k:k + 1])
-        scaled = row * scale
+        inverse = 1.0 / row[:, k:k + 1]
         for j in range(home, groups):
             block = blocks[j]
-            column = block[:, k:k + 1] * scale
+            column = block[:, k:k + 1] * inverse
             if j == home:
                 column = jnp.where(sub[:, :1] > place, column, 0.0)
-                block = jnp.where(sub == place, scaled, block - column * scaled)
-            else:
-                block = block - column * scaled
-            blocks[j] = block
+            blocks[j] = block - column * row
     for i in range(groups):
+        block = blocks[i]
+        pivots = jnp.sum(jnp.where(lane == sub + 8 * i, block, 0.0), axis=1, keepdims=True)
         keep = (lane >= order) | (lane >= sub + 8 * i)
-        out_ref[pl.ds(8 * i, 8), :] = jnp.where(keep, blocks[i], 0.0)
+        out_ref[pl.ds(8 * i, 8), :] = jnp.where(keep, block / jnp.sqrt(pivots), 0.0)
 
 
 def factor_and_inverse(gram):

time: 88.9 us -> 87.9 us (0.989)
  Pallas kernels: 7.58 us -> 6.66 us
    pallas_call x1, Pallas kernels: 7.58 us -> 6.66 us  [factor_and_inverse(): pl.pallas_call(factor_kernel, out_shape=jax.ShapeDtypeStruct(aug.shape, j...]
  transfers between devices with their start and end apart: 16 -> 16, of which waited for: 11 -> 11; matrix products, arithmetic and copies ran while one was open for 9% -> 10% of each run, Pallas kernels for 0% -> 0%
where the time goes in v6:
time: 87.9 us; the launch traced here: 87.6 us
  waiting for transfers between devices  36.7 us (42%)
  starting transfers between devices  22.1 us (25%)
  local copies, waits for them, and re-layouts  12.7 us (14%)
  Pallas kernels  6.66 us (8%)
  other arithmetic  5.77 us (7%)
  matrix products  2.76 us (3%)
  between operations  0.96 us (1%)
    ppermute x8, waiting for transfers between devices, butterfly_sum(): lax.ppermute(value, axis, [(i, partner(i)) for i in range(count)])  27.6 us
    ppermute x4, starting transfers between devices, faces(): lax.ppermute(head, axis, [((i + 1) % count, i) for i in range(count)])  10 us
    ppermute x8, starting transfers between devices, butterfly_sum(): lax.ppermute(value, axis, [(i, partner(i)) for i in range(count)])  8.58 us
    unnamed x20, local copies, waits for them, and re-layouts  7.76 us
    pallas_call x1, Pallas kernels, factor_and_inverse(): pl.pallas_call(factor_kernel, out_shape=jax.ShapeDtypeStruct(aug.shape, j...  6.66 us
    ppermute x4, waiting for transfers between devices, faces(): lax.ppermute(tail, axis, [(i, (i + 1) % count) for i in range(count)])  5.55 us
    ppermute x4, waiting for transfers between devices, faces(): lax.ppermute(head, axis, [((i + 1) % count, i) for i in range(count)])  3.59 us
    ppermute x4, starting transfers between devices, faces(): lax.ppermute(tail, axis, [(i, (i + 1) % count) for i in range(count)])  3.52 us
  transfers between devices with their start and end apart: 16, of which 11 were waited for; matrix products, arithmetic and copies ran while one was open for 10% of the time, Pallas kernels for 0%

profile of v6, /device:TPU:32, one launch (start us, length us, event | category | flops | bytes accessed | tf_op | source)
XLA Modules:
  0.0 87.6 jit_solution(13951913697167587169)
XLA Ops:
  0.6 1.4 %fusion.55 = (f32[64,2,8,128]{3,2,1,0:T(8,128)S(1)}, f32[64,2,8,128]{3,2,1,0:T(8,128)S(1)}) fusion(f32[64,4,8,128]{3,2,1,0:T(8,128)} %param.2), kind=kLoop, calls=%fused_computation.88 | loop fusion | bytes 2097152 | tf_op jit(solution)/shard_map/slice | solution.py:12
  2.5 2.0 %collective-permute-start.3 = (f32[64,4,2,128]{3,0,2,1:T(8,128)S(1)}, f32[64,4,2,128]{3,0,2,1:T(8,128)S(1)}, u32[]{:S(2)}, u32[]{:S(2)}) collective-permute-start(f32[64,4,2,128]{3,0,2,1:T(8,128)S(1)} %copy.44), channel_id=1, source_target_pairs={{0,1},{1,2},{2,3},{3,4},{4,5},{5,6},{6,7},{7,0},{8,9},{9,10},{10,1... | collective-permute-start | bytes 786440 | tf_op jit(solution)/shard_map/ppermute | solution.py:14
  4.7 4.8 %collective-permute-start = (f32[64,2,8,128]{3,0,2,1:T(8,128)S(1)}, f32[64,2,8,128]{3,0,2,1:T(8,128)S(1)}, u32[]{:S(2)}, u32[]{:S(2)}) collective-permute-start(f32[64,2,8,128]{3,0,2,1:T(8,128)S(1)} %copy.47), channel_id=1, source_target_pairs={{8,0},{16,8},{24,16},{32,24},{40,32},{48,40},{56,48},{64,56},{72,6... | collective-permute-start | bytes 1572872 | tf_op jit(solution)/shard_map/ppermute | solution.py:15
  17.5 2.5 %broadcast_multiply_fusion = (f32[64,4,8,128]{3,0,2,1:T(8,128)S(1)}, f32[64,4,8,128]{3,0,2,1:T(8,128)S(1)}) fusion(f32[4,8,128]{2,1,0:T(8,128)S(1)} %copy-done.1, f32[64,4,8,2]{3,0,2,1:T(8,128)S(1)} %copy.54, f32[64,4,8,126]{3,0,2,1:T(8,128)S(1)} %copy.55, f32[64,4,8,126]{3,0,2,1:T(8,128)S(1)} %copy.52, f32[64,4,8,2]{3,0,2,1:T(8,128)S(1)} %copy.53, ...), kind=kLoop, calls=%fused_computation.62 | loop fusion | flops 7602176 | bytes 15745024 | tf_op jit(solution)/shard_map/div | solution.py:92
  20.9 4.1 %collective-permute-start.4 = (f32[64,2,8,128]{3,0,2,1:T(8,128)S(1)}, f32[64,2,8,128]{3,0,2,1:T(8,128)S(1)}, u32[]{:S(2)}, u32[]{:S(2)}) collective-permute-start(f32[64,2,8,128]{3,0,2,1:T(8,128)S(1)} %get-tuple-element.18), channel_id=1, source_target_pairs={{8,0},{16,8},{24,16},{32,24},{40,32},{48,40},{56,48},{64,56},{72,6... | collective-permute-start | bytes 1572872 | tf_op jit(solution)/shard_map/ppermute | solution.py:15
  25.6 1.4 %collective-permute-start.7 = (f32[64,4,2,128]{3,0,2,1:T(8,128)S(1)}, f32[64,4,2,128]{3,0,2,1:T(8,128)S(1)}, u32[]{:S(2)}, u32[]{:S(2)}) collective-permute-start(f32[64,4,2,128]{3,0,2,1:T(8,128)S(1)} %get-tuple-element.21), channel_id=1, source_target_pairs={{0,1},{1,2},{2,3},{3,4},{4,5},{5,6},{6,7},{7,0},{8,9},{9,10},{10,1... | collective-permute-start | bytes 786440 | tf_op jit(solution)/shard_map/ppermute | solution.py:14
  27.8 3.6 %collective-permute-done.6 = f32[64,4,2,128]{3,0,2,1:T(8,128)S(1)} collective-permute-done((f32[64,4,2,128]{3,0,2,1:T(8,128)S(1)}, f32[64,4,2,128]{3,0,2,1:T(8,128)S(1)}, u32[]{:S(2)}, u32[]{:S(2)}) %collective-permute-start.6) | collective-permute-done | bytes 262176 | tf_op jit(solution)/shard_map/ppermute | solution.py:15
  31.4 2.3 %collective-permute-done.7 = f32[64,4,2,128]{3,0,2,1:T(8,128)S(1)} collective-permute-done((f32[64,4,2,128]{3,0,2,1:T(8,128)S(1)}, f32[64,4,2,128]{3,0,2,1:T(8,128)S(1)}, u32[]{:S(2)}, u32[]{:S(2)}) %collective-permute-start.7) | collective-permute-done | bytes 262176 | tf_op jit(solution)/shard_map/ppermute | solution.py:14
  33.7 3.2 %collective-permute-done.5 = f32[64,2,8,128]{3,0,2,1:T(8,128)S(1)} collective-permute-done((f32[64,2,8,128]{3,0,2,1:T(8,128)S(1)}, f32[64,2,8,128]{3,0,2,1:T(8,128)S(1)}, u32[]{:S(2)}, u32[]{:S(2)}) %collective-permute-start.5) | collective-permute-done | bytes 524320 | tf_op jit(solution)/shard_map/ppermute | solution.py:14
  37.0 2.5 %fusion.12 = f32[64,4,8,128]{3,0,2,1:T(8,128)S(1)} fusion(f32[64,4,2,128]{3,0,2,1:T(8,128)S(1)} %collective-permute-done.7, f32[64,4,8,128]{3,0,2,1:T(8,128)S(1)} %get-tuple-element.8, f32[64,4,2,128]{3,0,2,1:T(8,128)S(1)} %collective-permute-done.6, f32[64,2,8,128]{3,0,2,1:T(8,128)S(1)} %collective-permute-done.5, ...), kind=kLoop, calls=%fused_computation.21 | loop fusion | flops 9961472 | bytes 9977856 | tf_op jit(solution)/shard_map/sub | solution.py:94
  39.5 1.0 %fusion = f32[64,64]{1,0:T(8,128)S(1)} fusion(f32[64,4,8,128]{3,0,2,1:T(8,128)S(1)} %fusion.12), kind=kOutput, calls=%fused_computation.9 | convolution fusion | flops 201330688 | bytes 1064960 | tf_op jit(solution)/shard_map/kxyz,mxyz->km/dot_general | solution.py:98
  40.8 3.5 %collective-permute-done.8 = f32[32,128]{1,0:T(8,128)S(1)} collective-permute-done((f32[32,128]{1,0:T(8,128)S(1)}, f32[32,128]{1,0:T(8,128)S(1)}, u32[]{:S(2)}, u32[]{:S(2)}) %collective-permute-start.8) | collective-permute-done | bytes 16416 | tf_op jit(solution)/shard_map/ppermute | solution.py:87
  44.3 4.5 %collective-permute-start.9 = (f32[32,128]{1,0:T(8,128)S(1)}, f32[32,128]{1,0:T(8,128)S(1)}, u32[]{:S(2)}, u32[]{:S(2)}) collective-permute-start(f32[32,128]{1,0:T(8,128)S(1)} %add.107), channel_id=1, source_target_pairs={{0,2},{1,3},{2,0},{3,1},{4,6},{5,7},{6,4},{7,5},{8,10},{9,11},{10,... | collective-permute-start | bytes 49160 | tf_op jit(solution)/shard_map/ppermute | solution.py:87
  48.8 1.7 %collective-permute-done.9 = f32[32,128]{1,0:T(8,128)S(1)} collective-permute-done((f32[32,128]{1,0:T(8,128)S(1)}, f32[32,128]{1,0:T(8,128)S(1)}, u32[]{:S(2)}, u32[]{:S(2)}) %collective-permute-start.9) | collective-permute-done | bytes 16416 | tf_op jit(solution)/shard_map/ppermute | solution.py:87
  50.5 3.8 %collective-permute-start.10 = (f32[32,128]{1,0:T(8,128)S(1)}, f32[32,128]{1,0:T(8,128)S(1)}, u32[]{:S(2)}, u32[]{:S(2)}) collective-permute-start(f32[32,128]{1,0:T(8,128)S(1)} %add.108), channel_id=1, source_target_pairs={{0,4},{1,5},{2,6},{3,7},{4,0},{5,1},{6,2},{7,3},{8,12},{9,13},{10,... | collective-permute-start | bytes 49160 | tf_op jit(solution)/shard_map/ppermute | solution.py:87
  54.3 3.8 %collective-permute-done.10 = f32[32,128]{1,0:T(8,128)S(1)} collective-permute-done((f32[32,128]{1,0:T(8,128)S(1)}, f32[32,128]{1,0:T(8,128)S(1)}, u32[]{:S(2)}, u32[]{:S(2)}) %collective-permute-start.10) | collective-permute-done | bytes 16416 | tf_op jit(solution)/shard_map/ppermute | solution.py:87
  58.1 1.2 %collective-permute-done.11 = f32[32,128]{1,0:T(8,128)S(1)} collective-permute-done((f32[32,128]{1,0:T(8,128)S(1)}, f32[32,128]{1,0:T(8,128)S(1)}, u32[]{:S(2)}, u32[]{:S(2)}) %collective-permute-start.11) | collective-permute-done | bytes 16416 | tf_op jit(solution)/shard_map/ppermute | solution.py:87
  59.3 3.7 %collective-permute-done.12 = f32[32,128]{1,0:T(8,128)S(1)} collective-permute-done((f32[32,128]{1,0:T(8,128)S(1)}, f32[32,128]{1,0:T(8,128)S(1)}, u32[]{:S(2)}, u32[]{:S(2)}) %collective-permute-start.12) | collective-permute-done | bytes 16416 | tf_op jit(solution)/shard_map/ppermute | solution.py:87
  63.1 4.9 %collective-permute-done.13 = f32[32,128]{1,0:T(8,128)S(1)} collective-permute-done((f32[32,128]{1,0:T(8,128)S(1)}, f32[32,128]{1,0:T(8,128)S(1)}, u32[]{:S(2)}, u32[]{:S(2)}) %collective-permute-start.13) | collective-permute-done | bytes 16416 | tf_op jit(solution)/shard_map/ppermute | solution.py:87
  68.0 3.7 %collective-permute-done.14 = f32[32,128]{1,0:T(8,128)S(1)} collective-permute-done((f32[32,128]{1,0:T(8,128)S(1)}, f32[32,128]{1,0:T(8,128)S(1)}, u32[]{:S(2)}, u32[]{:S(2)}) %collective-permute-start.14) | collective-permute-done | bytes 16416 | tf_op jit(solution)/shard_map/ppermute | solution.py:87
  71.8 4.9 %collective-permute-done.15 = f32[32,128]{1,0:T(8,128)S(1)} collective-permute-done((f32[32,128]{1,0:T(8,128)S(1)}, f32[32,128]{1,0:T(8,128)S(1)}, u32[]{:S(2)}, u32[]{:S(2)}) %collective-permute-start.15) | collective-permute-done | bytes 16416 | tf_op jit(solution)/shard_map/ppermute | solution.py:87
  77.6 6.7 %shard_map.41 = f32[64,128]{1,0:T(8,128)} custom-call(f32[64,128]{1,0:T(8,128)} %pad_maximum_fusion.4.aug_ref), custom_call_target="tpu_custom_call" | custom-call | tf_op jit(solution)/shard_map/pallas_call | solution.py:59
  84.3 1.8 %fusion.42 = f32[64,4,8,128]{3,0,2,1:T(8,128)S(1)} fusion(f32[64,4,8,128]{3,0,2,1:T(8,128)S(1)} %fusion.12, f32[64,128]{1,0:T(8,128)} %shard_map.41), kind=kOutput, calls=%fused_computation.65 | convolution fusion | flops 201330688 | bytes 2129920 | tf_op jit(solution)/shard_map/mk,kxyz->mxyz/dot_general | solution.py:107
  86.1 1.6 %copy.35 = f32[64,4,8,128]{3,2,1,0:T(8,128)} copy(f32[64,4,8,128]{3,0,2,1:T(8,128)S(1)} %fusion.42) | data formatting | bytes 2097152
  (62 shorter events, 11.9 us)
Async XLA Ops:
  0.6 1.7 %copy-start = (f32[64,4,8,128]{3,2,1,0:T(8,128)S(1)}, f32[64,4,8,128]{3,2,1,0:T(8,128)}, u32[]{:S(2)}) copy-start(f32[64,4,8,128]{3,2,1,0:T(8,128)} %param.2) | copy-start | bytes 3145732
  2.2 14.5 %collective-permute-start.1 = (f32[64,2,8,128]{3,0,2,1:T(8,128)S(1)}, f32[64,2,8,128]{3,0,2,1:T(8,128)S(1)}, u32[]{:S(2)}, u32[]{:S(2)}) collective-permute-start(f32[64,2,8,128]{3,0,2,1:T(8,128)S(1)} %copy.46), channel_id=1, source_target_pairs={{0,8},{8,16},{16,24},{24,32},{32,40},{40,48},{48,56},{56,64},{64,7... | collective-permute-start | bytes 1572872 | tf_op jit(solution)/shard_map/ppermute | solution.py:14
  2.5 14.1 %collective-permute-start.3 = (f32[64,4,2,128]{3,0,2,1:T(8,128)S(1)}, f32[64,4,2,128]{3,0,2,1:T(8,128)S(1)}, u32[]{:S(2)}, u32[]{:S(2)}) collective-permute-start(f32[64,4,2,128]{3,0,2,1:T(8,128)S(1)} %copy.44), channel_id=1, source_target_pairs={{0,1},{1,2},{2,3},{3,4},{4,5},{5,6},{6,7},{7,0},{8,9},{9,10},{10,1... | collective-permute-start | bytes 786440 | tf_op jit(solution)/shard_map/ppermute | solution.py:14
  4.7 12.7 %collective-permute-start = (f32[64,2,8,128]{3,0,2,1:T(8,128)S(1)}, f32[64,2,8,128]{3,0,2,1:T(8,128)S(1)}, u32[]{:S(2)}, u32[]{:S(2)}) collective-permute-start(f32[64,2,8,128]{3,0,2,1:T(8,128)S(1)} %copy.47), channel_id=1, source_target_pairs={{8,0},{16,8},{24,16},{32,24},{40,32},{48,40},{56,48},{64,56},{72,6... | collective-permute-start | bytes 1572872 | tf_op jit(solution)/shard_map/ppermute | solution.py:15
  9.6 7.9 %collective-permute-start.2 = (f32[64,4,2,128]{3,0,2,1:T(8,128)S(1)}, f32[64,4,2,128]{3,0,2,1:T(8,128)S(1)}, u32[]{:S(2)}, u32[]{:S(2)}) collective-permute-start(f32[64,4,2,128]{3,0,2,1:T(8,128)S(1)} %copy.45), channel_id=1, source_target_pairs={{1,0},{2,1},{3,2},{4,3},{5,4},{6,5},{7,6},{0,7},{9,8},{10,9},{11,1... | collective-permute-start | bytes 786440 | tf_op jit(solution)/shard_map/ppermute | solution.py:15
  15.9 0.7 copy-start.1
  20.9 12.8 %collective-permute-start.4 = (f32[64,2,8,128]{3,0,2,1:T(8,128)S(1)}, f32[64,2,8,128]{3,0,2,1:T(8,128)S(1)}, u32[]{:S(2)}, u32[]{:S(2)}) collective-permute-start(f32[64,2,8,128]{3,0,2,1:T(8,128)S(1)} %get-tuple-element.18), channel_id=1, source_target_pairs={{8,0},{16,8},{24,16},{32,24},{40,32},{48,40},{56,48},{64,56},{72,6... | collective-permute-start | bytes 1572872 | tf_op jit(solution)/shard_map/ppermute | solution.py:15
  25.0 11.9 %collective-permute-start.5 = (f32[64,2,8,128]{3,0,2,1:T(8,128)S(1)}, f32[64,2,8,128]{3,0,2,1:T(8,128)S(1)}, u32[]{:S(2)}, u32[]{:S(2)}) collective-permute-start(f32[64,2,8,128]{3,0,2,1:T(8,128)S(1)} %get-tuple-element.19), channel_id=1, source_target_pairs={{0,8},{8,16},{16,24},{24,32},{32,40},{40,48},{48,56},{56,64},{64,7... | collective-permute-start | bytes 1572872 | tf_op jit(solution)/shard_map/ppermute | solution.py:14
  25.0 6.4 %collective-permute-start.6 = (f32[64,4,2,128]{3,0,2,1:T(8,128)S(1)}, f32[64,4,2,128]{3,0,2,1:T(8,128)S(1)}, u32[]{:S(2)}, u32[]{:S(2)}) collective-permute-start(f32[64,4,2,128]{3,0,2,1:T(8,128)S(1)} %get-tuple-element.20), channel_id=1, source_target_pairs={{1,0},{2,1},{3,2},{4,3},{5,4},{6,5},{7,6},{0,7},{9,8},{10,9},{11,1... | collective-permute-start | bytes 786440 | tf_op jit(solution)/shard_map/ppermute | solution.py:15
  25.6 8.1 %collective-permute-start.7 = (f32[64,4,2,128]{3,0,2,1:T(8,128)S(1)}, f32[64,4,2,128]{3,0,2,1:T(8,128)S(1)}, u32[]{:S(2)}, u32[]{:S(2)}) collective-permute-start(f32[64,4,2,128]{3,0,2,1:T(8,128)S(1)} %get-tuple-element.21), channel_id=1, source_target_pairs={{0,1},{1,2},{2,3},{3,4},{4,5},{5,6},{6,7},{7,0},{8,9},{9,10},{10,1... | collective-permute-start | bytes 786440 | tf_op jit(solution)/shard_map/ppermute | solution.py:14
  40.5 3.8 %collective-permute-start.8 = (f32[32,128]{1,0:T(8,128)S(1)}, f32[32,128]{1,0:T(8,128)S(1)}, u32[]{:S(2)}, u32[]{:S(2)}) collective-permute-start(f32[32,128]{1,0:T(8,128)S(1)} %reshape.11), channel_id=1, source_target_pairs={{0,1},{1,0},{2,3},{3,2},{4,5},{5,4},{6,7},{7,6},{8,9},{9,8},{10,11... | collective-permute-start | bytes 49160 | tf_op jit(solution)/shard_map/ppermute | solution.py:87
  44.3 6.2 %collective-permute-start.9 = (f32[32,128]{1,0:T(8,128)S(1)}, f32[32,128]{1,0:T(8,128)S(1)}, u32[]{:S(2)}, u32[]{:S(2)}) collective-permute-start(f32[32,128]{1,0:T(8,128)S(1)} %add.107), channel_id=1, source_target_pairs={{0,2},{1,3},{2,0},{3,1},{4,6},{5,7},{6,4},{7,5},{8,10},{9,11},{10,... | collective-permute-start | bytes 49160 | tf_op jit(solution)/shard_map/ppermute | solution.py:87
  50.5 7.6 %collective-permute-start.10 = (f32[32,128]{1,0:T(8,128)S(1)}, f32[32,128]{1,0:T(8,128)S(1)}, u32[]{:S(2)}, u32[]{:S(2)}) collective-permute-start(f32[32,128]{1,0:T(8,128)S(1)} %add.108), channel_id=1, source_target_pairs={{0,4},{1,5},{2,6},{3,7},{4,0},{5,1},{6,2},{7,3},{8,12},{9,13},{10,... | collective-permute-start | bytes 49160 | tf_op jit(solution)/shard_map/ppermute | solution.py:87
  58.1 1.2 %collective-permute-start.11 = (f32[32,128]{1,0:T(8,128)S(1)}, f32[32,128]{1,0:T(8,128)S(1)}, u32[]{:S(2)}, u32[]{:S(2)}) collective-permute-start(f32[32,128]{1,0:T(8,128)S(1)} %add.109), channel_id=1, source_target_pairs={{0,8},{8,0},{16,24},{24,16},{32,40},{40,32},{48,56},{56,48},{64,72... | collective-permute-start | bytes 49160 | tf_op jit(solution)/shard_map/ppermute | solution.py:87
  59.3 3.7 %collective-permute-start.12 = (f32[32,128]{1,0:T(8,128)S(1)}, f32[32,128]{1,0:T(8,128)S(1)}, u32[]{:S(2)}, u32[]{:S(2)}) collective-permute-start(f32[32,128]{1,0:T(8,128)S(1)} %add.110), channel_id=1, source_target_pairs={{0,16},{8,24},{16,0},{24,8},{32,48},{40,56},{48,32},{56,40},{64,80... | collective-permute-start | bytes 49160 | tf_op jit(solution)/shard_map/ppermute | solution.py:87
  63.1 4.9 %collective-permute-start.13 = (f32[32,128]{1,0:T(8,128)S(1)}, f32[32,128]{1,0:T(8,128)S(1)}, u32[]{:S(2)}, u32[]{:S(2)}) collective-permute-start(f32[32,128]{1,0:T(8,128)S(1)} %add.111), channel_id=1, source_target_pairs={{0,48},{8,56},{16,32},{24,40},{32,16},{40,24},{48,0},{56,8},{64,11... | collective-permute-start | bytes 49160 | tf_op jit(solution)/shard_map/ppermute | solution.py:87
  68.0 3.7 %collective-permute-start.14 = (f32[32,128]{1,0:T(8,128)S(1)}, f32[32,128]{1,0:T(8,128)S(1)}, u32[]{:S(2)}, u32[]{:S(2)}) collective-permute-start(f32[32,128]{1,0:T(8,128)S(1)} %add.112), channel_id=1, source_target_pairs={{0,64},{8,72},{16,80},{24,88},{32,96},{40,104},{48,112},{56,120},{... | collective-permute-start | bytes 49160 | tf_op jit(solution)/shard_map/ppermute | solution.py:87
  71.8 4.9 %collective-permute-start.15 = (f32[32,128]{1,0:T(8,128)S(1)}, f32[32,128]{1,0:T(8,128)S(1)}, u32[]{:S(2)}, u32[]{:S(2)}) collective-permute-start(f32[32,128]{1,0:T(8,128)S(1)} %add.113), channel_id=1, source_target_pairs={{0,192},{8,200},{16,208},{24,216},{32,224},{40,232},{48,240},{56,2... | collective-permute-start | bytes 49160 | tf_op jit(solution)/shard_map/ppermute | solution.py:87

commit v7 on v6

--- a/solution.py
+++ b/solution.py
@@ -24,8 +24,10 @@
     total = total - 1.0 / 12.0 * (along_x[:, 4:] + along_x[:, :-4])
     total = total + 4.0 / 3.0 * (along_y[:, :, 3:-1] + along_y[:, :, 1:-3])
     total = total - 1.0 / 12.0 * (along_y[:, :, 4:] + along_y[:, :, :-4])
-    total = total + 4.0 / 3.0 * (jnp.roll(core, 1, 3) + jnp.roll(core, -1, 3))
-    total = total - 1.0 / 12.0 * (jnp.roll(core, 2, 3) + jnp.roll(core, -2, 3))
+    size = core.shape[3]
+    along_z = jnp.concatenate([core[..., size - 2:], core, core[..., :2]], axis=3)
+    total = total + 4.0 / 3.0 * (along_z[..., 1:size + 1] + along_z[..., 3:size + 3])
+    total = total - 1.0 / 12.0 * (along_z[..., :size] + along_z[..., 4:])
     return -0.5 * total + pot[None] * core
 
 

time: 87.9 us -> 86.5 us (0.984)
  local copies, waits for them, and re-layouts: 12.7 us -> 5.47 us
  waiting for transfers between devices: 36.7 us -> 42.1 us
  starting transfers between devices: 22.1 us -> 23.4 us
    ppermute x4, waiting for transfers between devices: 5.55 us -> 9.78 us  [faces(): lax.ppermute(tail, axis, [(i, (i + 1) % count) for i in range(count)])]
    unnamed x20 -> x9, local copies, waits for them, and re-layouts: 7.76 us -> 4.2 us
    slice x8 -> x2, local copies, waits for them, and re-layouts: 2.97 us -> 0.74 us  [apply_ham(): core[..., size - 2:]]
    slice x4, local copies, waits for them, and re-layouts: 1.64 us -> 0.25 us  [faces(): head = lax.slice_in_dim(cells, 0, width, axis=dim)]
    ppermute x4, waiting for transfers between devices: 3.59 us -> 4.83 us  [faces(): lax.ppermute(head, axis, [((i + 1) % count, i) for i in range(count)])]
  transfers between devices with their start and end apart: 16 -> 16, of which waited for: 11 -> 14; matrix products, arithmetic and copies ran while one was open for 10% -> 2% of each run, Pallas kernels for 0% -> 0%
where the time goes in v7:
time: 86.5 us; the launch traced here: 86.2 us
  waiting for transfers between devices  42.1 us (49%)
  starting transfers between devices  23.4 us (27%)
  Pallas kernels  6.66 us (8%)
  local copies, waits for them, and re-layouts  5.47 us (6%)
  other arithmetic  4.97 us (6%)
  matrix products  2.76 us (3%)
    ppermute x8, waiting for transfers between devices, butterfly_sum(): lax.ppermute(value, axis, [(i, partner(i)) for i in range(count)])  27.5 us
    ppermute x4, starting transfers between devices, faces(): lax.ppermute(head, axis, [((i + 1) % count, i) for i in range(count)])  10.7 us
    ppermute x4, waiting for transfers between devices, faces(): lax.ppermute(tail, axis, [(i, (i + 1) % count) for i in range(count)])  9.78 us
    ppermute x8, starting transfers between devices, butterfly_sum(): lax.ppermute(value, axis, [(i, partner(i)) for i in range(count)])  8.84 us
    pallas_call x1, Pallas kernels, factor_and_inverse(): pl.pallas_call(factor_kernel, out_shape=jax.ShapeDtypeStruct(aug.shape, j...  6.66 us
    ppermute x4, waiting for transfers between devices, faces(): lax.ppermute(head, axis, [((i + 1) % count, i) for i in range(count)])  4.83 us
    unnamed x9, local copies, waits for them, and re-layouts  4.2 us
    ppermute x4, starting transfers between devices, faces(): lax.ppermute(tail, axis, [(i, (i + 1) % count) for i in range(count)])  3.81 us
  transfers between devices with their start and end apart: 16, of which 14 were waited for; matrix products, arithmetic and copies ran while one was open for 2% of the time, Pallas kernels for 0%

profile of v7, /device:TPU:32, one launch (start us, length us, event | category | flops | bytes accessed | tf_op | source)
XLA Modules:
  0.0 86.2 jit_solution(5818368001398644618)
XLA Ops:
  0.6 1.8 %copy.14 = f32[64,4,8,128]{3,0,2,1:T(8,128)S(1)} copy(f32[64,4,8,128]{3,2,1,0:T(8,128)} %param.2) | data formatting | bytes 2097152 | tf_op args[0]
  2.7 2.0 %collective-permute-start.3 = (f32[64,4,2,128]{3,0,2,1:T(8,128)S(1)}, f32[64,4,2,128]{3,0,2,1:T(8,128)S(1)}, u32[]{:S(2)}, u32[]{:S(2)}) collective-permute-start(f32[64,4,2,128]{3,0,2,1:T(8,128)S(1)} %get-tuple-element.23), channel_id=1, source_target_pairs={{0,1},{1,2},{2,3},{3,4},{4,5},{5,6},{6,7},{7,0},{8,9},{9,10},{10,1... | collective-permute-start | bytes 786440 | tf_op jit(solution)/shard_map/ppermute | solution.py:14
  4.7 4.8 %collective-permute-start = (f32[64,2,8,128]{3,0,2,1:T(8,128)S(1)}, f32[64,2,8,128]{3,0,2,1:T(8,128)S(1)}, u32[]{:S(2)}, u32[]{:S(2)}) collective-permute-start(f32[64,2,8,128]{3,0,2,1:T(8,128)S(1)} %get-tuple-element.16), channel_id=1, source_target_pairs={{8,0},{16,8},{24,16},{32,24},{40,32},{48,40},{56,48},{64,56},{72,6... | collective-permute-start | bytes 1572872 | tf_op jit(solution)/shard_map/ppermute | solution.py:15
  11.3 3.2 %collective-permute-done.1 = f32[64,2,8,128]{3,0,2,1:T(8,128)S(1)} collective-permute-done((f32[64,2,8,128]{3,0,2,1:T(8,128)S(1)}, f32[64,2,8,128]{3,0,2,1:T(8,128)S(1)}, u32[]{:S(2)}, u32[]{:S(2)}) %collective-permute-start.1) | collective-permute-done | bytes 524320 | tf_op jit(solution)/shard_map/ppermute | solution.py:14
  16.3 2.1 %broadcast_multiply_fusion = (f32[64,4,8,128]{3,0,2,1:T(8,128)S(1)}, f32[64,4,8,128]{3,0,2,1:T(8,128)S(1)}) fusion(f32[64,4,8,128]{3,0,2,1:T(8,128)S(1)} %copy.14, f32[4,8,128]{2,1,0:T(8,128)S(1)} %copy-done.1, f32[64,4,8,2]{3,0,2,1:T(8,128)S(1)} %get-tuple-element.25, f32[64,4,8,2]{3,0,2,1:T(8,128)S(1)} %get-tuple-element.24, ...), kind=kLoop, calls=%fused_computation.78 | loop fusion | flops 7602176 | bytes 11583488 | tf_op jit(solution)/shard_map/div | solution.py:94
  18.5 5.3 %collective-permute-start.4 = (f32[64,2,8,128]{3,0,2,1:T(8,128)S(1)}, f32[64,2,8,128]{3,0,2,1:T(8,128)S(1)}, u32[]{:S(2)}, u32[]{:S(2)}) collective-permute-start(f32[64,2,8,128]{3,0,2,1:T(8,128)S(1)} %get-tuple-element.12), channel_id=1, source_target_pairs={{8,0},{16,8},{24,16},{32,24},{40,32},{48,40},{56,48},{64,56},{72,6... | collective-permute-start | bytes 1572872 | tf_op jit(solution)/shard_map/ppermute | solution.py:15
  24.2 1.7 %collective-permute-start.7 = (f32[64,4,2,128]{3,0,2,1:T(8,128)S(1)}, f32[64,4,2,128]{3,0,2,1:T(8,128)S(1)}, u32[]{:S(2)}, u32[]{:S(2)}) collective-permute-start(f32[64,4,2,128]{3,0,2,1:T(8,128)S(1)} %get-tuple-element.15), channel_id=1, source_target_pairs={{0,1},{1,2},{2,3},{3,4},{4,5},{5,6},{6,7},{7,0},{8,9},{9,10},{10,1... | collective-permute-start | bytes 786440 | tf_op jit(solution)/shard_map/ppermute | solution.py:14
  26.3 4.0 %collective-permute-done.6 = f32[64,4,2,128]{3,0,2,1:T(8,128)S(1)} collective-permute-done((f32[64,4,2,128]{3,0,2,1:T(8,128)S(1)}, f32[64,4,2,128]{3,0,2,1:T(8,128)S(1)}, u32[]{:S(2)}, u32[]{:S(2)}) %collective-permute-start.6) | collective-permute-done | bytes 262176 | tf_op jit(solution)/shard_map/ppermute | solution.py:15
  30.3 2.4 %collective-permute-done.7 = f32[64,4,2,128]{3,0,2,1:T(8,128)S(1)} collective-permute-done((f32[64,4,2,128]{3,0,2,1:T(8,128)S(1)}, f32[64,4,2,128]{3,0,2,1:T(8,128)S(1)}, u32[]{:S(2)}, u32[]{:S(2)}) %collective-permute-start.7) | collective-permute-done | bytes 262176 | tf_op jit(solution)/shard_map/ppermute | solution.py:14
  32.6 3.0 %collective-permute-done.5 = f32[64,2,8,128]{3,0,2,1:T(8,128)S(1)} collective-permute-done((f32[64,2,8,128]{3,0,2,1:T(8,128)S(1)}, f32[64,2,8,128]{3,0,2,1:T(8,128)S(1)}, u32[]{:S(2)}, u32[]{:S(2)}) %collective-permute-start.5) | collective-permute-done | bytes 524320 | tf_op jit(solution)/shard_map/ppermute | solution.py:14
  35.7 2.1 %fusion.12 = f32[64,4,8,128]{3,0,2,1:T(8,128)S(1)} fusion(f32[64,4,2,128]{3,0,2,1:T(8,128)S(1)} %collective-permute-done.7, f32[64,4,8,128]{3,0,2,1:T(8,128)S(1)} %get-tuple-element.8, f32[64,4,2,128]{3,0,2,1:T(8,128)S(1)} %collective-permute-done.6, f32[64,2,8,128]{3,0,2,1:T(8,128)S(1)} %collective-permute-done.5, ...), kind=kLoop, calls=%fused_computation.29 | loop fusion | flops 9961472 | bytes 5816320 | tf_op jit(solution)/shard_map/sub | solution.py:96
  39.4 3.4 %collective-permute-done.8 = f32[32,128]{1,0:T(8,128)S(1)} collective-permute-done((f32[32,128]{1,0:T(8,128)S(1)}, f32[32,128]{1,0:T(8,128)S(1)}, u32[]{:S(2)}, u32[]{:S(2)}) %collective-permute-start.8) | collective-permute-done | bytes 16416 | tf_op jit(solution)/shard_map/ppermute | solution.py:89
  42.8 4.5 %collective-permute-start.9 = (f32[32,128]{1,0:T(8,128)S(1)}, f32[32,128]{1,0:T(8,128)S(1)}, u32[]{:S(2)}, u32[]{:S(2)}) collective-permute-start(f32[32,128]{1,0:T(8,128)S(1)} %add.107), channel_id=1, source_target_pairs={{0,2},{1,3},{2,0},{3,1},{4,6},{5,7},{6,4},{7,5},{8,10},{9,11},{10,... | collective-permute-start | bytes 49160 | tf_op jit(solution)/shard_map/ppermute | solution.py:89
  47.3 1.7 %collective-permute-done.9 = f32[32,128]{1,0:T(8,128)S(1)} collective-permute-done((f32[32,128]{1,0:T(8,128)S(1)}, f32[32,128]{1,0:T(8,128)S(1)}, u32[]{:S(2)}, u32[]{:S(2)}) %collective-permute-start.9) | collective-permute-done | bytes 16416 | tf_op jit(solution)/shard_map/ppermute | solution.py:89
  49.0 3.8 %collective-permute-start.10 = (f32[32,128]{1,0:T(8,128)S(1)}, f32[32,128]{1,0:T(8,128)S(1)}, u32[]{:S(2)}, u32[]{:S(2)}) collective-permute-start(f32[32,128]{1,0:T(8,128)S(1)} %add.108), channel_id=1, source_target_pairs={{0,4},{1,5},{2,6},{3,7},{4,0},{5,1},{6,2},{7,3},{8,12},{9,13},{10,... | collective-permute-start | bytes 49160 | tf_op jit(solution)/shard_map/ppermute | solution.py:89
  52.9 3.8 %collective-permute-done.10 = f32[32,128]{1,0:T(8,128)S(1)} collective-permute-done((f32[32,128]{1,0:T(8,128)S(1)}, f32[32,128]{1,0:T(8,128)S(1)}, u32[]{:S(2)}, u32[]{:S(2)}) %collective-permute-start.10) | collective-permute-done | bytes 16416 | tf_op jit(solution)/shard_map/ppermute | solution.py:89
  56.7 1.2 %collective-permute-done.11 = f32[32,128]{1,0:T(8,128)S(1)} collective-permute-done((f32[32,128]{1,0:T(8,128)S(1)}, f32[32,128]{1,0:T(8,128)S(1)}, u32[]{:S(2)}, u32[]{:S(2)}) %collective-permute-start.11) | collective-permute-done | bytes 16416 | tf_op jit(solution)/shard_map/ppermute | solution.py:89
  57.9 3.7 %collective-permute-done.12 = f32[32,128]{1,0:T(8,128)S(1)} collective-permute-done((f32[32,128]{1,0:T(8,128)S(1)}, f32[32,128]{1,0:T(8,128)S(1)}, u32[]{:S(2)}, u32[]{:S(2)}) %collective-permute-start.12) | collective-permute-done | bytes 16416 | tf_op jit(solution)/shard_map/ppermute | solution.py:89
  61.6 4.9 %collective-permute-done.13 = f32[32,128]{1,0:T(8,128)S(1)} collective-permute-done((f32[32,128]{1,0:T(8,128)S(1)}, f32[32,128]{1,0:T(8,128)S(1)}, u32[]{:S(2)}, u32[]{:S(2)}) %collective-permute-start.13) | collective-permute-done | bytes 16416 | tf_op jit(solution)/shard_map/ppermute | solution.py:89
  66.6 3.7 %collective-permute-done.14 = f32[32,128]{1,0:T(8,128)S(1)} collective-permute-done((f32[32,128]{1,0:T(8,128)S(1)}, f32[32,128]{1,0:T(8,128)S(1)}, u32[]{:S(2)}, u32[]{:S(2)}) %collective-permute-start.14) | collective-permute-done | bytes 16416 | tf_op jit(solution)/shard_map/ppermute | solution.py:89
  70.3 4.9 %collective-permute-done.15 = f32[32,128]{1,0:T(8,128)S(1)} collective-permute-done((f32[32,128]{1,0:T(8,128)S(1)}, f32[32,128]{1,0:T(8,128)S(1)}, u32[]{:S(2)}, u32[]{:S(2)}) %collective-permute-start.15) | collective-permute-done | bytes 16416 | tf_op jit(solution)/shard_map/ppermute | solution.py:89
  76.1 6.7 %shard_map.41 = f32[64,128]{1,0:T(8,128)} custom-call(f32[64,128]{1,0:T(8,128)} %pad_maximum_fusion.8.aug_ref), custom_call_target="tpu_custom_call" | custom-call | tf_op jit(solution)/shard_map/pallas_call | solution.py:61
  82.8 1.8 %fusion.50 = f32[64,4,8,128]{3,0,2,1:T(8,128)S(1)} fusion(f32[64,4,8,128]{3,0,2,1:T(8,128)S(1)} %fusion.12, f32[64,128]{1,0:T(8,128)} %shard_map.41), kind=kOutput, calls=%fused_computation.81 | convolution fusion | flops 201330688 | bytes 2129920 | tf_op jit(solution)/shard_map/mk,kxyz->mxyz/dot_general | solution.py:109
  84.6 1.6 %copy.31 = f32[64,4,8,128]{3,2,1,0:T(8,128)} copy(f32[64,4,8,128]{3,0,2,1:T(8,128)S(1)} %fusion.50) | data formatting | bytes 2097152
  (45 shorter events, 7.0 us)
Async XLA Ops:
  2.6 12.0 %collective-permute-start.1 = (f32[64,2,8,128]{3,0,2,1:T(8,128)S(1)}, f32[64,2,8,128]{3,0,2,1:T(8,128)S(1)}, u32[]{:S(2)}, u32[]{:S(2)}) collective-permute-start(f32[64,2,8,128]{3,0,2,1:T(8,128)S(1)} %get-tuple-element.17), channel_id=1, source_target_pairs={{0,8},{8,16},{16,24},{24,32},{32,40},{40,48},{48,56},{56,64},{64,7... | collective-permute-start | bytes 1572872 | tf_op jit(solution)/shard_map/ppermute | solution.py:14
  2.7 8.6 %collective-permute-start.3 = (f32[64,4,2,128]{3,0,2,1:T(8,128)S(1)}, f32[64,4,2,128]{3,0,2,1:T(8,128)S(1)}, u32[]{:S(2)}, u32[]{:S(2)}) collective-permute-start(f32[64,4,2,128]{3,0,2,1:T(8,128)S(1)} %get-tuple-element.23), channel_id=1, source_target_pairs={{0,1},{1,2},{2,3},{3,4},{4,5},{5,6},{6,7},{7,0},{8,9},{9,10},{10,1... | collective-permute-start | bytes 786440 | tf_op jit(solution)/shard_map/ppermute | solution.py:14
  4.7 11.5 %collective-permute-start = (f32[64,2,8,128]{3,0,2,1:T(8,128)S(1)}, f32[64,2,8,128]{3,0,2,1:T(8,128)S(1)}, u32[]{:S(2)}, u32[]{:S(2)}) collective-permute-start(f32[64,2,8,128]{3,0,2,1:T(8,128)S(1)} %get-tuple-element.16), channel_id=1, source_target_pairs={{8,0},{16,8},{24,16},{32,24},{40,32},{48,40},{56,48},{64,56},{72,6... | collective-permute-start | bytes 1572872 | tf_op jit(solution)/shard_map/ppermute | solution.py:15
  9.5 0.7 copy-start.1
  9.5 6.7 %collective-permute-start.2 = (f32[64,4,2,128]{3,0,2,1:T(8,128)S(1)}, f32[64,4,2,128]{3,0,2,1:T(8,128)S(1)}, u32[]{:S(2)}, u32[]{:S(2)}) collective-permute-start(f32[64,4,2,128]{3,0,2,1:T(8,128)S(1)} %get-tuple-element.22), channel_id=1, source_target_pairs={{1,0},{2,1},{3,2},{4,3},{5,4},{6,5},{7,6},{0,7},{9,8},{10,9},{11,1... | collective-permute-start | bytes 786440 | tf_op jit(solution)/shard_map/ppermute | solution.py:15
  10.2 4.4 %copy-start = (f32[64,4,8,128]{3,2,1,0:T(8,128)S(1)}, f32[64,4,8,128]{3,2,1,0:T(8,128)}, u32[]{:S(2)}) copy-start(f32[64,4,8,128]{3,2,1,0:T(8,128)} %param.2) | copy-start | bytes 3145732
  18.5 14.2 %collective-permute-start.4 = (f32[64,2,8,128]{3,0,2,1:T(8,128)S(1)}, f32[64,2,8,128]{3,0,2,1:T(8,128)S(1)}, u32[]{:S(2)}, u32[]{:S(2)}) collective-permute-start(f32[64,2,8,128]{3,0,2,1:T(8,128)S(1)} %get-tuple-element.12), channel_id=1, source_target_pairs={{8,0},{16,8},{24,16},{32,24},{40,32},{48,40},{56,48},{64,56},{72,6... | collective-permute-start | bytes 1572872 | tf_op jit(solution)/shard_map/ppermute | solution.py:15
  23.8 11.9 %collective-permute-start.5 = (f32[64,2,8,128]{3,0,2,1:T(8,128)S(1)}, f32[64,2,8,128]{3,0,2,1:T(8,128)S(1)}, u32[]{:S(2)}, u32[]{:S(2)}) collective-permute-start(f32[64,2,8,128]{3,0,2,1:T(8,128)S(1)} %get-tuple-element.13), channel_id=1, source_target_pairs={{0,8},{8,16},{16,24},{24,32},{32,40},{40,48},{48,56},{56,64},{64,7... | collective-permute-start | bytes 1572872 | tf_op jit(solution)/shard_map/ppermute | solution.py:14
  23.8 6.4 %collective-permute-start.6 = (f32[64,4,2,128]{3,0,2,1:T(8,128)S(1)}, f32[64,4,2,128]{3,0,2,1:T(8,128)S(1)}, u32[]{:S(2)}, u32[]{:S(2)}) collective-permute-start(f32[64,4,2,128]{3,0,2,1:T(8,128)S(1)} %get-tuple-element.14), channel_id=1, source_target_pairs={{1,0},{2,1},{3,2},{4,3},{5,4},{6,5},{7,6},{0,7},{9,8},{10,9},{11,1... | collective-permute-start | bytes 786440 | tf_op jit(solution)/shard_map/ppermute | solution.py:15
  24.2 8.5 %collective-permute-start.7 = (f32[64,4,2,128]{3,0,2,1:T(8,128)S(1)}, f32[64,4,2,128]{3,0,2,1:T(8,128)S(1)}, u32[]{:S(2)}, u32[]{:S(2)}) collective-permute-start(f32[64,4,2,128]{3,0,2,1:T(8,128)S(1)} %get-tuple-element.15), channel_id=1, source_target_pairs={{0,1},{1,2},{2,3},{3,4},{4,5},{5,6},{6,7},{7,0},{8,9},{9,10},{10,1... | collective-permute-start | bytes 786440 | tf_op jit(solution)/shard_map/ppermute | solution.py:14
  38.9 3.9 %collective-permute-start.8 = (f32[32,128]{1,0:T(8,128)S(1)}, f32[32,128]{1,0:T(8,128)S(1)}, u32[]{:S(2)}, u32[]{:S(2)}) collective-permute-start(f32[32,128]{1,0:T(8,128)S(1)} %reshape.11), channel_id=1, source_target_pairs={{0,1},{1,0},{2,3},{3,2},{4,5},{5,4},{6,7},{7,6},{8,9},{9,8},{10,11... | collective-permute-start | bytes 49160 | tf_op jit(solution)/shard_map/ppermute | solution.py:89
  42.8 6.2 %collective-permute-start.9 = (f32[32,128]{1,0:T(8,128)S(1)}, f32[32,128]{1,0:T(8,128)S(1)}, u32[]{:S(2)}, u32[]{:S(2)}) collective-permute-start(f32[32,128]{1,0:T(8,128)S(1)} %add.107), channel_id=1, source_target_pairs={{0,2},{1,3},{2,0},{3,1},{4,6},{5,7},{6,4},{7,5},{8,10},{9,11},{10,... | collective-permute-start | bytes 49160 | tf_op jit(solution)/shard_map/ppermute | solution.py:89
  49.0 7.6 %collective-permute-start.10 = (f32[32,128]{1,0:T(8,128)S(1)}, f32[32,128]{1,0:T(8,128)S(1)}, u32[]{:S(2)}, u32[]{:S(2)}) collective-permute-start(f32[32,128]{1,0:T(8,128)S(1)} %add.108), channel_id=1, source_target_pairs={{0,4},{1,5},{2,6},{3,7},{4,0},{5,1},{6,2},{7,3},{8,12},{9,13},{10,... | collective-permute-start | bytes 49160 | tf_op jit(solution)/shard_map/ppermute | solution.py:89
  56.7 1.2 %collective-permute-start.11 = (f32[32,128]{1,0:T(8,128)S(1)}, f32[32,128]{1,0:T(8,128)S(1)}, u32[]{:S(2)}, u32[]{:S(2)}) collective-permute-start(f32[32,128]{1,0:T(8,128)S(1)} %add.109), channel_id=1, source_target_pairs={{0,8},{8,0},{16,24},{24,16},{32,40},{40,32},{48,56},{56,48},{64,72... | collective-permute-start | bytes 49160 | tf_op jit(solution)/shard_map/ppermute | solution.py:89
  57.9 3.7 %collective-permute-start.12 = (f32[32,128]{1,0:T(8,128)S(1)}, f32[32,128]{1,0:T(8,128)S(1)}, u32[]{:S(2)}, u32[]{:S(2)}) collective-permute-start(f32[32,128]{1,0:T(8,128)S(1)} %add.110), channel_id=1, source_target_pairs={{0,16},{8,24},{16,0},{24,8},{32,48},{40,56},{48,32},{56,40},{64,80... | collective-permute-start | bytes 49160 | tf_op jit(solution)/shard_map/ppermute | solution.py:89
  61.6 4.9 %collective-permute-start.13 = (f32[32,128]{1,0:T(8,128)S(1)}, f32[32,128]{1,0:T(8,128)S(1)}, u32[]{:S(2)}, u32[]{:S(2)}) collective-permute-start(f32[32,128]{1,0:T(8,128)S(1)} %add.111), channel_id=1, source_target_pairs={{0,48},{8,56},{16,32},{24,40},{32,16},{40,24},{48,0},{56,8},{64,11... | collective-permute-start | bytes 49160 | tf_op jit(solution)/shard_map/ppermute | solution.py:89
  66.6 3.7 %collective-permute-start.14 = (f32[32,128]{1,0:T(8,128)S(1)}, f32[32,128]{1,0:T(8,128)S(1)}, u32[]{:S(2)}, u32[]{:S(2)}) collective-permute-start(f32[32,128]{1,0:T(8,128)S(1)} %add.112), channel_id=1, source_target_pairs={{0,64},{8,72},{16,80},{24,88},{32,96},{40,104},{48,112},{56,120},{... | collective-permute-start | bytes 49160 | tf_op jit(solution)/shard_map/ppermute | solution.py:89
  70.3 4.9 %collective-permute-start.15 = (f32[32,128]{1,0:T(8,128)S(1)}, f32[32,128]{1,0:T(8,128)S(1)}, u32[]{:S(2)}, u32[]{:S(2)}) collective-permute-start(f32[32,128]{1,0:T(8,128)S(1)} %add.113), channel_id=1, source_target_pairs={{0,192},{8,200},{16,208},{24,216},{32,224},{40,232},{48,240},{56,2... | collective-permute-start | bytes 49160 | tf_op jit(solution)/shard_map/ppermute | solution.py:89

commit v8 on v7

--- a/solution.py
+++ b/solution.py
@@ -37,16 +37,22 @@
     blocks = [aug_ref[pl.ds(8 * i, 8), :] for i in range(groups)]
     sub = lax.broadcasted_iota(jnp.int32, blocks[0].shape, 0)
     lane = lax.broadcasted_iota(jnp.int32, blocks[0].shape, 1)
-    for k in range(order):
+    for k in range(0, order, 2):
         home, place = divmod(k, 8)
-        row = blocks[home][place:place + 1, :]
-        inverse = 1.0 / row[:, k:k + 1]
+        first_row = blocks[home][place:place + 1, :]
+        first_inverse = 1.0 / first_row[:, k:k + 1]
+        second_row = blocks[home][place + 1:place + 2, :]
+        second_row = second_row - (second_row[:, k:k + 1] * first_inverse) * first_row
+        second_inverse = 1.0 / second_row[:, k + 1:k + 2]
+        coupling = first_row[:, k + 1:k + 2]
         for j in range(home, groups):
             block = blocks[j]
-            column = block[:, k:k + 1] * inverse
+            first_column = block[:, k:k + 1] * first_inverse
+            second_column = (block[:, k + 1:k + 2] - first_column * coupling) * second_inverse
             if j == home:
-                column = jnp.where(sub[:, :1] > place, column, 0.0)
-            blocks[j] = block - column * row
+                first_column = jnp.where(sub[:, :1] > place, first_column, 0.0)
+                second_column = jnp.where(sub[:, :1] > place + 1, second_column, 0.0)
+            blocks[j] = block - first_column * first_row - second_column * second_row
     for i in range(groups):
         block = blocks[i]
         pivots = jnp.sum(jnp.where(lane == sub + 8 * i, block, 0.0), axis=1, keepdims=True)

time: 86.5 us -> 87.8 us (1.015)
  Pallas kernels: 6.66 us -> 8.02 us
    pallas_call x1, Pallas kernels: 6.66 us -> 8.02 us  [factor_and_inverse(): pl.pallas_call(factor_kernel, out_shape=jax.ShapeDtypeStruct(aug.shape, j...]
where the time goes in v8:
time: 87.8 us; the launch traced here: 87.5 us
  waiting for transfers between devices  42.1 us (48%)
  starting transfers between devices  23.4 us (27%)
  Pallas kernels  8.02 us (9%)
  local copies, waits for them, and re-layouts  5.47 us (6%)
  other arithmetic  4.97 us (6%)
  matrix products  2.76 us (3%)
    ppermute x8, waiting for transfers between devices, butterfly_sum(): lax.ppermute(value, axis, [(i, partner(i)) for i in range(count)])  27.5 us
    ppermute x4, starting transfers between devices, faces(): lax.ppermute(head, axis, [((i + 1) % count, i) for i in range(count)])  10.7 us
    ppermute x4, waiting for transfers between devices, faces(): lax.ppermute(tail, axis, [(i, (i + 1) % count) for i in range(count)])  9.78 us
    ppermute x8, starting transfers between devices, butterfly_sum(): lax.ppermute(value, axis, [(i, partner(i)) for i in range(count)])  8.84 us
    pallas_call x1, Pallas kernels, factor_and_inverse(): pl.pallas_call(factor_kernel, out_shape=jax.ShapeDtypeStruct(aug.shape, j...  8.02 us
    ppermute x4, waiting for transfers between devices, faces(): lax.ppermute(head, axis, [((i + 1) % count, i) for i in range(count)])  4.83 us
    unnamed x9, local copies, waits for them, and re-layouts  4.2 us
    ppermute x4, starting transfers between devices, faces(): lax.ppermute(tail, axis, [(i, (i + 1) % count) for i in range(count)])  3.81 us
  transfers between devices with their start and end apart: 16, of which 14 were waited for; matrix products, arithmetic and copies ran while one was open for 2% of the time, Pallas kernels for 0%

profile of v8, /device:TPU:32, one launch (start us, length us, event | category | flops | bytes accessed | tf_op | source)
XLA Modules:
  0.0 87.5 jit_solution(1504149373525349238)
XLA Ops:
  0.6 1.8 %copy.14 = f32[64,4,8,128]{3,0,2,1:T(8,128)S(1)} copy(f32[64,4,8,128]{3,2,1,0:T(8,128)} %param.2) | data formatting | bytes 2097152 | tf_op args[0]
  2.7 2.0 %collective-permute-start.3 = (f32[64,4,2,128]{3,0,2,1:T(8,128)S(1)}, f32[64,4,2,128]{3,0,2,1:T(8,128)S(1)}, u32[]{:S(2)}, u32[]{:S(2)}) collective-permute-start(f32[64,4,2,128]{3,0,2,1:T(8,128)S(1)} %get-tuple-element.23), channel_id=1, source_target_pairs={{0,1},{1,2},{2,3},{3,4},{4,5},{5,6},{6,7},{7,0},{8,9},{9,10},{10,1... | collective-permute-start | bytes 786440 | tf_op jit(solution)/shard_map/ppermute | solution.py:14
  4.7 4.8 %collective-permute-start = (f32[64,2,8,128]{3,0,2,1:T(8,128)S(1)}, f32[64,2,8,128]{3,0,2,1:T(8,128)S(1)}, u32[]{:S(2)}, u32[]{:S(2)}) collective-permute-start(f32[64,2,8,128]{3,0,2,1:T(8,128)S(1)} %get-tuple-element.16), channel_id=1, source_target_pairs={{8,0},{16,8},{24,16},{32,24},{40,32},{48,40},{56,48},{64,56},{72,6... | collective-permute-start | bytes 1572872 | tf_op jit(solution)/shard_map/ppermute | solution.py:15
  11.3 3.2 %collective-permute-done.1 = f32[64,2,8,128]{3,0,2,1:T(8,128)S(1)} collective-permute-done((f32[64,2,8,128]{3,0,2,1:T(8,128)S(1)}, f32[64,2,8,128]{3,0,2,1:T(8,128)S(1)}, u32[]{:S(2)}, u32[]{:S(2)}) %collective-permute-start.1) | collective-permute-done | bytes 524320 | tf_op jit(solution)/shard_map/ppermute | solution.py:14
  16.3 2.1 %broadcast_multiply_fusion = (f32[64,4,8,128]{3,0,2,1:T(8,128)S(1)}, f32[64,4,8,128]{3,0,2,1:T(8,128)S(1)}) fusion(f32[64,4,8,128]{3,0,2,1:T(8,128)S(1)} %copy.14, f32[4,8,128]{2,1,0:T(8,128)S(1)} %copy-done.1, f32[64,4,8,2]{3,0,2,1:T(8,128)S(1)} %get-tuple-element.25, f32[64,4,8,2]{3,0,2,1:T(8,128)S(1)} %get-tuple-element.24, ...), kind=kLoop, calls=%fused_computation.78 | loop fusion | flops 7602176 | bytes 11583488 | tf_op jit(solution)/shard_map/div | solution.py:100
  18.5 5.3 %collective-permute-start.4 = (f32[64,2,8,128]{3,0,2,1:T(8,128)S(1)}, f32[64,2,8,128]{3,0,2,1:T(8,128)S(1)}, u32[]{:S(2)}, u32[]{:S(2)}) collective-permute-start(f32[64,2,8,128]{3,0,2,1:T(8,128)S(1)} %get-tuple-element.12), channel_id=1, source_target_pairs={{8,0},{16,8},{24,16},{32,24},{40,32},{48,40},{56,48},{64,56},{72,6... | collective-permute-start | bytes 1572872 | tf_op jit(solution)/shard_map/ppermute | solution.py:15
  24.2 1.7 %collective-permute-start.7 = (f32[64,4,2,128]{3,0,2,1:T(8,128)S(1)}, f32[64,4,2,128]{3,0,2,1:T(8,128)S(1)}, u32[]{:S(2)}, u32[]{:S(2)}) collective-permute-start(f32[64,4,2,128]{3,0,2,1:T(8,128)S(1)} %get-tuple-element.15), channel_id=1, source_target_pairs={{0,1},{1,2},{2,3},{3,4},{4,5},{5,6},{6,7},{7,0},{8,9},{9,10},{10,1... | collective-permute-start | bytes 786440 | tf_op jit(solution)/shard_map/ppermute | solution.py:14
  26.3 4.0 %collective-permute-done.6 = f32[64,4,2,128]{3,0,2,1:T(8,128)S(1)} collective-permute-done((f32[64,4,2,128]{3,0,2,1:T(8,128)S(1)}, f32[64,4,2,128]{3,0,2,1:T(8,128)S(1)}, u32[]{:S(2)}, u32[]{:S(2)}) %collective-permute-start.6) | collective-permute-done | bytes 262176 | tf_op jit(solution)/shard_map/ppermute | solution.py:15
  30.3 2.4 %collective-permute-done.7 = f32[64,4,2,128]{3,0,2,1:T(8,128)S(1)} collective-permute-done((f32[64,4,2,128]{3,0,2,1:T(8,128)S(1)}, f32[64,4,2,128]{3,0,2,1:T(8,128)S(1)}, u32[]{:S(2)}, u32[]{:S(2)}) %collective-permute-start.7) | collective-permute-done | bytes 262176 | tf_op jit(solution)/shard_map/ppermute | solution.py:14
  32.6 3.0 %collective-permute-done.5 = f32[64,2,8,128]{3,0,2,1:T(8,128)S(1)} collective-permute-done((f32[64,2,8,128]{3,0,2,1:T(8,128)S(1)}, f32[64,2,8,128]{3,0,2,1:T(8,128)S(1)}, u32[]{:S(2)}, u32[]{:S(2)}) %collective-permute-start.5) | collective-permute-done | bytes 524320 | tf_op jit(solution)/shard_map/ppermute | solution.py:14
  35.7 2.1 %fusion.12 = f32[64,4,8,128]{3,0,2,1:T(8,128)S(1)} fusion(f32[64,4,2,128]{3,0,2,1:T(8,128)S(1)} %collective-permute-done.7, f32[64,4,8,128]{3,0,2,1:T(8,128)S(1)} %get-tuple-element.8, f32[64,4,2,128]{3,0,2,1:T(8,128)S(1)} %collective-permute-done.6, f32[64,2,8,128]{3,0,2,1:T(8,128)S(1)} %collective-permute-done.5, ...), kind=kLoop, calls=%fused_computation.29 | loop fusion | flops 9961472 | bytes 5816320 | tf_op jit(solution)/shard_map/sub | solution.py:102
  39.4 3.4 %collective-permute-done.8 = f32[32,128]{1,0:T(8,128)S(1)} collective-permute-done((f32[32,128]{1,0:T(8,128)S(1)}, f32[32,128]{1,0:T(8,128)S(1)}, u32[]{:S(2)}, u32[]{:S(2)}) %collective-permute-start.8) | collective-permute-done | bytes 16416 | tf_op jit(solution)/shard_map/ppermute | solution.py:95
  42.8 4.5 %collective-permute-start.9 = (f32[32,128]{1,0:T(8,128)S(1)}, f32[32,128]{1,0:T(8,128)S(1)}, u32[]{:S(2)}, u32[]{:S(2)}) collective-permute-start(f32[32,128]{1,0:T(8,128)S(1)} %add.107), channel_id=1, source_target_pairs={{0,2},{1,3},{2,0},{3,1},{4,6},{5,7},{6,4},{7,5},{8,10},{9,11},{10,... | collective-permute-start | bytes 49160 | tf_op jit(solution)/shard_map/ppermute | solution.py:95
  47.3 1.7 %collective-permute-done.9 = f32[32,128]{1,0:T(8,128)S(1)} collective-permute-done((f32[32,128]{1,0:T(8,128)S(1)}, f32[32,128]{1,0:T(8,128)S(1)}, u32[]{:S(2)}, u32[]{:S(2)}) %collective-permute-start.9) | collective-permute-done | bytes 16416 | tf_op jit(solution)/shard_map/ppermute | solution.py:95
  49.0 3.8 %collective-permute-start.10 = (f32[32,128]{1,0:T(8,128)S(1)}, f32[32,128]{1,0:T(8,128)S(1)}, u32[]{:S(2)}, u32[]{:S(2)}) collective-permute-start(f32[32,128]{1,0:T(8,128)S(1)} %add.108), channel_id=1, source_target_pairs={{0,4},{1,5},{2,6},{3,7},{4,0},{5,1},{6,2},{7,3},{8,12},{9,13},{10,... | collective-permute-start | bytes 49160 | tf_op jit(solution)/shard_map/ppermute | solution.py:95
  52.9 3.8 %collective-permute-done.10 = f32[32,128]{1,0:T(8,128)S(1)} collective-permute-done((f32[32,128]{1,0:T(8,128)S(1)}, f32[32,128]{1,0:T(8,128)S(1)}, u32[]{:S(2)}, u32[]{:S(2)}) %collective-permute-start.10) | collective-permute-done | bytes 16416 | tf_op jit(solution)/shard_map/ppermute | solution.py:95
  56.7 1.2 %collective-permute-done.11 = f32[32,128]{1,0:T(8,128)S(1)} collective-permute-done((f32[32,128]{1,0:T(8,128)S(1)}, f32[32,128]{1,0:T(8,128)S(1)}, u32[]{:S(2)}, u32[]{:S(2)}) %collective-permute-start.11) | collective-permute-done | bytes 16416 | tf_op jit(solution)/shard_map/ppermute | solution.py:95
  57.9 3.7 %collective-permute-done.12 = f32[32,128]{1,0:T(8,128)S(1)} collective-permute-done((f32[32,128]{1,0:T(8,128)S(1)}, f32[32,128]{1,0:T(8,128)S(1)}, u32[]{:S(2)}, u32[]{:S(2)}) %collective-permute-start.12) | collective-permute-done | bytes 16416 | tf_op jit(solution)/shard_map/ppermute | solution.py:95
  61.6 4.9 %collective-permute-done.13 = f32[32,128]{1,0:T(8,128)S(1)} collective-permute-done((f32[32,128]{1,0:T(8,128)S(1)}, f32[32,128]{1,0:T(8,128)S(1)}, u32[]{:S(2)}, u32[]{:S(2)}) %collective-permute-start.13) | collective-permute-done | bytes 16416 | tf_op jit(solution)/shard_map/ppermute | solution.py:95
  66.6 3.7 %collective-permute-done.14 = f32[32,128]{1,0:T(8,128)S(1)} collective-permute-done((f32[32,128]{1,0:T(8,128)S(1)}, f32[32,128]{1,0:T(8,128)S(1)}, u32[]{:S(2)}, u32[]{:S(2)}) %collective-permute-start.14) | collective-permute-done | bytes 16416 | tf_op jit(solution)/shard_map/ppermute | solution.py:95
  70.3 4.9 %collective-permute-done.15 = f32[32,128]{1,0:T(8,128)S(1)} collective-permute-done((f32[32,128]{1,0:T(8,128)S(1)}, f32[32,128]{1,0:T(8,128)S(1)}, u32[]{:S(2)}, u32[]{:S(2)}) %collective-permute-start.15) | collective-permute-done | bytes 16416 | tf_op jit(solution)/shard_map/ppermute | solution.py:95
  76.1 8.0 %shard_map.41 = f32[64,128]{1,0:T(8,128)} custom-call(f32[64,128]{1,0:T(8,128)} %pad_maximum_fusion.8.aug_ref), custom_call_target="tpu_custom_call" | custom-call | tf_op jit(solution)/shard_map/pallas_call | solution.py:67
  84.2 1.8 %fusion.50 = f32[64,4,8,128]{3,0,2,1:T(8,128)S(1)} fusion(f32[64,4,8,128]{3,0,2,1:T(8,128)S(1)} %fusion.12, f32[64,128]{1,0:T(8,128)} %shard_map.41), kind=kOutput, calls=%fused_computation.81 | convolution fusion | flops 201330688 | bytes 2129920 | tf_op jit(solution)/shard_map/mk,kxyz->mxyz/dot_general | solution.py:115
  86.0 1.6 %copy.31 = f32[64,4,8,128]{3,2,1,0:T(8,128)} copy(f32[64,4,8,128]{3,0,2,1:T(8,128)S(1)} %fusion.50) | data formatting | bytes 2097152
  (45 shorter events, 7.0 us)
Async XLA Ops:
  2.6 12.0 %collective-permute-start.1 = (f32[64,2,8,128]{3,0,2,1:T(8,128)S(1)}, f32[64,2,8,128]{3,0,2,1:T(8,128)S(1)}, u32[]{:S(2)}, u32[]{:S(2)}) collective-permute-start(f32[64,2,8,128]{3,0,2,1:T(8,128)S(1)} %get-tuple-element.17), channel_id=1, source_target_pairs={{0,8},{8,16},{16,24},{24,32},{32,40},{40,48},{48,56},{56,64},{64,7... | collective-permute-start | bytes 1572872 | tf_op jit(solution)/shard_map/ppermute | solution.py:14
  2.7 8.6 %collective-permute-start.3 = (f32[64,4,2,128]{3,0,2,1:T(8,128)S(1)}, f32[64,4,2,128]{3,0,2,1:T(8,128)S(1)}, u32[]{:S(2)}, u32[]{:S(2)}) collective-permute-start(f32[64,4,2,128]{3,0,2,1:T(8,128)S(1)} %get-tuple-element.23), channel_id=1, source_target_pairs={{0,1},{1,2},{2,3},{3,4},{4,5},{5,6},{6,7},{7,0},{8,9},{9,10},{10,1... | collective-permute-start | bytes 786440 | tf_op jit(solution)/shard_map/ppermute | solution.py:14
  4.7 11.5 %collective-permute-start = (f32[64,2,8,128]{3,0,2,1:T(8,128)S(1)}, f32[64,2,8,128]{3,0,2,1:T(8,128)S(1)}, u32[]{:S(2)}, u32[]{:S(2)}) collective-permute-start(f32[64,2,8,128]{3,0,2,1:T(8,128)S(1)} %get-tuple-element.16), channel_id=1, source_target_pairs={{8,0},{16,8},{24,16},{32,24},{40,32},{48,40},{56,48},{64,56},{72,6... | collective-permute-start | bytes 1572872 | tf_op jit(solution)/shard_map/ppermute | solution.py:15
  9.5 0.7 copy-start.1
  9.5 6.7 %collective-permute-start.2 = (f32[64,4,2,128]{3,0,2,1:T(8,128)S(1)}, f32[64,4,2,128]{3,0,2,1:T(8,128)S(1)}, u32[]{:S(2)}, u32[]{:S(2)}) collective-permute-start(f32[64,4,2,128]{3,0,2,1:T(8,128)S(1)} %get-tuple-element.22), channel_id=1, source_target_pairs={{1,0},{2,1},{3,2},{4,3},{5,4},{6,5},{7,6},{0,7},{9,8},{10,9},{11,1... | collective-permute-start | bytes 786440 | tf_op jit(solution)/shard_map/ppermute | solution.py:15
  10.2 4.4 %copy-start = (f32[64,4,8,128]{3,2,1,0:T(8,128)S(1)}, f32[64,4,8,128]{3,2,1,0:T(8,128)}, u32[]{:S(2)}) copy-start(f32[64,4,8,128]{3,2,1,0:T(8,128)} %param.2) | copy-start | bytes 3145732
  18.5 14.2 %collective-permute-start.4 = (f32[64,2,8,128]{3,0,2,1:T(8,128)S(1)}, f32[64,2,8,128]{3,0,2,1:T(8,128)S(1)}, u32[]{:S(2)}, u32[]{:S(2)}) collective-permute-start(f32[64,2,8,128]{3,0,2,1:T(8,128)S(1)} %get-tuple-element.12), channel_id=1, source_target_pairs={{8,0},{16,8},{24,16},{32,24},{40,32},{48,40},{56,48},{64,56},{72,6... | collective-permute-start | bytes 1572872 | tf_op jit(solution)/shard_map/ppermute | solution.py:15
  23.8 11.9 %collective-permute-start.5 = (f32[64,2,8,128]{3,0,2,1:T(8,128)S(1)}, f32[64,2,8,128]{3,0,2,1:T(8,128)S(1)}, u32[]{:S(2)}, u32[]{:S(2)}) collective-permute-start(f32[64,2,8,128]{3,0,2,1:T(8,128)S(1)} %get-tuple-element.13), channel_id=1, source_target_pairs={{0,8},{8,16},{16,24},{24,32},{32,40},{40,48},{48,56},{56,64},{64,7... | collective-permute-start | bytes 1572872 | tf_op jit(solution)/shard_map/ppermute | solution.py:14
  23.8 6.4 %collective-permute-start.6 = (f32[64,4,2,128]{3,0,2,1:T(8,128)S(1)}, f32[64,4,2,128]{3,0,2,1:T(8,128)S(1)}, u32[]{:S(2)}, u32[]{:S(2)}) collective-permute-start(f32[64,4,2,128]{3,0,2,1:T(8,128)S(1)} %get-tuple-element.14), channel_id=1, source_target_pairs={{1,0},{2,1},{3,2},{4,3},{5,4},{6,5},{7,6},{0,7},{9,8},{10,9},{11,1... | collective-permute-start | bytes 786440 | tf_op jit(solution)/shard_map/ppermute | solution.py:15
  24.2 8.5 %collective-permute-start.7 = (f32[64,4,2,128]{3,0,2,1:T(8,128)S(1)}, f32[64,4,2,128]{3,0,2,1:T(8,128)S(1)}, u32[]{:S(2)}, u32[]{:S(2)}) collective-permute-start(f32[64,4,2,128]{3,0,2,1:T(8,128)S(1)} %get-tuple-element.15), channel_id=1, source_target_pairs={{0,1},{1,2},{2,3},{3,4},{4,5},{5,6},{6,7},{7,0},{8,9},{9,10},{10,1... | collective-permute-start | bytes 786440 | tf_op jit(solution)/shard_map/ppermute | solution.py:14
  38.9 3.9 %collective-permute-start.8 = (f32[32,128]{1,0:T(8,128)S(1)}, f32[32,128]{1,0:T(8,128)S(1)}, u32[]{:S(2)}, u32[]{:S(2)}) collective-permute-start(f32[32,128]{1,0:T(8,128)S(1)} %reshape.11), channel_id=1, source_target_pairs={{0,1},{1,0},{2,3},{3,2},{4,5},{5,4},{6,7},{7,6},{8,9},{9,8},{10,11... | collective-permute-start | bytes 49160 | tf_op jit(solution)/shard_map/ppermute | solution.py:95
  42.8 6.2 %collective-permute-start.9 = (f32[32,128]{1,0:T(8,128)S(1)}, f32[32,128]{1,0:T(8,128)S(1)}, u32[]{:S(2)}, u32[]{:S(2)}) collective-permute-start(f32[32,128]{1,0:T(8,128)S(1)} %add.107), channel_id=1, source_target_pairs={{0,2},{1,3},{2,0},{3,1},{4,6},{5,7},{6,4},{7,5},{8,10},{9,11},{10,... | collective-permute-start | bytes 49160 | tf_op jit(solution)/shard_map/ppermute | solution.py:95
  49.0 7.6 %collective-permute-start.10 = (f32[32,128]{1,0:T(8,128)S(1)}, f32[32,128]{1,0:T(8,128)S(1)}, u32[]{:S(2)}, u32[]{:S(2)}) collective-permute-start(f32[32,128]{1,0:T(8,128)S(1)} %add.108), channel_id=1, source_target_pairs={{0,4},{1,5},{2,6},{3,7},{4,0},{5,1},{6,2},{7,3},{8,12},{9,13},{10,... | collective-permute-start | bytes 49160 | tf_op jit(solution)/shard_map/ppermute | solution.py:95
  56.7 1.2 %collective-permute-start.11 = (f32[32,128]{1,0:T(8,128)S(1)}, f32[32,128]{1,0:T(8,128)S(1)}, u32[]{:S(2)}, u32[]{:S(2)}) collective-permute-start(f32[32,128]{1,0:T(8,128)S(1)} %add.109), channel_id=1, source_target_pairs={{0,8},{8,0},{16,24},{24,16},{32,40},{40,32},{48,56},{56,48},{64,72... | collective-permute-start | bytes 49160 | tf_op jit(solution)/shard_map/ppermute | solution.py:95
  57.9 3.7 %collective-permute-start.12 = (f32[32,128]{1,0:T(8,128)S(1)}, f32[32,128]{1,0:T(8,128)S(1)}, u32[]{:S(2)}, u32[]{:S(2)}) collective-permute-start(f32[32,128]{1,0:T(8,128)S(1)} %add.110), channel_id=1, source_target_pairs={{0,16},{8,24},{16,0},{24,8},{32,48},{40,56},{48,32},{56,40},{64,80... | collective-permute-start | bytes 49160 | tf_op jit(solution)/shard_map/ppermute | solution.py:95
  61.6 4.9 %collective-permute-start.13 = (f32[32,128]{1,0:T(8,128)S(1)}, f32[32,128]{1,0:T(8,128)S(1)}, u32[]{:S(2)}, u32[]{:S(2)}) collective-permute-start(f32[32,128]{1,0:T(8,128)S(1)} %add.111), channel_id=1, source_target_pairs={{0,48},{8,56},{16,32},{24,40},{32,16},{40,24},{48,0},{56,8},{64,11... | collective-permute-start | bytes 49160 | tf_op jit(solution)/shard_map/ppermute | solution.py:95
  66.6 3.7 %collective-permute-start.14 = (f32[32,128]{1,0:T(8,128)S(1)}, f32[32,128]{1,0:T(8,128)S(1)}, u32[]{:S(2)}, u32[]{:S(2)}) collective-permute-start(f32[32,128]{1,0:T(8,128)S(1)} %add.112), channel_id=1, source_target_pairs={{0,64},{8,72},{16,80},{24,88},{32,96},{40,104},{48,112},{56,120},{... | collective-permute-start | bytes 49160 | tf_op jit(solution)/shard_map/ppermute | solution.py:95
  70.3 4.9 %collective-permute-start.15 = (f32[32,128]{1,0:T(8,128)S(1)}, f32[32,128]{1,0:T(8,128)S(1)}, u32[]{:S(2)}, u32[]{:S(2)}) collective-permute-start(f32[32,128]{1,0:T(8,128)S(1)} %add.113), channel_id=1, source_target_pairs={{0,192},{8,200},{16,208},{24,216},{32,224},{40,232},{48,240},{56,2... | collective-permute-start | bytes 49160 | tf_op jit(solution)/shard_map/ppermute | solution.py:95

commit v9 on v7

--- a/solution.py
+++ b/solution.py
@@ -16,9 +16,13 @@
     return jnp.concatenate([before, cells, after], axis=dim)
 
 
-def apply_ham(core, pot):
-    along_x = faces(core, "gx", 1, 2)
-    along_y = faces(core, "gy", 2, 2)
+def apply_ham(core, pot, source=None):
+    source = core if source is None else source
+    along_x = faces(source, "gx", 1, 2)
+    along_y = faces(source, "gy", 2, 2)
+    if source is not core:
+        along_x = jnp.concatenate([along_x[:, :2], core, along_x[:, -2:]], axis=1)
+        along_y = jnp.concatenate([along_y[:, :, :2], core, along_y[:, :, -2:]], axis=2)
     total = -7.5 * core
     total = total + 4.0 / 3.0 * (along_x[:, 3:-1] + along_x[:, 1:-3])
     total = total - 1.0 / 12.0 * (along_x[:, 4:] + along_x[:, :-4])
@@ -91,9 +95,10 @@
 
 
 def shards(orbitals, potential):
-    first = (apply_ham(orbitals, potential) - 5.5 * orbitals) / 4.5
+    orbitals_here = lax.optimization_barrier(orbitals)
+    first = (apply_ham(orbitals_here, potential, orbitals) - 5.5 * orbitals_here) / 4.5
     applied = apply_ham(first, potential)
-    filtered = 2.0 * (applied - 5.5 * first) / 4.5 - orbitals
+    filtered = 2.0 * (applied - 5.5 * first) / 4.5 - orbitals_here
     count = filtered.shape[1] * filtered.shape[2] * filtered.shape[3]
     cells = count * lax.axis_size("gx") * lax.axis_size("gy")
     local_gram = (

time: 86.5 us -> 85.7 us (level)
  waiting for transfers between devices: 42.1 us -> 37.8 us
  starting transfers between devices: 23.4 us -> 26.6 us
    ppermute x4, waiting for transfers between devices: 4.83 us -> 1.99 us  [faces(): lax.ppermute(head, axis, [((i + 1) % count, i) for i in range(count)])]
    ppermute x4, starting transfers between devices: 10.7 us -> 12.5 us  [faces(): lax.ppermute(head, axis, [((i + 1) % count, i) for i in range(count)])]
    ppermute x4, waiting for transfers between devices: 9.78 us -> 8.37 us  [faces(): lax.ppermute(tail, axis, [(i, (i + 1) % count) for i in range(count)])]
    slice x4, local copies, waits for them, and re-layouts: 0.25 us -> 1.64 us  [faces(): head = lax.slice_in_dim(cells, 0, width, axis=dim)]
    unnamed x9 -> x12, local copies, waits for them, and re-layouts: 4.2 us -> 2.82 us
    ppermute x8, starting transfers between devices: 8.84 us -> 10 us  [butterfly_sum(): lax.ppermute(value, axis, [(i, partner(i)) for i in range(count)])]
  transfers between devices with their start and end apart: 16 -> 16, of which waited for: 14 -> 13; matrix products, arithmetic and copies ran while one was open for 2% -> 2% of each run, Pallas kernels for 0% -> 0%
where the time goes in v9:
time: 85.7 us; the launch traced here: 85.5 us
  waiting for transfers between devices  37.8 us (44%)
  starting transfers between devices  26.6 us (31%)
  Pallas kernels  6.66 us (8%)
  local copies, waits for them, and re-layouts  5.48 us (6%)
  other arithmetic  5.32 us (6%)
  matrix products  2.76 us (3%)
    ppermute x8, waiting for transfers between devices, butterfly_sum(): lax.ppermute(value, axis, [(i, partner(i)) for i in range(count)])  27.4 us
    ppermute x4, starting transfers between devices, faces(): lax.ppermute(head, axis, [((i + 1) % count, i) for i in range(count)])  12.5 us
    ppermute x8, starting transfers between devices, butterfly_sum(): lax.ppermute(value, axis, [(i, partner(i)) for i in range(count)])  10 us
    ppermute x4, waiting for transfers between devices, faces(): lax.ppermute(tail, axis, [(i, (i + 1) % count) for i in range(count)])  8.37 us
    pallas_call x1, Pallas kernels, factor_and_inverse(): pl.pallas_call(factor_kernel, out_shape=jax.ShapeDtypeStruct(aug.shape, j...  6.66 us
    ppermute x4, starting transfers between devices, faces(): lax.ppermute(tail, axis, [(i, (i + 1) % count) for i in range(count)])  4.15 us
    unnamed x12, local copies, waits for them, and re-layouts  2.82 us
    sub x1, other arithmetic, shards(): filtered = 2.0 * (applied - 5.5 * first) / 4.5 - orbitals_here  2.37 us
  transfers between devices with their start and end apart: 16, of which 13 were waited for; matrix products, arithmetic and copies ran while one was open for 2% of the time, Pallas kernels for 0%

profile of v9, /device:TPU:32, one launch (start us, length us, event | category | flops | bytes accessed | tf_op | source)
XLA Modules:
  0.0 85.5 jit_solution(14693521352269892080)
XLA Ops:
  0.6 1.4 %fusion.60 = (f32[64,2,8,128]{3,2,1,0:T(8,128)S(1)}, f32[64,2,8,128]{3,2,1,0:T(8,128)S(1)}) fusion(f32[64,4,8,128]{3,2,1,0:T(8,128)} %param.2), kind=kLoop, calls=%fused_computation.101 | loop fusion | bytes 2097152 | tf_op jit(solution)/shard_map/slice | solution.py:12
  2.5 2.0 %collective-permute-start.3 = (f32[64,4,2,128]{3,0,2,1:T(8,128)S(1)}, f32[64,4,2,128]{3,0,2,1:T(8,128)S(1)}, u32[]{:S(2)}, u32[]{:S(2)}) collective-permute-start(f32[64,4,2,128]{3,0,2,1:T(8,128)S(1)} %copy.37), channel_id=1, source_target_pairs={{0,1},{1,2},{2,3},{3,4},{4,5},{5,6},{6,7},{7,0},{8,9},{9,10},{10,1... | collective-permute-start | bytes 786440 | tf_op jit(solution)/shard_map/ppermute | solution.py:14
  4.9 4.7 %collective-permute-start = (f32[64,2,8,128]{3,0,2,1:T(8,128)S(1)}, f32[64,2,8,128]{3,0,2,1:T(8,128)S(1)}, u32[]{:S(2)}, u32[]{:S(2)}) collective-permute-start(f32[64,2,8,128]{3,0,2,1:T(8,128)S(1)} %copy.34), channel_id=1, source_target_pairs={{8,0},{16,8},{24,16},{32,24},{40,32},{48,40},{56,48},{64,56},{72,6... | collective-permute-start | bytes 1572872 | tf_op jit(solution)/shard_map/ppermute | solution.py:15
  9.7 1.4 %collective-permute-done.3 = f32[64,4,2,128]{3,0,2,1:T(8,128)S(1)} collective-permute-done((f32[64,4,2,128]{3,0,2,1:T(8,128)S(1)}, f32[64,4,2,128]{3,0,2,1:T(8,128)S(1)}, u32[]{:S(2)}, u32[]{:S(2)}) %collective-permute-start.3) | collective-permute-done | bytes 262176 | tf_op jit(solution)/shard_map/ppermute | solution.py:14
  11.2 3.0 %collective-permute-done.1 = f32[64,2,8,128]{3,0,2,1:T(8,128)S(1)} collective-permute-done((f32[64,2,8,128]{3,0,2,1:T(8,128)S(1)}, f32[64,2,8,128]{3,0,2,1:T(8,128)S(1)}, u32[]{:S(2)}, u32[]{:S(2)}) %collective-permute-start.1) | collective-permute-done | bytes 524320 | tf_op jit(solution)/shard_map/ppermute | solution.py:14
  16.4 2.2 %broadcast_multiply_fusion = (f32[64,4,8,128]{3,0,2,1:T(8,128)S(1)}, f32[64,4,8,128]{3,0,2,1:T(8,128)S(1)}) fusion(f32[64,4,8,128]{3,0,2,1:T(8,128)S(1)} %get-tuple-element.22, f32[4,8,128]{2,1,0:T(8,128)S(1)} %copy-done.1, f32[64,4,8,2]{3,0,2,1:T(8,128)S(1)} %get-tuple-element.26, f32[64,4,8,2]{3,0,2,1:T(8,128)S(1)} %get-tuple-element.25, ...), kind=kLoop, calls=%fused_computation.78 | loop fusion | flops 7602176 | bytes 11583488 | tf_op jit(solution)/shard_map/div | solution.py:99
  18.8 5.3 %collective-permute-start.4 = (f32[64,2,8,128]{3,0,2,1:T(8,128)S(1)}, f32[64,2,8,128]{3,0,2,1:T(8,128)S(1)}, u32[]{:S(2)}, u32[]{:S(2)}) collective-permute-start(f32[64,2,8,128]{3,0,2,1:T(8,128)S(1)} %get-tuple-element.12), channel_id=1, source_target_pairs={{8,0},{16,8},{24,16},{32,24},{40,32},{48,40},{56,48},{64,56},{72,6... | collective-permute-start | bytes 1572872 | tf_op jit(solution)/shard_map/ppermute | solution.py:15
  24.2 2.0 %collective-permute-start.7 = (f32[64,4,2,128]{3,0,2,1:T(8,128)S(1)}, f32[64,4,2,128]{3,0,2,1:T(8,128)S(1)}, u32[]{:S(2)}, u32[]{:S(2)}) collective-permute-start(f32[64,4,2,128]{3,0,2,1:T(8,128)S(1)} %get-tuple-element.15), channel_id=1, source_target_pairs={{0,1},{1,2},{2,3},{3,4},{4,5},{5,6},{6,7},{7,0},{8,9},{9,10},{10,1... | collective-permute-start | bytes 786440 | tf_op jit(solution)/shard_map/ppermute | solution.py:14
  26.2 2.2 %collective-permute-start.6 = (f32[64,4,2,128]{3,0,2,1:T(8,128)S(1)}, f32[64,4,2,128]{3,0,2,1:T(8,128)S(1)}, u32[]{:S(2)}, u32[]{:S(2)}) collective-permute-start(f32[64,4,2,128]{3,0,2,1:T(8,128)S(1)} %get-tuple-element.14), channel_id=1, source_target_pairs={{1,0},{2,1},{3,2},{4,3},{5,4},{6,5},{7,6},{0,7},{9,8},{10,9},{11,1... | collective-permute-start | bytes 786440 | tf_op jit(solution)/shard_map/ppermute | solution.py:15
  28.8 3.9 %collective-permute-done.7 = f32[64,4,2,128]{3,0,2,1:T(8,128)S(1)} collective-permute-done((f32[64,4,2,128]{3,0,2,1:T(8,128)S(1)}, f32[64,4,2,128]{3,0,2,1:T(8,128)S(1)}, u32[]{:S(2)}, u32[]{:S(2)}) %collective-permute-start.7) | collective-permute-done | bytes 262176 | tf_op jit(solution)/shard_map/ppermute | solution.py:14
  33.6 2.4 %fusion.12 = f32[64,4,8,128]{3,0,2,1:T(8,128)S(1)} fusion(f32[64,4,2,128]{3,0,2,1:T(8,128)S(1)} %collective-permute-done.7, f32[64,4,8,128]{3,0,2,1:T(8,128)S(1)} %get-tuple-element.8, f32[64,4,2,128]{3,0,2,1:T(8,128)S(1)} %collective-permute-done.6, f32[64,2,8,128]{3,0,2,1:T(8,128)S(1)} %collective-permute-done.5, ...), kind=kLoop, calls=%fused_computation.29 | loop fusion | flops 9961472 | bytes 5816320 | tf_op jit(solution)/shard_map/sub | solution.py:101
  37.1 2.5 %collective-permute-start.8 = (f32[32,128]{1,0:T(8,128)S(1)}, f32[32,128]{1,0:T(8,128)S(1)}, u32[]{:S(2)}, u32[]{:S(2)}) collective-permute-start(f32[32,128]{1,0:T(8,128)S(1)} %reshape.11), channel_id=1, source_target_pairs={{0,1},{1,0},{2,3},{3,2},{4,5},{5,4},{6,7},{7,6},{8,9},{9,8},{10,11... | collective-permute-start | bytes 49160 | tf_op jit(solution)/shard_map/ppermute | solution.py:93
  39.5 1.7 %collective-permute-done.8 = f32[32,128]{1,0:T(8,128)S(1)} collective-permute-done((f32[32,128]{1,0:T(8,128)S(1)}, f32[32,128]{1,0:T(8,128)S(1)}, u32[]{:S(2)}, u32[]{:S(2)}) %collective-permute-start.8) | collective-permute-done | bytes 16416 | tf_op jit(solution)/shard_map/ppermute | solution.py:93
  41.3 5.4 %collective-permute-start.9 = (f32[32,128]{1,0:T(8,128)S(1)}, f32[32,128]{1,0:T(8,128)S(1)}, u32[]{:S(2)}, u32[]{:S(2)}) collective-permute-start(f32[32,128]{1,0:T(8,128)S(1)} %add.107), channel_id=1, source_target_pairs={{0,2},{1,3},{2,0},{3,1},{4,6},{5,7},{6,4},{7,5},{8,10},{9,11},{10,... | collective-permute-start | bytes 49160 | tf_op jit(solution)/shard_map/ppermute | solution.py:93
  46.6 1.7 %collective-permute-done.9 = f32[32,128]{1,0:T(8,128)S(1)} collective-permute-done((f32[32,128]{1,0:T(8,128)S(1)}, f32[32,128]{1,0:T(8,128)S(1)}, u32[]{:S(2)}, u32[]{:S(2)}) %collective-permute-start.9) | collective-permute-done | bytes 16416 | tf_op jit(solution)/shard_map/ppermute | solution.py:93
  48.3 1.8 %collective-permute-start.10 = (f32[32,128]{1,0:T(8,128)S(1)}, f32[32,128]{1,0:T(8,128)S(1)}, u32[]{:S(2)}, u32[]{:S(2)}) collective-permute-start(f32[32,128]{1,0:T(8,128)S(1)} %add.108), channel_id=1, source_target_pairs={{0,4},{1,5},{2,6},{3,7},{4,0},{5,1},{6,2},{7,3},{8,12},{9,13},{10,... | collective-permute-start | bytes 49160 | tf_op jit(solution)/shard_map/ppermute | solution.py:93
  50.2 5.8 %collective-permute-done.10 = f32[32,128]{1,0:T(8,128)S(1)} collective-permute-done((f32[32,128]{1,0:T(8,128)S(1)}, f32[32,128]{1,0:T(8,128)S(1)}, u32[]{:S(2)}, u32[]{:S(2)}) %collective-permute-start.10) | collective-permute-done | bytes 16416 | tf_op jit(solution)/shard_map/ppermute | solution.py:93
  57.2 3.7 %collective-permute-done.12 = f32[32,128]{1,0:T(8,128)S(1)} collective-permute-done((f32[32,128]{1,0:T(8,128)S(1)}, f32[32,128]{1,0:T(8,128)S(1)}, u32[]{:S(2)}, u32[]{:S(2)}) %collective-permute-start.12) | collective-permute-done | bytes 16416 | tf_op jit(solution)/shard_map/ppermute | solution.py:93
  60.9 4.9 %collective-permute-done.13 = f32[32,128]{1,0:T(8,128)S(1)} collective-permute-done((f32[32,128]{1,0:T(8,128)S(1)}, f32[32,128]{1,0:T(8,128)S(1)}, u32[]{:S(2)}, u32[]{:S(2)}) %collective-permute-start.13) | collective-permute-done | bytes 16416 | tf_op jit(solution)/shard_map/ppermute | solution.py:93
  65.9 3.7 %collective-permute-done.14 = f32[32,128]{1,0:T(8,128)S(1)} collective-permute-done((f32[32,128]{1,0:T(8,128)S(1)}, f32[32,128]{1,0:T(8,128)S(1)}, u32[]{:S(2)}, u32[]{:S(2)}) %collective-permute-start.14) | collective-permute-done | bytes 16416 | tf_op jit(solution)/shard_map/ppermute | solution.py:93
  70.0 4.6 %collective-permute-done.15 = f32[32,128]{1,0:T(8,128)S(1)} collective-permute-done((f32[32,128]{1,0:T(8,128)S(1)}, f32[32,128]{1,0:T(8,128)S(1)}, u32[]{:S(2)}, u32[]{:S(2)}) %collective-permute-start.15) | collective-permute-done | bytes 16416 | tf_op jit(solution)/shard_map/ppermute | solution.py:93
  75.4 6.7 %shard_map.41 = f32[64,128]{1,0:T(8,128)} custom-call(f32[64,128]{1,0:T(8,128)} %pad_maximum_fusion.8.aug_ref), custom_call_target="tpu_custom_call" | custom-call | tf_op jit(solution)/shard_map/pallas_call | solution.py:65
  82.1 1.8 %fusion.50 = f32[64,4,8,128]{3,0,2,1:T(8,128)S(1)} fusion(f32[64,4,8,128]{3,0,2,1:T(8,128)S(1)} %fusion.12, f32[64,128]{1,0:T(8,128)} %shard_map.41), kind=kOutput, calls=%fused_computation.81 | convolution fusion | flops 201330688 | bytes 2129920 | tf_op jit(solution)/shard_map/mk,kxyz->mxyz/dot_general | solution.py:114
  83.9 1.6 %copy.31 = f32[64,4,8,128]{3,2,1,0:T(8,128)} copy(f32[64,4,8,128]{3,0,2,1:T(8,128)S(1)} %fusion.50) | data formatting | bytes 2097152
  (48 shorter events, 8.1 us)
Async XLA Ops:
  0.6 1.7 %copy-start = (f32[64,4,8,128]{3,2,1,0:T(8,128)S(1)}, f32[64,4,8,128]{3,2,1,0:T(8,128)}, u32[]{:S(2)}) copy-start(f32[64,4,8,128]{3,2,1,0:T(8,128)} %param.2) | copy-start | bytes 3145732
  2.2 7.5 %copy-start.1 = (f32[4,8,128]{2,1,0:T(8,128)S(1)}, f32[4,8,128]{2,1,0:T(8,128)}, u32[]{:S(2)}) copy-start(f32[4,8,128]{2,1,0:T(8,128)} %param.3) | copy-start | bytes 49156
  2.2 12.0 %collective-permute-start.1 = (f32[64,2,8,128]{3,0,2,1:T(8,128)S(1)}, f32[64,2,8,128]{3,0,2,1:T(8,128)S(1)}, u32[]{:S(2)}, u32[]{:S(2)}) collective-permute-start(f32[64,2,8,128]{3,0,2,1:T(8,128)S(1)} %copy.35), channel_id=1, source_target_pairs={{0,8},{8,16},{16,24},{24,32},{32,40},{40,48},{48,56},{56,64},{64,7... | collective-permute-start | bytes 1572872 | tf_op jit(solution)/shard_map/ppermute | solution.py:14
  2.5 8.6 %collective-permute-start.3 = (f32[64,4,2,128]{3,0,2,1:T(8,128)S(1)}, f32[64,4,2,128]{3,0,2,1:T(8,128)S(1)}, u32[]{:S(2)}, u32[]{:S(2)}) collective-permute-start(f32[64,4,2,128]{3,0,2,1:T(8,128)S(1)} %copy.37), channel_id=1, source_target_pairs={{0,1},{1,2},{2,3},{3,4},{4,5},{5,6},{6,7},{7,0},{8,9},{9,10},{10,1... | collective-permute-start | bytes 786440 | tf_op jit(solution)/shard_map/ppermute | solution.py:14
  4.6 10.4 %collective-permute-start.2 = (f32[64,4,2,128]{3,0,2,1:T(8,128)S(1)}, f32[64,4,2,128]{3,0,2,1:T(8,128)S(1)}, u32[]{:S(2)}, u32[]{:S(2)}) collective-permute-start(f32[64,4,2,128]{3,0,2,1:T(8,128)S(1)} %copy.36), channel_id=1, source_target_pairs={{1,0},{2,1},{3,2},{4,3},{5,4},{6,5},{7,6},{0,7},{9,8},{10,9},{11,1... | collective-permute-start | bytes 786440 | tf_op jit(solution)/shard_map/ppermute | solution.py:15
  4.9 11.4 %collective-permute-start = (f32[64,2,8,128]{3,0,2,1:T(8,128)S(1)}, f32[64,2,8,128]{3,0,2,1:T(8,128)S(1)}, u32[]{:S(2)}, u32[]{:S(2)}) collective-permute-start(f32[64,2,8,128]{3,0,2,1:T(8,128)S(1)} %copy.34), channel_id=1, source_target_pairs={{8,0},{16,8},{24,16},{32,24},{40,32},{48,40},{56,48},{64,56},{72,6... | collective-permute-start | bytes 1572872 | tf_op jit(solution)/shard_map/ppermute | solution.py:15
  18.7 14.9 %collective-permute-start.5 = (f32[64,2,8,128]{3,0,2,1:T(8,128)S(1)}, f32[64,2,8,128]{3,0,2,1:T(8,128)S(1)}, u32[]{:S(2)}, u32[]{:S(2)}) collective-permute-start(f32[64,2,8,128]{3,0,2,1:T(8,128)S(1)} %get-tuple-element.13), channel_id=1, source_target_pairs={{0,8},{8,16},{16,24},{24,32},{32,40},{40,48},{48,56},{56,64},{64,7... | collective-permute-start | bytes 1572872 | tf_op jit(solution)/shard_map/ppermute | solution.py:14
  18.8 14.8 %collective-permute-start.4 = (f32[64,2,8,128]{3,0,2,1:T(8,128)S(1)}, f32[64,2,8,128]{3,0,2,1:T(8,128)S(1)}, u32[]{:S(2)}, u32[]{:S(2)}) collective-permute-start(f32[64,2,8,128]{3,0,2,1:T(8,128)S(1)} %get-tuple-element.12), channel_id=1, source_target_pairs={{8,0},{16,8},{24,16},{32,24},{40,32},{48,40},{56,48},{64,56},{72,6... | collective-permute-start | bytes 1572872 | tf_op jit(solution)/shard_map/ppermute | solution.py:15
  24.2 8.5 %collective-permute-start.7 = (f32[64,4,2,128]{3,0,2,1:T(8,128)S(1)}, f32[64,4,2,128]{3,0,2,1:T(8,128)S(1)}, u32[]{:S(2)}, u32[]{:S(2)}) collective-permute-start(f32[64,4,2,128]{3,0,2,1:T(8,128)S(1)} %get-tuple-element.15), channel_id=1, source_target_pairs={{0,1},{1,2},{2,3},{3,4},{4,5},{5,6},{6,7},{7,0},{8,9},{9,10},{10,1... | collective-permute-start | bytes 786440 | tf_op jit(solution)/shard_map/ppermute | solution.py:14
  26.2 7.5 %collective-permute-start.6 = (f32[64,4,2,128]{3,0,2,1:T(8,128)S(1)}, f32[64,4,2,128]{3,0,2,1:T(8,128)S(1)}, u32[]{:S(2)}, u32[]{:S(2)}) collective-permute-start(f32[64,4,2,128]{3,0,2,1:T(8,128)S(1)} %get-tuple-element.14), channel_id=1, source_target_pairs={{1,0},{2,1},{3,2},{4,3},{5,4},{6,5},{7,6},{0,7},{9,8},{10,9},{11,1... | collective-permute-start | bytes 786440 | tf_op jit(solution)/shard_map/ppermute | solution.py:15
  37.1 4.2 %collective-permute-start.8 = (f32[32,128]{1,0:T(8,128)S(1)}, f32[32,128]{1,0:T(8,128)S(1)}, u32[]{:S(2)}, u32[]{:S(2)}) collective-permute-start(f32[32,128]{1,0:T(8,128)S(1)} %reshape.11), channel_id=1, source_target_pairs={{0,1},{1,0},{2,3},{3,2},{4,5},{5,4},{6,7},{7,6},{8,9},{9,8},{10,11... | collective-permute-start | bytes 49160 | tf_op jit(solution)/shard_map/ppermute | solution.py:93
  41.3 7.1 %collective-permute-start.9 = (f32[32,128]{1,0:T(8,128)S(1)}, f32[32,128]{1,0:T(8,128)S(1)}, u32[]{:S(2)}, u32[]{:S(2)}) collective-permute-start(f32[32,128]{1,0:T(8,128)S(1)} %add.107), channel_id=1, source_target_pairs={{0,2},{1,3},{2,0},{3,1},{4,6},{5,7},{6,4},{7,5},{8,10},{9,11},{10,... | collective-permute-start | bytes 49160 | tf_op jit(solution)/shard_map/ppermute | solution.py:93
  48.3 7.6 %collective-permute-start.10 = (f32[32,128]{1,0:T(8,128)S(1)}, f32[32,128]{1,0:T(8,128)S(1)}, u32[]{:S(2)}, u32[]{:S(2)}) collective-permute-start(f32[32,128]{1,0:T(8,128)S(1)} %add.108), channel_id=1, source_target_pairs={{0,4},{1,5},{2,6},{3,7},{4,0},{5,1},{6,2},{7,3},{8,12},{9,13},{10,... | collective-permute-start | bytes 49160 | tf_op jit(solution)/shard_map/ppermute | solution.py:93
  56.0 1.2 %collective-permute-start.11 = (f32[32,128]{1,0:T(8,128)S(1)}, f32[32,128]{1,0:T(8,128)S(1)}, u32[]{:S(2)}, u32[]{:S(2)}) collective-permute-start(f32[32,128]{1,0:T(8,128)S(1)} %add.109), channel_id=1, source_target_pairs={{0,8},{8,0},{16,24},{24,16},{32,40},{40,32},{48,56},{56,48},{64,72... | collective-permute-start | bytes 49160 | tf_op jit(solution)/shard_map/ppermute | solution.py:93
  57.2 3.7 %collective-permute-start.12 = (f32[32,128]{1,0:T(8,128)S(1)}, f32[32,128]{1,0:T(8,128)S(1)}, u32[]{:S(2)}, u32[]{:S(2)}) collective-permute-start(f32[32,128]{1,0:T(8,128)S(1)} %add.110), channel_id=1, source_target_pairs={{0,16},{8,24},{16,0},{24,8},{32,48},{40,56},{48,32},{56,40},{64,80... | collective-permute-start | bytes 49160 | tf_op jit(solution)/shard_map/ppermute | solution.py:93
  60.9 4.9 %collective-permute-start.13 = (f32[32,128]{1,0:T(8,128)S(1)}, f32[32,128]{1,0:T(8,128)S(1)}, u32[]{:S(2)}, u32[]{:S(2)}) collective-permute-start(f32[32,128]{1,0:T(8,128)S(1)} %add.111), channel_id=1, source_target_pairs={{0,48},{8,56},{16,32},{24,40},{32,16},{40,24},{48,0},{56,8},{64,11... | collective-permute-start | bytes 49160 | tf_op jit(solution)/shard_map/ppermute | solution.py:93
  65.9 3.7 %collective-permute-start.14 = (f32[32,128]{1,0:T(8,128)S(1)}, f32[32,128]{1,0:T(8,128)S(1)}, u32[]{:S(2)}, u32[]{:S(2)}) collective-permute-start(f32[32,128]{1,0:T(8,128)S(1)} %add.112), channel_id=1, source_target_pairs={{0,64},{8,72},{16,80},{24,88},{32,96},{40,104},{48,112},{56,120},{... | collective-permute-start | bytes 49160 | tf_op jit(solution)/shard_map/ppermute | solution.py:93
  69.6 4.9 %collective-permute-start.15 = (f32[32,128]{1,0:T(8,128)S(1)}, f32[32,128]{1,0:T(8,128)S(1)}, u32[]{:S(2)}, u32[]{:S(2)}) collective-permute-start(f32[32,128]{1,0:T(8,128)S(1)} %add.113), channel_id=1, source_target_pairs={{0,192},{8,200},{16,208},{24,216},{32,224},{40,232},{48,240},{56,2... | collective-permute-start | bytes 49160 | tf_op jit(solution)/shard_map/ppermute | solution.py:93

commit v10 on v9

--- a/solution.py
+++ b/solution.py
@@ -87,6 +87,8 @@
         return lax.psum(value, axis)
     if count == 32:
         rounds = [lambda i: i ^ 1] + ring_rounds(2) + ring_rounds(8)
+    elif count == 8:
+        rounds = [lambda i: i ^ 1] + ring_rounds(2)
     else:
         rounds = [lambda i, mask=1 << b: i ^ mask for b in range(count.bit_length() - 1)]
     for partner in rounds:

time: 85.7 us -> 83.9 us (0.979)
  waiting for transfers between devices: 37.8 us -> 35.6 us
    ppermute x8, waiting for transfers between devices: 27.4 us -> 25.2 us  [butterfly_sum(): lax.ppermute(value, axis, [(i, partner(i)) for i in range(count)])]
where the time goes in v10:
time: 83.9 us; the launch traced here: 83.7 us
  waiting for transfers between devices  35.6 us (42%)
  starting transfers between devices  27 us (32%)
  Pallas kernels  6.66 us (8%)
  local copies, waits for them, and re-layouts  5.48 us (7%)
  other arithmetic  5.32 us (6%)
  matrix products  2.76 us (3%)
  between operations  0.84 us (1%)
    ppermute x8, waiting for transfers between devices, butterfly_sum(): lax.ppermute(value, axis, [(i, partner(i)) for i in range(count)])  25.2 us
    ppermute x4, starting transfers between devices, faces(): lax.ppermute(head, axis, [((i + 1) % count, i) for i in range(count)])  12.5 us
    ppermute x8, starting transfers between devices, butterfly_sum(): lax.ppermute(value, axis, [(i, partner(i)) for i in range(count)])  10.4 us
    ppermute x4, waiting for transfers between devices, faces(): lax.ppermute(tail, axis, [(i, (i + 1) % count) for i in range(count)])  8.37 us
    pallas_call x1, Pallas kernels, factor_and_inverse(): pl.pallas_call(factor_kernel, out_shape=jax.ShapeDtypeStruct(aug.shape, j...  6.66 us
    ppermute x4, starting transfers between devices, faces(): lax.ppermute(tail, axis, [(i, (i + 1) % count) for i in range(count)])  4.15 us
    unnamed x12, local copies, waits for them, and re-layouts  2.82 us
    sub x1, other arithmetic, shards(): filtered = 2.0 * (applied - 5.5 * first) / 4.5 - orbitals_here  2.37 us
  transfers between devices with their start and end apart: 16, of which 13 were waited for; matrix products, arithmetic and copies ran while one was open for 2% of the time, Pallas kernels for 0%

profile of v10, /device:TPU:32, one launch (start us, length us, event | category | flops | bytes accessed | tf_op | source)
XLA Modules:
  0.0 83.7 jit_solution(5380128473057465531)
XLA Ops:
  0.6 1.4 %fusion.60 = (f32[64,2,8,128]{3,2,1,0:T(8,128)S(1)}, f32[64,2,8,128]{3,2,1,0:T(8,128)S(1)}) fusion(f32[64,4,8,128]{3,2,1,0:T(8,128)} %param.2), kind=kLoop, calls=%fused_computation.101 | loop fusion | bytes 2097152 | tf_op jit(solution)/shard_map/slice | solution.py:12
  2.5 2.0 %collective-permute-start.3 = (f32[64,4,2,128]{3,0,2,1:T(8,128)S(1)}, f32[64,4,2,128]{3,0,2,1:T(8,128)S(1)}, u32[]{:S(2)}, u32[]{:S(2)}) collective-permute-start(f32[64,4,2,128]{3,0,2,1:T(8,128)S(1)} %copy.37), channel_id=1, source_target_pairs={{0,1},{1,2},{2,3},{3,4},{4,5},{5,6},{6,7},{7,0},{8,9},{9,10},{10,1... | collective-permute-start | bytes 786440 | tf_op jit(solution)/shard_map/ppermute | solution.py:14
  4.9 4.7 %collective-permute-start = (f32[64,2,8,128]{3,0,2,1:T(8,128)S(1)}, f32[64,2,8,128]{3,0,2,1:T(8,128)S(1)}, u32[]{:S(2)}, u32[]{:S(2)}) collective-permute-start(f32[64,2,8,128]{3,0,2,1:T(8,128)S(1)} %copy.34), channel_id=1, source_target_pairs={{8,0},{16,8},{24,16},{32,24},{40,32},{48,40},{56,48},{64,56},{72,6... | collective-permute-start | bytes 1572872 | tf_op jit(solution)/shard_map/ppermute | solution.py:15
  9.7 1.4 %collective-permute-done.3 = f32[64,4,2,128]{3,0,2,1:T(8,128)S(1)} collective-permute-done((f32[64,4,2,128]{3,0,2,1:T(8,128)S(1)}, f32[64,4,2,128]{3,0,2,1:T(8,128)S(1)}, u32[]{:S(2)}, u32[]{:S(2)}) %collective-permute-start.3) | collective-permute-done | bytes 262176 | tf_op jit(solution)/shard_map/ppermute | solution.py:14
  11.2 3.0 %collective-permute-done.1 = f32[64,2,8,128]{3,0,2,1:T(8,128)S(1)} collective-permute-done((f32[64,2,8,128]{3,0,2,1:T(8,128)S(1)}, f32[64,2,8,128]{3,0,2,1:T(8,128)S(1)}, u32[]{:S(2)}, u32[]{:S(2)}) %collective-permute-start.1) | collective-permute-done | bytes 524320 | tf_op jit(solution)/shard_map/ppermute | solution.py:14
  16.4 2.2 %broadcast_multiply_fusion = (f32[64,4,8,128]{3,0,2,1:T(8,128)S(1)}, f32[64,4,8,128]{3,0,2,1:T(8,128)S(1)}) fusion(f32[64,4,8,128]{3,0,2,1:T(8,128)S(1)} %get-tuple-element.22, f32[4,8,128]{2,1,0:T(8,128)S(1)} %copy-done.1, f32[64,4,8,2]{3,0,2,1:T(8,128)S(1)} %get-tuple-element.26, f32[64,4,8,2]{3,0,2,1:T(8,128)S(1)} %get-tuple-element.25, ...), kind=kLoop, calls=%fused_computation.78 | loop fusion | flops 7602176 | bytes 11583488 | tf_op jit(solution)/shard_map/div | solution.py:101
  18.8 5.3 %collective-permute-start.4 = (f32[64,2,8,128]{3,0,2,1:T(8,128)S(1)}, f32[64,2,8,128]{3,0,2,1:T(8,128)S(1)}, u32[]{:S(2)}, u32[]{:S(2)}) collective-permute-start(f32[64,2,8,128]{3,0,2,1:T(8,128)S(1)} %get-tuple-element.12), channel_id=1, source_target_pairs={{8,0},{16,8},{24,16},{32,24},{40,32},{48,40},{56,48},{64,56},{72,6... | collective-permute-start | bytes 1572872 | tf_op jit(solution)/shard_map/ppermute | solution.py:15
  24.2 2.0 %collective-permute-start.7 = (f32[64,4,2,128]{3,0,2,1:T(8,128)S(1)}, f32[64,4,2,128]{3,0,2,1:T(8,128)S(1)}, u32[]{:S(2)}, u32[]{:S(2)}) collective-permute-start(f32[64,4,2,128]{3,0,2,1:T(8,128)S(1)} %get-tuple-element.15), channel_id=1, source_target_pairs={{0,1},{1,2},{2,3},{3,4},{4,5},{5,6},{6,7},{7,0},{8,9},{9,10},{10,1... | collective-permute-start | bytes 786440 | tf_op jit(solution)/shard_map/ppermute | solution.py:14
  26.2 2.2 %collective-permute-start.6 = (f32[64,4,2,128]{3,0,2,1:T(8,128)S(1)}, f32[64,4,2,128]{3,0,2,1:T(8,128)S(1)}, u32[]{:S(2)}, u32[]{:S(2)}) collective-permute-start(f32[64,4,2,128]{3,0,2,1:T(8,128)S(1)} %get-tuple-element.14), channel_id=1, source_target_pairs={{1,0},{2,1},{3,2},{4,3},{5,4},{6,5},{7,6},{0,7},{9,8},{10,9},{11,1... | collective-permute-start | bytes 786440 | tf_op jit(solution)/shard_map/ppermute | solution.py:15
  28.8 3.9 %collective-permute-done.7 = f32[64,4,2,128]{3,0,2,1:T(8,128)S(1)} collective-permute-done((f32[64,4,2,128]{3,0,2,1:T(8,128)S(1)}, f32[64,4,2,128]{3,0,2,1:T(8,128)S(1)}, u32[]{:S(2)}, u32[]{:S(2)}) %collective-permute-start.7) | collective-permute-done | bytes 262176 | tf_op jit(solution)/shard_map/ppermute | solution.py:14
  33.6 2.4 %fusion.12 = f32[64,4,8,128]{3,0,2,1:T(8,128)S(1)} fusion(f32[64,4,2,128]{3,0,2,1:T(8,128)S(1)} %collective-permute-done.7, f32[64,4,8,128]{3,0,2,1:T(8,128)S(1)} %get-tuple-element.8, f32[64,4,2,128]{3,0,2,1:T(8,128)S(1)} %collective-permute-done.6, f32[64,2,8,128]{3,0,2,1:T(8,128)S(1)} %collective-permute-done.5, ...), kind=kLoop, calls=%fused_computation.29 | loop fusion | flops 9961472 | bytes 5816320 | tf_op jit(solution)/shard_map/sub | solution.py:103
  37.1 2.5 %collective-permute-start.8 = (f32[32,128]{1,0:T(8,128)S(1)}, f32[32,128]{1,0:T(8,128)S(1)}, u32[]{:S(2)}, u32[]{:S(2)}) collective-permute-start(f32[32,128]{1,0:T(8,128)S(1)} %reshape.11), channel_id=1, source_target_pairs={{0,1},{1,0},{2,3},{3,2},{4,5},{5,4},{6,7},{7,6},{8,9},{9,8},{10,11... | collective-permute-start | bytes 49160 | tf_op jit(solution)/shard_map/ppermute | solution.py:95
  39.5 1.7 %collective-permute-done.8 = f32[32,128]{1,0:T(8,128)S(1)} collective-permute-done((f32[32,128]{1,0:T(8,128)S(1)}, f32[32,128]{1,0:T(8,128)S(1)}, u32[]{:S(2)}, u32[]{:S(2)}) %collective-permute-start.8) | collective-permute-done | bytes 16416 | tf_op jit(solution)/shard_map/ppermute | solution.py:95
  41.3 5.4 %collective-permute-start.9 = (f32[32,128]{1,0:T(8,128)S(1)}, f32[32,128]{1,0:T(8,128)S(1)}, u32[]{:S(2)}, u32[]{:S(2)}) collective-permute-start(f32[32,128]{1,0:T(8,128)S(1)} %add.107), channel_id=1, source_target_pairs={{0,2},{1,3},{2,0},{3,1},{4,6},{5,7},{6,4},{7,5},{8,10},{9,11},{10,... | collective-permute-start | bytes 49160 | tf_op jit(solution)/shard_map/ppermute | solution.py:95
  46.6 1.7 %collective-permute-done.9 = f32[32,128]{1,0:T(8,128)S(1)} collective-permute-done((f32[32,128]{1,0:T(8,128)S(1)}, f32[32,128]{1,0:T(8,128)S(1)}, u32[]{:S(2)}, u32[]{:S(2)}) %collective-permute-start.9) | collective-permute-done | bytes 16416 | tf_op jit(solution)/shard_map/ppermute | solution.py:95
  48.3 2.2 %collective-permute-start.10 = (f32[32,128]{1,0:T(8,128)S(1)}, f32[32,128]{1,0:T(8,128)S(1)}, u32[]{:S(2)}, u32[]{:S(2)}) collective-permute-start(f32[32,128]{1,0:T(8,128)S(1)} %add.108), channel_id=1, source_target_pairs={{0,6},{1,7},{2,4},{3,5},{4,2},{5,3},{6,0},{7,1},{8,14},{9,15},{10,... | collective-permute-start | bytes 49160 | tf_op jit(solution)/shard_map/ppermute | solution.py:95
  50.6 3.6 %collective-permute-done.10 = f32[32,128]{1,0:T(8,128)S(1)} collective-permute-done((f32[32,128]{1,0:T(8,128)S(1)}, f32[32,128]{1,0:T(8,128)S(1)}, u32[]{:S(2)}, u32[]{:S(2)}) %collective-permute-start.10) | collective-permute-done | bytes 16416 | tf_op jit(solution)/shard_map/ppermute | solution.py:95
  55.4 3.7 %collective-permute-done.12 = f32[32,128]{1,0:T(8,128)S(1)} collective-permute-done((f32[32,128]{1,0:T(8,128)S(1)}, f32[32,128]{1,0:T(8,128)S(1)}, u32[]{:S(2)}, u32[]{:S(2)}) %collective-permute-start.12) | collective-permute-done | bytes 16416 | tf_op jit(solution)/shard_map/ppermute | solution.py:95
  59.1 4.9 %collective-permute-done.13 = f32[32,128]{1,0:T(8,128)S(1)} collective-permute-done((f32[32,128]{1,0:T(8,128)S(1)}, f32[32,128]{1,0:T(8,128)S(1)}, u32[]{:S(2)}, u32[]{:S(2)}) %collective-permute-start.13) | collective-permute-done | bytes 16416 | tf_op jit(solution)/shard_map/ppermute | solution.py:95
  64.1 3.7 %collective-permute-done.14 = f32[32,128]{1,0:T(8,128)S(1)} collective-permute-done((f32[32,128]{1,0:T(8,128)S(1)}, f32[32,128]{1,0:T(8,128)S(1)}, u32[]{:S(2)}, u32[]{:S(2)}) %collective-permute-start.14) | collective-permute-done | bytes 16416 | tf_op jit(solution)/shard_map/ppermute | solution.py:95
  68.2 4.6 %collective-permute-done.15 = f32[32,128]{1,0:T(8,128)S(1)} collective-permute-done((f32[32,128]{1,0:T(8,128)S(1)}, f32[32,128]{1,0:T(8,128)S(1)}, u32[]{:S(2)}, u32[]{:S(2)}) %collective-permute-start.15) | collective-permute-done | bytes 16416 | tf_op jit(solution)/shard_map/ppermute | solution.py:95
  73.7 6.7 %shard_map.41 = f32[64,128]{1,0:T(8,128)} custom-call(f32[64,128]{1,0:T(8,128)} %pad_maximum_fusion.8.aug_ref), custom_call_target="tpu_custom_call" | custom-call | tf_op jit(solution)/shard_map/pallas_call | solution.py:65
  80.3 1.8 %fusion.50 = f32[64,4,8,128]{3,0,2,1:T(8,128)S(1)} fusion(f32[64,4,8,128]{3,0,2,1:T(8,128)S(1)} %fusion.12, f32[64,128]{1,0:T(8,128)} %shard_map.41), kind=kOutput, calls=%fused_computation.81 | convolution fusion | flops 201330688 | bytes 2129920 | tf_op jit(solution)/shard_map/mk,kxyz->mxyz/dot_general | solution.py:116
  82.1 1.6 %copy.31 = f32[64,4,8,128]{3,2,1,0:T(8,128)} copy(f32[64,4,8,128]{3,0,2,1:T(8,128)S(1)} %fusion.50) | data formatting | bytes 2097152
  (48 shorter events, 8.1 us)
Async XLA Ops:
  0.6 1.7 %copy-start = (f32[64,4,8,128]{3,2,1,0:T(8,128)S(1)}, f32[64,4,8,128]{3,2,1,0:T(8,128)}, u32[]{:S(2)}) copy-start(f32[64,4,8,128]{3,2,1,0:T(8,128)} %param.2) | copy-start | bytes 3145732
  2.2 7.5 %copy-start.1 = (f32[4,8,128]{2,1,0:T(8,128)S(1)}, f32[4,8,128]{2,1,0:T(8,128)}, u32[]{:S(2)}) copy-start(f32[4,8,128]{2,1,0:T(8,128)} %param.3) | copy-start | bytes 49156
  2.2 12.0 %collective-permute-start.1 = (f32[64,2,8,128]{3,0,2,1:T(8,128)S(1)}, f32[64,2,8,128]{3,0,2,1:T(8,128)S(1)}, u32[]{:S(2)}, u32[]{:S(2)}) collective-permute-start(f32[64,2,8,128]{3,0,2,1:T(8,128)S(1)} %copy.35), channel_id=1, source_target_pairs={{0,8},{8,16},{16,24},{24,32},{32,40},{40,48},{48,56},{56,64},{64,7... | collective-permute-start | bytes 1572872 | tf_op jit(solution)/shard_map/ppermute | solution.py:14
  2.5 8.6 %collective-permute-start.3 = (f32[64,4,2,128]{3,0,2,1:T(8,128)S(1)}, f32[64,4,2,128]{3,0,2,1:T(8,128)S(1)}, u32[]{:S(2)}, u32[]{:S(2)}) collective-permute-start(f32[64,4,2,128]{3,0,2,1:T(8,128)S(1)} %copy.37), channel_id=1, source_target_pairs={{0,1},{1,2},{2,3},{3,4},{4,5},{5,6},{6,7},{7,0},{8,9},{9,10},{10,1... | collective-permute-start | bytes 786440 | tf_op jit(solution)/shard_map/ppermute | solution.py:14
  4.6 10.4 %collective-permute-start.2 = (f32[64,4,2,128]{3,0,2,1:T(8,128)S(1)}, f32[64,4,2,128]{3,0,2,1:T(8,128)S(1)}, u32[]{:S(2)}, u32[]{:S(2)}) collective-permute-start(f32[64,4,2,128]{3,0,2,1:T(8,128)S(1)} %copy.36), channel_id=1, source_target_pairs={{1,0},{2,1},{3,2},{4,3},{5,4},{6,5},{7,6},{0,7},{9,8},{10,9},{11,1... | collective-permute-start | bytes 786440 | tf_op jit(solution)/shard_map/ppermute | solution.py:15
  4.9 11.4 %collective-permute-start = (f32[64,2,8,128]{3,0,2,1:T(8,128)S(1)}, f32[64,2,8,128]{3,0,2,1:T(8,128)S(1)}, u32[]{:S(2)}, u32[]{:S(2)}) collective-permute-start(f32[64,2,8,128]{3,0,2,1:T(8,128)S(1)} %copy.34), channel_id=1, source_target_pairs={{8,0},{16,8},{24,16},{32,24},{40,32},{48,40},{56,48},{64,56},{72,6... | collective-permute-start | bytes 1572872 | tf_op jit(solution)/shard_map/ppermute | solution.py:15
  18.7 14.9 %collective-permute-start.5 = (f32[64,2,8,128]{3,0,2,1:T(8,128)S(1)}, f32[64,2,8,128]{3,0,2,1:T(8,128)S(1)}, u32[]{:S(2)}, u32[]{:S(2)}) collective-permute-start(f32[64,2,8,128]{3,0,2,1:T(8,128)S(1)} %get-tuple-element.13), channel_id=1, source_target_pairs={{0,8},{8,16},{16,24},{24,32},{32,40},{40,48},{48,56},{56,64},{64,7... | collective-permute-start | bytes 1572872 | tf_op jit(solution)/shard_map/ppermute | solution.py:14
  18.8 14.8 %collective-permute-start.4 = (f32[64,2,8,128]{3,0,2,1:T(8,128)S(1)}, f32[64,2,8,128]{3,0,2,1:T(8,128)S(1)}, u32[]{:S(2)}, u32[]{:S(2)}) collective-permute-start(f32[64,2,8,128]{3,0,2,1:T(8,128)S(1)} %get-tuple-element.12), channel_id=1, source_target_pairs={{8,0},{16,8},{24,16},{32,24},{40,32},{48,40},{56,48},{64,56},{72,6... | collective-permute-start | bytes 1572872 | tf_op jit(solution)/shard_map/ppermute | solution.py:15
  24.2 8.5 %collective-permute-start.7 = (f32[64,4,2,128]{3,0,2,1:T(8,128)S(1)}, f32[64,4,2,128]{3,0,2,1:T(8,128)S(1)}, u32[]{:S(2)}, u32[]{:S(2)}) collective-permute-start(f32[64,4,2,128]{3,0,2,1:T(8,128)S(1)} %get-tuple-element.15), channel_id=1, source_target_pairs={{0,1},{1,2},{2,3},{3,4},{4,5},{5,6},{6,7},{7,0},{8,9},{9,10},{10,1... | collective-permute-start | bytes 786440 | tf_op jit(solution)/shard_map/ppermute | solution.py:14
  26.2 7.5 %collective-permute-start.6 = (f32[64,4,2,128]{3,0,2,1:T(8,128)S(1)}, f32[64,4,2,128]{3,0,2,1:T(8,128)S(1)}, u32[]{:S(2)}, u32[]{:S(2)}) collective-permute-start(f32[64,4,2,128]{3,0,2,1:T(8,128)S(1)} %get-tuple-element.14), channel_id=1, source_target_pairs={{1,0},{2,1},{3,2},{4,3},{5,4},{6,5},{7,6},{0,7},{9,8},{10,9},{11,1... | collective-permute-start | bytes 786440 | tf_op jit(solution)/shard_map/ppermute | solution.py:15
  37.1 4.2 %collective-permute-start.8 = (f32[32,128]{1,0:T(8,128)S(1)}, f32[32,128]{1,0:T(8,128)S(1)}, u32[]{:S(2)}, u32[]{:S(2)}) collective-permute-start(f32[32,128]{1,0:T(8,128)S(1)} %reshape.11), channel_id=1, source_target_pairs={{0,1},{1,0},{2,3},{3,2},{4,5},{5,4},{6,7},{7,6},{8,9},{9,8},{10,11... | collective-permute-start | bytes 49160 | tf_op jit(solution)/shard_map/ppermute | solution.py:95
  41.3 7.1 %collective-permute-start.9 = (f32[32,128]{1,0:T(8,128)S(1)}, f32[32,128]{1,0:T(8,128)S(1)}, u32[]{:S(2)}, u32[]{:S(2)}) collective-permute-start(f32[32,128]{1,0:T(8,128)S(1)} %add.107), channel_id=1, source_target_pairs={{0,2},{1,3},{2,0},{3,1},{4,6},{5,7},{6,4},{7,5},{8,10},{9,11},{10,... | collective-permute-start | bytes 49160 | tf_op jit(solution)/shard_map/ppermute | solution.py:95
  48.3 5.8 %collective-permute-start.10 = (f32[32,128]{1,0:T(8,128)S(1)}, f32[32,128]{1,0:T(8,128)S(1)}, u32[]{:S(2)}, u32[]{:S(2)}) collective-permute-start(f32[32,128]{1,0:T(8,128)S(1)} %add.108), channel_id=1, source_target_pairs={{0,6},{1,7},{2,4},{3,5},{4,2},{5,3},{6,0},{7,1},{8,14},{9,15},{10,... | collective-permute-start | bytes 49160 | tf_op jit(solution)/shard_map/ppermute | solution.py:95
  54.2 1.2 %collective-permute-start.11 = (f32[32,128]{1,0:T(8,128)S(1)}, f32[32,128]{1,0:T(8,128)S(1)}, u32[]{:S(2)}, u32[]{:S(2)}) collective-permute-start(f32[32,128]{1,0:T(8,128)S(1)} %add.109), channel_id=1, source_target_pairs={{0,8},{8,0},{16,24},{24,16},{32,40},{40,32},{48,56},{56,48},{64,72... | collective-permute-start | bytes 49160 | tf_op jit(solution)/shard_map/ppermute | solution.py:95
  55.4 3.7 %collective-permute-start.12 = (f32[32,128]{1,0:T(8,128)S(1)}, f32[32,128]{1,0:T(8,128)S(1)}, u32[]{:S(2)}, u32[]{:S(2)}) collective-permute-start(f32[32,128]{1,0:T(8,128)S(1)} %add.110), channel_id=1, source_target_pairs={{0,16},{8,24},{16,0},{24,8},{32,48},{40,56},{48,32},{56,40},{64,80... | collective-permute-start | bytes 49160 | tf_op jit(solution)/shard_map/ppermute | solution.py:95
  59.1 4.9 %collective-permute-start.13 = (f32[32,128]{1,0:T(8,128)S(1)}, f32[32,128]{1,0:T(8,128)S(1)}, u32[]{:S(2)}, u32[]{:S(2)}) collective-permute-start(f32[32,128]{1,0:T(8,128)S(1)} %add.111), channel_id=1, source_target_pairs={{0,48},{8,56},{16,32},{24,40},{32,16},{40,24},{48,0},{56,8},{64,11... | collective-permute-start | bytes 49160 | tf_op jit(solution)/shard_map/ppermute | solution.py:95
  64.1 3.7 %collective-permute-start.14 = (f32[32,128]{1,0:T(8,128)S(1)}, f32[32,128]{1,0:T(8,128)S(1)}, u32[]{:S(2)}, u32[]{:S(2)}) collective-permute-start(f32[32,128]{1,0:T(8,128)S(1)} %add.112), channel_id=1, source_target_pairs={{0,64},{8,72},{16,80},{24,88},{32,96},{40,104},{48,112},{56,120},{... | collective-permute-start | bytes 49160 | tf_op jit(solution)/shard_map/ppermute | solution.py:95
  67.8 4.9 %collective-permute-start.15 = (f32[32,128]{1,0:T(8,128)S(1)}, f32[32,128]{1,0:T(8,128)S(1)}, u32[]{:S(2)}, u32[]{:S(2)}) collective-permute-start(f32[32,128]{1,0:T(8,128)S(1)} %add.113), channel_id=1, source_target_pairs={{0,192},{8,200},{16,208},{24,216},{32,224},{40,232},{48,240},{56,2... | collective-permute-start | bytes 49160 | tf_op jit(solution)/shard_map/ppermute | solution.py:95

commit v11 on v10

--- a/solution.py
+++ b/solution.py
@@ -23,15 +23,16 @@
     if source is not core:
         along_x = jnp.concatenate([along_x[:, :2], core, along_x[:, -2:]], axis=1)
         along_y = jnp.concatenate([along_y[:, :, :2], core, along_y[:, :, -2:]], axis=2)
-    total = -7.5 * core
+    size = core.shape[3]
+    along_z = jnp.concatenate([core[..., size - 2:], core, core[..., :2]], axis=3)
+    local = -7.5 * core
+    local = local + 4.0 / 3.0 * (along_z[..., 1:size + 1] + along_z[..., 3:size + 3])
+    local = local - 1.0 / 12.0 * (along_z[..., :size] + along_z[..., 4:])
+    total = lax.optimization_barrier(local)
     total = total + 4.0 / 3.0 * (along_x[:, 3:-1] + along_x[:, 1:-3])
     total = total - 1.0 / 12.0 * (along_x[:, 4:] + along_x[:, :-4])
     total = total + 4.0 / 3.0 * (along_y[:, :, 3:-1] + along_y[:, :, 1:-3])
     total = total - 1.0 / 12.0 * (along_y[:, :, 4:] + along_y[:, :, :-4])
-    size = core.shape[3]
-    along_z = jnp.concatenate([core[..., size - 2:], core, core[..., :2]], axis=3)
-    total = total + 4.0 / 3.0 * (along_z[..., 1:size + 1] + along_z[..., 3:size + 3])
-    total = total - 1.0 / 12.0 * (along_z[..., :size] + along_z[..., 4:])
     return -0.5 * total + pot[None] * core
 
 

time: 83.9 us -> 82.3 us (0.981)
  starting transfers between devices: 27 us -> 24.1 us
  other arithmetic: 5.32 us -> 7.91 us
  waiting for transfers between devices: 35.6 us -> 34 us
    sub x0 -> x2, other arithmetic: none -> 3.92 us  [apply_ham(): local = local - 1.0 / 12.0 * (along_z[..., :size] + along_z[..., 4:])]
    ppermute x4, waiting for transfers between devices: 1.99 us -> 0.01 us  [faces(): lax.ppermute(head, axis, [((i + 1) % count, i) for i in range(count)])]
    ppermute x8, starting transfers between devices: 10.4 us -> 8.88 us  [butterfly_sum(): lax.ppermute(value, axis, [(i, partner(i)) for i in range(count)])]
    ppermute x4, starting transfers between devices: 12.5 us -> 11.2 us  [faces(): lax.ppermute(head, axis, [((i + 1) % count, i) for i in range(count)])]
    div x1, other arithmetic: 2.2 us -> 1.36 us  [shards(): (apply_ham(orbitals_here, potential, orbitals) - 5.5 * orbitals_here) / 4.5]
    unnamed x12 -> x11, local copies, waits for them, and re-layouts: 2.82 us -> 2.09 us
  transfers between devices with their start and end apart: 16 -> 16, of which waited for: 13 -> 11; matrix products, arithmetic and copies ran while one was open for 2% -> 7% of each run, Pallas kernels for 0% -> 0%
where the time goes in v11:
time: 82.3 us; the launch traced here: 81.9 us
  waiting for transfers between devices  34 us (41%)
  starting transfers between devices  24.1 us (29%)
  other arithmetic  7.91 us (10%)
  Pallas kernels  6.66 us (8%)
  local copies, waits for them, and re-layouts  5.56 us (7%)
  matrix products  2.76 us (3%)
  between operations  0.86 us (1%)
    ppermute x8, waiting for transfers between devices, butterfly_sum(): lax.ppermute(value, axis, [(i, partner(i)) for i in range(count)])  25 us
    ppermute x4, starting transfers between devices, faces(): lax.ppermute(head, axis, [((i + 1) % count, i) for i in range(count)])  11.2 us
    ppermute x4, waiting for transfers between devices, faces(): lax.ppermute(tail, axis, [(i, (i + 1) % count) for i in range(count)])  8.99 us
    ppermute x8, starting transfers between devices, butterfly_sum(): lax.ppermute(value, axis, [(i, partner(i)) for i in range(count)])  8.88 us
    pallas_call x1, Pallas kernels, factor_and_inverse(): pl.pallas_call(factor_kernel, out_shape=jax.ShapeDtypeStruct(aug.shape, j...  6.66 us
    ppermute x4, starting transfers between devices, faces(): lax.ppermute(tail, axis, [(i, (i + 1) % count) for i in range(count)])  4.08 us
    sub x2, other arithmetic, apply_ham(): local = local - 1.0 / 12.0 * (along_z[..., :size] + along_z[..., 4:])  3.92 us
    unnamed x11, local copies, waits for them, and re-layouts  2.09 us
  transfers between devices with their start and end apart: 16, of which 11 were waited for; matrix products, arithmetic and copies ran while one was open for 7% of the time, Pallas kernels for 0%

profile of v11, /device:TPU:32, one launch (start us, length us, event | category | flops | bytes accessed | tf_op | source)
XLA Modules:
  0.0 81.9 jit_solution(11117892946332057755)
XLA Ops:
  0.6 1.4 %fusion.62 = (f32[64,2,8,128]{3,2,1,0:T(8,128)S(1)}, f32[64,2,8,128]{3,2,1,0:T(8,128)S(1)}) fusion(f32[64,4,8,128]{3,2,1,0:T(8,128)} %param.2), kind=kLoop, calls=%fused_computation.103 | loop fusion | bytes 2097152 | tf_op jit(solution)/shard_map/slice | solution.py:12
  2.5 2.0 %collective-permute-start.3 = (f32[64,4,2,128]{3,0,2,1:T(8,128)S(1)}, f32[64,4,2,128]{3,0,2,1:T(8,128)S(1)}, u32[]{:S(2)}, u32[]{:S(2)}) collective-permute-start(f32[64,4,2,128]{3,0,2,1:T(8,128)S(1)} %copy.37), channel_id=1, source_target_pairs={{0,1},{1,2},{2,3},{3,4},{4,5},{5,6},{6,7},{7,0},{8,9},{9,10},{10,1... | collective-permute-start | bytes 786440 | tf_op jit(solution)/shard_map/ppermute | solution.py:14
  4.9 4.7 %collective-permute-start = (f32[64,2,8,128]{3,0,2,1:T(8,128)S(1)}, f32[64,2,8,128]{3,0,2,1:T(8,128)S(1)}, u32[]{:S(2)}, u32[]{:S(2)}) collective-permute-start(f32[64,2,8,128]{3,0,2,1:T(8,128)S(1)} %copy.34), channel_id=1, source_target_pairs={{8,0},{16,8},{24,16},{32,24},{40,32},{48,40},{56,48},{64,56},{72,6... | collective-permute-start | bytes 1572872 | tf_op jit(solution)/shard_map/ppermute | solution.py:15
  9.7 1.4 %collective-permute-done.3 = f32[64,4,2,128]{3,0,2,1:T(8,128)S(1)} collective-permute-done((f32[64,4,2,128]{3,0,2,1:T(8,128)S(1)}, f32[64,4,2,128]{3,0,2,1:T(8,128)S(1)}, u32[]{:S(2)}, u32[]{:S(2)}) %collective-permute-start.3) | collective-permute-done | bytes 262176 | tf_op jit(solution)/shard_map/ppermute | solution.py:14
  11.2 3.0 %collective-permute-done.1 = f32[64,2,8,128]{3,0,2,1:T(8,128)S(1)} collective-permute-done((f32[64,2,8,128]{3,0,2,1:T(8,128)S(1)}, f32[64,2,8,128]{3,0,2,1:T(8,128)S(1)}, u32[]{:S(2)}, u32[]{:S(2)}) %collective-permute-start.1) | collective-permute-done | bytes 524320 | tf_op jit(solution)/shard_map/ppermute | solution.py:14
  15.4 2.0 %fusion.28 = f32[64,4,8,128]{3,0,2,1:T(8,128)S(1)} fusion(f32[64,4,8,128]{3,0,2,1:T(8,128)S(1)} %get-tuple-element.18, f32[64,4,8,2]{3,0,2,1:T(8,128)S(1)} %get-tuple-element.17, f32[64,4,8,2]{3,0,2,1:T(8,128)S(1)} %get-tuple-element.16), kind=kLoop, calls=%fused_computation.45 | loop fusion | flops 2883584 | bytes 2129920 | tf_op jit(solution)/shard_map/sub | solution.py:30
  19.0 2.0 %collective-permute-start.7 = (f32[64,4,2,128]{3,0,2,1:T(8,128)S(1)}, f32[64,4,2,128]{3,0,2,1:T(8,128)S(1)}, u32[]{:S(2)}, u32[]{:S(2)}) collective-permute-start(f32[64,4,2,128]{3,0,2,1:T(8,128)S(1)} %get-tuple-element.15), channel_id=1, source_target_pairs={{0,1},{1,2},{2,3},{3,4},{4,5},{5,6},{6,7},{7,0},{8,9},{9,10},{10,1... | collective-permute-start | bytes 786440 | tf_op jit(solution)/shard_map/ppermute | solution.py:14
  22.2 5.1 %collective-permute-start.4 = (f32[64,2,8,128]{3,0,2,1:T(8,128)S(1)}, f32[64,2,8,128]{3,0,2,1:T(8,128)S(1)}, u32[]{:S(2)}, u32[]{:S(2)}) collective-permute-start(f32[64,2,8,128]{3,0,2,1:T(8,128)S(1)} %get-tuple-element.10), channel_id=1, source_target_pairs={{8,0},{16,8},{24,16},{32,24},{40,32},{48,40},{56,48},{64,56},{72,6... | collective-permute-start | bytes 1572872 | tf_op jit(solution)/shard_map/ppermute | solution.py:15
  27.6 2.0 %fusion.22 = f32[64,4,8,128]{3,0,2,1:T(8,128)S(1)} fusion(f32[64,4,8,128]{3,0,2,1:T(8,128)S(1)} %get-tuple-element.8, f32[64,4,8,2]{3,0,2,1:T(8,128)S(1)} %get-tuple-element.13, f32[64,4,8,2]{3,0,2,1:T(8,128)S(1)} %get-tuple-element.12, f32[64,4,8,128]{3,0,2,1:T(8,128)S(1)} %get-tuple-element.9), kind=kLoop, calls=%fused_computation.39 | loop fusion | flops 2883584 | bytes 3178496 | tf_op jit(solution)/shard_map/sub | solution.py:30
  29.6 4.5 %collective-permute-done.5 = f32[64,2,8,128]{3,0,2,1:T(8,128)S(1)} collective-permute-done((f32[64,2,8,128]{3,0,2,1:T(8,128)S(1)}, f32[64,2,8,128]{3,0,2,1:T(8,128)S(1)}, u32[]{:S(2)}, u32[]{:S(2)}) %collective-permute-start.5) | collective-permute-done | bytes 524320 | tf_op jit(solution)/shard_map/ppermute | solution.py:14
  34.1 1.9 %fusion.10 = f32[64,4,8,128]{3,0,2,1:T(8,128)S(1)} fusion(f32[64,4,2,128]{3,0,2,1:T(8,128)S(1)} %collective-permute-done.7, f32[64,4,8,128]{3,0,2,1:T(8,128)S(1)} %get-tuple-element.8, f32[64,4,2,128]{3,0,2,1:T(8,128)S(1)} %collective-permute-done.6, f32[64,4,8,128]{3,0,2,1:T(8,128)S(1)} %fusion.22, f32[64,2,8,128]{3,0,2,1:T(8,128)S(1)} %collective-permute-done.5, ...), kind=kLoop, calls=%fused_computation.27 | loop fusion | flops 7077888 | bytes 6832128 | tf_op jit(solution)/shard_map/sub | solution.py:104
  37.0 3.2 %collective-permute-start.8 = (f32[32,128]{1,0:T(8,128)S(1)}, f32[32,128]{1,0:T(8,128)S(1)}, u32[]{:S(2)}, u32[]{:S(2)}) collective-permute-start(f32[32,128]{1,0:T(8,128)S(1)} %reshape.11), channel_id=1, source_target_pairs={{0,1},{1,0},{2,3},{3,2},{4,5},{5,4},{6,7},{7,6},{8,9},{9,8},{10,11... | collective-permute-start | bytes 49160 | tf_op jit(solution)/shard_map/ppermute | solution.py:96
  40.2 1.7 %collective-permute-done.8 = f32[32,128]{1,0:T(8,128)S(1)} collective-permute-done((f32[32,128]{1,0:T(8,128)S(1)}, f32[32,128]{1,0:T(8,128)S(1)}, u32[]{:S(2)}, u32[]{:S(2)}) %collective-permute-start.8) | collective-permute-done | bytes 16416 | tf_op jit(solution)/shard_map/ppermute | solution.py:96
  41.9 2.2 %collective-permute-start.9 = (f32[32,128]{1,0:T(8,128)S(1)}, f32[32,128]{1,0:T(8,128)S(1)}, u32[]{:S(2)}, u32[]{:S(2)}) collective-permute-start(f32[32,128]{1,0:T(8,128)S(1)} %add.107), channel_id=1, source_target_pairs={{0,2},{1,3},{2,0},{3,1},{4,6},{5,7},{6,4},{7,5},{8,10},{9,11},{10,... | collective-permute-start | bytes 49160 | tf_op jit(solution)/shard_map/ppermute | solution.py:96
  44.1 2.5 %collective-permute-done.9 = f32[32,128]{1,0:T(8,128)S(1)} collective-permute-done((f32[32,128]{1,0:T(8,128)S(1)}, f32[32,128]{1,0:T(8,128)S(1)}, u32[]{:S(2)}, u32[]{:S(2)}) %collective-permute-start.9) | collective-permute-done | bytes 16416 | tf_op jit(solution)/shard_map/ppermute | solution.py:96
  46.6 3.2 %collective-permute-start.10 = (f32[32,128]{1,0:T(8,128)S(1)}, f32[32,128]{1,0:T(8,128)S(1)}, u32[]{:S(2)}, u32[]{:S(2)}) collective-permute-start(f32[32,128]{1,0:T(8,128)S(1)} %add.108), channel_id=1, source_target_pairs={{0,6},{1,7},{2,4},{3,5},{4,2},{5,3},{6,0},{7,1},{8,14},{9,15},{10,... | collective-permute-start | bytes 49160 | tf_op jit(solution)/shard_map/ppermute | solution.py:96
  49.8 2.7 %collective-permute-done.10 = f32[32,128]{1,0:T(8,128)S(1)} collective-permute-done((f32[32,128]{1,0:T(8,128)S(1)}, f32[32,128]{1,0:T(8,128)S(1)}, u32[]{:S(2)}, u32[]{:S(2)}) %collective-permute-start.10) | collective-permute-done | bytes 16416 | tf_op jit(solution)/shard_map/ppermute | solution.py:96
  53.6 3.7 %collective-permute-done.12 = f32[32,128]{1,0:T(8,128)S(1)} collective-permute-done((f32[32,128]{1,0:T(8,128)S(1)}, f32[32,128]{1,0:T(8,128)S(1)}, u32[]{:S(2)}, u32[]{:S(2)}) %collective-permute-start.12) | collective-permute-done | bytes 16416 | tf_op jit(solution)/shard_map/ppermute | solution.py:96
  57.4 4.9 %collective-permute-done.13 = f32[32,128]{1,0:T(8,128)S(1)} collective-permute-done((f32[32,128]{1,0:T(8,128)S(1)}, f32[32,128]{1,0:T(8,128)S(1)}, u32[]{:S(2)}, u32[]{:S(2)}) %collective-permute-start.13) | collective-permute-done | bytes 16416 | tf_op jit(solution)/shard_map/ppermute | solution.py:96
  62.3 3.7 %collective-permute-done.14 = f32[32,128]{1,0:T(8,128)S(1)} collective-permute-done((f32[32,128]{1,0:T(8,128)S(1)}, f32[32,128]{1,0:T(8,128)S(1)}, u32[]{:S(2)}, u32[]{:S(2)}) %collective-permute-start.14) | collective-permute-done | bytes 16416 | tf_op jit(solution)/shard_map/ppermute | solution.py:96
  66.4 4.6 %collective-permute-done.15 = f32[32,128]{1,0:T(8,128)S(1)} collective-permute-done((f32[32,128]{1,0:T(8,128)S(1)}, f32[32,128]{1,0:T(8,128)S(1)}, u32[]{:S(2)}, u32[]{:S(2)}) %collective-permute-start.15) | collective-permute-done | bytes 16416 | tf_op jit(solution)/shard_map/ppermute | solution.py:96
  71.9 6.7 %shard_map.41 = f32[64,128]{1,0:T(8,128)} custom-call(f32[64,128]{1,0:T(8,128)} %pad_maximum_fusion.8.aug_ref), custom_call_target="tpu_custom_call" | custom-call | tf_op jit(solution)/shard_map/pallas_call | solution.py:66
  78.5 1.8 %fusion.50 = f32[64,4,8,128]{3,0,2,1:T(8,128)S(1)} fusion(f32[64,4,8,128]{3,0,2,1:T(8,128)S(1)} %fusion.10, f32[64,128]{1,0:T(8,128)} %shard_map.41), kind=kOutput, calls=%fused_computation.81 | convolution fusion | flops 201330688 | bytes 2129920 | tf_op jit(solution)/shard_map/mk,kxyz->mxyz/dot_general | solution.py:117
  80.3 1.6 %copy.31 = f32[64,4,8,128]{3,2,1,0:T(8,128)} copy(f32[64,4,8,128]{3,0,2,1:T(8,128)S(1)} %fusion.50) | data formatting | bytes 2097152
  (50 shorter events, 8.7 us)
Async XLA Ops:
  0.6 1.7 %copy-start = (f32[64,4,8,128]{3,2,1,0:T(8,128)S(1)}, f32[64,4,8,128]{3,2,1,0:T(8,128)}, u32[]{:S(2)}) copy-start(f32[64,4,8,128]{3,2,1,0:T(8,128)} %param.2) | copy-start | bytes 3145732
  2.2 7.5 %copy-start.1 = (f32[4,8,128]{2,1,0:T(8,128)S(1)}, f32[4,8,128]{2,1,0:T(8,128)}, u32[]{:S(2)}) copy-start(f32[4,8,128]{2,1,0:T(8,128)} %param.3) | copy-start | bytes 49156
  2.2 12.0 %collective-permute-start.1 = (f32[64,2,8,128]{3,0,2,1:T(8,128)S(1)}, f32[64,2,8,128]{3,0,2,1:T(8,128)S(1)}, u32[]{:S(2)}, u32[]{:S(2)}) collective-permute-start(f32[64,2,8,128]{3,0,2,1:T(8,128)S(1)} %copy.35), channel_id=1, source_target_pairs={{0,8},{8,16},{16,24},{24,32},{32,40},{40,48},{48,56},{56,64},{64,7... | collective-permute-start | bytes 1572872 | tf_op jit(solution)/shard_map/ppermute | solution.py:14
  2.5 8.6 %collective-permute-start.3 = (f32[64,4,2,128]{3,0,2,1:T(8,128)S(1)}, f32[64,4,2,128]{3,0,2,1:T(8,128)S(1)}, u32[]{:S(2)}, u32[]{:S(2)}) collective-permute-start(f32[64,4,2,128]{3,0,2,1:T(8,128)S(1)} %copy.37), channel_id=1, source_target_pairs={{0,1},{1,2},{2,3},{3,4},{4,5},{5,6},{6,7},{7,0},{8,9},{9,10},{10,1... | collective-permute-start | bytes 786440 | tf_op jit(solution)/shard_map/ppermute | solution.py:14
  4.6 12.8 %collective-permute-start.2 = (f32[64,4,2,128]{3,0,2,1:T(8,128)S(1)}, f32[64,4,2,128]{3,0,2,1:T(8,128)S(1)}, u32[]{:S(2)}, u32[]{:S(2)}) collective-permute-start(f32[64,4,2,128]{3,0,2,1:T(8,128)S(1)} %copy.36), channel_id=1, source_target_pairs={{1,0},{2,1},{3,2},{4,3},{5,4},{6,5},{7,6},{0,7},{9,8},{10,9},{11,1... | collective-permute-start | bytes 786440 | tf_op jit(solution)/shard_map/ppermute | solution.py:15
  4.9 12.5 %collective-permute-start = (f32[64,2,8,128]{3,0,2,1:T(8,128)S(1)}, f32[64,2,8,128]{3,0,2,1:T(8,128)S(1)}, u32[]{:S(2)}, u32[]{:S(2)}) collective-permute-start(f32[64,2,8,128]{3,0,2,1:T(8,128)S(1)} %copy.34), channel_id=1, source_target_pairs={{8,0},{16,8},{24,16},{32,24},{40,32},{48,40},{56,48},{64,56},{72,6... | collective-permute-start | bytes 1572872 | tf_op jit(solution)/shard_map/ppermute | solution.py:15
  19.0 10.6 %collective-permute-start.7 = (f32[64,4,2,128]{3,0,2,1:T(8,128)S(1)}, f32[64,4,2,128]{3,0,2,1:T(8,128)S(1)}, u32[]{:S(2)}, u32[]{:S(2)}) collective-permute-start(f32[64,4,2,128]{3,0,2,1:T(8,128)S(1)} %get-tuple-element.15), channel_id=1, source_target_pairs={{0,1},{1,2},{2,3},{3,4},{4,5},{5,6},{6,7},{7,0},{8,9},{9,10},{10,1... | collective-permute-start | bytes 786440 | tf_op jit(solution)/shard_map/ppermute | solution.py:14
  21.0 8.6 %collective-permute-start.6 = (f32[64,4,2,128]{3,0,2,1:T(8,128)S(1)}, f32[64,4,2,128]{3,0,2,1:T(8,128)S(1)}, u32[]{:S(2)}, u32[]{:S(2)}) collective-permute-start(f32[64,4,2,128]{3,0,2,1:T(8,128)S(1)} %get-tuple-element.14), channel_id=1, source_target_pairs={{1,0},{2,1},{3,2},{4,3},{5,4},{6,5},{7,6},{0,7},{9,8},{10,9},{11,1... | collective-permute-start | bytes 786440 | tf_op jit(solution)/shard_map/ppermute | solution.py:15
  22.2 11.9 %collective-permute-start.5 = (f32[64,2,8,128]{3,0,2,1:T(8,128)S(1)}, f32[64,2,8,128]{3,0,2,1:T(8,128)S(1)}, u32[]{:S(2)}, u32[]{:S(2)}) collective-permute-start(f32[64,2,8,128]{3,0,2,1:T(8,128)S(1)} %get-tuple-element.11), channel_id=1, source_target_pairs={{0,8},{8,16},{16,24},{24,32},{32,40},{40,48},{48,56},{56,64},{64,7... | collective-permute-start | bytes 1572872 | tf_op jit(solution)/shard_map/ppermute | solution.py:14
  22.2 11.9 %collective-permute-start.4 = (f32[64,2,8,128]{3,0,2,1:T(8,128)S(1)}, f32[64,2,8,128]{3,0,2,1:T(8,128)S(1)}, u32[]{:S(2)}, u32[]{:S(2)}) collective-permute-start(f32[64,2,8,128]{3,0,2,1:T(8,128)S(1)} %get-tuple-element.10), channel_id=1, source_target_pairs={{8,0},{16,8},{24,16},{32,24},{40,32},{48,40},{56,48},{64,56},{72,6... | collective-permute-start | bytes 1572872 | tf_op jit(solution)/shard_map/ppermute | solution.py:15
  37.0 4.9 %collective-permute-start.8 = (f32[32,128]{1,0:T(8,128)S(1)}, f32[32,128]{1,0:T(8,128)S(1)}, u32[]{:S(2)}, u32[]{:S(2)}) collective-permute-start(f32[32,128]{1,0:T(8,128)S(1)} %reshape.11), channel_id=1, source_target_pairs={{0,1},{1,0},{2,3},{3,2},{4,5},{5,4},{6,7},{7,6},{8,9},{9,8},{10,11... | collective-permute-start | bytes 49160 | tf_op jit(solution)/shard_map/ppermute | solution.py:96
  41.9 4.6 %collective-permute-start.9 = (f32[32,128]{1,0:T(8,128)S(1)}, f32[32,128]{1,0:T(8,128)S(1)}, u32[]{:S(2)}, u32[]{:S(2)}) collective-permute-start(f32[32,128]{1,0:T(8,128)S(1)} %add.107), channel_id=1, source_target_pairs={{0,2},{1,3},{2,0},{3,1},{4,6},{5,7},{6,4},{7,5},{8,10},{9,11},{10,... | collective-permute-start | bytes 49160 | tf_op jit(solution)/shard_map/ppermute | solution.py:96
  46.6 5.8 %collective-permute-start.10 = (f32[32,128]{1,0:T(8,128)S(1)}, f32[32,128]{1,0:T(8,128)S(1)}, u32[]{:S(2)}, u32[]{:S(2)}) collective-permute-start(f32[32,128]{1,0:T(8,128)S(1)} %add.108), channel_id=1, source_target_pairs={{0,6},{1,7},{2,4},{3,5},{4,2},{5,3},{6,0},{7,1},{8,14},{9,15},{10,... | collective-permute-start | bytes 49160 | tf_op jit(solution)/shard_map/ppermute | solution.py:96
  52.4 1.2 %collective-permute-start.11 = (f32[32,128]{1,0:T(8,128)S(1)}, f32[32,128]{1,0:T(8,128)S(1)}, u32[]{:S(2)}, u32[]{:S(2)}) collective-permute-start(f32[32,128]{1,0:T(8,128)S(1)} %add.109), channel_id=1, source_target_pairs={{0,8},{8,0},{16,24},{24,16},{32,40},{40,32},{48,56},{56,48},{64,72... | collective-permute-start | bytes 49160 | tf_op jit(solution)/shard_map/ppermute | solution.py:96
  53.6 3.7 %collective-permute-start.12 = (f32[32,128]{1,0:T(8,128)S(1)}, f32[32,128]{1,0:T(8,128)S(1)}, u32[]{:S(2)}, u32[]{:S(2)}) collective-permute-start(f32[32,128]{1,0:T(8,128)S(1)} %add.110), channel_id=1, source_target_pairs={{0,16},{8,24},{16,0},{24,8},{32,48},{40,56},{48,32},{56,40},{64,80... | collective-permute-start | bytes 49160 | tf_op jit(solution)/shard_map/ppermute | solution.py:96
  57.4 4.9 %collective-permute-start.13 = (f32[32,128]{1,0:T(8,128)S(1)}, f32[32,128]{1,0:T(8,128)S(1)}, u32[]{:S(2)}, u32[]{:S(2)}) collective-permute-start(f32[32,128]{1,0:T(8,128)S(1)} %add.111), channel_id=1, source_target_pairs={{0,48},{8,56},{16,32},{24,40},{32,16},{40,24},{48,0},{56,8},{64,11... | collective-permute-start | bytes 49160 | tf_op jit(solution)/shard_map/ppermute | solution.py:96
  62.3 3.7 %collective-permute-start.14 = (f32[32,128]{1,0:T(8,128)S(1)}, f32[32,128]{1,0:T(8,128)S(1)}, u32[]{:S(2)}, u32[]{:S(2)}) collective-permute-start(f32[32,128]{1,0:T(8,128)S(1)} %add.112), channel_id=1, source_target_pairs={{0,64},{8,72},{16,80},{24,88},{32,96},{40,104},{48,112},{56,120},{... | collective-permute-start | bytes 49160 | tf_op jit(solution)/shard_map/ppermute | solution.py:96
  66.1 4.9 %collective-permute-start.15 = (f32[32,128]{1,0:T(8,128)S(1)}, f32[32,128]{1,0:T(8,128)S(1)}, u32[]{:S(2)}, u32[]{:S(2)}) collective-permute-start(f32[32,128]{1,0:T(8,128)S(1)} %add.113), channel_id=1, source_target_pairs={{0,192},{8,200},{16,208},{24,216},{32,224},{40,232},{48,240},{56,2... | collective-permute-start | bytes 49160 | tf_op jit(solution)/shard_map/ppermute | solution.py:96

commit v12 on v11

--- a/solution.py
+++ b/solution.py
@@ -112,7 +112,7 @@
         / cells
     )
     packed = local_gram.reshape(-1, 128)
-    gram = butterfly_sum(butterfly_sum(packed, "gy"), "gx").reshape(local_gram.shape)
+    gram = butterfly_sum(butterfly_sum(packed, "gx"), "gy").reshape(local_gram.shape)
     factor, lower_inverse = factor_and_inverse(gram)
     basis = jnp.einsum(
         "mk,kxyz->mxyz", lower_inverse * jnp.sqrt(jnp.float32(cells)), filtered,

time: 82.3 us -> 84 us (1.021)
  the two profiles are of different devices: /device:TPU:32 before, /device:TPU:30 now
where the time goes in v12:
time: 84 us; the launch traced here: 83.7 us
  waiting for transfers between devices  39.4 us (47%)
  starting transfers between devices  20.6 us (25%)
  other arithmetic  7.91 us (9%)
  Pallas kernels  6.66 us (8%)
  local copies, waits for them, and re-layouts  5.56 us (7%)
  matrix products  2.76 us (3%)
  between operations  0.86 us (1%)
    ppermute x8, waiting for transfers between devices, butterfly_sum(): lax.ppermute(value, axis, [(i, partner(i)) for i in range(count)])  30.1 us
    ppermute x4, waiting for transfers between devices, faces(): lax.ppermute(tail, axis, [(i, (i + 1) % count) for i in range(count)])  9.33 us
    ppermute x4, starting transfers between devices, faces(): lax.ppermute(head, axis, [((i + 1) % count, i) for i in range(count)])  8.78 us
    ppermute x8, starting transfers between devices, butterfly_sum(): lax.ppermute(value, axis, [(i, partner(i)) for i in range(count)])  7.86 us
    pallas_call x1, Pallas kernels, factor_and_inverse(): pl.pallas_call(factor_kernel, out_shape=jax.ShapeDtypeStruct(aug.shape, j...  6.66 us
    ppermute x4, starting transfers between devices, faces(): lax.ppermute(tail, axis, [(i, (i + 1) % count) for i in range(count)])  3.93 us
    sub x2, other arithmetic, apply_ham(): local = local - 1.0 / 12.0 * (along_z[..., :size] + along_z[..., 4:])  3.92 us
    unnamed x11, local copies, waits for them, and re-layouts  2.09 us
  transfers between devices with their start and end apart: 16, of which 11 were waited for; matrix products, arithmetic and copies ran while one was open for 7% of the time, Pallas kernels for 0%

profile of v12, /device:TPU:30, one launch (start us, length us, event | category | flops | bytes accessed | tf_op | source)
XLA Modules:
  0.0 83.7 jit_solution(17051119849163983696)
XLA Ops:
  0.6 1.4 %fusion.62 = (f32[64,2,8,128]{3,2,1,0:T(8,128)S(1)}, f32[64,2,8,128]{3,2,1,0:T(8,128)S(1)}) fusion(f32[64,4,8,128]{3,2,1,0:T(8,128)} %param.2), kind=kLoop, calls=%fused_computation.103 | loop fusion | bytes 2097152 | tf_op jit(solution)/shard_map/slice | solution.py:12
  2.5 2.0 %collective-permute-start.3 = (f32[64,4,2,128]{3,0,2,1:T(8,128)S(1)}, f32[64,4,2,128]{3,0,2,1:T(8,128)S(1)}, u32[]{:S(2)}, u32[]{:S(2)}) collective-permute-start(f32[64,4,2,128]{3,0,2,1:T(8,128)S(1)} %copy.37), channel_id=1, source_target_pairs={{0,1},{1,2},{2,3},{3,4},{4,5},{5,6},{6,7},{7,0},{8,9},{9,10},{10,1... | collective-permute-start | bytes 786440 | tf_op jit(solution)/shard_map/ppermute | solution.py:14
  4.6 4.0 %collective-permute-start.2 = (f32[64,4,2,128]{3,0,2,1:T(8,128)S(1)}, f32[64,4,2,128]{3,0,2,1:T(8,128)S(1)}, u32[]{:S(2)}, u32[]{:S(2)}) collective-permute-start(f32[64,4,2,128]{3,0,2,1:T(8,128)S(1)} %copy.36), channel_id=1, source_target_pairs={{1,0},{2,1},{3,2},{4,3},{5,4},{6,5},{7,6},{0,7},{9,8},{10,9},{11,1... | collective-permute-start | bytes 786440 | tf_op jit(solution)/shard_map/ppermute | solution.py:15
  8.8 1.5 %collective-permute-start = (f32[64,2,8,128]{3,0,2,1:T(8,128)S(1)}, f32[64,2,8,128]{3,0,2,1:T(8,128)S(1)}, u32[]{:S(2)}, u32[]{:S(2)}) collective-permute-start(f32[64,2,8,128]{3,0,2,1:T(8,128)S(1)} %copy.34), channel_id=1, source_target_pairs={{8,0},{16,8},{24,16},{32,24},{40,32},{48,40},{56,48},{64,56},{72,6... | collective-permute-start | bytes 1572872 | tf_op jit(solution)/shard_map/ppermute | solution.py:15
  10.3 4.8 %collective-permute-done.3 = f32[64,4,2,128]{3,0,2,1:T(8,128)S(1)} collective-permute-done((f32[64,4,2,128]{3,0,2,1:T(8,128)S(1)}, f32[64,4,2,128]{3,0,2,1:T(8,128)S(1)}, u32[]{:S(2)}, u32[]{:S(2)}) %collective-permute-start.3) | collective-permute-done | bytes 262176 | tf_op jit(solution)/shard_map/ppermute | solution.py:14
  16.4 2.0 %fusion.28 = f32[64,4,8,128]{3,0,2,1:T(8,128)S(1)} fusion(f32[64,4,8,128]{3,0,2,1:T(8,128)S(1)} %get-tuple-element.18, f32[64,4,8,2]{3,0,2,1:T(8,128)S(1)} %get-tuple-element.17, f32[64,4,8,2]{3,0,2,1:T(8,128)S(1)} %get-tuple-element.16), kind=kLoop, calls=%fused_computation.45 | loop fusion | flops 2883584 | bytes 2129920 | tf_op jit(solution)/shard_map/sub | solution.py:30
  20.1 3.2 %collective-permute-start.6 = (f32[64,4,2,128]{3,0,2,1:T(8,128)S(1)}, f32[64,4,2,128]{3,0,2,1:T(8,128)S(1)}, u32[]{:S(2)}, u32[]{:S(2)}) collective-permute-start(f32[64,4,2,128]{3,0,2,1:T(8,128)S(1)} %get-tuple-element.14), channel_id=1, source_target_pairs={{1,0},{2,1},{3,2},{4,3},{5,4},{6,5},{7,6},{0,7},{9,8},{10,9},{11,1... | collective-permute-start | bytes 786440 | tf_op jit(solution)/shard_map/ppermute | solution.py:15
  23.3 1.8 %collective-permute-start.5 = (f32[64,2,8,128]{3,0,2,1:T(8,128)S(1)}, f32[64,2,8,128]{3,0,2,1:T(8,128)S(1)}, u32[]{:S(2)}, u32[]{:S(2)}) collective-permute-start(f32[64,2,8,128]{3,0,2,1:T(8,128)S(1)} %get-tuple-element.11), channel_id=1, source_target_pairs={{0,8},{8,16},{16,24},{24,32},{32,40},{40,48},{48,56},{56,64},{64,7... | collective-permute-start | bytes 1572872 | tf_op jit(solution)/shard_map/ppermute | solution.py:14
  25.4 2.0 %fusion.22 = f32[64,4,8,128]{3,0,2,1:T(8,128)S(1)} fusion(f32[64,4,8,128]{3,0,2,1:T(8,128)S(1)} %get-tuple-element.8, f32[64,4,8,2]{3,0,2,1:T(8,128)S(1)} %get-tuple-element.13, f32[64,4,8,2]{3,0,2,1:T(8,128)S(1)} %get-tuple-element.12, f32[64,4,8,128]{3,0,2,1:T(8,128)S(1)} %get-tuple-element.9), kind=kLoop, calls=%fused_computation.39 | loop fusion | flops 2883584 | bytes 3178496 | tf_op jit(solution)/shard_map/sub | solution.py:30
  27.4 1.6 %collective-permute-done.7 = f32[64,4,2,128]{3,0,2,1:T(8,128)S(1)} collective-permute-done((f32[64,4,2,128]{3,0,2,1:T(8,128)S(1)}, f32[64,4,2,128]{3,0,2,1:T(8,128)S(1)}, u32[]{:S(2)}, u32[]{:S(2)}) %collective-permute-start.7) | collective-permute-done | bytes 262176 | tf_op jit(solution)/shard_map/ppermute | solution.py:14
  29.0 2.9 %collective-permute-done.5 = f32[64,2,8,128]{3,0,2,1:T(8,128)S(1)} collective-permute-done((f32[64,2,8,128]{3,0,2,1:T(8,128)S(1)}, f32[64,2,8,128]{3,0,2,1:T(8,128)S(1)}, u32[]{:S(2)}, u32[]{:S(2)}) %collective-permute-start.5) | collective-permute-done | bytes 524320 | tf_op jit(solution)/shard_map/ppermute | solution.py:14
  31.9 1.9 %fusion.10 = f32[64,4,8,128]{3,0,2,1:T(8,128)S(1)} fusion(f32[64,4,2,128]{3,0,2,1:T(8,128)S(1)} %collective-permute-done.7, f32[64,4,8,128]{3,0,2,1:T(8,128)S(1)} %get-tuple-element.8, f32[64,4,2,128]{3,0,2,1:T(8,128)S(1)} %collective-permute-done.6, f32[64,4,8,128]{3,0,2,1:T(8,128)S(1)} %fusion.22, f32[64,2,8,128]{3,0,2,1:T(8,128)S(1)} %collective-permute-done.5, ...), kind=kLoop, calls=%fused_computation.27 | loop fusion | flops 7077888 | bytes 6832128 | tf_op jit(solution)/shard_map/sub | solution.py:104
  34.8 5.5 %collective-permute-start.8 = (f32[32,128]{1,0:T(8,128)S(1)}, f32[32,128]{1,0:T(8,128)S(1)}, u32[]{:S(2)}, u32[]{:S(2)}) collective-permute-start(f32[32,128]{1,0:T(8,128)S(1)} %reshape.11), channel_id=1, source_target_pairs={{0,8},{8,0},{16,24},{24,16},{32,40},{40,32},{48,56},{56,48},{64,72... | collective-permute-start | bytes 49160 | tf_op jit(solution)/shard_map/ppermute | solution.py:96
  41.2 3.7 %collective-permute-done.9 = f32[32,128]{1,0:T(8,128)S(1)} collective-permute-done((f32[32,128]{1,0:T(8,128)S(1)}, f32[32,128]{1,0:T(8,128)S(1)}, u32[]{:S(2)}, u32[]{:S(2)}) %collective-permute-start.9) | collective-permute-done | bytes 16416 | tf_op jit(solution)/shard_map/ppermute | solution.py:96
  44.9 4.9 %collective-permute-done.10 = f32[32,128]{1,0:T(8,128)S(1)} collective-permute-done((f32[32,128]{1,0:T(8,128)S(1)}, f32[32,128]{1,0:T(8,128)S(1)}, u32[]{:S(2)}, u32[]{:S(2)}) %collective-permute-start.10) | collective-permute-done | bytes 16416 | tf_op jit(solution)/shard_map/ppermute | solution.py:96
  49.9 3.7 %collective-permute-done.11 = f32[32,128]{1,0:T(8,128)S(1)} collective-permute-done((f32[32,128]{1,0:T(8,128)S(1)}, f32[32,128]{1,0:T(8,128)S(1)}, u32[]{:S(2)}, u32[]{:S(2)}) %collective-permute-start.11) | collective-permute-done | bytes 16416 | tf_op jit(solution)/shard_map/ppermute | solution.py:96
  53.6 4.9 %collective-permute-done.12 = f32[32,128]{1,0:T(8,128)S(1)} collective-permute-done((f32[32,128]{1,0:T(8,128)S(1)}, f32[32,128]{1,0:T(8,128)S(1)}, u32[]{:S(2)}, u32[]{:S(2)}) %collective-permute-start.12) | collective-permute-done | bytes 16416 | tf_op jit(solution)/shard_map/ppermute | solution.py:96
  58.6 3.7 %collective-permute-done.13 = f32[32,128]{1,0:T(8,128)S(1)} collective-permute-done((f32[32,128]{1,0:T(8,128)S(1)}, f32[32,128]{1,0:T(8,128)S(1)}, u32[]{:S(2)}, u32[]{:S(2)}) %collective-permute-start.13) | collective-permute-done | bytes 16416 | tf_op jit(solution)/shard_map/ppermute | solution.py:96
  62.5 4.5 %collective-permute-done.14 = f32[32,128]{1,0:T(8,128)S(1)} collective-permute-done((f32[32,128]{1,0:T(8,128)S(1)}, f32[32,128]{1,0:T(8,128)S(1)}, u32[]{:S(2)}, u32[]{:S(2)}) %collective-permute-start.14) | collective-permute-done | bytes 16416 | tf_op jit(solution)/shard_map/ppermute | solution.py:96
  67.0 2.2 %collective-permute-start.15 = (f32[32,128]{1,0:T(8,128)S(1)}, f32[32,128]{1,0:T(8,128)S(1)}, u32[]{:S(2)}, u32[]{:S(2)}) collective-permute-start(f32[32,128]{1,0:T(8,128)S(1)} %add.113), channel_id=1, source_target_pairs={{0,6},{1,7},{2,4},{3,5},{4,2},{5,3},{6,0},{7,1},{8,14},{9,15},{10,... | collective-permute-start | bytes 49160 | tf_op jit(solution)/shard_map/ppermute | solution.py:96
  69.2 3.7 %collective-permute-done.15 = f32[32,128]{1,0:T(8,128)S(1)} collective-permute-done((f32[32,128]{1,0:T(8,128)S(1)}, f32[32,128]{1,0:T(8,128)S(1)}, u32[]{:S(2)}, u32[]{:S(2)}) %collective-permute-start.15) | collective-permute-done | bytes 16416 | tf_op jit(solution)/shard_map/ppermute | solution.py:96
  73.7 6.7 %shard_map.41 = f32[64,128]{1,0:T(8,128)} custom-call(f32[64,128]{1,0:T(8,128)} %pad_maximum_fusion.8.aug_ref), custom_call_target="tpu_custom_call" | custom-call | tf_op jit(solution)/shard_map/pallas_call | solution.py:66
  80.4 1.8 %fusion.50 = f32[64,4,8,128]{3,0,2,1:T(8,128)S(1)} fusion(f32[64,4,8,128]{3,0,2,1:T(8,128)S(1)} %fusion.10, f32[64,128]{1,0:T(8,128)} %shard_map.41), kind=kOutput, calls=%fused_computation.81 | convolution fusion | flops 201330688 | bytes 2129920 | tf_op jit(solution)/shard_map/mk,kxyz->mxyz/dot_general | solution.py:117
  82.2 1.6 %copy.31 = f32[64,4,8,128]{3,2,1,0:T(8,128)} copy(f32[64,4,8,128]{3,0,2,1:T(8,128)S(1)} %fusion.50) | data formatting | bytes 2097152
  (50 shorter events, 6.9 us)
Async XLA Ops:
  0.6 1.7 %copy-start = (f32[64,4,8,128]{3,2,1,0:T(8,128)S(1)}, f32[64,4,8,128]{3,2,1,0:T(8,128)}, u32[]{:S(2)}) copy-start(f32[64,4,8,128]{3,2,1,0:T(8,128)} %param.2) | copy-start | bytes 3145732
  2.2 8.1 %copy-start.1 = (f32[4,8,128]{2,1,0:T(8,128)S(1)}, f32[4,8,128]{2,1,0:T(8,128)}, u32[]{:S(2)}) copy-start(f32[4,8,128]{2,1,0:T(8,128)} %param.3) | copy-start | bytes 49156
  2.2 13.0 %collective-permute-start.1 = (f32[64,2,8,128]{3,0,2,1:T(8,128)S(1)}, f32[64,2,8,128]{3,0,2,1:T(8,128)S(1)}, u32[]{:S(2)}, u32[]{:S(2)}) collective-permute-start(f32[64,2,8,128]{3,0,2,1:T(8,128)S(1)} %copy.35), channel_id=1, source_target_pairs={{0,8},{8,16},{16,24},{24,32},{32,40},{40,48},{48,56},{56,64},{64,7... | collective-permute-start | bytes 1572872 | tf_op jit(solution)/shard_map/ppermute | solution.py:14
  2.5 12.6 %collective-permute-start.3 = (f32[64,4,2,128]{3,0,2,1:T(8,128)S(1)}, f32[64,4,2,128]{3,0,2,1:T(8,128)S(1)}, u32[]{:S(2)}, u32[]{:S(2)}) collective-permute-start(f32[64,4,2,128]{3,0,2,1:T(8,128)S(1)} %copy.37), channel_id=1, source_target_pairs={{0,1},{1,2},{2,3},{3,4},{4,5},{5,6},{6,7},{7,0},{8,9},{9,10},{10,1... | collective-permute-start | bytes 786440 | tf_op jit(solution)/shard_map/ppermute | solution.py:14
  4.6 13.8 %collective-permute-start.2 = (f32[64,4,2,128]{3,0,2,1:T(8,128)S(1)}, f32[64,4,2,128]{3,0,2,1:T(8,128)S(1)}, u32[]{:S(2)}, u32[]{:S(2)}) collective-permute-start(f32[64,4,2,128]{3,0,2,1:T(8,128)S(1)} %copy.36), channel_id=1, source_target_pairs={{1,0},{2,1},{3,2},{4,3},{5,4},{6,5},{7,6},{0,7},{9,8},{10,9},{11,1... | collective-permute-start | bytes 786440 | tf_op jit(solution)/shard_map/ppermute | solution.py:15
  8.8 9.6 %collective-permute-start = (f32[64,2,8,128]{3,0,2,1:T(8,128)S(1)}, f32[64,2,8,128]{3,0,2,1:T(8,128)S(1)}, u32[]{:S(2)}, u32[]{:S(2)}) collective-permute-start(f32[64,2,8,128]{3,0,2,1:T(8,128)S(1)} %copy.34), channel_id=1, source_target_pairs={{8,0},{16,8},{24,16},{32,24},{40,32},{48,40},{56,48},{64,56},{72,6... | collective-permute-start | bytes 1572872 | tf_op jit(solution)/shard_map/ppermute | solution.py:15
  20.0 9.1 %collective-permute-start.7 = (f32[64,4,2,128]{3,0,2,1:T(8,128)S(1)}, f32[64,4,2,128]{3,0,2,1:T(8,128)S(1)}, u32[]{:S(2)}, u32[]{:S(2)}) collective-permute-start(f32[64,4,2,128]{3,0,2,1:T(8,128)S(1)} %get-tuple-element.15), channel_id=1, source_target_pairs={{0,1},{1,2},{2,3},{3,4},{4,5},{5,6},{6,7},{7,0},{8,9},{9,10},{10,1... | collective-permute-start | bytes 786440 | tf_op jit(solution)/shard_map/ppermute | solution.py:14
  20.1 9.0 %collective-permute-start.6 = (f32[64,4,2,128]{3,0,2,1:T(8,128)S(1)}, f32[64,4,2,128]{3,0,2,1:T(8,128)S(1)}, u32[]{:S(2)}, u32[]{:S(2)}) collective-permute-start(f32[64,4,2,128]{3,0,2,1:T(8,128)S(1)} %get-tuple-element.14), channel_id=1, source_target_pairs={{1,0},{2,1},{3,2},{4,3},{5,4},{6,5},{7,6},{0,7},{9,8},{10,9},{11,1... | collective-permute-start | bytes 786440 | tf_op jit(solution)/shard_map/ppermute | solution.py:15
  23.3 8.6 %collective-permute-start.5 = (f32[64,2,8,128]{3,0,2,1:T(8,128)S(1)}, f32[64,2,8,128]{3,0,2,1:T(8,128)S(1)}, u32[]{:S(2)}, u32[]{:S(2)}) collective-permute-start(f32[64,2,8,128]{3,0,2,1:T(8,128)S(1)} %get-tuple-element.11), channel_id=1, source_target_pairs={{0,8},{8,16},{16,24},{24,32},{32,40},{40,48},{48,56},{56,64},{64,7... | collective-permute-start | bytes 1572872 | tf_op jit(solution)/shard_map/ppermute | solution.py:14
  25.1 6.8 %collective-permute-start.4 = (f32[64,2,8,128]{3,0,2,1:T(8,128)S(1)}, f32[64,2,8,128]{3,0,2,1:T(8,128)S(1)}, u32[]{:S(2)}, u32[]{:S(2)}) collective-permute-start(f32[64,2,8,128]{3,0,2,1:T(8,128)S(1)} %get-tuple-element.10), channel_id=1, source_target_pairs={{8,0},{16,8},{24,16},{32,24},{40,32},{48,40},{56,48},{64,56},{72,6... | collective-permute-start | bytes 1572872 | tf_op jit(solution)/shard_map/ppermute | solution.py:15
  34.8 6.4 %collective-permute-start.8 = (f32[32,128]{1,0:T(8,128)S(1)}, f32[32,128]{1,0:T(8,128)S(1)}, u32[]{:S(2)}, u32[]{:S(2)}) collective-permute-start(f32[32,128]{1,0:T(8,128)S(1)} %reshape.11), channel_id=1, source_target_pairs={{0,8},{8,0},{16,24},{24,16},{32,40},{40,32},{48,56},{56,48},{64,72... | collective-permute-start | bytes 49160 | tf_op jit(solution)/shard_map/ppermute | solution.py:96
  41.2 3.7 %collective-permute-start.9 = (f32[32,128]{1,0:T(8,128)S(1)}, f32[32,128]{1,0:T(8,128)S(1)}, u32[]{:S(2)}, u32[]{:S(2)}) collective-permute-start(f32[32,128]{1,0:T(8,128)S(1)} %add.107), channel_id=1, source_target_pairs={{0,16},{8,24},{16,0},{24,8},{32,48},{40,56},{48,32},{56,40},{64,80... | collective-permute-start | bytes 49160 | tf_op jit(solution)/shard_map/ppermute | solution.py:96
  44.9 4.9 %collective-permute-start.10 = (f32[32,128]{1,0:T(8,128)S(1)}, f32[32,128]{1,0:T(8,128)S(1)}, u32[]{:S(2)}, u32[]{:S(2)}) collective-permute-start(f32[32,128]{1,0:T(8,128)S(1)} %add.108), channel_id=1, source_target_pairs={{0,48},{8,56},{16,32},{24,40},{32,16},{40,24},{48,0},{56,8},{64,11... | collective-permute-start | bytes 49160 | tf_op jit(solution)/shard_map/ppermute | solution.py:96
  49.9 3.7 %collective-permute-start.11 = (f32[32,128]{1,0:T(8,128)S(1)}, f32[32,128]{1,0:T(8,128)S(1)}, u32[]{:S(2)}, u32[]{:S(2)}) collective-permute-start(f32[32,128]{1,0:T(8,128)S(1)} %add.109), channel_id=1, source_target_pairs={{0,64},{8,72},{16,80},{24,88},{32,96},{40,104},{48,112},{56,120},{... | collective-permute-start | bytes 49160 | tf_op jit(solution)/shard_map/ppermute | solution.py:96
  53.6 4.9 %collective-permute-start.12 = (f32[32,128]{1,0:T(8,128)S(1)}, f32[32,128]{1,0:T(8,128)S(1)}, u32[]{:S(2)}, u32[]{:S(2)}) collective-permute-start(f32[32,128]{1,0:T(8,128)S(1)} %add.110), channel_id=1, source_target_pairs={{0,192},{8,200},{16,208},{24,216},{32,224},{40,232},{48,240},{56,2... | collective-permute-start | bytes 49160 | tf_op jit(solution)/shard_map/ppermute | solution.py:96
  58.6 3.7 %collective-permute-start.13 = (f32[32,128]{1,0:T(8,128)S(1)}, f32[32,128]{1,0:T(8,128)S(1)}, u32[]{:S(2)}, u32[]{:S(2)}) collective-permute-start(f32[32,128]{1,0:T(8,128)S(1)} %add.111), channel_id=1, source_target_pairs={{0,1},{1,0},{2,3},{3,2},{4,5},{5,4},{6,7},{7,6},{8,9},{9,8},{10,11... | collective-permute-start | bytes 49160 | tf_op jit(solution)/shard_map/ppermute | solution.py:96
  62.3 4.6 %collective-permute-start.14 = (f32[32,128]{1,0:T(8,128)S(1)}, f32[32,128]{1,0:T(8,128)S(1)}, u32[]{:S(2)}, u32[]{:S(2)}) collective-permute-start(f32[32,128]{1,0:T(8,128)S(1)} %add.112), channel_id=1, source_target_pairs={{0,2},{1,3},{2,0},{3,1},{4,6},{5,7},{6,4},{7,5},{8,10},{9,11},{10,... | collective-permute-start | bytes 49160 | tf_op jit(solution)/shard_map/ppermute | solution.py:96
  67.0 5.8 %collective-permute-start.15 = (f32[32,128]{1,0:T(8,128)S(1)}, f32[32,128]{1,0:T(8,128)S(1)}, u32[]{:S(2)}, u32[]{:S(2)}) collective-permute-start(f32[32,128]{1,0:T(8,128)S(1)} %add.113), channel_id=1, source_target_pairs={{0,6},{1,7},{2,4},{3,5},{4,2},{5,3},{6,0},{7,1},{8,14},{9,15},{10,... | collective-permute-start | bytes 49160 | tf_op jit(solution)/shard_map/ppermute | solution.py:96

commit v13 on v11

--- a/solution.py
+++ b/solution.py
@@ -36,40 +36,42 @@
     return -0.5 * total + pot[None] * core
 
 
-def factor_kernel(aug_ref, out_ref):
-    order = aug_ref.shape[0]
+def factor_kernel(gram_ref, flipped_ref, factor_ref, inverse_ref):
+    order = gram_ref.shape[0]
     groups = order // 8
-    blocks = [aug_ref[pl.ds(8 * i, 8), :] for i in range(groups)]
-    sub = lax.broadcasted_iota(jnp.int32, blocks[0].shape, 0)
-    lane = lax.broadcasted_iota(jnp.int32, blocks[0].shape, 1)
+    sub = lax.broadcasted_iota(jnp.int32, (8, order), 0)
+    lane = lax.broadcasted_iota(jnp.int32, (8, order), 1)
+    left = [
+        0.5 * (gram_ref[pl.ds(8 * i, 8), :] + flipped_ref[pl.ds(8 * i, 8), :])
+        for i in range(groups)
+    ]
+    right = [jnp.where(lane == sub + 8 * i, 1.0, 0.0) for i in range(groups)]
     for k in range(order):
         home, place = divmod(k, 8)
-        row = blocks[home][place:place + 1, :]
+        row = left[home][place:place + 1, :]
+        row_right = right[home][place:place + 1, :]
         inverse = 1.0 / row[:, k:k + 1]
         for j in range(home, groups):
-            block = blocks[j]
-            column = block[:, k:k + 1] * inverse
+            column = left[j][:, k:k + 1] * inverse
             if j == home:
                 column = jnp.where(sub[:, :1] > place, column, 0.0)
-            blocks[j] = block - column * row
+            left[j] = left[j] - column * row
+            right[j] = right[j] - column * row_right
     for i in range(groups):
-        block = blocks[i]
-        pivots = jnp.sum(jnp.where(lane == sub + 8 * i, block, 0.0), axis=1, keepdims=True)
-        keep = (lane >= order) | (lane >= sub + 8 * i)
-        out_ref[pl.ds(8 * i, 8), :] = jnp.where(keep, block / jnp.sqrt(pivots), 0.0)
+        pivots = jnp.sum(jnp.where(lane == sub + 8 * i, left[i], 0.0), axis=1, keepdims=True)
+        scale = 1.0 / jnp.sqrt(pivots)
+        factor_ref[pl.ds(8 * i, 8), :] = jnp.where(lane >= sub + 8 * i, left[i] * scale, 0.0)
+        inverse_ref[pl.ds(8 * i, 8), :] = right[i] * scale
 
 
 def factor_and_inverse(gram):
-    order = gram.shape[0]
-    sym = 0.5 * (gram + gram.T)
-    aug = jnp.concatenate([sym, jnp.eye(order, dtype=jnp.float32)], axis=1)
-    out = pl.pallas_call(
+    shape = jax.ShapeDtypeStruct(gram.shape, jnp.float32)
+    return pl.pallas_call(
         factor_kernel,
-        out_shape=jax.ShapeDtypeStruct(aug.shape, jnp.float32),
-        in_specs=[pl.BlockSpec(memory_space=pltpu.VMEM)],
-        out_specs=pl.BlockSpec(memory_space=pltpu.VMEM),
-    )(aug)
-    return out[:, :order], out[:, order:]
+        out_shape=(shape, shape),
+        in_specs=[pl.BlockSpec(memory_space=pltpu.VMEM)] * 2,
+        out_specs=(pl.BlockSpec(memory_space=pltpu.VMEM),) * 2,
+    )(gram, gram.T)
 
 
 def ring_rounds(stride):

time: 82.3 us -> 81.9 us (level)
  other arithmetic: 7.91 us -> 6.76 us
    unnamed x11 -> x13, local copies, waits for them, and re-layouts: 2.09 us -> 2.1 us
where the time goes in v13:
time: 81.9 us; the launch traced here: 81.4 us
  waiting for transfers between devices  34 us (42%)
  starting transfers between devices  24.1 us (29%)
  other arithmetic  6.76 us (8%)
  Pallas kernels  6.69 us (8%)
  local copies, waits for them, and re-layouts  6.19 us (8%)
  matrix products  2.77 us (3%)
  between operations  0.86 us (1%)
    ppermute x8, waiting for transfers between devices, butterfly_sum(): lax.ppermute(value, axis, [(i, partner(i)) for i in range(count)])  25.1 us
    ppermute x4, starting transfers between devices, faces(): lax.ppermute(head, axis, [((i + 1) % count, i) for i in range(count)])  11.2 us
    ppermute x4, waiting for transfers between devices, faces(): lax.ppermute(tail, axis, [(i, (i + 1) % count) for i in range(count)])  8.97 us
    ppermute x8, starting transfers between devices, butterfly_sum(): lax.ppermute(value, axis, [(i, partner(i)) for i in range(count)])  8.87 us
    pallas_call x1, Pallas kernels, factor_and_inverse(): pl.pallas_call(factor_kernel, out_shape=(shape, shape), in_specs=[pl.Bloc...  6.69 us
    ppermute x4, starting transfers between devices, faces(): lax.ppermute(tail, axis, [(i, (i + 1) % count) for i in range(count)])  4.08 us
    sub x2, other arithmetic, apply_ham(): local = local - 1.0 / 12.0 * (along_z[..., :size] + along_z[..., 4:])  3.92 us
    unnamed x13, local copies, waits for them, and re-layouts  2.1 us
  transfers between devices with their start and end apart: 16, of which 11 were waited for; matrix products, arithmetic and copies ran while one was open for 7% of the time, Pallas kernels for 0%

profile of v13, /device:TPU:32, one launch (start us, length us, event | category | flops | bytes accessed | tf_op | source)
XLA Modules:
  0.0 81.4 jit_solution(16055282020456086054)
XLA Ops:
  0.6 1.4 %fusion.60 = (f32[64,2,8,128]{3,2,1,0:T(8,128)S(1)}, f32[64,2,8,128]{3,2,1,0:T(8,128)S(1)}) fusion(f32[64,4,8,128]{3,2,1,0:T(8,128)} %param.2), kind=kLoop, calls=%fused_computation.98 | loop fusion | bytes 2097152 | tf_op jit(solution)/shard_map/slice | solution.py:12
  2.5 2.0 %collective-permute-start.3 = (f32[64,4,2,128]{3,0,2,1:T(8,128)S(1)}, f32[64,4,2,128]{3,0,2,1:T(8,128)S(1)}, u32[]{:S(2)}, u32[]{:S(2)}) collective-permute-start(f32[64,4,2,128]{3,0,2,1:T(8,128)S(1)} %copy.37), channel_id=1, source_target_pairs={{0,1},{1,2},{2,3},{3,4},{4,5},{5,6},{6,7},{7,0},{8,9},{9,10},{10,1... | collective-permute-start | bytes 786440 | tf_op jit(solution)/shard_map/ppermute | solution.py:14
  4.9 4.7 %collective-permute-start = (f32[64,2,8,128]{3,0,2,1:T(8,128)S(1)}, f32[64,2,8,128]{3,0,2,1:T(8,128)S(1)}, u32[]{:S(2)}, u32[]{:S(2)}) collective-permute-start(f32[64,2,8,128]{3,0,2,1:T(8,128)S(1)} %copy.34), channel_id=1, source_target_pairs={{8,0},{16,8},{24,16},{32,24},{40,32},{48,40},{56,48},{64,56},{72,6... | collective-permute-start | bytes 1572872 | tf_op jit(solution)/shard_map/ppermute | solution.py:15
  9.7 1.4 %collective-permute-done.3 = f32[64,4,2,128]{3,0,2,1:T(8,128)S(1)} collective-permute-done((f32[64,4,2,128]{3,0,2,1:T(8,128)S(1)}, f32[64,4,2,128]{3,0,2,1:T(8,128)S(1)}, u32[]{:S(2)}, u32[]{:S(2)}) %collective-permute-start.3) | collective-permute-done | bytes 262176 | tf_op jit(solution)/shard_map/ppermute | solution.py:14
  11.2 3.0 %collective-permute-done.1 = f32[64,2,8,128]{3,0,2,1:T(8,128)S(1)} collective-permute-done((f32[64,2,8,128]{3,0,2,1:T(8,128)S(1)}, f32[64,2,8,128]{3,0,2,1:T(8,128)S(1)}, u32[]{:S(2)}, u32[]{:S(2)}) %collective-permute-start.1) | collective-permute-done | bytes 524320 | tf_op jit(solution)/shard_map/ppermute | solution.py:14
  15.4 2.0 %fusion.28 = f32[64,4,8,128]{3,0,2,1:T(8,128)S(1)} fusion(f32[64,4,8,128]{3,0,2,1:T(8,128)S(1)} %get-tuple-element.22, f32[64,4,8,2]{3,0,2,1:T(8,128)S(1)} %get-tuple-element.21, f32[64,4,8,2]{3,0,2,1:T(8,128)S(1)} %get-tuple-element.20), kind=kLoop, calls=%fused_computation.45 | loop fusion | flops 2883584 | bytes 2129920 | tf_op jit(solution)/shard_map/sub | solution.py:30
  18.8 2.0 %collective-permute-start.7 = (f32[64,4,2,128]{3,0,2,1:T(8,128)S(1)}, f32[64,4,2,128]{3,0,2,1:T(8,128)S(1)}, u32[]{:S(2)}, u32[]{:S(2)}) collective-permute-start(f32[64,4,2,128]{3,0,2,1:T(8,128)S(1)} %get-tuple-element.19), channel_id=1, source_target_pairs={{0,1},{1,2},{2,3},{3,4},{4,5},{5,6},{6,7},{7,0},{8,9},{9,10},{10,1... | collective-permute-start | bytes 786440 | tf_op jit(solution)/shard_map/ppermute | solution.py:14
  21.9 5.1 %collective-permute-start.4 = (f32[64,2,8,128]{3,0,2,1:T(8,128)S(1)}, f32[64,2,8,128]{3,0,2,1:T(8,128)S(1)}, u32[]{:S(2)}, u32[]{:S(2)}) collective-permute-start(f32[64,2,8,128]{3,0,2,1:T(8,128)S(1)} %get-tuple-element.14), channel_id=1, source_target_pairs={{8,0},{16,8},{24,16},{32,24},{40,32},{48,40},{56,48},{64,56},{72,6... | collective-permute-start | bytes 1572872 | tf_op jit(solution)/shard_map/ppermute | solution.py:15
  27.4 2.0 %fusion.22 = f32[64,4,8,128]{3,0,2,1:T(8,128)S(1)} fusion(f32[64,4,8,128]{3,0,2,1:T(8,128)S(1)} %get-tuple-element.12, f32[64,4,8,2]{3,0,2,1:T(8,128)S(1)} %get-tuple-element.17, f32[64,4,8,2]{3,0,2,1:T(8,128)S(1)} %get-tuple-element.16, f32[64,4,8,128]{3,0,2,1:T(8,128)S(1)} %get-tuple-element.13), kind=kLoop, calls=%fused_computation.39 | loop fusion | flops 2883584 | bytes 3178496 | tf_op jit(solution)/shard_map/sub | solution.py:30
  29.4 4.5 %collective-permute-done.5 = f32[64,2,8,128]{3,0,2,1:T(8,128)S(1)} collective-permute-done((f32[64,2,8,128]{3,0,2,1:T(8,128)S(1)}, f32[64,2,8,128]{3,0,2,1:T(8,128)S(1)}, u32[]{:S(2)}, u32[]{:S(2)}) %collective-permute-start.5) | collective-permute-done | bytes 524320 | tf_op jit(solution)/shard_map/ppermute | solution.py:14
  33.9 1.7 %fusion.10 = f32[64,4,8,128]{3,0,2,1:T(8,128)S(1)} fusion(f32[64,4,2,128]{3,0,2,1:T(8,128)S(1)} %collective-permute-done.7, f32[64,4,8,128]{3,0,2,1:T(8,128)S(1)} %get-tuple-element.12, f32[64,4,2,128]{3,0,2,1:T(8,128)S(1)} %collective-permute-done.6, f32[64,4,8,128]{3,0,2,1:T(8,128)S(1)} %fusion.22, f32[64,2,8,128]{3,0,2,1:T(8,128)S(1)} %collective-permute-done.5, ...), kind=kLoop, calls=%fused_computation.27 | loop fusion | flops 7077888 | bytes 6832128 | tf_op jit(solution)/shard_map/sub | solution.py:106
  36.6 3.2 %collective-permute-start.8 = (f32[32,128]{1,0:T(8,128)S(1)}, f32[32,128]{1,0:T(8,128)S(1)}, u32[]{:S(2)}, u32[]{:S(2)}) collective-permute-start(f32[32,128]{1,0:T(8,128)S(1)} %reshape.11), channel_id=1, source_target_pairs={{0,1},{1,0},{2,3},{3,2},{4,5},{5,4},{6,7},{7,6},{8,9},{9,8},{10,11... | collective-permute-start | bytes 49160 | tf_op jit(solution)/shard_map/ppermute | solution.py:98
  39.8 1.7 %collective-permute-done.8 = f32[32,128]{1,0:T(8,128)S(1)} collective-permute-done((f32[32,128]{1,0:T(8,128)S(1)}, f32[32,128]{1,0:T(8,128)S(1)}, u32[]{:S(2)}, u32[]{:S(2)}) %collective-permute-start.8) | collective-permute-done | bytes 16416 | tf_op jit(solution)/shard_map/ppermute | solution.py:98
  41.5 2.2 %collective-permute-start.9 = (f32[32,128]{1,0:T(8,128)S(1)}, f32[32,128]{1,0:T(8,128)S(1)}, u32[]{:S(2)}, u32[]{:S(2)}) collective-permute-start(f32[32,128]{1,0:T(8,128)S(1)} %add.104), channel_id=1, source_target_pairs={{0,2},{1,3},{2,0},{3,1},{4,6},{5,7},{6,4},{7,5},{8,10},{9,11},{10,... | collective-permute-start | bytes 49160 | tf_op jit(solution)/shard_map/ppermute | solution.py:98
  43.7 2.5 %collective-permute-done.9 = f32[32,128]{1,0:T(8,128)S(1)} collective-permute-done((f32[32,128]{1,0:T(8,128)S(1)}, f32[32,128]{1,0:T(8,128)S(1)}, u32[]{:S(2)}, u32[]{:S(2)}) %collective-permute-start.9) | collective-permute-done | bytes 16416 | tf_op jit(solution)/shard_map/ppermute | solution.py:98
  46.1 3.2 %collective-permute-start.10 = (f32[32,128]{1,0:T(8,128)S(1)}, f32[32,128]{1,0:T(8,128)S(1)}, u32[]{:S(2)}, u32[]{:S(2)}) collective-permute-start(f32[32,128]{1,0:T(8,128)S(1)} %add.105), channel_id=1, source_target_pairs={{0,6},{1,7},{2,4},{3,5},{4,2},{5,3},{6,0},{7,1},{8,14},{9,15},{10,... | collective-permute-start | bytes 49160 | tf_op jit(solution)/shard_map/ppermute | solution.py:98
  49.3 2.7 %collective-permute-done.10 = f32[32,128]{1,0:T(8,128)S(1)} collective-permute-done((f32[32,128]{1,0:T(8,128)S(1)}, f32[32,128]{1,0:T(8,128)S(1)}, u32[]{:S(2)}, u32[]{:S(2)}) %collective-permute-start.10) | collective-permute-done | bytes 16416 | tf_op jit(solution)/shard_map/ppermute | solution.py:98
  53.2 3.7 %collective-permute-done.12 = f32[32,128]{1,0:T(8,128)S(1)} collective-permute-done((f32[32,128]{1,0:T(8,128)S(1)}, f32[32,128]{1,0:T(8,128)S(1)}, u32[]{:S(2)}, u32[]{:S(2)}) %collective-permute-start.12) | collective-permute-done | bytes 16416 | tf_op jit(solution)/shard_map/ppermute | solution.py:98
  56.9 4.9 %collective-permute-done.13 = f32[32,128]{1,0:T(8,128)S(1)} collective-permute-done((f32[32,128]{1,0:T(8,128)S(1)}, f32[32,128]{1,0:T(8,128)S(1)}, u32[]{:S(2)}, u32[]{:S(2)}) %collective-permute-start.13) | collective-permute-done | bytes 16416 | tf_op jit(solution)/shard_map/ppermute | solution.py:98
  61.9 3.7 %collective-permute-done.14 = f32[32,128]{1,0:T(8,128)S(1)} collective-permute-done((f32[32,128]{1,0:T(8,128)S(1)}, f32[32,128]{1,0:T(8,128)S(1)}, u32[]{:S(2)}, u32[]{:S(2)}) %collective-permute-start.14) | collective-permute-done | bytes 16416 | tf_op jit(solution)/shard_map/ppermute | solution.py:98
  66.0 4.6 %collective-permute-done.15 = f32[32,128]{1,0:T(8,128)S(1)} collective-permute-done((f32[32,128]{1,0:T(8,128)S(1)}, f32[32,128]{1,0:T(8,128)S(1)}, u32[]{:S(2)}, u32[]{:S(2)}) %collective-permute-start.15) | collective-permute-done | bytes 16416 | tf_op jit(solution)/shard_map/ppermute | solution.py:98
  71.4 6.7 %shard_map.41 = (f32[64,64]{1,0:T(8,128)}, f32[64,64]{1,0:T(8,128)}) custom-call(f32[64,64]{1,0:T(8,128)} %copy-done.1, f32[64,64]{1,0:T(8,128)} %bitcast.15), custom_call_target="tpu_custom_call" | custom-call | tf_op jit(solution)/shard_map/pallas_call | solution.py:69
  78.0 1.8 %fusion.49 = f32[64,4,8,128]{3,0,2,1:T(8,128)S(1)} fusion(f32[64,4,8,128]{3,0,2,1:T(8,128)S(1)} %fusion.10, f32[64,64]{1,0:T(8,128)} %get-tuple-element.4), kind=kOutput, calls=%fused_computation.79 | convolution fusion | flops 201330688 | bytes 2113536 | tf_op jit(solution)/shard_map/mk,kxyz->mxyz/dot_general | solution.py:119
  79.9 1.6 %copy.31 = f32[64,4,8,128]{3,2,1,0:T(8,128)} copy(f32[64,4,8,128]{3,0,2,1:T(8,128)S(1)} %fusion.49) | data formatting | bytes 2097152
  (49 shorter events, 8.4 us)
Async XLA Ops:
  0.6 1.7 %copy-start = (f32[64,4,8,128]{3,2,1,0:T(8,128)S(1)}, f32[64,4,8,128]{3,2,1,0:T(8,128)}, u32[]{:S(2)}) copy-start(f32[64,4,8,128]{3,2,1,0:T(8,128)} %param.2) | copy-start | bytes 3145732
  2.2 7.5 %copy-start.2 = (f32[4,8,128]{2,1,0:T(8,128)S(1)}, f32[4,8,128]{2,1,0:T(8,128)}, u32[]{:S(2)}) copy-start(f32[4,8,128]{2,1,0:T(8,128)} %param.3) | copy-start | bytes 49156
  2.2 12.0 %collective-permute-start.1 = (f32[64,2,8,128]{3,0,2,1:T(8,128)S(1)}, f32[64,2,8,128]{3,0,2,1:T(8,128)S(1)}, u32[]{:S(2)}, u32[]{:S(2)}) collective-permute-start(f32[64,2,8,128]{3,0,2,1:T(8,128)S(1)} %copy.35), channel_id=1, source_target_pairs={{0,8},{8,16},{16,24},{24,32},{32,40},{40,48},{48,56},{56,64},{64,7... | collective-permute-start | bytes 1572872 | tf_op jit(solution)/shard_map/ppermute | solution.py:14
  2.5 8.6 %collective-permute-start.3 = (f32[64,4,2,128]{3,0,2,1:T(8,128)S(1)}, f32[64,4,2,128]{3,0,2,1:T(8,128)S(1)}, u32[]{:S(2)}, u32[]{:S(2)}) collective-permute-start(f32[64,4,2,128]{3,0,2,1:T(8,128)S(1)} %copy.37), channel_id=1, source_target_pairs={{0,1},{1,2},{2,3},{3,4},{4,5},{5,6},{6,7},{7,0},{8,9},{9,10},{10,1... | collective-permute-start | bytes 786440 | tf_op jit(solution)/shard_map/ppermute | solution.py:14
  4.6 12.8 %collective-permute-start.2 = (f32[64,4,2,128]{3,0,2,1:T(8,128)S(1)}, f32[64,4,2,128]{3,0,2,1:T(8,128)S(1)}, u32[]{:S(2)}, u32[]{:S(2)}) collective-permute-start(f32[64,4,2,128]{3,0,2,1:T(8,128)S(1)} %copy.36), channel_id=1, source_target_pairs={{1,0},{2,1},{3,2},{4,3},{5,4},{6,5},{7,6},{0,7},{9,8},{10,9},{11,1... | collective-permute-start | bytes 786440 | tf_op jit(solution)/shard_map/ppermute | solution.py:15
  4.9 12.5 %collective-permute-start = (f32[64,2,8,128]{3,0,2,1:T(8,128)S(1)}, f32[64,2,8,128]{3,0,2,1:T(8,128)S(1)}, u32[]{:S(2)}, u32[]{:S(2)}) collective-permute-start(f32[64,2,8,128]{3,0,2,1:T(8,128)S(1)} %copy.34), channel_id=1, source_target_pairs={{8,0},{16,8},{24,16},{32,24},{40,32},{48,40},{56,48},{64,56},{72,6... | collective-permute-start | bytes 1572872 | tf_op jit(solution)/shard_map/ppermute | solution.py:15
  18.8 10.6 %collective-permute-start.7 = (f32[64,4,2,128]{3,0,2,1:T(8,128)S(1)}, f32[64,4,2,128]{3,0,2,1:T(8,128)S(1)}, u32[]{:S(2)}, u32[]{:S(2)}) collective-permute-start(f32[64,4,2,128]{3,0,2,1:T(8,128)S(1)} %get-tuple-element.19), channel_id=1, source_target_pairs={{0,1},{1,2},{2,3},{3,4},{4,5},{5,6},{6,7},{7,0},{8,9},{9,10},{10,1... | collective-permute-start | bytes 786440 | tf_op jit(solution)/shard_map/ppermute | solution.py:14
  20.7 8.6 %collective-permute-start.6 = (f32[64,4,2,128]{3,0,2,1:T(8,128)S(1)}, f32[64,4,2,128]{3,0,2,1:T(8,128)S(1)}, u32[]{:S(2)}, u32[]{:S(2)}) collective-permute-start(f32[64,4,2,128]{3,0,2,1:T(8,128)S(1)} %get-tuple-element.18), channel_id=1, source_target_pairs={{1,0},{2,1},{3,2},{4,3},{5,4},{6,5},{7,6},{0,7},{9,8},{10,9},{11,1... | collective-permute-start | bytes 786440 | tf_op jit(solution)/shard_map/ppermute | solution.py:15
  21.9 11.9 %collective-permute-start.5 = (f32[64,2,8,128]{3,0,2,1:T(8,128)S(1)}, f32[64,2,8,128]{3,0,2,1:T(8,128)S(1)}, u32[]{:S(2)}, u32[]{:S(2)}) collective-permute-start(f32[64,2,8,128]{3,0,2,1:T(8,128)S(1)} %get-tuple-element.15), channel_id=1, source_target_pairs={{0,8},{8,16},{16,24},{24,32},{32,40},{40,48},{48,56},{56,64},{64,7... | collective-permute-start | bytes 1572872 | tf_op jit(solution)/shard_map/ppermute | solution.py:14
  21.9 11.9 %collective-permute-start.4 = (f32[64,2,8,128]{3,0,2,1:T(8,128)S(1)}, f32[64,2,8,128]{3,0,2,1:T(8,128)S(1)}, u32[]{:S(2)}, u32[]{:S(2)}) collective-permute-start(f32[64,2,8,128]{3,0,2,1:T(8,128)S(1)} %get-tuple-element.14), channel_id=1, source_target_pairs={{8,0},{16,8},{24,16},{32,24},{40,32},{48,40},{56,48},{64,56},{72,6... | collective-permute-start | bytes 1572872 | tf_op jit(solution)/shard_map/ppermute | solution.py:15
  36.6 4.9 %collective-permute-start.8 = (f32[32,128]{1,0:T(8,128)S(1)}, f32[32,128]{1,0:T(8,128)S(1)}, u32[]{:S(2)}, u32[]{:S(2)}) collective-permute-start(f32[32,128]{1,0:T(8,128)S(1)} %reshape.11), channel_id=1, source_target_pairs={{0,1},{1,0},{2,3},{3,2},{4,5},{5,4},{6,7},{7,6},{8,9},{9,8},{10,11... | collective-permute-start | bytes 49160 | tf_op jit(solution)/shard_map/ppermute | solution.py:98
  41.5 4.6 %collective-permute-start.9 = (f32[32,128]{1,0:T(8,128)S(1)}, f32[32,128]{1,0:T(8,128)S(1)}, u32[]{:S(2)}, u32[]{:S(2)}) collective-permute-start(f32[32,128]{1,0:T(8,128)S(1)} %add.104), channel_id=1, source_target_pairs={{0,2},{1,3},{2,0},{3,1},{4,6},{5,7},{6,4},{7,5},{8,10},{9,11},{10,... | collective-permute-start | bytes 49160 | tf_op jit(solution)/shard_map/ppermute | solution.py:98
  46.1 5.8 %collective-permute-start.10 = (f32[32,128]{1,0:T(8,128)S(1)}, f32[32,128]{1,0:T(8,128)S(1)}, u32[]{:S(2)}, u32[]{:S(2)}) collective-permute-start(f32[32,128]{1,0:T(8,128)S(1)} %add.105), channel_id=1, source_target_pairs={{0,6},{1,7},{2,4},{3,5},{4,2},{5,3},{6,0},{7,1},{8,14},{9,15},{10,... | collective-permute-start | bytes 49160 | tf_op jit(solution)/shard_map/ppermute | solution.py:98
  52.0 1.2 %collective-permute-start.11 = (f32[32,128]{1,0:T(8,128)S(1)}, f32[32,128]{1,0:T(8,128)S(1)}, u32[]{:S(2)}, u32[]{:S(2)}) collective-permute-start(f32[32,128]{1,0:T(8,128)S(1)} %add.106), channel_id=1, source_target_pairs={{0,8},{8,0},{16,24},{24,16},{32,40},{40,32},{48,56},{56,48},{64,72... | collective-permute-start | bytes 49160 | tf_op jit(solution)/shard_map/ppermute | solution.py:98
  53.2 3.7 %collective-permute-start.12 = (f32[32,128]{1,0:T(8,128)S(1)}, f32[32,128]{1,0:T(8,128)S(1)}, u32[]{:S(2)}, u32[]{:S(2)}) collective-permute-start(f32[32,128]{1,0:T(8,128)S(1)} %add.107), channel_id=1, source_target_pairs={{0,16},{8,24},{16,0},{24,8},{32,48},{40,56},{48,32},{56,40},{64,80... | collective-permute-start | bytes 49160 | tf_op jit(solution)/shard_map/ppermute | solution.py:98
  56.9 4.9 %collective-permute-start.13 = (f32[32,128]{1,0:T(8,128)S(1)}, f32[32,128]{1,0:T(8,128)S(1)}, u32[]{:S(2)}, u32[]{:S(2)}) collective-permute-start(f32[32,128]{1,0:T(8,128)S(1)} %add.108), channel_id=1, source_target_pairs={{0,48},{8,56},{16,32},{24,40},{32,16},{40,24},{48,0},{56,8},{64,11... | collective-permute-start | bytes 49160 | tf_op jit(solution)/shard_map/ppermute | solution.py:98
  61.9 3.7 %collective-permute-start.14 = (f32[32,128]{1,0:T(8,128)S(1)}, f32[32,128]{1,0:T(8,128)S(1)}, u32[]{:S(2)}, u32[]{:S(2)}) collective-permute-start(f32[32,128]{1,0:T(8,128)S(1)} %add.109), channel_id=1, source_target_pairs={{0,64},{8,72},{16,80},{24,88},{32,96},{40,104},{48,112},{56,120},{... | collective-permute-start | bytes 49160 | tf_op jit(solution)/shard_map/ppermute | solution.py:98
  65.6 4.9 %collective-permute-start.15 = (f32[32,128]{1,0:T(8,128)S(1)}, f32[32,128]{1,0:T(8,128)S(1)}, u32[]{:S(2)}, u32[]{:S(2)}) collective-permute-start(f32[32,128]{1,0:T(8,128)S(1)} %add.110), channel_id=1, source_target_pairs={{0,192},{8,200},{16,208},{24,216},{32,224},{40,232},{48,240},{56,2... | collective-permute-start | bytes 49160 | tf_op jit(solution)/shard_map/ppermute | solution.py:98
  70.7 0.7 copy-start.1

commit v14 on v13

--- a/solution.py
+++ b/solution.py
@@ -36,15 +36,14 @@
     return -0.5 * total + pot[None] * core
 
 
-def factor_kernel(gram_ref, flipped_ref, factor_ref, inverse_ref):
+def factor_kernel(gram_ref, factor_ref, inverse_ref):
     order = gram_ref.shape[0]
     groups = order // 8
     sub = lax.broadcasted_iota(jnp.int32, (8, order), 0)
     lane = lax.broadcasted_iota(jnp.int32, (8, order), 1)
-    left = [
-        0.5 * (gram_ref[pl.ds(8 * i, 8), :] + flipped_ref[pl.ds(8 * i, 8), :])
-        for i in range(groups)
-    ]
+    gram = gram_ref[...]
+    sym = 0.5 * (gram + gram.T)
+    left = [sym[8 * i:8 * i + 8, :] for i in range(groups)]
     right = [jnp.where(lane == sub + 8 * i, 1.0, 0.0) for i in range(groups)]
     for k in range(order):
         home, place = divmod(k, 8)
@@ -69,9 +68,9 @@
     return pl.pallas_call(
         factor_kernel,
         out_shape=(shape, shape),
-        in_specs=[pl.BlockSpec(memory_space=pltpu.VMEM)] * 2,
+        in_specs=[pl.BlockSpec(memory_space=pltpu.VMEM)],
         out_specs=(pl.BlockSpec(memory_space=pltpu.VMEM),) * 2,
-    )(gram, gram.T)
+    )(gram)
 
 
 def ring_rounds(stride):

time: 81.9 us -> 81.9 us (level)
    unnamed x13 -> x11, local copies, waits for them, and re-layouts: 2.1 us -> 2.09 us
where the time goes in v14:
time: 81.9 us; the launch traced here: 81.4 us
  waiting for transfers between devices  34 us (42%)
  starting transfers between devices  24.1 us (29%)
  Pallas kernels  6.78 us (8%)
  other arithmetic  6.76 us (8%)
  local copies, waits for them, and re-layouts  6.11 us (7%)
  matrix products  2.77 us (3%)
  between operations  0.86 us (1%)
    ppermute x8, waiting for transfers between devices, butterfly_sum(): lax.ppermute(value, axis, [(i, partner(i)) for i in range(count)])  25.1 us
    ppermute x4, starting transfers between devices, faces(): lax.ppermute(head, axis, [((i + 1) % count, i) for i in range(count)])  11.2 us
    ppermute x4, waiting for transfers between devices, faces(): lax.ppermute(tail, axis, [(i, (i + 1) % count) for i in range(count)])  8.97 us
    ppermute x8, starting transfers between devices, butterfly_sum(): lax.ppermute(value, axis, [(i, partner(i)) for i in range(count)])  8.87 us
    pallas_call x1, Pallas kernels, factor_and_inverse(): pl.pallas_call(factor_kernel, out_shape=(shape, shape), in_specs=[pl.Bloc...  6.78 us
    ppermute x4, starting transfers between devices, faces(): lax.ppermute(tail, axis, [(i, (i + 1) % count) for i in range(count)])  4.08 us
    sub x2, other arithmetic, apply_ham(): local = local - 1.0 / 12.0 * (along_z[..., :size] + along_z[..., 4:])  3.92 us
    unnamed x11, local copies, waits for them, and re-layouts  2.09 us
  transfers between devices with their start and end apart: 16, of which 11 were waited for; matrix products, arithmetic and copies ran while one was open for 7% of the time, Pallas kernels for 0%

profile of v14, /device:TPU:32, one launch (start us, length us, event | category | flops | bytes accessed | tf_op | source)
XLA Modules:
  0.0 81.4 jit_solution(16217083274351003473)
XLA Ops:
  0.6 1.4 %fusion.60 = (f32[64,2,8,128]{3,2,1,0:T(8,128)S(1)}, f32[64,2,8,128]{3,2,1,0:T(8,128)S(1)}) fusion(f32[64,4,8,128]{3,2,1,0:T(8,128)} %param.2), kind=kLoop, calls=%fused_computation.98 | loop fusion | bytes 2097152 | tf_op jit(solution)/shard_map/slice | solution.py:12
  2.5 2.0 %collective-permute-start.3 = (f32[64,4,2,128]{3,0,2,1:T(8,128)S(1)}, f32[64,4,2,128]{3,0,2,1:T(8,128)S(1)}, u32[]{:S(2)}, u32[]{:S(2)}) collective-permute-start(f32[64,4,2,128]{3,0,2,1:T(8,128)S(1)} %copy.30), channel_id=1, source_target_pairs={{0,1},{1,2},{2,3},{3,4},{4,5},{5,6},{6,7},{7,0},{8,9},{9,10},{10,1... | collective-permute-start | bytes 786440 | tf_op jit(solution)/shard_map/ppermute | solution.py:14
  4.9 4.7 %collective-permute-start = (f32[64,2,8,128]{3,0,2,1:T(8,128)S(1)}, f32[64,2,8,128]{3,0,2,1:T(8,128)S(1)}, u32[]{:S(2)}, u32[]{:S(2)}) collective-permute-start(f32[64,2,8,128]{3,0,2,1:T(8,128)S(1)} %copy.27), channel_id=1, source_target_pairs={{8,0},{16,8},{24,16},{32,24},{40,32},{48,40},{56,48},{64,56},{72,6... | collective-permute-start | bytes 1572872 | tf_op jit(solution)/shard_map/ppermute | solution.py:15
  9.7 1.4 %collective-permute-done.3 = f32[64,4,2,128]{3,0,2,1:T(8,128)S(1)} collective-permute-done((f32[64,4,2,128]{3,0,2,1:T(8,128)S(1)}, f32[64,4,2,128]{3,0,2,1:T(8,128)S(1)}, u32[]{:S(2)}, u32[]{:S(2)}) %collective-permute-start.3) | collective-permute-done | bytes 262176 | tf_op jit(solution)/shard_map/ppermute | solution.py:14
  11.2 3.0 %collective-permute-done.1 = f32[64,2,8,128]{3,0,2,1:T(8,128)S(1)} collective-permute-done((f32[64,2,8,128]{3,0,2,1:T(8,128)S(1)}, f32[64,2,8,128]{3,0,2,1:T(8,128)S(1)}, u32[]{:S(2)}, u32[]{:S(2)}) %collective-permute-start.1) | collective-permute-done | bytes 524320 | tf_op jit(solution)/shard_map/ppermute | solution.py:14
  15.4 2.0 %fusion.28 = f32[64,4,8,128]{3,0,2,1:T(8,128)S(1)} fusion(f32[64,4,8,128]{3,0,2,1:T(8,128)S(1)} %get-tuple-element.20, f32[64,4,8,2]{3,0,2,1:T(8,128)S(1)} %get-tuple-element.19, f32[64,4,8,2]{3,0,2,1:T(8,128)S(1)} %get-tuple-element.18), kind=kLoop, calls=%fused_computation.45 | loop fusion | flops 2883584 | bytes 2129920 | tf_op jit(solution)/shard_map/sub | solution.py:30
  18.8 2.0 %collective-permute-start.7 = (f32[64,4,2,128]{3,0,2,1:T(8,128)S(1)}, f32[64,4,2,128]{3,0,2,1:T(8,128)S(1)}, u32[]{:S(2)}, u32[]{:S(2)}) collective-permute-start(f32[64,4,2,128]{3,0,2,1:T(8,128)S(1)} %get-tuple-element.17), channel_id=1, source_target_pairs={{0,1},{1,2},{2,3},{3,4},{4,5},{5,6},{6,7},{7,0},{8,9},{9,10},{10,1... | collective-permute-start | bytes 786440 | tf_op jit(solution)/shard_map/ppermute | solution.py:14
  21.9 5.1 %collective-permute-start.4 = (f32[64,2,8,128]{3,0,2,1:T(8,128)S(1)}, f32[64,2,8,128]{3,0,2,1:T(8,128)S(1)}, u32[]{:S(2)}, u32[]{:S(2)}) collective-permute-start(f32[64,2,8,128]{3,0,2,1:T(8,128)S(1)} %get-tuple-element.12), channel_id=1, source_target_pairs={{8,0},{16,8},{24,16},{32,24},{40,32},{48,40},{56,48},{64,56},{72,6... | collective-permute-start | bytes 1572872 | tf_op jit(solution)/shard_map/ppermute | solution.py:15
  27.4 2.0 %fusion.22 = f32[64,4,8,128]{3,0,2,1:T(8,128)S(1)} fusion(f32[64,4,8,128]{3,0,2,1:T(8,128)S(1)} %get-tuple-element.10, f32[64,4,8,2]{3,0,2,1:T(8,128)S(1)} %get-tuple-element.15, f32[64,4,8,2]{3,0,2,1:T(8,128)S(1)} %get-tuple-element.14, f32[64,4,8,128]{3,0,2,1:T(8,128)S(1)} %get-tuple-element.11), kind=kLoop, calls=%fused_computation.39 | loop fusion | flops 2883584 | bytes 3178496 | tf_op jit(solution)/shard_map/sub | solution.py:30
  29.4 4.5 %collective-permute-done.5 = f32[64,2,8,128]{3,0,2,1:T(8,128)S(1)} collective-permute-done((f32[64,2,8,128]{3,0,2,1:T(8,128)S(1)}, f32[64,2,8,128]{3,0,2,1:T(8,128)S(1)}, u32[]{:S(2)}, u32[]{:S(2)}) %collective-permute-start.5) | collective-permute-done | bytes 524320 | tf_op jit(solution)/shard_map/ppermute | solution.py:14
  33.9 1.7 %fusion.10 = f32[64,4,8,128]{3,0,2,1:T(8,128)S(1)} fusion(f32[64,4,2,128]{3,0,2,1:T(8,128)S(1)} %collective-permute-done.7, f32[64,4,8,128]{3,0,2,1:T(8,128)S(1)} %get-tuple-element.10, f32[64,4,2,128]{3,0,2,1:T(8,128)S(1)} %collective-permute-done.6, f32[64,4,8,128]{3,0,2,1:T(8,128)S(1)} %fusion.22, f32[64,2,8,128]{3,0,2,1:T(8,128)S(1)} %collective-permute-done.5, ...), kind=kLoop, calls=%fused_computation.27 | loop fusion | flops 7077888 | bytes 6832128 | tf_op jit(solution)/shard_map/sub | solution.py:105
  36.6 3.2 %collective-permute-start.8 = (f32[32,128]{1,0:T(8,128)S(1)}, f32[32,128]{1,0:T(8,128)S(1)}, u32[]{:S(2)}, u32[]{:S(2)}) collective-permute-start(f32[32,128]{1,0:T(8,128)S(1)} %reshape.11), channel_id=1, source_target_pairs={{0,1},{1,0},{2,3},{3,2},{4,5},{5,4},{6,7},{7,6},{8,9},{9,8},{10,11... | collective-permute-start | bytes 49160 | tf_op jit(solution)/shard_map/ppermute | solution.py:97
  39.8 1.7 %collective-permute-done.8 = f32[32,128]{1,0:T(8,128)S(1)} collective-permute-done((f32[32,128]{1,0:T(8,128)S(1)}, f32[32,128]{1,0:T(8,128)S(1)}, u32[]{:S(2)}, u32[]{:S(2)}) %collective-permute-start.8) | collective-permute-done | bytes 16416 | tf_op jit(solution)/shard_map/ppermute | solution.py:97
  41.5 2.2 %collective-permute-start.9 = (f32[32,128]{1,0:T(8,128)S(1)}, f32[32,128]{1,0:T(8,128)S(1)}, u32[]{:S(2)}, u32[]{:S(2)}) collective-permute-start(f32[32,128]{1,0:T(8,128)S(1)} %add.104), channel_id=1, source_target_pairs={{0,2},{1,3},{2,0},{3,1},{4,6},{5,7},{6,4},{7,5},{8,10},{9,11},{10,... | collective-permute-start | bytes 49160 | tf_op jit(solution)/shard_map/ppermute | solution.py:97
  43.7 2.5 %collective-permute-done.9 = f32[32,128]{1,0:T(8,128)S(1)} collective-permute-done((f32[32,128]{1,0:T(8,128)S(1)}, f32[32,128]{1,0:T(8,128)S(1)}, u32[]{:S(2)}, u32[]{:S(2)}) %collective-permute-start.9) | collective-permute-done | bytes 16416 | tf_op jit(solution)/shard_map/ppermute | solution.py:97
  46.1 3.2 %collective-permute-start.10 = (f32[32,128]{1,0:T(8,128)S(1)}, f32[32,128]{1,0:T(8,128)S(1)}, u32[]{:S(2)}, u32[]{:S(2)}) collective-permute-start(f32[32,128]{1,0:T(8,128)S(1)} %add.105), channel_id=1, source_target_pairs={{0,6},{1,7},{2,4},{3,5},{4,2},{5,3},{6,0},{7,1},{8,14},{9,15},{10,... | collective-permute-start | bytes 49160 | tf_op jit(solution)/shard_map/ppermute | solution.py:97
  49.3 2.7 %collective-permute-done.10 = f32[32,128]{1,0:T(8,128)S(1)} collective-permute-done((f32[32,128]{1,0:T(8,128)S(1)}, f32[32,128]{1,0:T(8,128)S(1)}, u32[]{:S(2)}, u32[]{:S(2)}) %collective-permute-start.10) | collective-permute-done | bytes 16416 | tf_op jit(solution)/shard_map/ppermute | solution.py:97
  53.2 3.7 %collective-permute-done.12 = f32[32,128]{1,0:T(8,128)S(1)} collective-permute-done((f32[32,128]{1,0:T(8,128)S(1)}, f32[32,128]{1,0:T(8,128)S(1)}, u32[]{:S(2)}, u32[]{:S(2)}) %collective-permute-start.12) | collective-permute-done | bytes 16416 | tf_op jit(solution)/shard_map/ppermute | solution.py:97
  56.9 4.9 %collective-permute-done.13 = f32[32,128]{1,0:T(8,128)S(1)} collective-permute-done((f32[32,128]{1,0:T(8,128)S(1)}, f32[32,128]{1,0:T(8,128)S(1)}, u32[]{:S(2)}, u32[]{:S(2)}) %collective-permute-start.13) | collective-permute-done | bytes 16416 | tf_op jit(solution)/shard_map/ppermute | solution.py:97
  61.9 3.7 %collective-permute-done.14 = f32[32,128]{1,0:T(8,128)S(1)} collective-permute-done((f32[32,128]{1,0:T(8,128)S(1)}, f32[32,128]{1,0:T(8,128)S(1)}, u32[]{:S(2)}, u32[]{:S(2)}) %collective-permute-start.14) | collective-permute-done | bytes 16416 | tf_op jit(solution)/shard_map/ppermute | solution.py:97
  66.0 4.6 %collective-permute-done.15 = f32[32,128]{1,0:T(8,128)S(1)} collective-permute-done((f32[32,128]{1,0:T(8,128)S(1)}, f32[32,128]{1,0:T(8,128)S(1)}, u32[]{:S(2)}, u32[]{:S(2)}) %collective-permute-start.15) | collective-permute-done | bytes 16416 | tf_op jit(solution)/shard_map/ppermute | solution.py:97
  71.3 6.8 %shard_map.41 = (f32[64,64]{1,0:T(8,128)}, f32[64,64]{1,0:T(8,128)}) custom-call(f32[64,64]{1,0:T(8,128)} %reshape.12.gram_ref), custom_call_target="tpu_custom_call" | custom-call | tf_op jit(solution)/shard_map/pallas_call | solution.py:68
  78.1 1.8 %fusion.49 = f32[64,4,8,128]{3,0,2,1:T(8,128)S(1)} fusion(f32[64,4,8,128]{3,0,2,1:T(8,128)S(1)} %fusion.10, f32[64,64]{1,0:T(8,128)} %get-tuple-element.4), kind=kOutput, calls=%fused_computation.79 | convolution fusion | flops 201330688 | bytes 2113536 | tf_op jit(solution)/shard_map/mk,kxyz->mxyz/dot_general | solution.py:118
  79.9 1.6 %copy.24 = f32[64,4,8,128]{3,2,1,0:T(8,128)} copy(f32[64,4,8,128]{3,0,2,1:T(8,128)S(1)} %fusion.49) | data formatting | bytes 2097152
  (46 shorter events, 8.3 us)
Async XLA Ops:
  0.6 1.7 %copy-start = (f32[64,4,8,128]{3,2,1,0:T(8,128)S(1)}, f32[64,4,8,128]{3,2,1,0:T(8,128)}, u32[]{:S(2)}) copy-start(f32[64,4,8,128]{3,2,1,0:T(8,128)} %param.2) | copy-start | bytes 3145732
  2.2 7.5 %copy-start.1 = (f32[4,8,128]{2,1,0:T(8,128)S(1)}, f32[4,8,128]{2,1,0:T(8,128)}, u32[]{:S(2)}) copy-start(f32[4,8,128]{2,1,0:T(8,128)} %param.3) | copy-start | bytes 49156
  2.2 12.0 %collective-permute-start.1 = (f32[64,2,8,128]{3,0,2,1:T(8,128)S(1)}, f32[64,2,8,128]{3,0,2,1:T(8,128)S(1)}, u32[]{:S(2)}, u32[]{:S(2)}) collective-permute-start(f32[64,2,8,128]{3,0,2,1:T(8,128)S(1)} %copy.28), channel_id=1, source_target_pairs={{0,8},{8,16},{16,24},{24,32},{32,40},{40,48},{48,56},{56,64},{64,7... | collective-permute-start | bytes 1572872 | tf_op jit(solution)/shard_map/ppermute | solution.py:14
  2.5 8.6 %collective-permute-start.3 = (f32[64,4,2,128]{3,0,2,1:T(8,128)S(1)}, f32[64,4,2,128]{3,0,2,1:T(8,128)S(1)}, u32[]{:S(2)}, u32[]{:S(2)}) collective-permute-start(f32[64,4,2,128]{3,0,2,1:T(8,128)S(1)} %copy.30), channel_id=1, source_target_pairs={{0,1},{1,2},{2,3},{3,4},{4,5},{5,6},{6,7},{7,0},{8,9},{9,10},{10,1... | collective-permute-start | bytes 786440 | tf_op jit(solution)/shard_map/ppermute | solution.py:14
  4.6 12.8 %collective-permute-start.2 = (f32[64,4,2,128]{3,0,2,1:T(8,128)S(1)}, f32[64,4,2,128]{3,0,2,1:T(8,128)S(1)}, u32[]{:S(2)}, u32[]{:S(2)}) collective-permute-start(f32[64,4,2,128]{3,0,2,1:T(8,128)S(1)} %copy.29), channel_id=1, source_target_pairs={{1,0},{2,1},{3,2},{4,3},{5,4},{6,5},{7,6},{0,7},{9,8},{10,9},{11,1... | collective-permute-start | bytes 786440 | tf_op jit(solution)/shard_map/ppermute | solution.py:15
  4.9 12.5 %collective-permute-start = (f32[64,2,8,128]{3,0,2,1:T(8,128)S(1)}, f32[64,2,8,128]{3,0,2,1:T(8,128)S(1)}, u32[]{:S(2)}, u32[]{:S(2)}) collective-permute-start(f32[64,2,8,128]{3,0,2,1:T(8,128)S(1)} %copy.27), channel_id=1, source_target_pairs={{8,0},{16,8},{24,16},{32,24},{40,32},{48,40},{56,48},{64,56},{72,6... | collective-permute-start | bytes 1572872 | tf_op jit(solution)/shard_map/ppermute | solution.py:15
  18.8 10.6 %collective-permute-start.7 = (f32[64,4,2,128]{3,0,2,1:T(8,128)S(1)}, f32[64,4,2,128]{3,0,2,1:T(8,128)S(1)}, u32[]{:S(2)}, u32[]{:S(2)}) collective-permute-start(f32[64,4,2,128]{3,0,2,1:T(8,128)S(1)} %get-tuple-element.17), channel_id=1, source_target_pairs={{0,1},{1,2},{2,3},{3,4},{4,5},{5,6},{6,7},{7,0},{8,9},{9,10},{10,1... | collective-permute-start | bytes 786440 | tf_op jit(solution)/shard_map/ppermute | solution.py:14
  20.7 8.6 %collective-permute-start.6 = (f32[64,4,2,128]{3,0,2,1:T(8,128)S(1)}, f32[64,4,2,128]{3,0,2,1:T(8,128)S(1)}, u32[]{:S(2)}, u32[]{:S(2)}) collective-permute-start(f32[64,4,2,128]{3,0,2,1:T(8,128)S(1)} %get-tuple-element.16), channel_id=1, source_target_pairs={{1,0},{2,1},{3,2},{4,3},{5,4},{6,5},{7,6},{0,7},{9,8},{10,9},{11,1... | collective-permute-start | bytes 786440 | tf_op jit(solution)/shard_map/ppermute | solution.py:15
  21.9 11.9 %collective-permute-start.5 = (f32[64,2,8,128]{3,0,2,1:T(8,128)S(1)}, f32[64,2,8,128]{3,0,2,1:T(8,128)S(1)}, u32[]{:S(2)}, u32[]{:S(2)}) collective-permute-start(f32[64,2,8,128]{3,0,2,1:T(8,128)S(1)} %get-tuple-element.13), channel_id=1, source_target_pairs={{0,8},{8,16},{16,24},{24,32},{32,40},{40,48},{48,56},{56,64},{64,7... | collective-permute-start | bytes 1572872 | tf_op jit(solution)/shard_map/ppermute | solution.py:14
  21.9 11.9 %collective-permute-start.4 = (f32[64,2,8,128]{3,0,2,1:T(8,128)S(1)}, f32[64,2,8,128]{3,0,2,1:T(8,128)S(1)}, u32[]{:S(2)}, u32[]{:S(2)}) collective-permute-start(f32[64,2,8,128]{3,0,2,1:T(8,128)S(1)} %get-tuple-element.12), channel_id=1, source_target_pairs={{8,0},{16,8},{24,16},{32,24},{40,32},{48,40},{56,48},{64,56},{72,6... | collective-permute-start | bytes 1572872 | tf_op jit(solution)/shard_map/ppermute | solution.py:15
  36.6 4.9 %collective-permute-start.8 = (f32[32,128]{1,0:T(8,128)S(1)}, f32[32,128]{1,0:T(8,128)S(1)}, u32[]{:S(2)}, u32[]{:S(2)}) collective-permute-start(f32[32,128]{1,0:T(8,128)S(1)} %reshape.11), channel_id=1, source_target_pairs={{0,1},{1,0},{2,3},{3,2},{4,5},{5,4},{6,7},{7,6},{8,9},{9,8},{10,11... | collective-permute-start | bytes 49160 | tf_op jit(solution)/shard_map/ppermute | solution.py:97
  41.5 4.6 %collective-permute-start.9 = (f32[32,128]{1,0:T(8,128)S(1)}, f32[32,128]{1,0:T(8,128)S(1)}, u32[]{:S(2)}, u32[]{:S(2)}) collective-permute-start(f32[32,128]{1,0:T(8,128)S(1)} %add.104), channel_id=1, source_target_pairs={{0,2},{1,3},{2,0},{3,1},{4,6},{5,7},{6,4},{7,5},{8,10},{9,11},{10,... | collective-permute-start | bytes 49160 | tf_op jit(solution)/shard_map/ppermute | solution.py:97
  46.1 5.8 %collective-permute-start.10 = (f32[32,128]{1,0:T(8,128)S(1)}, f32[32,128]{1,0:T(8,128)S(1)}, u32[]{:S(2)}, u32[]{:S(2)}) collective-permute-start(f32[32,128]{1,0:T(8,128)S(1)} %add.105), channel_id=1, source_target_pairs={{0,6},{1,7},{2,4},{3,5},{4,2},{5,3},{6,0},{7,1},{8,14},{9,15},{10,... | collective-permute-start | bytes 49160 | tf_op jit(solution)/shard_map/ppermute | solution.py:97
  52.0 1.2 %collective-permute-start.11 = (f32[32,128]{1,0:T(8,128)S(1)}, f32[32,128]{1,0:T(8,128)S(1)}, u32[]{:S(2)}, u32[]{:S(2)}) collective-permute-start(f32[32,128]{1,0:T(8,128)S(1)} %add.106), channel_id=1, source_target_pairs={{0,8},{8,0},{16,24},{24,16},{32,40},{40,32},{48,56},{56,48},{64,72... | collective-permute-start | bytes 49160 | tf_op jit(solution)/shard_map/ppermute | solution.py:97
  53.2 3.7 %collective-permute-start.12 = (f32[32,128]{1,0:T(8,128)S(1)}, f32[32,128]{1,0:T(8,128)S(1)}, u32[]{:S(2)}, u32[]{:S(2)}) collective-permute-start(f32[32,128]{1,0:T(8,128)S(1)} %add.107), channel_id=1, source_target_pairs={{0,16},{8,24},{16,0},{24,8},{32,48},{40,56},{48,32},{56,40},{64,80... | collective-permute-start | bytes 49160 | tf_op jit(solution)/shard_map/ppermute | solution.py:97
  56.9 4.9 %collective-permute-start.13 = (f32[32,128]{1,0:T(8,128)S(1)}, f32[32,128]{1,0:T(8,128)S(1)}, u32[]{:S(2)}, u32[]{:S(2)}) collective-permute-start(f32[32,128]{1,0:T(8,128)S(1)} %add.108), channel_id=1, source_target_pairs={{0,48},{8,56},{16,32},{24,40},{32,16},{40,24},{48,0},{56,8},{64,11... | collective-permute-start | bytes 49160 | tf_op jit(solution)/shard_map/ppermute | solution.py:97
  61.9 3.7 %collective-permute-start.14 = (f32[32,128]{1,0:T(8,128)S(1)}, f32[32,128]{1,0:T(8,128)S(1)}, u32[]{:S(2)}, u32[]{:S(2)}) collective-permute-start(f32[32,128]{1,0:T(8,128)S(1)} %add.109), channel_id=1, source_target_pairs={{0,64},{8,72},{16,80},{24,88},{32,96},{40,104},{48,112},{56,120},{... | collective-permute-start | bytes 49160 | tf_op jit(solution)/shard_map/ppermute | solution.py:97
  65.6 4.9 %collective-permute-start.15 = (f32[32,128]{1,0:T(8,128)S(1)}, f32[32,128]{1,0:T(8,128)S(1)}, u32[]{:S(2)}, u32[]{:S(2)}) collective-permute-start(f32[32,128]{1,0:T(8,128)S(1)} %add.110), channel_id=1, source_target_pairs={{0,192},{8,200},{16,208},{24,216},{32,224},{40,232},{48,240},{56,2... | collective-permute-start | bytes 49160 | tf_op jit(solution)/shard_map/ppermute | solution.py:97

commit v15 on v14

--- a/solution.py
+++ b/solution.py
@@ -37,11 +37,16 @@
 
 
 def factor_kernel(gram_ref, factor_ref, inverse_ref):
-    order = gram_ref.shape[0]
+    half = gram_ref.shape[1] // 2
+    order = gram_ref.shape[0] * gram_ref.shape[1] // half
     groups = order // 8
     sub = lax.broadcasted_iota(jnp.int32, (8, order), 0)
     lane = lax.broadcasted_iota(jnp.int32, (8, order), 1)
-    gram = gram_ref[...]
+    packed = gram_ref[...]
+    gram = jnp.concatenate(
+        [piece for r in range(packed.shape[0]) for piece in (packed[r:r + 1, :half], packed[r:r + 1, half:])],
+        axis=0,
+    )
     sym = 0.5 * (gram + gram.T)
     left = [sym[8 * i:8 * i + 8, :] for i in range(groups)]
     right = [jnp.where(lane == sub + 8 * i, 1.0, 0.0) for i in range(groups)]
@@ -63,14 +68,14 @@
         inverse_ref[pl.ds(8 * i, 8), :] = right[i] * scale
 
 
-def factor_and_inverse(gram):
-    shape = jax.ShapeDtypeStruct(gram.shape, jnp.float32)
+def factor_and_inverse(packed, order):
+    shape = jax.ShapeDtypeStruct((order, order), jnp.float32)
     return pl.pallas_call(
         factor_kernel,
         out_shape=(shape, shape),
         in_specs=[pl.BlockSpec(memory_space=pltpu.VMEM)],
         out_specs=(pl.BlockSpec(memory_space=pltpu.VMEM),) * 2,
-    )(gram)
+    )(packed)
 
 
 def ring_rounds(stride):
@@ -113,8 +118,8 @@
         / cells
     )
     packed = local_gram.reshape(-1, 128)
-    gram = butterfly_sum(butterfly_sum(packed, "gy"), "gx").reshape(local_gram.shape)
-    factor, lower_inverse = factor_and_inverse(gram)
+    gram = butterfly_sum(butterfly_sum(packed, "gy"), "gx")
+    factor, lower_inverse = factor_and_inverse(gram, local_gram.shape[0])
     basis = jnp.einsum(
         "mk,kxyz->mxyz", lower_inverse * jnp.sqrt(jnp.float32(cells)), filtered,
         precision=lax.Precision.HIGHEST, preferred_element_type=jnp.float32,

time: 81.9 us -> 81.8 us (level)
  no operation moved by 1% of the time
where the time goes in v15:
time: 81.8 us; the launch traced here: 81.4 us
  waiting for transfers between devices  34 us (42%)
  starting transfers between devices  24.1 us (29%)
  other arithmetic  7.36 us (9%)
  Pallas kernels  6.82 us (8%)
  local copies, waits for them, and re-layouts  5.42 us (7%)
  matrix products  2.77 us (3%)
  between operations  0.85 us (1%)
    ppermute x8, waiting for transfers between devices, butterfly_sum(): lax.ppermute(value, axis, [(i, partner(i)) for i in range(count)])  25.1 us
    ppermute x4, starting transfers between devices, faces(): lax.ppermute(head, axis, [((i + 1) % count, i) for i in range(count)])  11.2 us
    ppermute x4, waiting for transfers between devices, faces(): lax.ppermute(tail, axis, [(i, (i + 1) % count) for i in range(count)])  8.97 us
    ppermute x8, starting transfers between devices, butterfly_sum(): lax.ppermute(value, axis, [(i, partner(i)) for i in range(count)])  8.87 us
    pallas_call x1, Pallas kernels, factor_and_inverse(): pl.pallas_call(factor_kernel, out_shape=(shape, shape), in_specs=[pl.Bloc...  6.82 us
    ppermute x4, starting transfers between devices, faces(): lax.ppermute(tail, axis, [(i, (i + 1) % count) for i in range(count)])  4.08 us
    sub x2, other arithmetic, apply_ham(): local = local - 1.0 / 12.0 * (along_z[..., :size] + along_z[..., 4:])  3.92 us
    unnamed x11, local copies, waits for them, and re-layouts  2.09 us
  transfers between devices with their start and end apart: 16, of which 11 were waited for; matrix products, arithmetic and copies ran while one was open for 7% of the time, Pallas kernels for 0%

profile of v15, /device:TPU:32, one launch (start us, length us, event | category | flops | bytes accessed | tf_op | source)
XLA Modules:
  0.0 81.4 jit_solution(9160591611408362300)
XLA Ops:
  0.6 1.4 %fusion.60 = (f32[64,2,8,128]{3,2,1,0:T(8,128)S(1)}, f32[64,2,8,128]{3,2,1,0:T(8,128)S(1)}) fusion(f32[64,4,8,128]{3,2,1,0:T(8,128)} %param.2), kind=kLoop, calls=%fused_computation.98 | loop fusion | bytes 2097152 | tf_op jit(solution)/shard_map/slice | solution.py:12
  2.5 2.0 %collective-permute-start.3 = (f32[64,4,2,128]{3,0,2,1:T(8,128)S(1)}, f32[64,4,2,128]{3,0,2,1:T(8,128)S(1)}, u32[]{:S(2)}, u32[]{:S(2)}) collective-permute-start(f32[64,4,2,128]{3,0,2,1:T(8,128)S(1)} %copy.30), channel_id=1, source_target_pairs={{0,1},{1,2},{2,3},{3,4},{4,5},{5,6},{6,7},{7,0},{8,9},{9,10},{10,1... | collective-permute-start | bytes 786440 | tf_op jit(solution)/shard_map/ppermute | solution.py:14
  4.9 4.7 %collective-permute-start = (f32[64,2,8,128]{3,0,2,1:T(8,128)S(1)}, f32[64,2,8,128]{3,0,2,1:T(8,128)S(1)}, u32[]{:S(2)}, u32[]{:S(2)}) collective-permute-start(f32[64,2,8,128]{3,0,2,1:T(8,128)S(1)} %copy.27), channel_id=1, source_target_pairs={{8,0},{16,8},{24,16},{32,24},{40,32},{48,40},{56,48},{64,56},{72,6... | collective-permute-start | bytes 1572872 | tf_op jit(solution)/shard_map/ppermute | solution.py:15
  9.7 1.4 %collective-permute-done.3 = f32[64,4,2,128]{3,0,2,1:T(8,128)S(1)} collective-permute-done((f32[64,4,2,128]{3,0,2,1:T(8,128)S(1)}, f32[64,4,2,128]{3,0,2,1:T(8,128)S(1)}, u32[]{:S(2)}, u32[]{:S(2)}) %collective-permute-start.3) | collective-permute-done | bytes 262176 | tf_op jit(solution)/shard_map/ppermute | solution.py:14
  11.2 3.0 %collective-permute-done.1 = f32[64,2,8,128]{3,0,2,1:T(8,128)S(1)} collective-permute-done((f32[64,2,8,128]{3,0,2,1:T(8,128)S(1)}, f32[64,2,8,128]{3,0,2,1:T(8,128)S(1)}, u32[]{:S(2)}, u32[]{:S(2)}) %collective-permute-start.1) | collective-permute-done | bytes 524320 | tf_op jit(solution)/shard_map/ppermute | solution.py:14
  15.4 2.0 %fusion.28 = f32[64,4,8,128]{3,0,2,1:T(8,128)S(1)} fusion(f32[64,4,8,128]{3,0,2,1:T(8,128)S(1)} %get-tuple-element.20, f32[64,4,8,2]{3,0,2,1:T(8,128)S(1)} %get-tuple-element.19, f32[64,4,8,2]{3,0,2,1:T(8,128)S(1)} %get-tuple-element.18), kind=kLoop, calls=%fused_computation.45 | loop fusion | flops 2883584 | bytes 2129920 | tf_op jit(solution)/shard_map/sub | solution.py:30
  18.8 2.0 %collective-permute-start.7 = (f32[64,4,2,128]{3,0,2,1:T(8,128)S(1)}, f32[64,4,2,128]{3,0,2,1:T(8,128)S(1)}, u32[]{:S(2)}, u32[]{:S(2)}) collective-permute-start(f32[64,4,2,128]{3,0,2,1:T(8,128)S(1)} %get-tuple-element.17), channel_id=1, source_target_pairs={{0,1},{1,2},{2,3},{3,4},{4,5},{5,6},{6,7},{7,0},{8,9},{9,10},{10,1... | collective-permute-start | bytes 786440 | tf_op jit(solution)/shard_map/ppermute | solution.py:14
  21.9 5.1 %collective-permute-start.4 = (f32[64,2,8,128]{3,0,2,1:T(8,128)S(1)}, f32[64,2,8,128]{3,0,2,1:T(8,128)S(1)}, u32[]{:S(2)}, u32[]{:S(2)}) collective-permute-start(f32[64,2,8,128]{3,0,2,1:T(8,128)S(1)} %get-tuple-element.12), channel_id=1, source_target_pairs={{8,0},{16,8},{24,16},{32,24},{40,32},{48,40},{56,48},{64,56},{72,6... | collective-permute-start | bytes 1572872 | tf_op jit(solution)/shard_map/ppermute | solution.py:15
  27.4 2.0 %fusion.22 = f32[64,4,8,128]{3,0,2,1:T(8,128)S(1)} fusion(f32[64,4,8,128]{3,0,2,1:T(8,128)S(1)} %get-tuple-element.10, f32[64,4,8,2]{3,0,2,1:T(8,128)S(1)} %get-tuple-element.15, f32[64,4,8,2]{3,0,2,1:T(8,128)S(1)} %get-tuple-element.14, f32[64,4,8,128]{3,0,2,1:T(8,128)S(1)} %get-tuple-element.11), kind=kLoop, calls=%fused_computation.39 | loop fusion | flops 2883584 | bytes 3178496 | tf_op jit(solution)/shard_map/sub | solution.py:30
  29.4 4.5 %collective-permute-done.5 = f32[64,2,8,128]{3,0,2,1:T(8,128)S(1)} collective-permute-done((f32[64,2,8,128]{3,0,2,1:T(8,128)S(1)}, f32[64,2,8,128]{3,0,2,1:T(8,128)S(1)}, u32[]{:S(2)}, u32[]{:S(2)}) %collective-permute-start.5) | collective-permute-done | bytes 524320 | tf_op jit(solution)/shard_map/ppermute | solution.py:14
  33.9 1.7 %fusion.10 = f32[64,4,8,128]{3,0,2,1:T(8,128)S(1)} fusion(f32[64,4,2,128]{3,0,2,1:T(8,128)S(1)} %collective-permute-done.7, f32[64,4,8,128]{3,0,2,1:T(8,128)S(1)} %get-tuple-element.10, f32[64,4,2,128]{3,0,2,1:T(8,128)S(1)} %collective-permute-done.6, f32[64,4,8,128]{3,0,2,1:T(8,128)S(1)} %fusion.22, f32[64,2,8,128]{3,0,2,1:T(8,128)S(1)} %collective-permute-done.5, ...), kind=kLoop, calls=%fused_computation.27 | loop fusion | flops 7077888 | bytes 6832128 | tf_op jit(solution)/shard_map/sub | solution.py:110
  36.6 3.2 %collective-permute-start.8 = (f32[32,128]{1,0:T(8,128)S(1)}, f32[32,128]{1,0:T(8,128)S(1)}, u32[]{:S(2)}, u32[]{:S(2)}) collective-permute-start(f32[32,128]{1,0:T(8,128)S(1)} %reshape.8), channel_id=1, source_target_pairs={{0,1},{1,0},{2,3},{3,2},{4,5},{5,4},{6,7},{7,6},{8,9},{9,8},{10,11... | collective-permute-start | bytes 49160 | tf_op jit(solution)/shard_map/ppermute | solution.py:102
  39.8 1.7 %collective-permute-done.8 = f32[32,128]{1,0:T(8,128)S(1)} collective-permute-done((f32[32,128]{1,0:T(8,128)S(1)}, f32[32,128]{1,0:T(8,128)S(1)}, u32[]{:S(2)}, u32[]{:S(2)}) %collective-permute-start.8) | collective-permute-done | bytes 16416 | tf_op jit(solution)/shard_map/ppermute | solution.py:102
  41.5 2.2 %collective-permute-start.9 = (f32[32,128]{1,0:T(8,128)S(1)}, f32[32,128]{1,0:T(8,128)S(1)}, u32[]{:S(2)}, u32[]{:S(2)}) collective-permute-start(f32[32,128]{1,0:T(8,128)S(1)} %add.104), channel_id=1, source_target_pairs={{0,2},{1,3},{2,0},{3,1},{4,6},{5,7},{6,4},{7,5},{8,10},{9,11},{10,... | collective-permute-start | bytes 49160 | tf_op jit(solution)/shard_map/ppermute | solution.py:102
  43.7 2.5 %collective-permute-done.9 = f32[32,128]{1,0:T(8,128)S(1)} collective-permute-done((f32[32,128]{1,0:T(8,128)S(1)}, f32[32,128]{1,0:T(8,128)S(1)}, u32[]{:S(2)}, u32[]{:S(2)}) %collective-permute-start.9) | collective-permute-done | bytes 16416 | tf_op jit(solution)/shard_map/ppermute | solution.py:102
  46.1 3.2 %collective-permute-start.10 = (f32[32,128]{1,0:T(8,128)S(1)}, f32[32,128]{1,0:T(8,128)S(1)}, u32[]{:S(2)}, u32[]{:S(2)}) collective-permute-start(f32[32,128]{1,0:T(8,128)S(1)} %add.105), channel_id=1, source_target_pairs={{0,6},{1,7},{2,4},{3,5},{4,2},{5,3},{6,0},{7,1},{8,14},{9,15},{10,... | collective-permute-start | bytes 49160 | tf_op jit(solution)/shard_map/ppermute | solution.py:102
  49.3 2.7 %collective-permute-done.10 = f32[32,128]{1,0:T(8,128)S(1)} collective-permute-done((f32[32,128]{1,0:T(8,128)S(1)}, f32[32,128]{1,0:T(8,128)S(1)}, u32[]{:S(2)}, u32[]{:S(2)}) %collective-permute-start.10) | collective-permute-done | bytes 16416 | tf_op jit(solution)/shard_map/ppermute | solution.py:102
  53.2 3.7 %collective-permute-done.12 = f32[32,128]{1,0:T(8,128)S(1)} collective-permute-done((f32[32,128]{1,0:T(8,128)S(1)}, f32[32,128]{1,0:T(8,128)S(1)}, u32[]{:S(2)}, u32[]{:S(2)}) %collective-permute-start.12) | collective-permute-done | bytes 16416 | tf_op jit(solution)/shard_map/ppermute | solution.py:102
  56.9 4.9 %collective-permute-done.13 = f32[32,128]{1,0:T(8,128)S(1)} collective-permute-done((f32[32,128]{1,0:T(8,128)S(1)}, f32[32,128]{1,0:T(8,128)S(1)}, u32[]{:S(2)}, u32[]{:S(2)}) %collective-permute-start.13) | collective-permute-done | bytes 16416 | tf_op jit(solution)/shard_map/ppermute | solution.py:102
  61.9 3.7 %collective-permute-done.14 = f32[32,128]{1,0:T(8,128)S(1)} collective-permute-done((f32[32,128]{1,0:T(8,128)S(1)}, f32[32,128]{1,0:T(8,128)S(1)}, u32[]{:S(2)}, u32[]{:S(2)}) %collective-permute-start.14) | collective-permute-done | bytes 16416 | tf_op jit(solution)/shard_map/ppermute | solution.py:102
  66.0 4.6 %collective-permute-done.15 = f32[32,128]{1,0:T(8,128)S(1)} collective-permute-done((f32[32,128]{1,0:T(8,128)S(1)}, f32[32,128]{1,0:T(8,128)S(1)}, u32[]{:S(2)}, u32[]{:S(2)}) %collective-permute-start.15) | collective-permute-done | bytes 16416 | tf_op jit(solution)/shard_map/ppermute | solution.py:102
  71.2 6.8 %shard_map.41 = (f32[64,64]{1,0:T(8,128)}, f32[64,64]{1,0:T(8,128)}) custom-call(f32[32,128]{1,0:T(8,128)} %add.111.gram_ref), custom_call_target="tpu_custom_call" | custom-call | tf_op jit(solution)/shard_map/pallas_call | solution.py:73
  78.0 1.8 %fusion.49 = f32[64,4,8,128]{3,0,2,1:T(8,128)S(1)} fusion(f32[64,4,8,128]{3,0,2,1:T(8,128)S(1)} %fusion.10, f32[64,64]{1,0:T(8,128)} %get-tuple-element.4), kind=kOutput, calls=%fused_computation.79 | convolution fusion | flops 201330688 | bytes 2113536 | tf_op jit(solution)/shard_map/mk,kxyz->mxyz/dot_general | solution.py:123
  79.8 1.6 %copy.24 = f32[64,4,8,128]{3,2,1,0:T(8,128)} copy(f32[64,4,8,128]{3,0,2,1:T(8,128)S(1)} %fusion.49) | data formatting | bytes 2097152
  (45 shorter events, 8.2 us)
Async XLA Ops:
  0.6 1.7 %copy-start = (f32[64,4,8,128]{3,2,1,0:T(8,128)S(1)}, f32[64,4,8,128]{3,2,1,0:T(8,128)}, u32[]{:S(2)}) copy-start(f32[64,4,8,128]{3,2,1,0:T(8,128)} %param.2) | copy-start | bytes 3145732
  2.2 7.5 %copy-start.1 = (f32[4,8,128]{2,1,0:T(8,128)S(1)}, f32[4,8,128]{2,1,0:T(8,128)}, u32[]{:S(2)}) copy-start(f32[4,8,128]{2,1,0:T(8,128)} %param.3) | copy-start | bytes 49156
  2.2 12.0 %collective-permute-start.1 = (f32[64,2,8,128]{3,0,2,1:T(8,128)S(1)}, f32[64,2,8,128]{3,0,2,1:T(8,128)S(1)}, u32[]{:S(2)}, u32[]{:S(2)}) collective-permute-start(f32[64,2,8,128]{3,0,2,1:T(8,128)S(1)} %copy.28), channel_id=1, source_target_pairs={{0,8},{8,16},{16,24},{24,32},{32,40},{40,48},{48,56},{56,64},{64,7... | collective-permute-start | bytes 1572872 | tf_op jit(solution)/shard_map/ppermute | solution.py:14
  2.5 8.6 %collective-permute-start.3 = (f32[64,4,2,128]{3,0,2,1:T(8,128)S(1)}, f32[64,4,2,128]{3,0,2,1:T(8,128)S(1)}, u32[]{:S(2)}, u32[]{:S(2)}) collective-permute-start(f32[64,4,2,128]{3,0,2,1:T(8,128)S(1)} %copy.30), channel_id=1, source_target_pairs={{0,1},{1,2},{2,3},{3,4},{4,5},{5,6},{6,7},{7,0},{8,9},{9,10},{10,1... | collective-permute-start | bytes 786440 | tf_op jit(solution)/shard_map/ppermute | solution.py:14
  4.6 12.8 %collective-permute-start.2 = (f32[64,4,2,128]{3,0,2,1:T(8,128)S(1)}, f32[64,4,2,128]{3,0,2,1:T(8,128)S(1)}, u32[]{:S(2)}, u32[]{:S(2)}) collective-permute-start(f32[64,4,2,128]{3,0,2,1:T(8,128)S(1)} %copy.29), channel_id=1, source_target_pairs={{1,0},{2,1},{3,2},{4,3},{5,4},{6,5},{7,6},{0,7},{9,8},{10,9},{11,1... | collective-permute-start | bytes 786440 | tf_op jit(solution)/shard_map/ppermute | solution.py:15
  4.9 12.5 %collective-permute-start = (f32[64,2,8,128]{3,0,2,1:T(8,128)S(1)}, f32[64,2,8,128]{3,0,2,1:T(8,128)S(1)}, u32[]{:S(2)}, u32[]{:S(2)}) collective-permute-start(f32[64,2,8,128]{3,0,2,1:T(8,128)S(1)} %copy.27), channel_id=1, source_target_pairs={{8,0},{16,8},{24,16},{32,24},{40,32},{48,40},{56,48},{64,56},{72,6... | collective-permute-start | bytes 1572872 | tf_op jit(solution)/shard_map/ppermute | solution.py:15
  18.8 10.6 %collective-permute-start.7 = (f32[64,4,2,128]{3,0,2,1:T(8,128)S(1)}, f32[64,4,2,128]{3,0,2,1:T(8,128)S(1)}, u32[]{:S(2)}, u32[]{:S(2)}) collective-permute-start(f32[64,4,2,128]{3,0,2,1:T(8,128)S(1)} %get-tuple-element.17), channel_id=1, source_target_pairs={{0,1},{1,2},{2,3},{3,4},{4,5},{5,6},{6,7},{7,0},{8,9},{9,10},{10,1... | collective-permute-start | bytes 786440 | tf_op jit(solution)/shard_map/ppermute | solution.py:14
  20.7 8.6 %collective-permute-start.6 = (f32[64,4,2,128]{3,0,2,1:T(8,128)S(1)}, f32[64,4,2,128]{3,0,2,1:T(8,128)S(1)}, u32[]{:S(2)}, u32[]{:S(2)}) collective-permute-start(f32[64,4,2,128]{3,0,2,1:T(8,128)S(1)} %get-tuple-element.16), channel_id=1, source_target_pairs={{1,0},{2,1},{3,2},{4,3},{5,4},{6,5},{7,6},{0,7},{9,8},{10,9},{11,1... | collective-permute-start | bytes 786440 | tf_op jit(solution)/shard_map/ppermute | solution.py:15
  21.9 11.9 %collective-permute-start.5 = (f32[64,2,8,128]{3,0,2,1:T(8,128)S(1)}, f32[64,2,8,128]{3,0,2,1:T(8,128)S(1)}, u32[]{:S(2)}, u32[]{:S(2)}) collective-permute-start(f32[64,2,8,128]{3,0,2,1:T(8,128)S(1)} %get-tuple-element.13), channel_id=1, source_target_pairs={{0,8},{8,16},{16,24},{24,32},{32,40},{40,48},{48,56},{56,64},{64,7... | collective-permute-start | bytes 1572872 | tf_op jit(solution)/shard_map/ppermute | solution.py:14
  21.9 11.9 %collective-permute-start.4 = (f32[64,2,8,128]{3,0,2,1:T(8,128)S(1)}, f32[64,2,8,128]{3,0,2,1:T(8,128)S(1)}, u32[]{:S(2)}, u32[]{:S(2)}) collective-permute-start(f32[64,2,8,128]{3,0,2,1:T(8,128)S(1)} %get-tuple-element.12), channel_id=1, source_target_pairs={{8,0},{16,8},{24,16},{32,24},{40,32},{48,40},{56,48},{64,56},{72,6... | collective-permute-start | bytes 1572872 | tf_op jit(solution)/shard_map/ppermute | solution.py:15
  36.6 4.9 %collective-permute-start.8 = (f32[32,128]{1,0:T(8,128)S(1)}, f32[32,128]{1,0:T(8,128)S(1)}, u32[]{:S(2)}, u32[]{:S(2)}) collective-permute-start(f32[32,128]{1,0:T(8,128)S(1)} %reshape.8), channel_id=1, source_target_pairs={{0,1},{1,0},{2,3},{3,2},{4,5},{5,4},{6,7},{7,6},{8,9},{9,8},{10,11... | collective-permute-start | bytes 49160 | tf_op jit(solution)/shard_map/ppermute | solution.py:102
  41.5 4.6 %collective-permute-start.9 = (f32[32,128]{1,0:T(8,128)S(1)}, f32[32,128]{1,0:T(8,128)S(1)}, u32[]{:S(2)}, u32[]{:S(2)}) collective-permute-start(f32[32,128]{1,0:T(8,128)S(1)} %add.104), channel_id=1, source_target_pairs={{0,2},{1,3},{2,0},{3,1},{4,6},{5,7},{6,4},{7,5},{8,10},{9,11},{10,... | collective-permute-start | bytes 49160 | tf_op jit(solution)/shard_map/ppermute | solution.py:102
  46.1 5.8 %collective-permute-start.10 = (f32[32,128]{1,0:T(8,128)S(1)}, f32[32,128]{1,0:T(8,128)S(1)}, u32[]{:S(2)}, u32[]{:S(2)}) collective-permute-start(f32[32,128]{1,0:T(8,128)S(1)} %add.105), channel_id=1, source_target_pairs={{0,6},{1,7},{2,4},{3,5},{4,2},{5,3},{6,0},{7,1},{8,14},{9,15},{10,... | collective-permute-start | bytes 49160 | tf_op jit(solution)/shard_map/ppermute | solution.py:102
  52.0 1.2 %collective-permute-start.11 = (f32[32,128]{1,0:T(8,128)S(1)}, f32[32,128]{1,0:T(8,128)S(1)}, u32[]{:S(2)}, u32[]{:S(2)}) collective-permute-start(f32[32,128]{1,0:T(8,128)S(1)} %add.106), channel_id=1, source_target_pairs={{0,8},{8,0},{16,24},{24,16},{32,40},{40,32},{48,56},{56,48},{64,72... | collective-permute-start | bytes 49160 | tf_op jit(solution)/shard_map/ppermute | solution.py:102
  53.2 3.7 %collective-permute-start.12 = (f32[32,128]{1,0:T(8,128)S(1)}, f32[32,128]{1,0:T(8,128)S(1)}, u32[]{:S(2)}, u32[]{:S(2)}) collective-permute-start(f32[32,128]{1,0:T(8,128)S(1)} %add.107), channel_id=1, source_target_pairs={{0,16},{8,24},{16,0},{24,8},{32,48},{40,56},{48,32},{56,40},{64,80... | collective-permute-start | bytes 49160 | tf_op jit(solution)/shard_map/ppermute | solution.py:102
  56.9 4.9 %collective-permute-start.13 = (f32[32,128]{1,0:T(8,128)S(1)}, f32[32,128]{1,0:T(8,128)S(1)}, u32[]{:S(2)}, u32[]{:S(2)}) collective-permute-start(f32[32,128]{1,0:T(8,128)S(1)} %add.108), channel_id=1, source_target_pairs={{0,48},{8,56},{16,32},{24,40},{32,16},{40,24},{48,0},{56,8},{64,11... | collective-permute-start | bytes 49160 | tf_op jit(solution)/shard_map/ppermute | solution.py:102
  61.9 3.7 %collective-permute-start.14 = (f32[32,128]{1,0:T(8,128)S(1)}, f32[32,128]{1,0:T(8,128)S(1)}, u32[]{:S(2)}, u32[]{:S(2)}) collective-permute-start(f32[32,128]{1,0:T(8,128)S(1)} %add.109), channel_id=1, source_target_pairs={{0,64},{8,72},{16,80},{24,88},{32,96},{40,104},{48,112},{56,120},{... | collective-permute-start | bytes 49160 | tf_op jit(solution)/shard_map/ppermute | solution.py:102
  65.6 4.9 %collective-permute-start.15 = (f32[32,128]{1,0:T(8,128)S(1)}, f32[32,128]{1,0:T(8,128)S(1)}, u32[]{:S(2)}, u32[]{:S(2)}) collective-permute-start(f32[32,128]{1,0:T(8,128)S(1)} %add.110), channel_id=1, source_target_pairs={{0,192},{8,200},{16,208},{24,216},{32,224},{40,232},{48,240},{56,2... | collective-permute-start | bytes 49160 | tf_op jit(solution)/shard_map/ppermute | solution.py:102

commit v16 on v15

--- a/solution.py
+++ b/solution.py
@@ -36,13 +36,13 @@
     return -0.5 * total + pot[None] * core
 
 
-def factor_kernel(gram_ref, factor_ref, inverse_ref):
+def factor_kernel(gram_ref, received_ref, factor_ref, inverse_ref):
     half = gram_ref.shape[1] // 2
     order = gram_ref.shape[0] * gram_ref.shape[1] // half
     groups = order // 8
     sub = lax.broadcasted_iota(jnp.int32, (8, order), 0)
     lane = lax.broadcasted_iota(jnp.int32, (8, order), 1)
-    packed = gram_ref[...]
+    packed = gram_ref[...] + received_ref[...]
     gram = jnp.concatenate(
         [piece for r in range(packed.shape[0]) for piece in (packed[r:r + 1, :half], packed[r:r + 1, half:])],
         axis=0,
@@ -68,14 +68,14 @@
         inverse_ref[pl.ds(8 * i, 8), :] = right[i] * scale
 
 
-def factor_and_inverse(packed, order):
+def factor_and_inverse(packed, received, order):
     shape = jax.ShapeDtypeStruct((order, order), jnp.float32)
     return pl.pallas_call(
         factor_kernel,
         out_shape=(shape, shape),
-        in_specs=[pl.BlockSpec(memory_space=pltpu.VMEM)],
+        in_specs=[pl.BlockSpec(memory_space=pltpu.VMEM)] * 2,
         out_specs=(pl.BlockSpec(memory_space=pltpu.VMEM),) * 2,
-    )(packed)
+    )(packed, received)
 
 
 def ring_rounds(stride):
@@ -88,18 +88,22 @@
     return [flip, mirror]
 
 
-def butterfly_sum(value, axis):
+def butterfly_sum(value, axis, open_last=False):
     count = lax.axis_size(axis)
     if count & (count - 1):
-        return lax.psum(value, axis)
+        total = lax.psum(value, axis)
+        return (total, jnp.zeros_like(total)) if open_last else total
     if count == 32:
         rounds = [lambda i: i ^ 1] + ring_rounds(2) + ring_rounds(8)
     elif count == 8:
         rounds = [lambda i: i ^ 1] + ring_rounds(2)
     else:
         rounds = [lambda i, mask=1 << b: i ^ mask for b in range(count.bit_length() - 1)]
-    for partner in rounds:
-        value = value + lax.ppermute(value, axis, [(i, partner(i)) for i in range(count)])
+    for step, partner in enumerate(rounds):
+        received = lax.ppermute(value, axis, [(i, partner(i)) for i in range(count)])
+        if open_last and step == len(rounds) - 1:
+            return value, received
+        value = value + received
     return value
 
 
@@ -118,8 +122,8 @@
         / cells
     )
     packed = local_gram.reshape(-1, 128)
-    gram = butterfly_sum(butterfly_sum(packed, "gy"), "gx")
-    factor, lower_inverse = factor_and_inverse(gram, local_gram.shape[0])
+    gram, received = butterfly_sum(butterfly_sum(packed, "gy"), "gx", open_last=True)
+    factor, lower_inverse = factor_and_inverse(gram, received, local_gram.shape[0])
     basis = jnp.einsum(
         "mk,kxyz->mxyz", lower_inverse * jnp.sqrt(jnp.float32(cells)), filtered,
         precision=lax.Precision.HIGHEST, preferred_element_type=jnp.float32,

time: 81.8 us -> 81.9 us (level)
    unnamed x11 -> x15, local copies, waits for them, and re-layouts: 2.09 us -> 2.69 us
where the time goes in v16:
time: 81.9 us; the launch traced here: 81.4 us
  waiting for transfers between devices  34 us (42%)
  starting transfers between devices  24.1 us (29%)
  Pallas kernels  6.84 us (8%)
  other arithmetic  6.76 us (8%)
  local copies, waits for them, and re-layouts  6.02 us (7%)
  matrix products  2.76 us (3%)
  between operations  0.86 us (1%)
    ppermute x8, waiting for transfers between devices, butterfly_sum(): lax.ppermute(value, axis, [(i, partner(i)) for i in range(count)])  25.1 us
    ppermute x4, starting transfers between devices, faces(): lax.ppermute(head, axis, [((i + 1) % count, i) for i in range(count)])  11.2 us
    ppermute x4, waiting for transfers between devices, faces(): lax.ppermute(tail, axis, [(i, (i + 1) % count) for i in range(count)])  8.97 us
    ppermute x8, starting transfers between devices, butterfly_sum(): lax.ppermute(value, axis, [(i, partner(i)) for i in range(count)])  8.87 us
    pallas_call x1, Pallas kernels, factor_and_inverse(): pl.pallas_call(factor_kernel, out_shape=(shape, shape), in_specs=[pl.Bloc...  6.84 us
    ppermute x4, starting transfers between devices, faces(): lax.ppermute(tail, axis, [(i, (i + 1) % count) for i in range(count)])  4.08 us
    sub x2, other arithmetic, apply_ham(): local = local - 1.0 / 12.0 * (along_z[..., :size] + along_z[..., 4:])  3.92 us
    unnamed x15, local copies, waits for them, and re-layouts  2.69 us
  transfers between devices with their start and end apart: 16, of which 11 were waited for; matrix products, arithmetic and copies ran while one was open for 7% of the time, Pallas kernels for 0%

profile of v16, /device:TPU:32, one launch (start us, length us, event | category | flops | bytes accessed | tf_op | source)
XLA Modules:
  0.0 81.4 jit_solution(14484547552896639833)
XLA Ops:
  0.6 1.4 %fusion.60 = (f32[64,2,8,128]{3,2,1,0:T(8,128)S(1)}, f32[64,2,8,128]{3,2,1,0:T(8,128)S(1)}) fusion(f32[64,4,8,128]{3,2,1,0:T(8,128)} %param.2), kind=kLoop, calls=%fused_computation.98 | loop fusion | bytes 2097152 | tf_op jit(solution)/shard_map/slice | solution.py:12
  2.5 2.0 %collective-permute-start.3 = (f32[64,4,2,128]{3,0,2,1:T(8,128)S(1)}, f32[64,4,2,128]{3,0,2,1:T(8,128)S(1)}, u32[]{:S(2)}, u32[]{:S(2)}) collective-permute-start(f32[64,4,2,128]{3,0,2,1:T(8,128)S(1)} %copy.30), channel_id=1, source_target_pairs={{0,1},{1,2},{2,3},{3,4},{4,5},{5,6},{6,7},{7,0},{8,9},{9,10},{10,1... | collective-permute-start | bytes 786440 | tf_op jit(solution)/shard_map/ppermute | solution.py:14
  4.9 4.7 %collective-permute-start = (f32[64,2,8,128]{3,0,2,1:T(8,128)S(1)}, f32[64,2,8,128]{3,0,2,1:T(8,128)S(1)}, u32[]{:S(2)}, u32[]{:S(2)}) collective-permute-start(f32[64,2,8,128]{3,0,2,1:T(8,128)S(1)} %copy.27), channel_id=1, source_target_pairs={{8,0},{16,8},{24,16},{32,24},{40,32},{48,40},{56,48},{64,56},{72,6... | collective-permute-start | bytes 1572872 | tf_op jit(solution)/shard_map/ppermute | solution.py:15
  9.7 1.4 %collective-permute-done.3 = f32[64,4,2,128]{3,0,2,1:T(8,128)S(1)} collective-permute-done((f32[64,4,2,128]{3,0,2,1:T(8,128)S(1)}, f32[64,4,2,128]{3,0,2,1:T(8,128)S(1)}, u32[]{:S(2)}, u32[]{:S(2)}) %collective-permute-start.3) | collective-permute-done | bytes 262176 | tf_op jit(solution)/shard_map/ppermute | solution.py:14
  11.2 3.0 %collective-permute-done.1 = f32[64,2,8,128]{3,0,2,1:T(8,128)S(1)} collective-permute-done((f32[64,2,8,128]{3,0,2,1:T(8,128)S(1)}, f32[64,2,8,128]{3,0,2,1:T(8,128)S(1)}, u32[]{:S(2)}, u32[]{:S(2)}) %collective-permute-start.1) | collective-permute-done | bytes 524320 | tf_op jit(solution)/shard_map/ppermute | solution.py:14
  15.4 2.0 %fusion.28 = f32[64,4,8,128]{3,0,2,1:T(8,128)S(1)} fusion(f32[64,4,8,128]{3,0,2,1:T(8,128)S(1)} %get-tuple-element.20, f32[64,4,8,2]{3,0,2,1:T(8,128)S(1)} %get-tuple-element.19, f32[64,4,8,2]{3,0,2,1:T(8,128)S(1)} %get-tuple-element.18), kind=kLoop, calls=%fused_computation.45 | loop fusion | flops 2883584 | bytes 2129920 | tf_op jit(solution)/shard_map/sub | solution.py:30
  18.8 2.0 %collective-permute-start.7 = (f32[64,4,2,128]{3,0,2,1:T(8,128)S(1)}, f32[64,4,2,128]{3,0,2,1:T(8,128)S(1)}, u32[]{:S(2)}, u32[]{:S(2)}) collective-permute-start(f32[64,4,2,128]{3,0,2,1:T(8,128)S(1)} %get-tuple-element.17), channel_id=1, source_target_pairs={{0,1},{1,2},{2,3},{3,4},{4,5},{5,6},{6,7},{7,0},{8,9},{9,10},{10,1... | collective-permute-start | bytes 786440 | tf_op jit(solution)/shard_map/ppermute | solution.py:14
  21.9 5.1 %collective-permute-start.4 = (f32[64,2,8,128]{3,0,2,1:T(8,128)S(1)}, f32[64,2,8,128]{3,0,2,1:T(8,128)S(1)}, u32[]{:S(2)}, u32[]{:S(2)}) collective-permute-start(f32[64,2,8,128]{3,0,2,1:T(8,128)S(1)} %get-tuple-element.12), channel_id=1, source_target_pairs={{8,0},{16,8},{24,16},{32,24},{40,32},{48,40},{56,48},{64,56},{72,6... | collective-permute-start | bytes 1572872 | tf_op jit(solution)/shard_map/ppermute | solution.py:15
  27.4 2.0 %fusion.22 = f32[64,4,8,128]{3,0,2,1:T(8,128)S(1)} fusion(f32[64,4,8,128]{3,0,2,1:T(8,128)S(1)} %get-tuple-element.10, f32[64,4,8,2]{3,0,2,1:T(8,128)S(1)} %get-tuple-element.15, f32[64,4,8,2]{3,0,2,1:T(8,128)S(1)} %get-tuple-element.14, f32[64,4,8,128]{3,0,2,1:T(8,128)S(1)} %get-tuple-element.11), kind=kLoop, calls=%fused_computation.39 | loop fusion | flops 2883584 | bytes 3178496 | tf_op jit(solution)/shard_map/sub | solution.py:30
  29.4 4.5 %collective-permute-done.5 = f32[64,2,8,128]{3,0,2,1:T(8,128)S(1)} collective-permute-done((f32[64,2,8,128]{3,0,2,1:T(8,128)S(1)}, f32[64,2,8,128]{3,0,2,1:T(8,128)S(1)}, u32[]{:S(2)}, u32[]{:S(2)}) %collective-permute-start.5) | collective-permute-done | bytes 524320 | tf_op jit(solution)/shard_map/ppermute | solution.py:14
  33.9 1.7 %fusion.10 = f32[64,4,8,128]{3,0,2,1:T(8,128)S(1)} fusion(f32[64,4,2,128]{3,0,2,1:T(8,128)S(1)} %collective-permute-done.7, f32[64,4,8,128]{3,0,2,1:T(8,128)S(1)} %get-tuple-element.10, f32[64,4,2,128]{3,0,2,1:T(8,128)S(1)} %collective-permute-done.6, f32[64,4,8,128]{3,0,2,1:T(8,128)S(1)} %fusion.22, f32[64,2,8,128]{3,0,2,1:T(8,128)S(1)} %collective-permute-done.5, ...), kind=kLoop, calls=%fused_computation.27 | loop fusion | flops 7077888 | bytes 6832128 | tf_op jit(solution)/shard_map/sub | solution.py:114
  36.6 3.2 %collective-permute-start.8 = (f32[32,128]{1,0:T(8,128)S(1)}, f32[32,128]{1,0:T(8,128)S(1)}, u32[]{:S(2)}, u32[]{:S(2)}) collective-permute-start(f32[32,128]{1,0:T(8,128)S(1)} %reshape.8), channel_id=1, source_target_pairs={{0,1},{1,0},{2,3},{3,2},{4,5},{5,4},{6,7},{7,6},{8,9},{9,8},{10,11... | collective-permute-start | bytes 49160 | tf_op jit(solution)/shard_map/ppermute | solution.py:103
  39.8 1.7 %collective-permute-done.8 = f32[32,128]{1,0:T(8,128)S(1)} collective-permute-done((f32[32,128]{1,0:T(8,128)S(1)}, f32[32,128]{1,0:T(8,128)S(1)}, u32[]{:S(2)}, u32[]{:S(2)}) %collective-permute-start.8) | collective-permute-done | bytes 16416 | tf_op jit(solution)/shard_map/ppermute | solution.py:103
  41.5 2.2 %collective-permute-start.9 = (f32[32,128]{1,0:T(8,128)S(1)}, f32[32,128]{1,0:T(8,128)S(1)}, u32[]{:S(2)}, u32[]{:S(2)}) collective-permute-start(f32[32,128]{1,0:T(8,128)S(1)} %add.101), channel_id=1, source_target_pairs={{0,2},{1,3},{2,0},{3,1},{4,6},{5,7},{6,4},{7,5},{8,10},{9,11},{10,... | collective-permute-start | bytes 49160 | tf_op jit(solution)/shard_map/ppermute | solution.py:103
  43.7 2.5 %collective-permute-done.9 = f32[32,128]{1,0:T(8,128)S(1)} collective-permute-done((f32[32,128]{1,0:T(8,128)S(1)}, f32[32,128]{1,0:T(8,128)S(1)}, u32[]{:S(2)}, u32[]{:S(2)}) %collective-permute-start.9) | collective-permute-done | bytes 16416 | tf_op jit(solution)/shard_map/ppermute | solution.py:103
  46.1 3.2 %collective-permute-start.10 = (f32[32,128]{1,0:T(8,128)S(1)}, f32[32,128]{1,0:T(8,128)S(1)}, u32[]{:S(2)}, u32[]{:S(2)}) collective-permute-start(f32[32,128]{1,0:T(8,128)S(1)} %add.102), channel_id=1, source_target_pairs={{0,6},{1,7},{2,4},{3,5},{4,2},{5,3},{6,0},{7,1},{8,14},{9,15},{10,... | collective-permute-start | bytes 49160 | tf_op jit(solution)/shard_map/ppermute | solution.py:103
  49.3 2.7 %collective-permute-done.10 = f32[32,128]{1,0:T(8,128)S(1)} collective-permute-done((f32[32,128]{1,0:T(8,128)S(1)}, f32[32,128]{1,0:T(8,128)S(1)}, u32[]{:S(2)}, u32[]{:S(2)}) %collective-permute-start.10) | collective-permute-done | bytes 16416 | tf_op jit(solution)/shard_map/ppermute | solution.py:103
  53.2 3.7 %collective-permute-done.12 = f32[32,128]{1,0:T(8,128)S(1)} collective-permute-done((f32[32,128]{1,0:T(8,128)S(1)}, f32[32,128]{1,0:T(8,128)S(1)}, u32[]{:S(2)}, u32[]{:S(2)}) %collective-permute-start.12) | collective-permute-done | bytes 16416 | tf_op jit(solution)/shard_map/ppermute | solution.py:103
  56.9 4.9 %collective-permute-done.13 = f32[32,128]{1,0:T(8,128)S(1)} collective-permute-done((f32[32,128]{1,0:T(8,128)S(1)}, f32[32,128]{1,0:T(8,128)S(1)}, u32[]{:S(2)}, u32[]{:S(2)}) %collective-permute-start.13) | collective-permute-done | bytes 16416 | tf_op jit(solution)/shard_map/ppermute | solution.py:103
  61.9 3.7 %collective-permute-done.14 = f32[32,128]{1,0:T(8,128)S(1)} collective-permute-done((f32[32,128]{1,0:T(8,128)S(1)}, f32[32,128]{1,0:T(8,128)S(1)}, u32[]{:S(2)}, u32[]{:S(2)}) %collective-permute-start.14) | collective-permute-done | bytes 16416 | tf_op jit(solution)/shard_map/ppermute | solution.py:103
  66.0 4.6 %collective-permute-done.15.received_ref = f32[32,128]{1,0:T(8,128)S(1)} collective-permute-done((f32[32,128]{1,0:T(8,128)S(1)}, f32[32,128]{1,0:T(8,128)S(1)}, u32[]{:S(2)}, u32[]{:S(2)}) %collective-permute-start.15) | collective-permute-done | bytes 16416 | tf_op jit(solution)/shard_map/ppermute | solution.py:103
  71.2 6.8 %shard_map.41 = (f32[64,64]{1,0:T(8,128)}, f32[64,64]{1,0:T(8,128)}) custom-call(f32[32,128]{1,0:T(8,128)} %copy-done.2, f32[32,128]{1,0:T(8,128)} %copy-done.3), custom_call_target="tpu_custom_call" | custom-call | tf_op jit(solution)/shard_map/pallas_call | solution.py:73
  78.0 1.8 %fusion.49 = f32[64,4,8,128]{3,0,2,1:T(8,128)S(1)} fusion(f32[64,4,8,128]{3,0,2,1:T(8,128)S(1)} %fusion.10, f32[64,64]{1,0:T(8,128)} %get-tuple-element.4), kind=kOutput, calls=%fused_computation.79 | convolution fusion | flops 201330688 | bytes 2113536 | tf_op jit(solution)/shard_map/mk,kxyz->mxyz/dot_general | solution.py:127
  79.8 1.6 %copy.24 = f32[64,4,8,128]{3,2,1,0:T(8,128)} copy(f32[64,4,8,128]{3,0,2,1:T(8,128)S(1)} %fusion.49) | data formatting | bytes 2097152
  (48 shorter events, 8.2 us)
Async XLA Ops:
  0.6 1.7 %copy-start = (f32[64,4,8,128]{3,2,1,0:T(8,128)S(1)}, f32[64,4,8,128]{3,2,1,0:T(8,128)}, u32[]{:S(2)}) copy-start(f32[64,4,8,128]{3,2,1,0:T(8,128)} %param.2) | copy-start | bytes 3145732
  2.2 7.5 %copy-start.1 = (f32[4,8,128]{2,1,0:T(8,128)S(1)}, f32[4,8,128]{2,1,0:T(8,128)}, u32[]{:S(2)}) copy-start(f32[4,8,128]{2,1,0:T(8,128)} %param.3) | copy-start | bytes 49156
  2.2 12.0 %collective-permute-start.1 = (f32[64,2,8,128]{3,0,2,1:T(8,128)S(1)}, f32[64,2,8,128]{3,0,2,1:T(8,128)S(1)}, u32[]{:S(2)}, u32[]{:S(2)}) collective-permute-start(f32[64,2,8,128]{3,0,2,1:T(8,128)S(1)} %copy.28), channel_id=1, source_target_pairs={{0,8},{8,16},{16,24},{24,32},{32,40},{40,48},{48,56},{56,64},{64,7... | collective-permute-start | bytes 1572872 | tf_op jit(solution)/shard_map/ppermute | solution.py:14
  2.5 8.6 %collective-permute-start.3 = (f32[64,4,2,128]{3,0,2,1:T(8,128)S(1)}, f32[64,4,2,128]{3,0,2,1:T(8,128)S(1)}, u32[]{:S(2)}, u32[]{:S(2)}) collective-permute-start(f32[64,4,2,128]{3,0,2,1:T(8,128)S(1)} %copy.30), channel_id=1, source_target_pairs={{0,1},{1,2},{2,3},{3,4},{4,5},{5,6},{6,7},{7,0},{8,9},{9,10},{10,1... | collective-permute-start | bytes 786440 | tf_op jit(solution)/shard_map/ppermute | solution.py:14
  4.6 12.8 %collective-permute-start.2 = (f32[64,4,2,128]{3,0,2,1:T(8,128)S(1)}, f32[64,4,2,128]{3,0,2,1:T(8,128)S(1)}, u32[]{:S(2)}, u32[]{:S(2)}) collective-permute-start(f32[64,4,2,128]{3,0,2,1:T(8,128)S(1)} %copy.29), channel_id=1, source_target_pairs={{1,0},{2,1},{3,2},{4,3},{5,4},{6,5},{7,6},{0,7},{9,8},{10,9},{11,1... | collective-permute-start | bytes 786440 | tf_op jit(solution)/shard_map/ppermute | solution.py:15
  4.9 12.5 %collective-permute-start = (f32[64,2,8,128]{3,0,2,1:T(8,128)S(1)}, f32[64,2,8,128]{3,0,2,1:T(8,128)S(1)}, u32[]{:S(2)}, u32[]{:S(2)}) collective-permute-start(f32[64,2,8,128]{3,0,2,1:T(8,128)S(1)} %copy.27), channel_id=1, source_target_pairs={{8,0},{16,8},{24,16},{32,24},{40,32},{48,40},{56,48},{64,56},{72,6... | collective-permute-start | bytes 1572872 | tf_op jit(solution)/shard_map/ppermute | solution.py:15
  18.8 10.6 %collective-permute-start.7 = (f32[64,4,2,128]{3,0,2,1:T(8,128)S(1)}, f32[64,4,2,128]{3,0,2,1:T(8,128)S(1)}, u32[]{:S(2)}, u32[]{:S(2)}) collective-permute-start(f32[64,4,2,128]{3,0,2,1:T(8,128)S(1)} %get-tuple-element.17), channel_id=1, source_target_pairs={{0,1},{1,2},{2,3},{3,4},{4,5},{5,6},{6,7},{7,0},{8,9},{9,10},{10,1... | collective-permute-start | bytes 786440 | tf_op jit(solution)/shard_map/ppermute | solution.py:14
  20.7 8.6 %collective-permute-start.6 = (f32[64,4,2,128]{3,0,2,1:T(8,128)S(1)}, f32[64,4,2,128]{3,0,2,1:T(8,128)S(1)}, u32[]{:S(2)}, u32[]{:S(2)}) collective-permute-start(f32[64,4,2,128]{3,0,2,1:T(8,128)S(1)} %get-tuple-element.16), channel_id=1, source_target_pairs={{1,0},{2,1},{3,2},{4,3},{5,4},{6,5},{7,6},{0,7},{9,8},{10,9},{11,1... | collective-permute-start | bytes 786440 | tf_op jit(solution)/shard_map/ppermute | solution.py:15
  21.9 11.9 %collective-permute-start.5 = (f32[64,2,8,128]{3,0,2,1:T(8,128)S(1)}, f32[64,2,8,128]{3,0,2,1:T(8,128)S(1)}, u32[]{:S(2)}, u32[]{:S(2)}) collective-permute-start(f32[64,2,8,128]{3,0,2,1:T(8,128)S(1)} %get-tuple-element.13), channel_id=1, source_target_pairs={{0,8},{8,16},{16,24},{24,32},{32,40},{40,48},{48,56},{56,64},{64,7... | collective-permute-start | bytes 1572872 | tf_op jit(solution)/shard_map/ppermute | solution.py:14
  21.9 11.9 %collective-permute-start.4 = (f32[64,2,8,128]{3,0,2,1:T(8,128)S(1)}, f32[64,2,8,128]{3,0,2,1:T(8,128)S(1)}, u32[]{:S(2)}, u32[]{:S(2)}) collective-permute-start(f32[64,2,8,128]{3,0,2,1:T(8,128)S(1)} %get-tuple-element.12), channel_id=1, source_target_pairs={{8,0},{16,8},{24,16},{32,24},{40,32},{48,40},{56,48},{64,56},{72,6... | collective-permute-start | bytes 1572872 | tf_op jit(solution)/shard_map/ppermute | solution.py:15
  36.6 4.9 %collective-permute-start.8 = (f32[32,128]{1,0:T(8,128)S(1)}, f32[32,128]{1,0:T(8,128)S(1)}, u32[]{:S(2)}, u32[]{:S(2)}) collective-permute-start(f32[32,128]{1,0:T(8,128)S(1)} %reshape.8), channel_id=1, source_target_pairs={{0,1},{1,0},{2,3},{3,2},{4,5},{5,4},{6,7},{7,6},{8,9},{9,8},{10,11... | collective-permute-start | bytes 49160 | tf_op jit(solution)/shard_map/ppermute | solution.py:103
  41.5 4.6 %collective-permute-start.9 = (f32[32,128]{1,0:T(8,128)S(1)}, f32[32,128]{1,0:T(8,128)S(1)}, u32[]{:S(2)}, u32[]{:S(2)}) collective-permute-start(f32[32,128]{1,0:T(8,128)S(1)} %add.101), channel_id=1, source_target_pairs={{0,2},{1,3},{2,0},{3,1},{4,6},{5,7},{6,4},{7,5},{8,10},{9,11},{10,... | collective-permute-start | bytes 49160 | tf_op jit(solution)/shard_map/ppermute | solution.py:103
  46.1 5.8 %collective-permute-start.10 = (f32[32,128]{1,0:T(8,128)S(1)}, f32[32,128]{1,0:T(8,128)S(1)}, u32[]{:S(2)}, u32[]{:S(2)}) collective-permute-start(f32[32,128]{1,0:T(8,128)S(1)} %add.102), channel_id=1, source_target_pairs={{0,6},{1,7},{2,4},{3,5},{4,2},{5,3},{6,0},{7,1},{8,14},{9,15},{10,... | collective-permute-start | bytes 49160 | tf_op jit(solution)/shard_map/ppermute | solution.py:103
  52.0 1.2 %collective-permute-start.11 = (f32[32,128]{1,0:T(8,128)S(1)}, f32[32,128]{1,0:T(8,128)S(1)}, u32[]{:S(2)}, u32[]{:S(2)}) collective-permute-start(f32[32,128]{1,0:T(8,128)S(1)} %add.103), channel_id=1, source_target_pairs={{0,8},{8,0},{16,24},{24,16},{32,40},{40,32},{48,56},{56,48},{64,72... | collective-permute-start | bytes 49160 | tf_op jit(solution)/shard_map/ppermute | solution.py:103
  53.2 3.7 %collective-permute-start.12 = (f32[32,128]{1,0:T(8,128)S(1)}, f32[32,128]{1,0:T(8,128)S(1)}, u32[]{:S(2)}, u32[]{:S(2)}) collective-permute-start(f32[32,128]{1,0:T(8,128)S(1)} %add.104), channel_id=1, source_target_pairs={{0,16},{8,24},{16,0},{24,8},{32,48},{40,56},{48,32},{56,40},{64,80... | collective-permute-start | bytes 49160 | tf_op jit(solution)/shard_map/ppermute | solution.py:103
  56.9 4.9 %collective-permute-start.13 = (f32[32,128]{1,0:T(8,128)S(1)}, f32[32,128]{1,0:T(8,128)S(1)}, u32[]{:S(2)}, u32[]{:S(2)}) collective-permute-start(f32[32,128]{1,0:T(8,128)S(1)} %add.105), channel_id=1, source_target_pairs={{0,48},{8,56},{16,32},{24,40},{32,16},{40,24},{48,0},{56,8},{64,11... | collective-permute-start | bytes 49160 | tf_op jit(solution)/shard_map/ppermute | solution.py:103
  61.9 3.7 %collective-permute-start.14 = (f32[32,128]{1,0:T(8,128)S(1)}, f32[32,128]{1,0:T(8,128)S(1)}, u32[]{:S(2)}, u32[]{:S(2)}) collective-permute-start(f32[32,128]{1,0:T(8,128)S(1)} %add.106), channel_id=1, source_target_pairs={{0,64},{8,72},{16,80},{24,88},{32,96},{40,104},{48,112},{56,120},{... | collective-permute-start | bytes 49160 | tf_op jit(solution)/shard_map/ppermute | solution.py:103
  65.6 5.0 %copy-start.2 = (f32[32,128]{1,0:T(8,128)}, f32[32,128]{1,0:T(8,128)S(1)}, u32[]{:S(2)}) copy-start(f32[32,128]{1,0:T(8,128)S(1)} %add.107.gram_ref) | copy-start | bytes 49156
  65.6 4.9 %collective-permute-start.15 = (f32[32,128]{1,0:T(8,128)S(1)}, f32[32,128]{1,0:T(8,128)S(1)}, u32[]{:S(2)}, u32[]{:S(2)}) collective-permute-start(f32[32,128]{1,0:T(8,128)S(1)} %add.107.gram_ref), channel_id=1, source_target_pairs={{0,192},{8,200},{16,208},{24,216},{32,224},{40,232},{48,240},{56,2... | collective-permute-start | bytes 49160 | tf_op jit(solution)/shard_map/ppermute | solution.py:103
  70.6 0.6 copy-start.3

commit v17 on v14

--- a/solution.py
+++ b/solution.py
@@ -28,12 +28,12 @@
     local = -7.5 * core
     local = local + 4.0 / 3.0 * (along_z[..., 1:size + 1] + along_z[..., 3:size + 3])
     local = local - 1.0 / 12.0 * (along_z[..., :size] + along_z[..., 4:])
-    total = lax.optimization_barrier(local)
-    total = total + 4.0 / 3.0 * (along_x[:, 3:-1] + along_x[:, 1:-3])
+    shifted = lax.optimization_barrier(-0.5 * local + pot[None] * core - 5.5 * core)
+    total = 4.0 / 3.0 * (along_x[:, 3:-1] + along_x[:, 1:-3])
     total = total - 1.0 / 12.0 * (along_x[:, 4:] + along_x[:, :-4])
     total = total + 4.0 / 3.0 * (along_y[:, :, 3:-1] + along_y[:, :, 1:-3])
     total = total - 1.0 / 12.0 * (along_y[:, :, 4:] + along_y[:, :, :-4])
-    return -0.5 * total + pot[None] * core
+    return shifted - 0.5 * total
 
 
 def factor_kernel(gram_ref, factor_ref, inverse_ref):
@@ -100,9 +100,8 @@
 
 def shards(orbitals, potential):
     orbitals_here = lax.optimization_barrier(orbitals)
-    first = (apply_ham(orbitals_here, potential, orbitals) - 5.5 * orbitals_here) / 4.5
-    applied = apply_ham(first, potential)
-    filtered = 2.0 * (applied - 5.5 * first) / 4.5 - orbitals_here
+    first = apply_ham(orbitals_here, potential, orbitals) / 4.5
+    filtered = 2.0 * apply_ham(first, potential) / 4.5 - orbitals_here
     count = filtered.shape[1] * filtered.shape[2] * filtered.shape[3]
     cells = count * lax.axis_size("gx") * lax.axis_size("gy")
     local_gram = (

time: 81.9 us -> 85.6 us (1.045)
  waiting for transfers between devices: 34 us -> 38.6 us
    ppermute x4, waiting for transfers between devices: 0.01 us -> 4.34 us  [faces(): lax.ppermute(head, axis, [((i + 1) % count, i) for i in range(count)])]
    ppermute x4, starting transfers between devices: 4.08 us -> 2.08 us  [faces(): lax.ppermute(tail, axis, [(i, (i + 1) % count) for i in range(count)])]
    ppermute x4, starting transfers between devices: 11.2 us -> 13 us  [faces(): lax.ppermute(head, axis, [((i + 1) % count, i) for i in range(count)])]
    unnamed x11 -> x12, local copies, waits for them, and re-layouts: 2.09 us -> 2.86 us
  transfers between devices with their start and end apart: 16 -> 16, of which waited for: 11 -> 12; matrix products, arithmetic and copies ran while one was open for 7% -> 7% of each run, Pallas kernels for 0% -> 0%
where the time goes in v17:
time: 85.6 us; the launch traced here: 85.4 us
  waiting for transfers between devices  38.6 us (45%)
  starting transfers between devices  23.9 us (28%)
  Pallas kernels  6.78 us (8%)
  other arithmetic  6.39 us (7%)
  local copies, waits for them, and re-layouts  6.07 us (7%)
  matrix products  2.77 us (3%)
  between operations  0.86 us (1%)
    ppermute x8, waiting for transfers between devices, butterfly_sum(): lax.ppermute(value, axis, [(i, partner(i)) for i in range(count)])  24.5 us
    ppermute x4, starting transfers between devices, faces(): lax.ppermute(head, axis, [((i + 1) % count, i) for i in range(count)])  13 us
    ppermute x4, waiting for transfers between devices, faces(): lax.ppermute(tail, axis, [(i, (i + 1) % count) for i in range(count)])  9.72 us
    ppermute x8, starting transfers between devices, butterfly_sum(): lax.ppermute(value, axis, [(i, partner(i)) for i in range(count)])  8.82 us
    pallas_call x1, Pallas kernels, factor_and_inverse(): pl.pallas_call(factor_kernel, out_shape=(shape, shape), in_specs=[pl.Bloc...  6.78 us
    ppermute x4, waiting for transfers between devices, faces(): lax.ppermute(head, axis, [((i + 1) % count, i) for i in range(count)])  4.34 us
    sub x2, other arithmetic, apply_ham(): -0.5 * local + pot[None] * core - 5.5 * core  3.93 us
    unnamed x12, local copies, waits for them, and re-layouts  2.86 us
  transfers between devices with their start and end apart: 16, of which 12 were waited for; matrix products, arithmetic and copies ran while one was open for 7% of the time, Pallas kernels for 0%

profile of v17, /device:TPU:32, one launch (start us, length us, event | category | flops | bytes accessed | tf_op | source)
XLA Modules:
  0.0 85.4 jit_solution(11492316926598299292)
XLA Ops:
  2.5 2.0 %collective-permute-start.3 = (f32[64,4,2,128]{3,0,2,1:T(8,128)S(1)}, f32[64,4,2,128]{3,0,2,1:T(8,128)S(1)}, u32[]{:S(2)}, u32[]{:S(2)}) collective-permute-start(f32[64,4,2,128]{3,0,2,1:T(8,128)S(1)} %copy.30), channel_id=1, source_target_pairs={{0,1},{1,2},{2,3},{3,4},{4,5},{5,6},{6,7},{7,0},{8,9},{9,10},{10,1... | collective-permute-start | bytes 786440 | tf_op jit(solution)/shard_map/ppermute | solution.py:14
  4.9 4.7 %collective-permute-start = (f32[64,2,8,128]{3,0,2,1:T(8,128)S(1)}, f32[64,2,8,128]{3,0,2,1:T(8,128)S(1)}, u32[]{:S(2)}, u32[]{:S(2)}) collective-permute-start(f32[64,2,8,128]{3,0,2,1:T(8,128)S(1)} %copy.27), channel_id=1, source_target_pairs={{8,0},{16,8},{24,16},{32,24},{40,32},{48,40},{56,48},{64,56},{72,6... | collective-permute-start | bytes 1572872 | tf_op jit(solution)/shard_map/ppermute | solution.py:15
  9.7 1.4 %collective-permute-done.3 = f32[64,4,2,128]{3,0,2,1:T(8,128)S(1)} collective-permute-done((f32[64,4,2,128]{3,0,2,1:T(8,128)S(1)}, f32[64,4,2,128]{3,0,2,1:T(8,128)S(1)}, u32[]{:S(2)}, u32[]{:S(2)}) %collective-permute-start.3) | collective-permute-done | bytes 262176 | tf_op jit(solution)/shard_map/ppermute | solution.py:14
  11.2 3.0 %collective-permute-done.1 = f32[64,2,8,128]{3,0,2,1:T(8,128)S(1)} collective-permute-done((f32[64,2,8,128]{3,0,2,1:T(8,128)S(1)}, f32[64,2,8,128]{3,0,2,1:T(8,128)S(1)}, u32[]{:S(2)}, u32[]{:S(2)}) %collective-permute-start.1) | collective-permute-done | bytes 524320 | tf_op jit(solution)/shard_map/ppermute | solution.py:14
  15.4 2.0 %fusion.32 = f32[64,4,8,128]{3,0,2,1:T(8,128)S(1)} fusion(f32[64,4,8,128]{3,0,2,1:T(8,128)S(1)} %get-tuple-element.24, f32[64,4,8,2]{3,0,2,1:T(8,128)S(1)} %get-tuple-element.28, f32[64,4,8,2]{3,0,2,1:T(8,128)S(1)} %get-tuple-element.27, f32[4,8,128]{2,1,0:T(8,128)S(1)} %copy-done.1), kind=kLoop, calls=%fused_computation.49 | loop fusion | flops 4194304 | bytes 2146304 | tf_op jit(solution)/shard_map/sub | solution.py:31
  18.5 3.1 %collective-permute-start.6 = (f32[64,4,2,128]{3,0,2,1:T(8,128)S(1)}, f32[64,4,2,128]{3,0,2,1:T(8,128)S(1)}, u32[]{:S(2)}, u32[]{:S(2)}) collective-permute-start(f32[64,4,2,128]{3,0,2,1:T(8,128)S(1)} %get-tuple-element.14), channel_id=1, source_target_pairs={{1,0},{2,1},{3,2},{4,3},{5,4},{6,5},{7,6},{0,7},{9,8},{10,9},{11,1... | collective-permute-start | bytes 786440 | tf_op jit(solution)/shard_map/ppermute | solution.py:15
  21.7 4.9 %collective-permute-start.4 = (f32[64,2,8,128]{3,0,2,1:T(8,128)S(1)}, f32[64,2,8,128]{3,0,2,1:T(8,128)S(1)}, u32[]{:S(2)}, u32[]{:S(2)}) collective-permute-start(f32[64,2,8,128]{3,0,2,1:T(8,128)S(1)} %get-tuple-element.12), channel_id=1, source_target_pairs={{8,0},{16,8},{24,16},{32,24},{40,32},{48,40},{56,48},{64,56},{72,6... | collective-permute-start | bytes 1572872 | tf_op jit(solution)/shard_map/ppermute | solution.py:15
  27.0 2.0 %fusion.23 = f32[64,4,8,128]{3,0,2,1:T(8,128)S(1)} fusion(f32[64,4,8,128]{3,0,2,1:T(8,128)S(1)} %get-tuple-element.10, f32[64,4,8,2]{3,0,2,1:T(8,128)S(1)} %get-tuple-element.17, f32[64,4,8,2]{3,0,2,1:T(8,128)S(1)} %get-tuple-element.16, f32[64,4,8,128]{3,0,2,1:T(8,128)S(1)} %get-tuple-element.11, f32[4,8,128]{2,1,0:T(8,128)S(1)} %broadcast_multiply_fusion.1), kind=kLoop, calls=%fused_computation.40 | loop fusion | flops 4194304 | bytes 3194880 | tf_op jit(solution)/shard_map/sub | solution.py:31
  29.0 4.3 %collective-permute-done.4 = f32[64,2,8,128]{3,0,2,1:T(8,128)S(1)} collective-permute-done((f32[64,2,8,128]{3,0,2,1:T(8,128)S(1)}, f32[64,2,8,128]{3,0,2,1:T(8,128)S(1)}, u32[]{:S(2)}, u32[]{:S(2)}) %collective-permute-start.4) | collective-permute-done | bytes 524320 | tf_op jit(solution)/shard_map/ppermute | solution.py:15
  33.3 5.2 %collective-permute-done.5 = f32[64,2,8,128]{3,0,2,1:T(8,128)S(1)} collective-permute-done((f32[64,2,8,128]{3,0,2,1:T(8,128)S(1)}, f32[64,2,8,128]{3,0,2,1:T(8,128)S(1)}, u32[]{:S(2)}, u32[]{:S(2)}) %collective-permute-start.5) | collective-permute-done | bytes 524320 | tf_op jit(solution)/shard_map/ppermute | solution.py:14
  38.5 1.5 %fusion.9 = f32[64,4,8,128]{3,0,2,1:T(8,128)S(1)} fusion(f32[64,4,8,128]{3,0,2,1:T(8,128)S(1)} %fusion.23, f32[64,4,2,128]{3,0,2,1:T(8,128)S(1)} %collective-permute-done.7, f32[64,4,8,128]{3,0,2,1:T(8,128)S(1)} %get-tuple-element.10, f32[64,4,2,128]{3,0,2,1:T(8,128)S(1)} %collective-permute-done.6, f32[64,2,8,128]{3,0,2,1:T(8,128)S(1)} %collective-permute-done.5, ...), kind=kLoop, calls=%fused_computation.26 | loop fusion | flops 6029312 | bytes 5767168 | tf_op jit(solution)/shard_map/sub | solution.py:104
  41.1 1.8 %collective-permute-start.8 = (f32[32,128]{1,0:T(8,128)S(1)}, f32[32,128]{1,0:T(8,128)S(1)}, u32[]{:S(2)}, u32[]{:S(2)}) collective-permute-start(f32[32,128]{1,0:T(8,128)S(1)} %reshape.11), channel_id=1, source_target_pairs={{0,1},{1,0},{2,3},{3,2},{4,5},{5,4},{6,7},{7,6},{8,9},{9,8},{10,11... | collective-permute-start | bytes 49160 | tf_op jit(solution)/shard_map/ppermute | solution.py:97
  42.9 2.0 %collective-permute-done.8 = f32[32,128]{1,0:T(8,128)S(1)} collective-permute-done((f32[32,128]{1,0:T(8,128)S(1)}, f32[32,128]{1,0:T(8,128)S(1)}, u32[]{:S(2)}, u32[]{:S(2)}) %collective-permute-start.8) | collective-permute-done | bytes 16416 | tf_op jit(solution)/shard_map/ppermute | solution.py:97
  44.9 3.5 %collective-permute-start.9 = (f32[32,128]{1,0:T(8,128)S(1)}, f32[32,128]{1,0:T(8,128)S(1)}, u32[]{:S(2)}, u32[]{:S(2)}) collective-permute-start(f32[32,128]{1,0:T(8,128)S(1)} %add.96), channel_id=1, source_target_pairs={{0,2},{1,3},{2,0},{3,1},{4,6},{5,7},{6,4},{7,5},{8,10},{9,11},{10,... | collective-permute-start | bytes 49160 | tf_op jit(solution)/shard_map/ppermute | solution.py:97
  48.4 1.7 %collective-permute-done.9 = f32[32,128]{1,0:T(8,128)S(1)} collective-permute-done((f32[32,128]{1,0:T(8,128)S(1)}, f32[32,128]{1,0:T(8,128)S(1)}, u32[]{:S(2)}, u32[]{:S(2)}) %collective-permute-start.9) | collective-permute-done | bytes 16416 | tf_op jit(solution)/shard_map/ppermute | solution.py:97
  50.1 3.6 %collective-permute-start.10 = (f32[32,128]{1,0:T(8,128)S(1)}, f32[32,128]{1,0:T(8,128)S(1)}, u32[]{:S(2)}, u32[]{:S(2)}) collective-permute-start(f32[32,128]{1,0:T(8,128)S(1)} %add.97), channel_id=1, source_target_pairs={{0,6},{1,7},{2,4},{3,5},{4,2},{5,3},{6,0},{7,1},{8,14},{9,15},{10,... | collective-permute-start | bytes 49160 | tf_op jit(solution)/shard_map/ppermute | solution.py:97
  53.6 2.3 %collective-permute-done.10 = f32[32,128]{1,0:T(8,128)S(1)} collective-permute-done((f32[32,128]{1,0:T(8,128)S(1)}, f32[32,128]{1,0:T(8,128)S(1)}, u32[]{:S(2)}, u32[]{:S(2)}) %collective-permute-start.10) | collective-permute-done | bytes 16416 | tf_op jit(solution)/shard_map/ppermute | solution.py:97
  57.1 3.7 %collective-permute-done.12 = f32[32,128]{1,0:T(8,128)S(1)} collective-permute-done((f32[32,128]{1,0:T(8,128)S(1)}, f32[32,128]{1,0:T(8,128)S(1)}, u32[]{:S(2)}, u32[]{:S(2)}) %collective-permute-start.12) | collective-permute-done | bytes 16416 | tf_op jit(solution)/shard_map/ppermute | solution.py:97
  60.9 4.9 %collective-permute-done.13 = f32[32,128]{1,0:T(8,128)S(1)} collective-permute-done((f32[32,128]{1,0:T(8,128)S(1)}, f32[32,128]{1,0:T(8,128)S(1)}, u32[]{:S(2)}, u32[]{:S(2)}) %collective-permute-start.13) | collective-permute-done | bytes 16416 | tf_op jit(solution)/shard_map/ppermute | solution.py:97
  65.8 3.7 %collective-permute-done.14 = f32[32,128]{1,0:T(8,128)S(1)} collective-permute-done((f32[32,128]{1,0:T(8,128)S(1)}, f32[32,128]{1,0:T(8,128)S(1)}, u32[]{:S(2)}, u32[]{:S(2)}) %collective-permute-start.14) | collective-permute-done | bytes 16416 | tf_op jit(solution)/shard_map/ppermute | solution.py:97
  69.6 4.9 %collective-permute-done.15 = f32[32,128]{1,0:T(8,128)S(1)} collective-permute-done((f32[32,128]{1,0:T(8,128)S(1)}, f32[32,128]{1,0:T(8,128)S(1)}, u32[]{:S(2)}, u32[]{:S(2)}) %collective-permute-start.15) | collective-permute-done | bytes 16416 | tf_op jit(solution)/shard_map/ppermute | solution.py:97
  75.2 6.8 %shard_map.41 = (f32[64,64]{1,0:T(8,128)}, f32[64,64]{1,0:T(8,128)}) custom-call(f32[64,64]{1,0:T(8,128)} %reshape.12.gram_ref), custom_call_target="tpu_custom_call" | custom-call | tf_op jit(solution)/shard_map/pallas_call | solution.py:68
  82.0 1.8 %fusion.51 = f32[64,4,8,128]{3,0,2,1:T(8,128)S(1)} fusion(f32[64,4,8,128]{3,0,2,1:T(8,128)S(1)} %fusion.9, f32[64,64]{1,0:T(8,128)} %get-tuple-element.4), kind=kOutput, calls=%fused_computation.81 | convolution fusion | flops 201330688 | bytes 2113536 | tf_op jit(solution)/shard_map/mk,kxyz->mxyz/dot_general | solution.py:117
  83.8 1.6 %copy.24 = f32[64,4,8,128]{3,2,1,0:T(8,128)} copy(f32[64,4,8,128]{3,0,2,1:T(8,128)S(1)} %fusion.51) | data formatting | bytes 2097152
  (46 shorter events, 7.9 us)
Async XLA Ops:
  0.6 1.7 %copy-start = (f32[64,4,8,128]{3,2,1,0:T(8,128)S(1)}, f32[64,4,8,128]{3,2,1,0:T(8,128)}, u32[]{:S(2)}) copy-start(f32[64,4,8,128]{3,2,1,0:T(8,128)} %param.2) | copy-start | bytes 3145732
  2.2 7.5 %copy-start.1 = (f32[4,8,128]{2,1,0:T(8,128)S(1)}, f32[4,8,128]{2,1,0:T(8,128)}, u32[]{:S(2)}) copy-start(f32[4,8,128]{2,1,0:T(8,128)} %param.3) | copy-start | bytes 49156
  2.2 12.0 %collective-permute-start.1 = (f32[64,2,8,128]{3,0,2,1:T(8,128)S(1)}, f32[64,2,8,128]{3,0,2,1:T(8,128)S(1)}, u32[]{:S(2)}, u32[]{:S(2)}) collective-permute-start(f32[64,2,8,128]{3,0,2,1:T(8,128)S(1)} %copy.28), channel_id=1, source_target_pairs={{0,8},{8,16},{16,24},{24,32},{32,40},{40,48},{48,56},{56,64},{64,7... | collective-permute-start | bytes 1572872 | tf_op jit(solution)/shard_map/ppermute | solution.py:14
  2.5 8.6 %collective-permute-start.3 = (f32[64,4,2,128]{3,0,2,1:T(8,128)S(1)}, f32[64,4,2,128]{3,0,2,1:T(8,128)S(1)}, u32[]{:S(2)}, u32[]{:S(2)}) collective-permute-start(f32[64,4,2,128]{3,0,2,1:T(8,128)S(1)} %copy.30), channel_id=1, source_target_pairs={{0,1},{1,2},{2,3},{3,4},{4,5},{5,6},{6,7},{7,0},{8,9},{9,10},{10,1... | collective-permute-start | bytes 786440 | tf_op jit(solution)/shard_map/ppermute | solution.py:14
  4.6 12.8 %collective-permute-start.2 = (f32[64,4,2,128]{3,0,2,1:T(8,128)S(1)}, f32[64,4,2,128]{3,0,2,1:T(8,128)S(1)}, u32[]{:S(2)}, u32[]{:S(2)}) collective-permute-start(f32[64,4,2,128]{3,0,2,1:T(8,128)S(1)} %copy.29), channel_id=1, source_target_pairs={{1,0},{2,1},{3,2},{4,3},{5,4},{6,5},{7,6},{0,7},{9,8},{10,9},{11,1... | collective-permute-start | bytes 786440 | tf_op jit(solution)/shard_map/ppermute | solution.py:15
  4.9 12.4 %collective-permute-start = (f32[64,2,8,128]{3,0,2,1:T(8,128)S(1)}, f32[64,2,8,128]{3,0,2,1:T(8,128)S(1)}, u32[]{:S(2)}, u32[]{:S(2)}) collective-permute-start(f32[64,2,8,128]{3,0,2,1:T(8,128)S(1)} %copy.27), channel_id=1, source_target_pairs={{8,0},{16,8},{24,16},{32,24},{40,32},{48,40},{56,48},{64,56},{72,6... | collective-permute-start | bytes 1572872 | tf_op jit(solution)/shard_map/ppermute | solution.py:15
  18.5 10.4 %collective-permute-start.6 = (f32[64,4,2,128]{3,0,2,1:T(8,128)S(1)}, f32[64,4,2,128]{3,0,2,1:T(8,128)S(1)}, u32[]{:S(2)}, u32[]{:S(2)}) collective-permute-start(f32[64,4,2,128]{3,0,2,1:T(8,128)S(1)} %get-tuple-element.14), channel_id=1, source_target_pairs={{1,0},{2,1},{3,2},{4,3},{5,4},{6,5},{7,6},{0,7},{9,8},{10,9},{11,1... | collective-permute-start | bytes 786440 | tf_op jit(solution)/shard_map/ppermute | solution.py:15
  21.7 7.3 %collective-permute-start.7 = (f32[64,4,2,128]{3,0,2,1:T(8,128)S(1)}, f32[64,4,2,128]{3,0,2,1:T(8,128)S(1)}, u32[]{:S(2)}, u32[]{:S(2)}) collective-permute-start(f32[64,4,2,128]{3,0,2,1:T(8,128)S(1)} %get-tuple-element.15), channel_id=1, source_target_pairs={{0,1},{1,2},{2,3},{3,4},{4,5},{5,6},{6,7},{7,0},{8,9},{9,10},{10,1... | collective-permute-start | bytes 786440 | tf_op jit(solution)/shard_map/ppermute | solution.py:14
  21.7 11.6 %collective-permute-start.4 = (f32[64,2,8,128]{3,0,2,1:T(8,128)S(1)}, f32[64,2,8,128]{3,0,2,1:T(8,128)S(1)}, u32[]{:S(2)}, u32[]{:S(2)}) collective-permute-start(f32[64,2,8,128]{3,0,2,1:T(8,128)S(1)} %get-tuple-element.12), channel_id=1, source_target_pairs={{8,0},{16,8},{24,16},{32,24},{40,32},{48,40},{56,48},{64,56},{72,6... | collective-permute-start | bytes 1572872 | tf_op jit(solution)/shard_map/ppermute | solution.py:15
  26.6 11.9 %collective-permute-start.5 = (f32[64,2,8,128]{3,0,2,1:T(8,128)S(1)}, f32[64,2,8,128]{3,0,2,1:T(8,128)S(1)}, u32[]{:S(2)}, u32[]{:S(2)}) collective-permute-start(f32[64,2,8,128]{3,0,2,1:T(8,128)S(1)} %get-tuple-element.13), channel_id=1, source_target_pairs={{0,8},{8,16},{16,24},{24,32},{32,40},{40,48},{48,56},{56,64},{64,7... | collective-permute-start | bytes 1572872 | tf_op jit(solution)/shard_map/ppermute | solution.py:14
  41.1 3.8 %collective-permute-start.8 = (f32[32,128]{1,0:T(8,128)S(1)}, f32[32,128]{1,0:T(8,128)S(1)}, u32[]{:S(2)}, u32[]{:S(2)}) collective-permute-start(f32[32,128]{1,0:T(8,128)S(1)} %reshape.11), channel_id=1, source_target_pairs={{0,1},{1,0},{2,3},{3,2},{4,5},{5,4},{6,7},{7,6},{8,9},{9,8},{10,11... | collective-permute-start | bytes 49160 | tf_op jit(solution)/shard_map/ppermute | solution.py:97
  44.9 5.2 %collective-permute-start.9 = (f32[32,128]{1,0:T(8,128)S(1)}, f32[32,128]{1,0:T(8,128)S(1)}, u32[]{:S(2)}, u32[]{:S(2)}) collective-permute-start(f32[32,128]{1,0:T(8,128)S(1)} %add.96), channel_id=1, source_target_pairs={{0,2},{1,3},{2,0},{3,1},{4,6},{5,7},{6,4},{7,5},{8,10},{9,11},{10,... | collective-permute-start | bytes 49160 | tf_op jit(solution)/shard_map/ppermute | solution.py:97
  50.1 5.8 %collective-permute-start.10 = (f32[32,128]{1,0:T(8,128)S(1)}, f32[32,128]{1,0:T(8,128)S(1)}, u32[]{:S(2)}, u32[]{:S(2)}) collective-permute-start(f32[32,128]{1,0:T(8,128)S(1)} %add.97), channel_id=1, source_target_pairs={{0,6},{1,7},{2,4},{3,5},{4,2},{5,3},{6,0},{7,1},{8,14},{9,15},{10,... | collective-permute-start | bytes 49160 | tf_op jit(solution)/shard_map/ppermute | solution.py:97
  55.9 1.2 %collective-permute-start.11 = (f32[32,128]{1,0:T(8,128)S(1)}, f32[32,128]{1,0:T(8,128)S(1)}, u32[]{:S(2)}, u32[]{:S(2)}) collective-permute-start(f32[32,128]{1,0:T(8,128)S(1)} %add.98), channel_id=1, source_target_pairs={{0,8},{8,0},{16,24},{24,16},{32,40},{40,32},{48,56},{56,48},{64,72... | collective-permute-start | bytes 49160 | tf_op jit(solution)/shard_map/ppermute | solution.py:97
  57.1 3.7 %collective-permute-start.12 = (f32[32,128]{1,0:T(8,128)S(1)}, f32[32,128]{1,0:T(8,128)S(1)}, u32[]{:S(2)}, u32[]{:S(2)}) collective-permute-start(f32[32,128]{1,0:T(8,128)S(1)} %add.99), channel_id=1, source_target_pairs={{0,16},{8,24},{16,0},{24,8},{32,48},{40,56},{48,32},{56,40},{64,80... | collective-permute-start | bytes 49160 | tf_op jit(solution)/shard_map/ppermute | solution.py:97
  60.9 4.9 %collective-permute-start.13 = (f32[32,128]{1,0:T(8,128)S(1)}, f32[32,128]{1,0:T(8,128)S(1)}, u32[]{:S(2)}, u32[]{:S(2)}) collective-permute-start(f32[32,128]{1,0:T(8,128)S(1)} %add.100), channel_id=1, source_target_pairs={{0,48},{8,56},{16,32},{24,40},{32,16},{40,24},{48,0},{56,8},{64,11... | collective-permute-start | bytes 49160 | tf_op jit(solution)/shard_map/ppermute | solution.py:97
  65.8 3.7 %collective-permute-start.14 = (f32[32,128]{1,0:T(8,128)S(1)}, f32[32,128]{1,0:T(8,128)S(1)}, u32[]{:S(2)}, u32[]{:S(2)}) collective-permute-start(f32[32,128]{1,0:T(8,128)S(1)} %add.101), channel_id=1, source_target_pairs={{0,64},{8,72},{16,80},{24,88},{32,96},{40,104},{48,112},{56,120},{... | collective-permute-start | bytes 49160 | tf_op jit(solution)/shard_map/ppermute | solution.py:97
  69.6 4.9 %collective-permute-start.15 = (f32[32,128]{1,0:T(8,128)S(1)}, f32[32,128]{1,0:T(8,128)S(1)}, u32[]{:S(2)}, u32[]{:S(2)}) collective-permute-start(f32[32,128]{1,0:T(8,128)S(1)} %add.102), channel_id=1, source_target_pairs={{0,192},{8,200},{16,208},{24,216},{32,224},{40,232},{48,240},{56,2... | collective-permute-start | bytes 49160 | tf_op jit(solution)/shard_map/ppermute | solution.py:97

commit v18 on v14

--- a/solution.py
+++ b/solution.py
@@ -25,10 +25,9 @@
         along_y = jnp.concatenate([along_y[:, :, :2], core, along_y[:, :, -2:]], axis=2)
     size = core.shape[3]
     along_z = jnp.concatenate([core[..., size - 2:], core, core[..., :2]], axis=3)
-    local = -7.5 * core
-    local = local + 4.0 / 3.0 * (along_z[..., 1:size + 1] + along_z[..., 3:size + 3])
+    local = 4.0 / 3.0 * (along_z[..., 1:size + 1] + along_z[..., 3:size + 3])
     local = local - 1.0 / 12.0 * (along_z[..., :size] + along_z[..., 4:])
-    total = lax.optimization_barrier(local)
+    total = lax.optimization_barrier(local) - 7.5 * core
     total = total + 4.0 / 3.0 * (along_x[:, 3:-1] + along_x[:, 1:-3])
     total = total - 1.0 / 12.0 * (along_x[:, 4:] + along_x[:, :-4])
     total = total + 4.0 / 3.0 * (along_y[:, :, 3:-1] + along_y[:, :, 1:-3])

time: 81.9 us -> 82 us (level)
  starting transfers between devices: 24.1 us -> 26 us
  waiting for transfers between devices: 34 us -> 32.5 us
    ppermute x4, waiting for transfers between devices: 8.97 us -> 6.23 us  [faces(): lax.ppermute(tail, axis, [(i, (i + 1) % count) for i in range(count)])]
    ppermute x8, starting transfers between devices: 8.87 us -> 10.2 us  [butterfly_sum(): lax.ppermute(value, axis, [(i, partner(i)) for i in range(count)])]
    ppermute x4, waiting for transfers between devices: 0.01 us -> 1 us  [faces(): lax.ppermute(head, axis, [((i + 1) % count, i) for i in range(count)])]
  transfers between devices with their start and end apart: 16 -> 16, of which waited for: 11 -> 12; matrix products, arithmetic and copies ran while one was open for 7% -> 7% of each run, Pallas kernels for 0% -> 0%
where the time goes in v18:
time: 82 us; the launch traced here: 81.7 us
  waiting for transfers between devices  32.5 us (40%)
  starting transfers between devices  26 us (32%)
  Pallas kernels  6.78 us (8%)
  other arithmetic  6.77 us (8%)
  local copies, waits for them, and re-layouts  6.09 us (7%)
  matrix products  2.77 us (3%)
  between operations  0.85 us (1%)
    ppermute x8, waiting for transfers between devices, butterfly_sum(): lax.ppermute(value, axis, [(i, partner(i)) for i in range(count)])  25.3 us
    ppermute x4, starting transfers between devices, faces(): lax.ppermute(head, axis, [((i + 1) % count, i) for i in range(count)])  11.6 us
    ppermute x8, starting transfers between devices, butterfly_sum(): lax.ppermute(value, axis, [(i, partner(i)) for i in range(count)])  10.2 us
    pallas_call x1, Pallas kernels, factor_and_inverse(): pl.pallas_call(factor_kernel, out_shape=(shape, shape), in_specs=[pl.Bloc...  6.78 us
    ppermute x4, waiting for transfers between devices, faces(): lax.ppermute(tail, axis, [(i, (i + 1) % count) for i in range(count)])  6.23 us
    ppermute x4, starting transfers between devices, faces(): lax.ppermute(tail, axis, [(i, (i + 1) % count) for i in range(count)])  4.16 us
    sub x2, other arithmetic, apply_ham(): local = local - 1.0 / 12.0 * (along_z[..., :size] + along_z[..., 4:])  3.92 us
    unnamed x11, local copies, waits for them, and re-layouts  2.1 us
  transfers between devices with their start and end apart: 16, of which 12 were waited for; matrix products, arithmetic and copies ran while one was open for 7% of the time, Pallas kernels for 0%

profile of v18, /device:TPU:32, one launch (start us, length us, event | category | flops | bytes accessed | tf_op | source)
XLA Modules:
  0.0 81.7 jit_solution(11052096371797843508)
XLA Ops:
  2.5 2.0 %collective-permute-start.3 = (f32[64,4,2,128]{3,0,2,1:T(8,128)S(1)}, f32[64,4,2,128]{3,0,2,1:T(8,128)S(1)}, u32[]{:S(2)}, u32[]{:S(2)}) collective-permute-start(f32[64,4,2,128]{3,0,2,1:T(8,128)S(1)} %copy.30), channel_id=1, source_target_pairs={{0,1},{1,2},{2,3},{3,4},{4,5},{5,6},{6,7},{7,0},{8,9},{9,10},{10,1... | collective-permute-start | bytes 786440 | tf_op jit(solution)/shard_map/ppermute | solution.py:14
  4.9 4.7 %collective-permute-start = (f32[64,2,8,128]{3,0,2,1:T(8,128)S(1)}, f32[64,2,8,128]{3,0,2,1:T(8,128)S(1)}, u32[]{:S(2)}, u32[]{:S(2)}) collective-permute-start(f32[64,2,8,128]{3,0,2,1:T(8,128)S(1)} %copy.27), channel_id=1, source_target_pairs={{8,0},{16,8},{24,16},{32,24},{40,32},{48,40},{56,48},{64,56},{72,6... | collective-permute-start | bytes 1572872 | tf_op jit(solution)/shard_map/ppermute | solution.py:15
  9.7 1.4 %collective-permute-done.3 = f32[64,4,2,128]{3,0,2,1:T(8,128)S(1)} collective-permute-done((f32[64,4,2,128]{3,0,2,1:T(8,128)S(1)}, f32[64,4,2,128]{3,0,2,1:T(8,128)S(1)}, u32[]{:S(2)}, u32[]{:S(2)}) %collective-permute-start.3) | collective-permute-done | bytes 262176 | tf_op jit(solution)/shard_map/ppermute | solution.py:14
  11.2 3.0 %collective-permute-done.1 = f32[64,2,8,128]{3,0,2,1:T(8,128)S(1)} collective-permute-done((f32[64,2,8,128]{3,0,2,1:T(8,128)S(1)}, f32[64,2,8,128]{3,0,2,1:T(8,128)S(1)}, u32[]{:S(2)}, u32[]{:S(2)}) %collective-permute-start.1) | collective-permute-done | bytes 524320 | tf_op jit(solution)/shard_map/ppermute | solution.py:14
  15.4 2.0 %fusion.26 = f32[64,4,8,128]{3,0,2,1:T(8,128)S(1)} fusion(f32[64,4,8,128]{3,0,2,1:T(8,128)S(1)} %get-tuple-element.20, f32[64,4,8,2]{3,0,2,1:T(8,128)S(1)} %get-tuple-element.19, f32[64,4,8,2]{3,0,2,1:T(8,128)S(1)} %get-tuple-element.18), kind=kLoop, calls=%fused_computation.43 | loop fusion | flops 2359296 | bytes 2129920 | tf_op jit(solution)/shard_map/sub | solution.py:29
  18.8 5.1 %collective-permute-start.4 = (f32[64,2,8,128]{3,0,2,1:T(8,128)S(1)}, f32[64,2,8,128]{3,0,2,1:T(8,128)S(1)}, u32[]{:S(2)}, u32[]{:S(2)}) collective-permute-start(f32[64,2,8,128]{3,0,2,1:T(8,128)S(1)} %get-tuple-element.14), channel_id=1, source_target_pairs={{8,0},{16,8},{24,16},{32,24},{40,32},{48,40},{56,48},{64,56},{72,6... | collective-permute-start | bytes 1572872 | tf_op jit(solution)/shard_map/ppermute | solution.py:15
  23.9 2.0 %collective-permute-start.7 = (f32[64,4,2,128]{3,0,2,1:T(8,128)S(1)}, f32[64,4,2,128]{3,0,2,1:T(8,128)S(1)}, u32[]{:S(2)}, u32[]{:S(2)}) collective-permute-start(f32[64,4,2,128]{3,0,2,1:T(8,128)S(1)} %get-tuple-element.17), channel_id=1, source_target_pairs={{0,1},{1,2},{2,3},{3,4},{4,5},{5,6},{6,7},{7,0},{8,9},{9,10},{10,1... | collective-permute-start | bytes 786440 | tf_op jit(solution)/shard_map/ppermute | solution.py:14
  25.9 1.6 %collective-permute-start.6 = (f32[64,4,2,128]{3,0,2,1:T(8,128)S(1)}, f32[64,4,2,128]{3,0,2,1:T(8,128)S(1)}, u32[]{:S(2)}, u32[]{:S(2)}) collective-permute-start(f32[64,4,2,128]{3,0,2,1:T(8,128)S(1)} %get-tuple-element.16), channel_id=1, source_target_pairs={{1,0},{2,1},{3,2},{4,3},{5,4},{6,5},{7,6},{0,7},{9,8},{10,9},{11,1... | collective-permute-start | bytes 786440 | tf_op jit(solution)/shard_map/ppermute | solution.py:15
  27.9 2.0 %fusion.21 = f32[64,4,8,128]{3,0,2,1:T(8,128)S(1)} fusion(f32[64,4,8,128]{3,0,2,1:T(8,128)S(1)} %get-tuple-element.10, f32[64,4,8,2]{3,0,2,1:T(8,128)S(1)} %get-tuple-element.13, f32[64,4,8,2]{3,0,2,1:T(8,128)S(1)} %get-tuple-element.12), kind=kLoop, calls=%fused_computation.38 | loop fusion | flops 2359296 | bytes 2129920 | tf_op jit(solution)/shard_map/sub | solution.py:29
  29.9 1.7 %collective-permute-done.7 = f32[64,4,2,128]{3,0,2,1:T(8,128)S(1)} collective-permute-done((f32[64,4,2,128]{3,0,2,1:T(8,128)S(1)}, f32[64,4,2,128]{3,0,2,1:T(8,128)S(1)}, u32[]{:S(2)}, u32[]{:S(2)}) %collective-permute-start.7) | collective-permute-done | bytes 262176 | tf_op jit(solution)/shard_map/ppermute | solution.py:14
  32.6 1.7 %fusion.10 = f32[64,4,8,128]{3,0,2,1:T(8,128)S(1)} fusion(f32[64,4,2,128]{3,0,2,1:T(8,128)S(1)} %collective-permute-done.7, f32[64,4,8,128]{3,0,2,1:T(8,128)S(1)} %get-tuple-element.10, f32[64,4,2,128]{3,0,2,1:T(8,128)S(1)} %collective-permute-done.6, f32[64,2,8,128]{3,0,2,1:T(8,128)S(1)} %collective-permute-done.5, ...), kind=kLoop, calls=%fused_computation.27 | loop fusion | flops 7602176 | bytes 6832128 | tf_op jit(solution)/shard_map/sub | solution.py:104
  35.3 2.3 %collective-permute-start.8 = (f32[32,128]{1,0:T(8,128)S(1)}, f32[32,128]{1,0:T(8,128)S(1)}, u32[]{:S(2)}, u32[]{:S(2)}) collective-permute-start(f32[32,128]{1,0:T(8,128)S(1)} %reshape.11), channel_id=1, source_target_pairs={{0,1},{1,0},{2,3},{3,2},{4,5},{5,4},{6,7},{7,6},{8,9},{9,8},{10,11... | collective-permute-start | bytes 49160 | tf_op jit(solution)/shard_map/ppermute | solution.py:96
  37.6 1.7 %collective-permute-done.8 = f32[32,128]{1,0:T(8,128)S(1)} collective-permute-done((f32[32,128]{1,0:T(8,128)S(1)}, f32[32,128]{1,0:T(8,128)S(1)}, u32[]{:S(2)}, u32[]{:S(2)}) %collective-permute-start.8) | collective-permute-done | bytes 16416 | tf_op jit(solution)/shard_map/ppermute | solution.py:96
  39.4 5.4 %collective-permute-start.9 = (f32[32,128]{1,0:T(8,128)S(1)}, f32[32,128]{1,0:T(8,128)S(1)}, u32[]{:S(2)}, u32[]{:S(2)}) collective-permute-start(f32[32,128]{1,0:T(8,128)S(1)} %add.96), channel_id=1, source_target_pairs={{0,2},{1,3},{2,0},{3,1},{4,6},{5,7},{6,4},{7,5},{8,10},{9,11},{10,... | collective-permute-start | bytes 49160 | tf_op jit(solution)/shard_map/ppermute | solution.py:96
  44.7 1.7 %collective-permute-done.9 = f32[32,128]{1,0:T(8,128)S(1)} collective-permute-done((f32[32,128]{1,0:T(8,128)S(1)}, f32[32,128]{1,0:T(8,128)S(1)}, u32[]{:S(2)}, u32[]{:S(2)}) %collective-permute-start.9) | collective-permute-done | bytes 16416 | tf_op jit(solution)/shard_map/ppermute | solution.py:96
  46.4 2.2 %collective-permute-start.10 = (f32[32,128]{1,0:T(8,128)S(1)}, f32[32,128]{1,0:T(8,128)S(1)}, u32[]{:S(2)}, u32[]{:S(2)}) collective-permute-start(f32[32,128]{1,0:T(8,128)S(1)} %add.97), channel_id=1, source_target_pairs={{0,6},{1,7},{2,4},{3,5},{4,2},{5,3},{6,0},{7,1},{8,14},{9,15},{10,... | collective-permute-start | bytes 49160 | tf_op jit(solution)/shard_map/ppermute | solution.py:96
  48.7 3.6 %collective-permute-done.10 = f32[32,128]{1,0:T(8,128)S(1)} collective-permute-done((f32[32,128]{1,0:T(8,128)S(1)}, f32[32,128]{1,0:T(8,128)S(1)}, u32[]{:S(2)}, u32[]{:S(2)}) %collective-permute-start.10) | collective-permute-done | bytes 16416 | tf_op jit(solution)/shard_map/ppermute | solution.py:96
  53.5 3.7 %collective-permute-done.12 = f32[32,128]{1,0:T(8,128)S(1)} collective-permute-done((f32[32,128]{1,0:T(8,128)S(1)}, f32[32,128]{1,0:T(8,128)S(1)}, u32[]{:S(2)}, u32[]{:S(2)}) %collective-permute-start.12) | collective-permute-done | bytes 16416 | tf_op jit(solution)/shard_map/ppermute | solution.py:96
  57.2 4.9 %collective-permute-done.13 = f32[32,128]{1,0:T(8,128)S(1)} collective-permute-done((f32[32,128]{1,0:T(8,128)S(1)}, f32[32,128]{1,0:T(8,128)S(1)}, u32[]{:S(2)}, u32[]{:S(2)}) %collective-permute-start.13) | collective-permute-done | bytes 16416 | tf_op jit(solution)/shard_map/ppermute | solution.py:96
  62.2 3.7 %collective-permute-done.14 = f32[32,128]{1,0:T(8,128)S(1)} collective-permute-done((f32[32,128]{1,0:T(8,128)S(1)}, f32[32,128]{1,0:T(8,128)S(1)}, u32[]{:S(2)}, u32[]{:S(2)}) %collective-permute-start.14) | collective-permute-done | bytes 16416 | tf_op jit(solution)/shard_map/ppermute | solution.py:96
  66.3 4.6 %collective-permute-done.15 = f32[32,128]{1,0:T(8,128)S(1)} collective-permute-done((f32[32,128]{1,0:T(8,128)S(1)}, f32[32,128]{1,0:T(8,128)S(1)}, u32[]{:S(2)}, u32[]{:S(2)}) %collective-permute-start.15) | collective-permute-done | bytes 16416 | tf_op jit(solution)/shard_map/ppermute | solution.py:96
  71.6 6.8 %shard_map.41 = (f32[64,64]{1,0:T(8,128)}, f32[64,64]{1,0:T(8,128)}) custom-call(f32[64,64]{1,0:T(8,128)} %reshape.12.gram_ref), custom_call_target="tpu_custom_call" | custom-call | tf_op jit(solution)/shard_map/pallas_call | solution.py:67
  78.4 1.8 %fusion.47 = f32[64,4,8,128]{3,0,2,1:T(8,128)S(1)} fusion(f32[64,4,8,128]{3,0,2,1:T(8,128)S(1)} %fusion.10, f32[64,64]{1,0:T(8,128)} %get-tuple-element.4), kind=kOutput, calls=%fused_computation.77 | convolution fusion | flops 201330688 | bytes 2113536 | tf_op jit(solution)/shard_map/mk,kxyz->mxyz/dot_general | solution.py:117
  80.2 1.6 %copy.24 = f32[64,4,8,128]{3,2,1,0:T(8,128)} copy(f32[64,4,8,128]{3,0,2,1:T(8,128)S(1)} %fusion.47) | data formatting | bytes 2097152
  (46 shorter events, 9.5 us)
Async XLA Ops:
  0.6 1.7 %copy-start = (f32[64,4,8,128]{3,2,1,0:T(8,128)S(1)}, f32[64,4,8,128]{3,2,1,0:T(8,128)}, u32[]{:S(2)}) copy-start(f32[64,4,8,128]{3,2,1,0:T(8,128)} %param.2) | copy-start | bytes 3145732
  2.2 7.5 %copy-start.1 = (f32[4,8,128]{2,1,0:T(8,128)S(1)}, f32[4,8,128]{2,1,0:T(8,128)}, u32[]{:S(2)}) copy-start(f32[4,8,128]{2,1,0:T(8,128)} %param.3) | copy-start | bytes 49156
  2.2 12.0 %collective-permute-start.1 = (f32[64,2,8,128]{3,0,2,1:T(8,128)S(1)}, f32[64,2,8,128]{3,0,2,1:T(8,128)S(1)}, u32[]{:S(2)}, u32[]{:S(2)}) collective-permute-start(f32[64,2,8,128]{3,0,2,1:T(8,128)S(1)} %copy.28), channel_id=1, source_target_pairs={{0,8},{8,16},{16,24},{24,32},{32,40},{40,48},{48,56},{56,64},{64,7... | collective-permute-start | bytes 1572872 | tf_op jit(solution)/shard_map/ppermute | solution.py:14
  2.5 8.6 %collective-permute-start.3 = (f32[64,4,2,128]{3,0,2,1:T(8,128)S(1)}, f32[64,4,2,128]{3,0,2,1:T(8,128)S(1)}, u32[]{:S(2)}, u32[]{:S(2)}) collective-permute-start(f32[64,4,2,128]{3,0,2,1:T(8,128)S(1)} %copy.30), channel_id=1, source_target_pairs={{0,1},{1,2},{2,3},{3,4},{4,5},{5,6},{6,7},{7,0},{8,9},{9,10},{10,1... | collective-permute-start | bytes 786440 | tf_op jit(solution)/shard_map/ppermute | solution.py:14
  4.6 12.8 %collective-permute-start.2 = (f32[64,4,2,128]{3,0,2,1:T(8,128)S(1)}, f32[64,4,2,128]{3,0,2,1:T(8,128)S(1)}, u32[]{:S(2)}, u32[]{:S(2)}) collective-permute-start(f32[64,4,2,128]{3,0,2,1:T(8,128)S(1)} %copy.29), channel_id=1, source_target_pairs={{1,0},{2,1},{3,2},{4,3},{5,4},{6,5},{7,6},{0,7},{9,8},{10,9},{11,1... | collective-permute-start | bytes 786440 | tf_op jit(solution)/shard_map/ppermute | solution.py:15
  4.9 12.5 %collective-permute-start = (f32[64,2,8,128]{3,0,2,1:T(8,128)S(1)}, f32[64,2,8,128]{3,0,2,1:T(8,128)S(1)}, u32[]{:S(2)}, u32[]{:S(2)}) collective-permute-start(f32[64,2,8,128]{3,0,2,1:T(8,128)S(1)} %copy.27), channel_id=1, source_target_pairs={{8,0},{16,8},{24,16},{32,24},{40,32},{48,40},{56,48},{64,56},{72,6... | collective-permute-start | bytes 1572872 | tf_op jit(solution)/shard_map/ppermute | solution.py:15
  18.7 13.9 %collective-permute-start.5 = (f32[64,2,8,128]{3,0,2,1:T(8,128)S(1)}, f32[64,2,8,128]{3,0,2,1:T(8,128)S(1)}, u32[]{:S(2)}, u32[]{:S(2)}) collective-permute-start(f32[64,2,8,128]{3,0,2,1:T(8,128)S(1)} %get-tuple-element.15), channel_id=1, source_target_pairs={{0,8},{8,16},{16,24},{24,32},{32,40},{40,48},{48,56},{56,64},{64,7... | collective-permute-start | bytes 1572872 | tf_op jit(solution)/shard_map/ppermute | solution.py:14
  18.8 13.8 %collective-permute-start.4 = (f32[64,2,8,128]{3,0,2,1:T(8,128)S(1)}, f32[64,2,8,128]{3,0,2,1:T(8,128)S(1)}, u32[]{:S(2)}, u32[]{:S(2)}) collective-permute-start(f32[64,2,8,128]{3,0,2,1:T(8,128)S(1)} %get-tuple-element.14), channel_id=1, source_target_pairs={{8,0},{16,8},{24,16},{32,24},{40,32},{48,40},{56,48},{64,56},{72,6... | collective-permute-start | bytes 1572872 | tf_op jit(solution)/shard_map/ppermute | solution.py:15
  23.9 7.7 %collective-permute-start.7 = (f32[64,4,2,128]{3,0,2,1:T(8,128)S(1)}, f32[64,4,2,128]{3,0,2,1:T(8,128)S(1)}, u32[]{:S(2)}, u32[]{:S(2)}) collective-permute-start(f32[64,4,2,128]{3,0,2,1:T(8,128)S(1)} %get-tuple-element.17), channel_id=1, source_target_pairs={{0,1},{1,2},{2,3},{3,4},{4,5},{5,6},{6,7},{7,0},{8,9},{9,10},{10,1... | collective-permute-start | bytes 786440 | tf_op jit(solution)/shard_map/ppermute | solution.py:14
  25.9 6.7 %collective-permute-start.6 = (f32[64,4,2,128]{3,0,2,1:T(8,128)S(1)}, f32[64,4,2,128]{3,0,2,1:T(8,128)S(1)}, u32[]{:S(2)}, u32[]{:S(2)}) collective-permute-start(f32[64,4,2,128]{3,0,2,1:T(8,128)S(1)} %get-tuple-element.16), channel_id=1, source_target_pairs={{1,0},{2,1},{3,2},{4,3},{5,4},{6,5},{7,6},{0,7},{9,8},{10,9},{11,1... | collective-permute-start | bytes 786440 | tf_op jit(solution)/shard_map/ppermute | solution.py:15
  35.3 4.0 %collective-permute-start.8 = (f32[32,128]{1,0:T(8,128)S(1)}, f32[32,128]{1,0:T(8,128)S(1)}, u32[]{:S(2)}, u32[]{:S(2)}) collective-permute-start(f32[32,128]{1,0:T(8,128)S(1)} %reshape.11), channel_id=1, source_target_pairs={{0,1},{1,0},{2,3},{3,2},{4,5},{5,4},{6,7},{7,6},{8,9},{9,8},{10,11... | collective-permute-start | bytes 49160 | tf_op jit(solution)/shard_map/ppermute | solution.py:96
  39.4 7.1 %collective-permute-start.9 = (f32[32,128]{1,0:T(8,128)S(1)}, f32[32,128]{1,0:T(8,128)S(1)}, u32[]{:S(2)}, u32[]{:S(2)}) collective-permute-start(f32[32,128]{1,0:T(8,128)S(1)} %add.96), channel_id=1, source_target_pairs={{0,2},{1,3},{2,0},{3,1},{4,6},{5,7},{6,4},{7,5},{8,10},{9,11},{10,... | collective-permute-start | bytes 49160 | tf_op jit(solution)/shard_map/ppermute | solution.py:96
  46.4 5.8 %collective-permute-start.10 = (f32[32,128]{1,0:T(8,128)S(1)}, f32[32,128]{1,0:T(8,128)S(1)}, u32[]{:S(2)}, u32[]{:S(2)}) collective-permute-start(f32[32,128]{1,0:T(8,128)S(1)} %add.97), channel_id=1, source_target_pairs={{0,6},{1,7},{2,4},{3,5},{4,2},{5,3},{6,0},{7,1},{8,14},{9,15},{10,... | collective-permute-start | bytes 49160 | tf_op jit(solution)/shard_map/ppermute | solution.py:96
  52.3 1.2 %collective-permute-start.11 = (f32[32,128]{1,0:T(8,128)S(1)}, f32[32,128]{1,0:T(8,128)S(1)}, u32[]{:S(2)}, u32[]{:S(2)}) collective-permute-start(f32[32,128]{1,0:T(8,128)S(1)} %add.98), channel_id=1, source_target_pairs={{0,8},{8,0},{16,24},{24,16},{32,40},{40,32},{48,56},{56,48},{64,72... | collective-permute-start | bytes 49160 | tf_op jit(solution)/shard_map/ppermute | solution.py:96
  53.5 3.7 %collective-permute-start.12 = (f32[32,128]{1,0:T(8,128)S(1)}, f32[32,128]{1,0:T(8,128)S(1)}, u32[]{:S(2)}, u32[]{:S(2)}) collective-permute-start(f32[32,128]{1,0:T(8,128)S(1)} %add.99), channel_id=1, source_target_pairs={{0,16},{8,24},{16,0},{24,8},{32,48},{40,56},{48,32},{56,40},{64,80... | collective-permute-start | bytes 49160 | tf_op jit(solution)/shard_map/ppermute | solution.py:96
  57.2 4.9 %collective-permute-start.13 = (f32[32,128]{1,0:T(8,128)S(1)}, f32[32,128]{1,0:T(8,128)S(1)}, u32[]{:S(2)}, u32[]{:S(2)}) collective-permute-start(f32[32,128]{1,0:T(8,128)S(1)} %add.100), channel_id=1, source_target_pairs={{0,48},{8,56},{16,32},{24,40},{32,16},{40,24},{48,0},{56,8},{64,11... | collective-permute-start | bytes 49160 | tf_op jit(solution)/shard_map/ppermute | solution.py:96
  62.2 3.7 %collective-permute-start.14 = (f32[32,128]{1,0:T(8,128)S(1)}, f32[32,128]{1,0:T(8,128)S(1)}, u32[]{:S(2)}, u32[]{:S(2)}) collective-permute-start(f32[32,128]{1,0:T(8,128)S(1)} %add.101), channel_id=1, source_target_pairs={{0,64},{8,72},{16,80},{24,88},{32,96},{40,104},{48,112},{56,120},{... | collective-permute-start | bytes 49160 | tf_op jit(solution)/shard_map/ppermute | solution.py:96
  65.9 4.9 %collective-permute-start.15 = (f32[32,128]{1,0:T(8,128)S(1)}, f32[32,128]{1,0:T(8,128)S(1)}, u32[]{:S(2)}, u32[]{:S(2)}) collective-permute-start(f32[32,128]{1,0:T(8,128)S(1)} %add.102), channel_id=1, source_target_pairs={{0,192},{8,200},{16,208},{24,216},{32,224},{40,232},{48,240},{56,2... | collective-permute-start | bytes 49160 | tf_op jit(solution)/shard_map/ppermute | solution.py:96
